TPU v7x, 32 devices: a whole 2x2x4 slice. The times are simulated.
32 devices in a mesh: box: 8 (over z, y), rep: 4 (over x, core).
Axes of the slice: x: 2, y: 2, z: 4, core: 2. Of those that a mesh axis runs over, the one named last changes fastest.
Arguments:
- targets: float32 [128, 256], P('box'), may hold values from -6 to 6
- noise_var: float32 [128, 256], P('box'), may hold values from 1 to 4
- near_tiles: bfloat16 [128, 8, 256, 256], P('box', 'rep'), may hold values from -1 to 1
- near_partners: int32 [128, 8], P('box', 'rep'), may hold values from -1 to 127, as said below
- leaf_bases: bfloat16 [128, 64, 256], P('box'), may hold values from -0.375 to 0.375
- transfer: bfloat16 [128, 64, 64], P('box'), may hold values from -0.375 to 0.375
- parents: int32 [128], P('box'), may hold values from 0 to 31, as said below
- coupling: bfloat16 [160, 16, 64, 64], P('box', 'rep'), may hold values from -0.109375 to 0.109375
- coupling_partners: int32 [160, 16], P('box', 'rep'), may hold values from -1 to 159, as said below
Outputs:
- weights: float32 [128, 256], P('box')
- residual: float32 [128, 256], P('box')
Inputs may be any that keep to these rules, and one draw needn't show every extreme that they name: `near_partners`: the first slot of each box's row is the box itself; every other entry is -1 or a box at most 16 boxes after the row's box. `coupling_partners`: each entry is -1 or a node of the same level as the row's node (leaf box or parent) with a higher number. The parents of the boxes of one index of box are that index's 4 parents. Along those boxes the parent number never decreases, so each parent's children are one contiguous run of one box or more.
All inputs are finite; a program needn't handle non-finite values.
Results may differ from a plain program's by a relative error of at most 0.006.
Values may be sent and summed in bfloat16 or wider, within the bound.
No kernel may reach another device: no remote copies, remote signals or barrier semaphores. Data moves between devices by JAX's collectives and lax.ppermute only.
A program may use at most 64 MiB of HBM per device.

v0:
```python
import jax
import jax.numpy as jnp
from jax import lax
from jax.sharding import PartitionSpec as P

ITERS = 2


def shifted(shard, axis, by):
    devices = lax.axis_size(axis)
    pairs = [(i, i + by) for i in range(devices) if 0 <= i + by < devices]
    return lax.ppermute(shard, axis, pairs)


def local(
    targets,
    noise_var,
    near_tiles,
    near_partners,
    leaf_bases,
    transfer,
    parents,
    coupling,
    coupling_partners,
):
    box_count = targets.shape[0]
    node_count = coupling.shape[0]
    group_count = node_count - box_count
    rank_width = coupling.shape[2]
    box_rank = lax.axis_index("box")
    all_nodes = lax.axis_size("box") * node_count
    near_valid = near_partners >= 0
    near_local = jnp.where(near_valid, near_partners - box_rank * box_count, 0)
    near_onehot = (
        (jnp.arange(2 * box_count, dtype=jnp.int32)[:, None] == near_local.reshape(1, -1))
        & near_valid.reshape(1, -1)
    ).astype(jnp.float32)
    parent_local = parents - box_rank * group_count
    parent_onehot = (
        jnp.arange(group_count, dtype=jnp.int32)[:, None] == parent_local[None, :]
    ).astype(jnp.float32)
    far_valid = coupling_partners >= 0
    far_index = jnp.where(far_valid, coupling_partners, 0)
    bf_zero = jnp.zeros((), jnp.bfloat16)

    def squares(vector):
        return lax.psum(jnp.sum(vector * vector), "box")

    weights = jnp.zeros_like(targets)
    residual = targets
    direction = targets
    norm_now = squares(residual)
    for iteration in range(ITERS):
        rounded = direction.astype(jnp.bfloat16)
        following = shifted(rounded, "box", -1)
        extended = jnp.concatenate([rounded, following], axis=0)
        near_in = jnp.where(near_valid[:, :, None], extended[near_local], bf_zero)
        forward = jnp.einsum(
            "bsij,bsj->bi", near_tiles, near_in, preferred_element_type=jnp.float32
        )
        mirrored = jnp.einsum(
            "bsij,bi->bsj", near_tiles, rounded, preferred_element_type=jnp.float32
        )
        landed = jnp.dot(
            near_onehot, mirrored.reshape(-1, mirrored.shape[2]), precision=lax.Precision.HIGHEST
        )
        arrived = shifted(landed[box_count:], "box", 1)
        near_part = forward + landed[:box_count] + arrived
        leaf_coef = jnp.einsum(
            "brl,bl->br", leaf_bases, rounded, preferred_element_type=jnp.float32
        ).astype(jnp.bfloat16)
        upward = jnp.einsum("brq,br->bq", transfer, leaf_coef, preferred_element_type=jnp.float32)
        group_coef = jnp.dot(parent_onehot, upward, precision=lax.Precision.HIGHEST).astype(
            jnp.bfloat16
        )
        node_coef = jnp.concatenate([leaf_coef, group_coef], axis=0)
        every_coef = lax.all_gather(node_coef, "box", axis=0, tiled=True)
        partner_coef = jnp.where(far_valid[:, :, None], every_coef[far_index], bf_zero)
        far_forward = jnp.einsum(
            "nsab,nsb->na", coupling, partner_coef, preferred_element_type=jnp.float32
        )
        far_mirror = jnp.einsum(
            "nsab,na->nsb", coupling, node_coef, preferred_element_type=jnp.float32
        )
        far_mirror = far_mirror * far_valid[:, :, None].astype(jnp.float32)
        spread = (
            jnp.zeros((all_nodes, rank_width), jnp.float32)
            .at[far_index.reshape(-1)]
            .add(far_mirror.reshape(-1, rank_width))
        )
        node_sums = lax.psum_scatter(spread, "box", scatter_dimension=0, tiled=True)
        near_total, far_total = lax.psum((near_part, node_sums + far_forward), "rep")
        group_out = far_total[box_count:].astype(jnp.bfloat16)
        from_parent = jnp.einsum(
            "brq,bq->br", transfer, group_out[parent_local], preferred_element_type=jnp.float32
        )
        downward = (far_total[:box_count] + from_parent).astype(jnp.bfloat16)
        far_field = jnp.einsum(
            "brl,br->bl", leaf_bases, downward, preferred_element_type=jnp.float32
        )
        image_vec = noise_var * direction + near_total + far_field
        step_size = norm_now / lax.psum(jnp.sum(direction * image_vec), "box")
        weights = weights + step_size * direction
        residual = residual - step_size * image_vec
        norm_next = squares(residual)
        direction = residual + norm_next / norm_now * direction
        norm_now = norm_next
    return (weights, residual)


def solution(mesh):
    placed = (
        P("box", None),
        P("box", None),
        P("box", "rep", None, None),
        P("box", "rep"),
        P("box", None, None),
        P("box", None, None),
        P("box"),
        P("box", "rep", None, None),
        P("box", "rep"),
    )
    return jax.shard_map(
        local,
        mesh=mesh,
        in_specs=placed,
        out_specs=(P("box", None), P("box", None)),
        check_vma=False,
    )
```

profile of v0, /device:TPU:0, one launch (start us, length us, event | category | flops | bytes accessed | tf_op | source)
XLA Modules:
  0.0 256.1 jit_solution(12259696300122468750)
XLA Ops:
  0.7 0.9 convert_bitcast_fusion.1
  1.6 2.8 %fusion.22 = f32[16,1,2,256]{3,1,2,0:T(1,128)S(1)} fusion(bf16[16,2,256,256]{3,2,1,0:T(8,128)(2,1)} %param.11, bf16[16,256,1,1]{1,0,2,3:T(8,128)(2,1)S(1)} %convert_bitcast_fusion.1), kind=kOutput, calls=%fused_computation.46 | convolution fusion | flops 4194304 | bytes 4235264 | tf_op jit(solution)/shard_map/bsij,bi->bsj/dot_general | solution.py:61
  5.1 4.9 %collective-permute-start.1 = (f32[16,256]{1,0:T(8,128)S(1)}, f32[16,256]{1,0:T(8,128)S(1)}, u32[]{:S(2)}, u32[]{:S(2)}) collective-permute-start(f32[16,256]{1,0:T(8,128)S(1)} %slice.47), channel_id=1, source_target_pairs={{0,4},{4,8},{8,12},{12,16},{16,20},{20,24},{24,28},{1,5},{5,9},{9,... | collective-permute-start | bytes 49160 | tf_op jit(solution)/shard_map/ppermute | solution.py:12
  10.0 1.3 collective-permute-start
  12.7 0.9 scatter_custom_fusion
  13.6 39.5 %all-reduce = f32[160,64]{1,0:T(8,128)S(1)} all-reduce(f32[160,64]{1,0:T(8,128)S(1)} %scatter_custom_fusion), channel_id=2, replica_groups=mesh['box'=8,'rep'=4] {'box'}, use_global_device_ids=true, to_apply=%region_4.5.clone | all-reduce | flops 10240 | bytes 81920
  53.1 30.7 %all-gather = bf16[8,20,64]{2,1,0:T(8,128)(2,1)S(1)} all-gather(bf16[1,20,64]{2,1,0:T(8,128)(2,1)S(1)} %get-tuple-element.23), channel_id=1, replica_groups=mesh['box'=8,'rep'=4] {'box'}, dimensions={0}, use_global_device_ids=true | all-gather | bytes 23040 | tf_op jit(solution)/shard_map/all_gather | solution.py:77
  84.0 0.7 gather_fusion.1
  86.7 0.6 gather_fusion
  87.5 3.4 %fusion.10 = f32[16,1,256,1]{2,1,3,0:T(1,128)S(1)} fusion(bf16[16,2,256,256]{3,2,1,0:T(8,128)(2,1)} %param.11, bf16[16,2,256,1]{2,1,0,3:T(2,128)(2,1)S(1)} %fusion.12), kind=kOutput, calls=%fused_computation.22 | convolution fusion | flops 4194304 | bytes 4227072 | tf_op jit(solution)/shard_map/bsij,bsj->bi/dot_general | solution.py:58
  90.9 10.3 %all-reduce.4 = (f32[20,64]{1,0:T(8,128)S(1)}, f32[16,256]{1,0:T(8,128)S(1)}) all-reduce(f32[20,64]{1,0:T(8,128)S(1)} %dynamic-slice_add_fusion.1, f32[16,256]{1,0:T(8,128)S(1)} %fusion.15), channel_id=1, replica_groups=mesh['box'=8,'rep'=4] {'rep'}, use_global_device_ids=true, to_apply=%region_5.6 | all-reduce | flops 5376 | bytes 43008 | tf_op jit(solution)/shard_map/psum | solution.py:92
  102.8 17.8 %all-reduce.2 = (f32[]{:T(128)}, f32[]{:T(128)}) all-reduce(f32[]{:T(128)} %get-tuple-element.3, f32[]{:T(128)} %get-tuple-element.2), channel_id=1, replica_groups=mesh['box'=8,'rep'=4] {'box'}, use_global_device_ids=true, to_apply=%region_1.2 | all-reduce | flops 2 | bytes 16 | tf_op jit(solution)/shard_map/psum | solution.py:47
  122.5 19.7 %psum.60 = f32[]{:T(128)} all-reduce(f32[]{:T(128)} %get-tuple-element.10), channel_id=1, replica_groups=mesh['box'=8,'rep'=4] {'box'}, use_global_device_ids=true, to_apply=%region_9.10 | all-reduce | flops 1 | bytes 8 | tf_op jit(solution)/shard_map/psum | solution.py:47
  143.8 1.3 collective-permute-start.2
  145.9 0.9 scatter_custom_fusion.1
  146.7 36.5 %all-reduce.1 = f32[160,64]{1,0:T(8,128)S(1)} all-reduce(f32[160,64]{1,0:T(8,128)S(1)} %scatter_custom_fusion.1), channel_id=3, replica_groups=mesh['box'=8,'rep'=4] {'box'}, use_global_device_ids=true, to_apply=%region_12.13.clone | all-reduce | flops 10240 | bytes 81920
  183.2 30.7 %all-gather.1 = bf16[8,20,64]{2,1,0:T(8,128)(2,1)S(1)} all-gather(bf16[1,20,64]{2,1,0:T(8,128)(2,1)S(1)} %get-tuple-element.21), channel_id=1, replica_groups=mesh['box'=8,'rep'=4] {'box'}, dimensions={0}, use_global_device_ids=true | all-gather | bytes 23040 | tf_op jit(solution)/shard_map/all_gather | solution.py:77
  213.9 0.7 gather_fusion.4
  215.1 2.9 %fusion.18 = f32[16,1,2,256]{3,1,2,0:T(1,128)S(1)} fusion(bf16[16,2,256,256]{3,2,1,0:T(8,128)(2,1)} %param.11, bf16[16,256,1,1]{1,0,2,3:T(8,128)(2,1)S(1)} %bitcast.105), kind=kOutput, calls=%fused_computation.42 | convolution fusion | flops 4194304 | bytes 4235264 | tf_op jit(solution)/shard_map/bsij,bi->bsj/dot_general | solution.py:61
  218.1 1.3 collective-permute-start.3
  219.5 0.6 gather_fusion.3
  220.2 3.4 %fusion.8 = f32[16,1,256,1]{2,1,3,0:T(1,128)S(1)} fusion(bf16[16,2,256,256]{3,2,1,0:T(8,128)(2,1)} %param.11, bf16[16,2,256,1]{2,1,0,3:T(2,128)(2,1)S(1)} %fusion.13), kind=kOutput, calls=%fused_computation.19 | convolution fusion | flops 4194304 | bytes 4227072 | tf_op jit(solution)/shard_map/bsij,bsj->bi/dot_general | solution.py:58
  223.6 10.3 %all-reduce.3 = (f32[20,64]{1,0:T(8,128)S(1)}, f32[16,256]{1,0:T(8,128)S(1)}) all-reduce(f32[20,64]{1,0:T(8,128)S(1)} %dynamic-slice_add_fusion, f32[16,256]{1,0:T(8,128)S(1)} %fusion.14), channel_id=1, replica_groups=mesh['box'=8,'rep'=4] {'rep'}, use_global_device_ids=true, to_apply=%region_13.14 | all-reduce | flops 5376 | bytes 43008 | tf_op jit(solution)/shard_map/psum | solution.py:92
  235.6 18.6 %psum.63 = f32[]{:T(128)} all-reduce(f32[]{:T(128)} %multiply_reduce_fusion), channel_id=1, replica_groups=mesh['box'=8,'rep'=4] {'box'}, use_global_device_ids=true, to_apply=%region_15.16 | all-reduce | flops 1 | bytes 8 | tf_op jit(solution)/shard_map/psum | solution.py:102
  (101 shorter events, 10.0 us)
Async XLA Ops:
  0.6 11.7 %copy-start = (bf16[20,4,64,64]{3,2,1,0:T(8,128)(2,1)S(1)}, bf16[20,4,64,64]{3,2,1,0:T(8,128)(2,1)}, u32[]{:S(2)}) copy-start(bf16[20,4,64,64]{3,2,1,0:T(8,128)(2,1)} %param.16) | copy-start | bytes 1966084
  0.6 9.3 %copy-start.2 = (f32[16,256]{1,0:T(8,128)S(1)}, f32[16,256]{1,0:T(8,128)}, u32[]{:S(2)}) copy-start(f32[16,256]{1,0:T(8,128)} %param.9) | copy-start | bytes 49156
  0.7 3.8 %copy-start.5 = (s32[16,2]{0,1:T(2,128)S(1)}, s32[16,2]{0,1:T(2,128)}, u32[]{:S(2)}) copy-start(s32[16,2]{0,1:T(2,128)} %param.12) | copy-start | bytes 388
  0.7 10.6 %copy-start.1 = (bf16[16,64,256]{2,1,0:T(8,128)(2,1)S(1)}, bf16[16,64,256]{2,1,0:T(8,128)(2,1)}, u32[]{:S(2)}) copy-start(bf16[16,64,256]{2,1,0:T(8,128)(2,1)} %param.13) | copy-start | bytes 1572868
  0.7 10.9 %copy-start.4 = (s32[20,4]{0,1:T(4,128)S(1)}, s32[20,4]{0,1:T(4,128)}, u32[]{:S(2)}) copy-start(s32[20,4]{0,1:T(4,128)} %param.17) | copy-start | bytes 964
  0.7 11.3 %copy-start.7 = (bf16[16,64,64]{2,1,0:T(8,128)(2,1)S(1)}, bf16[16,64,64]{2,1,0:T(8,128)(2,1)}, u32[]{:S(2)}) copy-start(bf16[16,64,64]{2,1,0:T(8,128)(2,1)} %param.14) | copy-start | bytes 393220
  0.7 11.5 %copy-start.6 = (s32[16]{0:T(128)S(1)}, s32[16]{0:T(128)}, u32[]{:S(2)}) copy-start(s32[16]{0:T(128)} %param.15) | copy-start | bytes 196
  1.6 83.9 %copy-start.8 = (u32[32]{0:T(128)S(1)}, u32[32]{0:T(128)}, u32[]{:S(2)}) copy-start(u32[32]{0:T(128)} %constant.33) | copy-start | bytes 388
  5.1 85.8 %collective-permute-start.1 = (f32[16,256]{1,0:T(8,128)S(1)}, f32[16,256]{1,0:T(8,128)S(1)}, u32[]{:S(2)}, u32[]{:S(2)}) collective-permute-start(f32[16,256]{1,0:T(8,128)S(1)} %slice.47), channel_id=1, source_target_pairs={{0,4},{4,8},{8,12},{12,16},{16,20},{20,24},{24,28},{1,5},{5,9},{9,... | collective-permute-start | bytes 49160 | tf_op jit(solution)/shard_map/ppermute | solution.py:12
  10.0 76.7 %collective-permute-start = (bf16[16,256]{1,0:T(8,128)(2,1)S(1)}, bf16[16,256]{1,0:T(8,128)(2,1)S(1)}, u32[]{:S(2)}, u32[]{:S(2)}) collective-permute-start(bf16[16,256]{1,0:T(8,128)(2,1)S(1)} %convert_element_type.33), channel_id=1, source_target_pairs={{4,0},{8,4},{12,8},{16,12},{20,16},{24,20},{28,24},{5,1},{9,5},{13... | collective-permute-start | bytes 24584 | tf_op jit(solution)/shard_map/ppermute | solution.py:12
  12.6 89.6 %copy-start.3 = (f32[16,256]{1,0:T(8,128)S(1)}, f32[16,256]{1,0:T(8,128)}, u32[]{:S(2)}) copy-start(f32[16,256]{1,0:T(8,128)} %param.10) | copy-start | bytes 49156
  143.8 75.6 %collective-permute-start.2 = (bf16[16,256]{1,0:T(8,128)(2,1)S(1)}, bf16[16,256]{1,0:T(8,128)(2,1)S(1)}, u32[]{:S(2)}, u32[]{:S(2)}) collective-permute-start(bf16[16,256]{1,0:T(8,128)(2,1)S(1)} %fusion.57), channel_id=1, source_target_pairs={{4,0},{8,4},{12,8},{16,12},{20,16},{24,20},{28,24},{5,1},{9,5},{13... | collective-permute-start | bytes 24584 | tf_op jit(solution)/shard_map/ppermute | solution.py:12
  218.1 5.5 %collective-permute-start.3 = (f32[16,256]{1,0:T(8,128)S(1)}, f32[16,256]{1,0:T(8,128)S(1)}, u32[]{:S(2)}, u32[]{:S(2)}) collective-permute-start(f32[16,256]{1,0:T(8,128)S(1)} %slice.51), channel_id=1, source_target_pairs={{0,4},{4,8},{8,12},{12,16},{16,20},{20,24},{24,28},{1,5},{5,9},{9,... | collective-permute-start | bytes 49160 | tf_op jit(solution)/shard_map/ppermute | solution.py:12
where the time goes:
time: 257 us; the launch traced here: 256 us
  blocking collectives  214 us (83%)
  matrix products  16.1 us (6%)
  starting transfers between devices  8.75 us (3%)
  between operations  5.83 us (2%)
  other arithmetic  5.79 us (2%)
  local copies, waits for them, and re-layouts  5.68 us (2%)
    unnamed x2, blocking collectives  76 us
    all_gather x2, blocking collectives, local(): every_coef = lax.all_gather(node_coef, 'box', axis=0, tiled=True)  61.3 us
    psum x2, blocking collectives, squares(): return lax.psum(jnp.sum(vector * vector), 'box')  37.5 us
    psum x2, blocking collectives, local(): lax.psum((near_part, node_sums + far_forward), 'rep')  20.6 us
    psum x1, blocking collectives, local(): step_size = norm_now / lax.psum(jnp.sum(direction * image_vec), 'box')  18.6 us
    ppermute x4, starting transfers between devices, shifted(): return lax.ppermute(shard, axis, pairs)  8.75 us
    dot_general x2, matrix products, local(): jnp.einsum('bsij,bsj->bi', near_tiles, near_in, preferred_element_type=jn...  6.73 us
    dot_general x2, matrix products, local(): jnp.einsum('bsij,bi->bsj', near_tiles, rounded, preferred_element_type=jn...  5.7 us
  transfers between devices with their start and end apart: 4, of which 0 were waited for; matrix products, arithmetic and copies ran while one was open for 7% of the time, Pallas kernels for 0%

commit v1 on v0

v1 whole, which is shorter than its diff:
```python
import jax
import jax.numpy as jnp
from jax import lax
from jax.sharding import PartitionSpec as P

ITERS = 2


def rep_sum(vector):
    count = lax.axis_size("rep")
    me = lax.axis_index("rep")
    pieces = [vector]
    for shift in range(1, count):
        pairs = [(i, (i + shift) % count) for i in range(count)]
        pieces.append(lax.ppermute(vector, "rep", pairs))
    stacked = jnp.stack(pieces)
    order = (me - jnp.arange(count)) % count
    ordered = stacked[order]
    total = ordered[0]
    for i in range(1, count):
        total = total + ordered[i]
    return total


def box_sum(values):
    count = lax.axis_size("box")
    sent = jnp.broadcast_to(values[None, :], (count, values.shape[0]))
    got = lax.all_to_all(sent, "box", 0, 0, tiled=True)
    total = got[0]
    for i in range(1, count):
        total = total + got[i]
    return total


def local(
    targets,
    noise_var,
    near_tiles,
    near_partners,
    leaf_bases,
    transfer,
    parents,
    coupling,
    coupling_partners,
):
    box_count, leaf = targets.shape
    node_count = coupling.shape[0]
    group_count = node_count - box_count
    rank_width = coupling.shape[2]
    box_devices = lax.axis_size("box")
    box_rank = lax.axis_index("box")
    all_nodes = box_devices * node_count
    near_valid = near_partners >= 0
    near_local = jnp.where(near_valid, near_partners - box_rank * box_count, 0)
    near_onehot = (
        (jnp.arange(2 * box_count, dtype=jnp.int32)[:, None] == near_local.reshape(1, -1))
        & near_valid.reshape(1, -1)
    ).astype(jnp.float32)
    parent_local = parents - box_rank * group_count
    parent_onehot = (
        jnp.arange(group_count, dtype=jnp.int32)[:, None] == parent_local[None, :]
    ).astype(jnp.float32)
    far_valid = coupling_partners >= 0
    far_index = jnp.where(far_valid, coupling_partners, 0)
    bf_zero = jnp.zeros((), jnp.bfloat16)
    devices = jnp.arange(box_devices, dtype=jnp.int32)
    below = (devices < box_rank)[:, None, None]
    above = (devices > box_rank)[:, None, None]
    is_next = (devices == box_rank + 1)[:, None, None]
    is_prev = (devices == box_rank - 1)[:, None, None]
    near_size = box_count * leaf
    far_size = node_count * rank_width

    weights = jnp.zeros_like(targets)
    residual = targets
    direction = targets
    norm_start = jnp.sum(targets * targets)
    norm_now = None
    for iteration in range(ITERS):
        rounded = direction.astype(jnp.bfloat16)
        mirrored = jnp.einsum(
            "bsij,bi->bsj", near_tiles, rounded, preferred_element_type=jnp.float32
        )
        landed = jnp.dot(
            near_onehot, mirrored.reshape(-1, mirrored.shape[2]), precision=lax.Precision.HIGHEST
        )
        leaf_coef = jnp.einsum(
            "brl,bl->br", leaf_bases, rounded, preferred_element_type=jnp.float32
        ).astype(jnp.bfloat16)
        upward = jnp.einsum("brq,br->bq", transfer, leaf_coef, preferred_element_type=jnp.float32)
        group_coef = jnp.dot(parent_onehot, upward, precision=lax.Precision.HIGHEST).astype(
            jnp.bfloat16
        )
        node_coef = jnp.concatenate([leaf_coef, group_coef], axis=0)
        far_mirror = jnp.einsum(
            "nsab,na->nsb", coupling, node_coef, preferred_element_type=jnp.float32
        )
        far_mirror = far_mirror * far_valid[:, :, None].astype(jnp.float32)
        spread = (
            jnp.zeros((all_nodes, rank_width), jnp.float32)
            .at[far_index.reshape(-1)]
            .add(far_mirror.reshape(-1, rank_width))
        ).reshape(box_devices, node_count, rank_width)
        coef_wide = node_coef.astype(jnp.float32)
        far_send = jnp.where(below, coef_wide[None], spread)
        near_send = jnp.where(
            is_prev,
            rounded.astype(jnp.float32)[None],
            jnp.where(is_next, landed[box_count:][None], 0.0),
        )
        send = jnp.concatenate(
            [near_send.reshape(box_devices, near_size), far_send.reshape(box_devices, far_size)],
            axis=1,
        )
        got = lax.all_to_all(send, "box", 0, 0, tiled=True)
        got_near = got[:, :near_size].reshape(box_devices, box_count, leaf)
        got_far = got[:, near_size:].reshape(box_devices, node_count, rank_width)
        following = jnp.sum(jnp.where(is_next, got_near, 0.0), axis=0).astype(jnp.bfloat16)
        arrived = jnp.sum(jnp.where(is_prev, got_near, 0.0), axis=0)
        mirror_in = jnp.sum(jnp.where(below, got_far, 0.0), axis=0)
        every_coef = jnp.where(
            above, got_far, jnp.where(devices[:, None, None] == box_rank, coef_wide[None], 0.0)
        ).astype(jnp.bfloat16).reshape(all_nodes, rank_width)

        extended = jnp.concatenate([rounded, following], axis=0)
        near_in = jnp.where(near_valid[:, :, None], extended[near_local], bf_zero)
        forward = jnp.einsum(
            "bsij,bsj->bi", near_tiles, near_in, preferred_element_type=jnp.float32
        )
        near_part = forward + landed[:box_count] + arrived
        partner_coef = jnp.where(far_valid[:, :, None], every_coef[far_index], bf_zero)
        far_forward = jnp.einsum(
            "nsab,nsb->na", coupling, partner_coef, preferred_element_type=jnp.float32
        )
        far_part = far_forward + spread[box_rank] + mirror_in
        both = rep_sum(jnp.concatenate([near_part.reshape(-1), far_part.reshape(-1)]))
        near_total = both[:near_size].reshape(box_count, leaf)
        far_total = both[near_size:].reshape(node_count, rank_width)
        group_out = far_total[box_count:].astype(jnp.bfloat16)
        from_parent = jnp.einsum(
            "brq,bq->br", transfer, group_out[parent_local], preferred_element_type=jnp.float32
        )
        downward = (far_total[:box_count] + from_parent).astype(jnp.bfloat16)
        far_field = jnp.einsum(
            "brl,br->bl", leaf_bases, downward, preferred_element_type=jnp.float32
        )
        image_vec = noise_var * direction + near_total + far_field
        curvature = jnp.sum(direction * image_vec)
        if norm_now is None:
            sums = box_sum(jnp.stack([curvature, norm_start]))
            curvature, norm_now = sums[0], sums[1]
        else:
            curvature = box_sum(curvature[None])[0]
        step_size = norm_now / curvature
        weights = weights + step_size * direction
        residual = residual - step_size * image_vec
        if iteration + 1 < ITERS:
            norm_next = box_sum(jnp.sum(residual * residual)[None])[0]
            direction = residual + norm_next / norm_now * direction
            norm_now = norm_next
    return (weights, residual)


def solution(mesh):
    placed = (
        P("box", None),
        P("box", None),
        P("box", "rep", None, None),
        P("box", "rep"),
        P("box", None, None),
        P("box", None, None),
        P("box"),
        P("box", "rep", None, None),
        P("box", "rep"),
    )
    return jax.shard_map(
        local,
        mesh=mesh,
        in_specs=placed,
        out_specs=(P("box", None), P("box", None)),
        check_vma=False,
    )
```

time: 257 us -> 117 us (0.46)
  blocking collectives: 214 us -> 26.8 us
  waiting for transfers between devices: 0.01 us -> 17.3 us
  between operations: 5.83 us -> 13.4 us
  starting transfers between devices: 8.75 us -> 16.3 us
  local copies, waits for them, and re-layouts: 5.68 us -> 12.9 us
  other arithmetic: 5.79 us -> 11.2 us
    psum x5 -> x0, blocking collectives: 76.6 us -> none  [the longest x2 37.5 us: squares(): return lax.psum(jnp.sum(vector * vector), 'box')]
    unnamed x2 -> x0, blocking collectives: 76 us -> none
    all_gather x2 -> x0, blocking collectives: 61.3 us -> none  [local(): every_coef = lax.all_gather(node_coef, 'box', axis=0, tiled=True)]
    all_to_all x0 -> x3, blocking collectives: none -> 26.8 us  [box_sum(): got = lax.all_to_all(sent, 'box', 0, 0, tiled=True)]
    all_to_all x0 -> x2, waiting for transfers between devices: none -> 14.2 us  [local(): got = lax.all_to_all(send, 'box', 0, 0, tiled=True)]
    all_to_all x0 -> x2, starting transfers between devices: none -> 10.7 us  [local(): got = lax.all_to_all(send, 'box', 0, 0, tiled=True)]
    ppermute x4 -> x6, starting transfers between devices: 8.75 us -> 5.54 us  [rep_sum(): pieces.append(lax.ppermute(vector, 'rep', pairs))]
    ppermute x4 -> x6, waiting for transfers between devices: 0.01 us -> 3.14 us  [rep_sum(): pieces.append(lax.ppermute(vector, 'rep', pairs))]
  transfers between devices with their start and end apart: 4 -> 8, of which waited for: 0 -> 7; matrix products, arithmetic and copies ran while one was open for 7% -> 1% of each run, Pallas kernels for 0% -> 0%
where the time goes in v1:
time: 117 us; the launch traced here: 116 us
  blocking collectives  26.8 us (23%)
  matrix products  18 us (15%)
  waiting for transfers between devices  17.3 us (15%)
  starting transfers between devices  16.3 us (14%)
  between operations  13.4 us (11%)
  local copies, waits for them, and re-layouts  12.9 us (11%)
  other arithmetic  11.2 us (10%)
    all_to_all x3, blocking collectives, box_sum(): got = lax.all_to_all(sent, 'box', 0, 0, tiled=True)  26.8 us
    all_to_all x2, waiting for transfers between devices, local(): got = lax.all_to_all(send, 'box', 0, 0, tiled=True)  14.2 us
    all_to_all x2, starting transfers between devices, local(): got = lax.all_to_all(send, 'box', 0, 0, tiled=True)  10.7 us
    dot_general x2, matrix products, local(): jnp.einsum('bsij,bsj->bi', near_tiles, near_in, preferred_element_type=jn...  6.73 us
    dot_general x2, matrix products, local(): jnp.einsum('bsij,bi->bsj', near_tiles, rounded, preferred_element_type=jn...  5.68 us
    ppermute x6, starting transfers between devices, rep_sum(): pieces.append(lax.ppermute(vector, 'rep', pairs))  5.54 us
    ppermute x6, waiting for transfers between devices, rep_sum(): pieces.append(lax.ppermute(vector, 'rep', pairs))  3.14 us
  transfers between devices with their start and end apart: 8, of which 7 were waited for; matrix products, arithmetic and copies ran while one was open for 1% of the time, Pallas kernels for 0%

profile of v1, /device:TPU:0, one launch (start us, length us, event | category | flops | bytes accessed | tf_op | source)
XLA Modules:
  0.0 116.0 jit_solution(3834208017236521656)
XLA Ops:
  0.6 0.8 convert_bitcast_fusion.1
  1.5 1.3 %fusion.22 = f32[16,1,64]{2,1,0:T(1,128)S(1)} fusion(bf16[16,64,256]{2,1,0:T(8,128)(2,1)} %param.13, bf16[16,256,1]{1,0,2:T(8,128)(2,1)S(1)} %bitcast.152), kind=kOutput, calls=%fused_computation.76 | convolution fusion | flops 524288 | bytes 536576 | tf_op jit(solution)/shard_map/brl,bl->br/dot_general | solution.py:87
  4.5 1.1 fusion.47
  6.1 0.9 scatter_custom_fusion
  8.7 2.8 %fusion.24 = f32[16,1,2,256]{3,1,2,0:T(1,128)S(1)} fusion(bf16[16,2,256,256]{3,2,1,0:T(8,128)(2,1)} %param.11, bf16[16,256,1,1]{1,0,2,3:T(8,128)(2,1)S(1)} %bitcast.153), kind=kOutput, calls=%fused_computation.78 | convolution fusion | flops 4194304 | bytes 4235264 | tf_op jit(solution)/shard_map/bsij,bi->bsj/dot_general | solution.py:81
  12.2 0.8 copy.32
  13.0 7.4 %all-to-all-start = ((f32[8,1,5376]{2,1,0:T(1,128)}), f32[8,1,5376]{2,1,0:T(1,128)S(1)}, u32[]{:S(2)}, u32[]{:S(2)}) async-start(f32[8,1,5376]{2,1,0:T(1,128)} %copy.32), calls=%async_computation | async-start | bytes 344064 | tf_op jit(solution)/shard_map/all_to_all | solution.py:115
  21.3 6.7 %all-to-all-done = f32[8,1,5376]{2,1,0:T(1,128)S(1)} async-done(((f32[8,1,5376]{2,1,0:T(1,128)}), f32[8,1,5376]{2,1,0:T(1,128)S(1)}, u32[]{:S(2)}, u32[]{:S(2)}) %all-to-all-start) | async-done | bytes 172064 | tf_op jit(solution)/shard_map/all_to_all | solution.py:115
  30.7 3.4 %fusion.10 = f32[16,1,256,1]{2,1,3,0:T(1,128)S(1)} fusion(bf16[16,2,256,256]{3,2,1,0:T(8,128)(2,1)} %param.11, bf16[16,2,256,1]{2,1,0,3:T(2,128)(2,1)S(1)} %fusion.12), kind=kOutput, calls=%fused_computation.39 | convolution fusion | flops 4194304 | bytes 4227072 | tf_op jit(solution)/shard_map/bsij,bsj->bi/dot_general | solution.py:127
  34.2 1.6 %collective-permute-start.1 = (f32[5376]{0:T(1024)S(1)}, f32[5376]{0:T(1024)S(1)}, u32[]{:S(2)}, u32[]{:S(2)}) collective-permute-start(f32[5376]{0:T(1024)S(1)} %constant_dynamic-update-slice_fusion), channel_id=1, source_target_pairs={{0,2},{1,3},{2,0},{3,1},{4,6},{5,7},{6,4},{7,5},{8,10},{9,11},{10,... | collective-permute-start | bytes 64520 | tf_op jit(solution)/shard_map/ppermute | solution.py:15
  35.8 1.4 %collective-permute-start.2 = (f32[5376]{0:T(1024)S(1)}, f32[5376]{0:T(1024)S(1)}, u32[]{:S(2)}, u32[]{:S(2)}) collective-permute-start(f32[5376]{0:T(1024)S(1)} %constant_dynamic-update-slice_fusion), channel_id=1, source_target_pairs={{0,3},{1,0},{2,1},{3,2},{4,7},{5,4},{6,5},{7,6},{8,11},{9,8},{10,9... | collective-permute-start | bytes 64520 | tf_op jit(solution)/shard_map/ppermute | solution.py:15
  41.4 1.4 %pad_maximum_fusion.6 = f32[2]{0:T(128)S(1)} fusion(f32[1]{0:T(128)} %bitcast.29, f32[1]{0:T(128)} %bitcast.28), kind=kLoop, calls=%fused_computation.169 | loop fusion | flops 2 | bytes 16 | tf_op jit(solution)/shard_map/stack | solution.py:150
  42.8 9.2 %all_to_all.42 = f32[8,1,2]{2,1,0:T(1,128)S(1)} all-to-all(f32[8,1,2]{2,1,0:T(1,128)S(1)} %broadcast_in_dim.290), channel_id=1, replica_groups=mesh['box'=8,'rep'=4] {'box'}, dimensions={0} | all-to-all | bytes 128 | tf_op jit(solution)/shard_map/all_to_all | solution.py:28
  55.1 8.8 %all_to_all.43 = f32[8,1,1]{2,1,0:T(1,128)S(1)} all-to-all(f32[8,1,1]{2,1,0:T(1,128)S(1)} %broadcast_in_dim.291), channel_id=1, replica_groups=mesh['box'=8,'rep'=4] {'box'}, dimensions={0} | all-to-all | bytes 64 | tf_op jit(solution)/shard_map/all_to_all | solution.py:28
  70.5 2.8 %fusion.20 = f32[16,1,2,256]{3,1,2,0:T(1,128)S(1)} fusion(bf16[16,2,256,256]{3,2,1,0:T(8,128)(2,1)} %param.11, bf16[16,256,1,1]{1,0,2,3:T(8,128)(2,1)S(1)} %bitcast.155), kind=kOutput, calls=%fused_computation.74 | convolution fusion | flops 4194304 | bytes 4235264 | tf_op jit(solution)/shard_map/bsij,bi->bsj/dot_general | solution.py:81
  74.4 0.9 scatter_custom_fusion.1
  75.5 0.8 copy.36
  76.3 3.4 %all-to-all-start.3 = ((f32[8,1,5376]{2,1,0:T(1,128)}), f32[8,1,5376]{2,1,0:T(1,128)S(1)}, u32[]{:S(2)}, u32[]{:S(2)}) async-start(f32[8,1,5376]{2,1,0:T(1,128)} %copy.36), calls=%async_computation.3 | async-start | bytes 344064 | tf_op jit(solution)/shard_map/all_to_all | solution.py:115
  79.8 7.5 %all-to-all-done.3 = f32[8,1,5376]{2,1,0:T(1,128)S(1)} async-done(((f32[8,1,5376]{2,1,0:T(1,128)}), f32[8,1,5376]{2,1,0:T(1,128)S(1)}, u32[]{:S(2)}, u32[]{:S(2)}) %all-to-all-start.3) | async-done | bytes 172064 | tf_op jit(solution)/shard_map/all_to_all | solution.py:115
  89.9 3.4 %fusion.8 = f32[16,1,256,1]{2,1,3,0:T(1,128)S(1)} fusion(bf16[16,2,256,256]{3,2,1,0:T(8,128)(2,1)} %param.11, bf16[16,2,256,1]{2,1,0,3:T(2,128)(2,1)S(1)} %fusion.13), kind=kOutput, calls=%fused_computation.36 | convolution fusion | flops 4194304 | bytes 4227072 | tf_op jit(solution)/shard_map/bsij,bsj->bi/dot_general | solution.py:127
  93.4 1.0 collective-permute-start.4
  94.4 1.4 %collective-permute-start.5 = (f32[5376]{0:T(1024)S(1)}, f32[5376]{0:T(1024)S(1)}, u32[]{:S(2)}, u32[]{:S(2)}) collective-permute-start(f32[5376]{0:T(1024)S(1)} %constant_dynamic-update-slice_fusion.1), channel_id=1, source_target_pairs={{0,3},{1,0},{2,1},{3,2},{4,7},{5,4},{6,5},{7,6},{8,11},{9,8},{10,9... | collective-permute-start | bytes 64520 | tf_op jit(solution)/shard_map/ppermute | solution.py:15
  96.7 0.9 collective-permute-done.4
  100.9 8.8 %all_to_all.44 = f32[8,1,1]{2,1,0:T(1,128)S(1)} all-to-all(f32[8,1,1]{2,1,0:T(1,128)S(1)} %broadcast_in_dim.300), channel_id=1, replica_groups=mesh['box'=8,'rep'=4] {'box'}, dimensions={0} | all-to-all | bytes 64 | tf_op jit(solution)/shard_map/all_to_all | solution.py:28
  (182 shorter events, 24.1 us)
Async XLA Ops:
  0.6 5.1 %copy-start = (bf16[20,4,64,64]{3,2,1,0:T(8,128)(2,1)S(1)}, bf16[20,4,64,64]{3,2,1,0:T(8,128)(2,1)}, u32[]{:S(2)}) copy-start(bf16[20,4,64,64]{3,2,1,0:T(8,128)(2,1)} %param.16) | copy-start | bytes 1966084
  13.0 15.0 %all-to-all-start = ((f32[8,1,5376]{2,1,0:T(1,128)}), f32[8,1,5376]{2,1,0:T(1,128)S(1)}, u32[]{:S(2)}, u32[]{:S(2)}) async-start(f32[8,1,5376]{2,1,0:T(1,128)} %copy.32), calls=%async_computation | async-start | bytes 344064 | tf_op jit(solution)/shard_map/all_to_all | solution.py:115
  21.3 18.9 %copy-start.4 = (bf16[16,64,64]{2,1,0:T(8,128)(2,1)S(1)}, bf16[16,64,64]{2,1,0:T(8,128)(2,1)}, u32[]{:S(2)}) copy-start(bf16[16,64,64]{2,1,0:T(8,128)(2,1)} %param.14) | copy-start | bytes 393220
  28.1 12.4 %copy-start.1 = (bf16[16,64,256]{2,1,0:T(8,128)(2,1)S(1)}, bf16[16,64,256]{2,1,0:T(8,128)(2,1)}, u32[]{:S(2)}) copy-start(bf16[16,64,256]{2,1,0:T(8,128)(2,1)} %param.13) | copy-start | bytes 1572868
  29.3 11.5 %copy-start.2 = (f32[16,256]{1,0:T(8,128)S(1)}, f32[16,256]{1,0:T(8,128)}, u32[]{:S(2)}) copy-start(f32[16,256]{1,0:T(8,128)} %param.9) | copy-start | bytes 49156
  29.3 11.5 %copy-start.3 = (f32[16,256]{1,0:T(8,128)S(1)}, f32[16,256]{1,0:T(8,128)}, u32[]{:S(2)}) copy-start(f32[16,256]{1,0:T(8,128)} %param.10) | copy-start | bytes 49156
  34.1 3.3 %collective-permute-start = (f32[5376]{0:T(1024)S(1)}, f32[5376]{0:T(1024)S(1)}, u32[]{:S(2)}, u32[]{:S(2)}) collective-permute-start(f32[5376]{0:T(1024)S(1)} %constant_dynamic-update-slice_fusion), channel_id=1, source_target_pairs={{0,1},{1,2},{2,3},{3,0},{4,5},{5,6},{6,7},{7,4},{8,9},{9,10},{10,1... | collective-permute-start | bytes 64520 | tf_op jit(solution)/shard_map/ppermute | solution.py:15
  34.2 3.9 %collective-permute-start.1 = (f32[5376]{0:T(1024)S(1)}, f32[5376]{0:T(1024)S(1)}, u32[]{:S(2)}, u32[]{:S(2)}) collective-permute-start(f32[5376]{0:T(1024)S(1)} %constant_dynamic-update-slice_fusion), channel_id=1, source_target_pairs={{0,2},{1,3},{2,0},{3,1},{4,6},{5,7},{6,4},{7,5},{8,10},{9,11},{10,... | collective-permute-start | bytes 64520 | tf_op jit(solution)/shard_map/ppermute | solution.py:15
  35.8 2.9 %collective-permute-start.2 = (f32[5376]{0:T(1024)S(1)}, f32[5376]{0:T(1024)S(1)}, u32[]{:S(2)}, u32[]{:S(2)}) collective-permute-start(f32[5376]{0:T(1024)S(1)} %constant_dynamic-update-slice_fusion), channel_id=1, source_target_pairs={{0,3},{1,0},{2,1},{3,2},{4,7},{5,4},{6,5},{7,6},{8,11},{9,8},{10,9... | collective-permute-start | bytes 64520 | tf_op jit(solution)/shard_map/ppermute | solution.py:15
  76.3 10.9 %all-to-all-start.3 = ((f32[8,1,5376]{2,1,0:T(1,128)}), f32[8,1,5376]{2,1,0:T(1,128)S(1)}, u32[]{:S(2)}, u32[]{:S(2)}) async-start(f32[8,1,5376]{2,1,0:T(1,128)} %copy.36), calls=%async_computation.3 | async-start | bytes 344064 | tf_op jit(solution)/shard_map/all_to_all | solution.py:115
  93.3 3.3 %collective-permute-start.3 = (f32[5376]{0:T(1024)S(1)}, f32[5376]{0:T(1024)S(1)}, u32[]{:S(2)}, u32[]{:S(2)}) collective-permute-start(f32[5376]{0:T(1024)S(1)} %constant_dynamic-update-slice_fusion.1), channel_id=1, source_target_pairs={{0,1},{1,2},{2,3},{3,0},{4,5},{5,6},{6,7},{7,4},{8,9},{9,10},{10,1... | collective-permute-start | bytes 64520 | tf_op jit(solution)/shard_map/ppermute | solution.py:15
  93.4 4.1 %collective-permute-start.4 = (f32[5376]{0:T(1024)S(1)}, f32[5376]{0:T(1024)S(1)}, u32[]{:S(2)}, u32[]{:S(2)}) collective-permute-start(f32[5376]{0:T(1024)S(1)} %constant_dynamic-update-slice_fusion.1), channel_id=1, source_target_pairs={{0,2},{1,3},{2,0},{3,1},{4,6},{5,7},{6,4},{7,5},{8,10},{9,11},{10,... | collective-permute-start | bytes 64520 | tf_op jit(solution)/shard_map/ppermute | solution.py:15
  94.4 3.1 %collective-permute-start.5 = (f32[5376]{0:T(1024)S(1)}, f32[5376]{0:T(1024)S(1)}, u32[]{:S(2)}, u32[]{:S(2)}) collective-permute-start(f32[5376]{0:T(1024)S(1)} %constant_dynamic-update-slice_fusion.1), channel_id=1, source_target_pairs={{0,3},{1,0},{2,1},{3,2},{4,7},{5,4},{6,5},{7,6},{8,11},{9,8},{10,9... | collective-permute-start | bytes 64520 | tf_op jit(solution)/shard_map/ppermute | solution.py:15

commit v2 on v1

--- a/solution.py
+++ b/solution.py
@@ -8,28 +8,27 @@
 
 def rep_sum(vector):
     count = lax.axis_size("rep")
+    if count & (count - 1) == 0:
+        stride = 1
+        while stride < count:
+            pairs = [(i, i ^ stride) for i in range(count)]
+            vector = vector + lax.ppermute(vector, "rep", pairs)
+            stride *= 2
+        return vector
     me = lax.axis_index("rep")
     pieces = [vector]
     for shift in range(1, count):
         pairs = [(i, (i + shift) % count) for i in range(count)]
         pieces.append(lax.ppermute(vector, "rep", pairs))
-    stacked = jnp.stack(pieces)
-    order = (me - jnp.arange(count)) % count
-    ordered = stacked[order]
-    total = ordered[0]
-    for i in range(1, count):
-        total = total + ordered[i]
-    return total
+    ordered = jnp.stack(pieces)[(me - jnp.arange(count)) % count]
+    return jnp.sum(ordered, axis=0)
 
 
 def box_sum(values):
     count = lax.axis_size("box")
     sent = jnp.broadcast_to(values[None, :], (count, values.shape[0]))
     got = lax.all_to_all(sent, "box", 0, 0, tiled=True)
-    total = got[0]
-    for i in range(1, count):
-        total = total + got[i]
-    return total
+    return jnp.sum(got, axis=0)
 
 
 def local(
@@ -66,15 +65,12 @@
     devices = jnp.arange(box_devices, dtype=jnp.int32)
     below = (devices < box_rank)[:, None, None]
     above = (devices > box_rank)[:, None, None]
-    is_next = (devices == box_rank + 1)[:, None, None]
-    is_prev = (devices == box_rank - 1)[:, None, None]
     near_size = box_count * leaf
     far_size = node_count * rank_width
 
     weights = jnp.zeros_like(targets)
     residual = targets
     direction = targets
-    norm_start = jnp.sum(targets * targets)
     norm_now = None
     for iteration in range(ITERS):
         rounded = direction.astype(jnp.bfloat16)
@@ -101,22 +97,17 @@
             .at[far_index.reshape(-1)]
             .add(far_mirror.reshape(-1, rank_width))
         ).reshape(box_devices, node_count, rank_width)
+        following = lax.ppermute(
+            rounded, "box", [(i, i - 1) for i in range(1, box_devices)]
+        )
+        arrived = lax.ppermute(
+            landed[box_count:], "box", [(i, i + 1) for i in range(box_devices - 1)]
+        )
         coef_wide = node_coef.astype(jnp.float32)
         far_send = jnp.where(below, coef_wide[None], spread)
-        near_send = jnp.where(
-            is_prev,
-            rounded.astype(jnp.float32)[None],
-            jnp.where(is_next, landed[box_count:][None], 0.0),
-        )
-        send = jnp.concatenate(
-            [near_send.reshape(box_devices, near_size), far_send.reshape(box_devices, far_size)],
-            axis=1,
-        )
-        got = lax.all_to_all(send, "box", 0, 0, tiled=True)
-        got_near = got[:, :near_size].reshape(box_devices, box_count, leaf)
-        got_far = got[:, near_size:].reshape(box_devices, node_count, rank_width)
-        following = jnp.sum(jnp.where(is_next, got_near, 0.0), axis=0).astype(jnp.bfloat16)
-        arrived = jnp.sum(jnp.where(is_prev, got_near, 0.0), axis=0)
+        got_far = lax.all_to_all(
+            far_send.reshape(box_devices, far_size), "box", 0, 0, tiled=True
+        ).reshape(box_devices, node_count, rank_width)
         mirror_in = jnp.sum(jnp.where(below, got_far, 0.0), axis=0)
         every_coef = jnp.where(
             above, got_far, jnp.where(devices[:, None, None] == box_rank, coef_wide[None], 0.0)
@@ -145,18 +136,17 @@
             "brl,br->bl", leaf_bases, downward, preferred_element_type=jnp.float32
         )
         image_vec = noise_var * direction + near_total + far_field
-        curvature = jnp.sum(direction * image_vec)
         if norm_now is None:
-            sums = box_sum(jnp.stack([curvature, norm_start]))
-            curvature, norm_now = sums[0], sums[1]
+            sums = box_sum(jnp.sum(jnp.stack([direction * image_vec, targets * targets]), axis=(1, 2)))
+            curvature, norm_now = sums[0:1], sums[1:2]
         else:
-            curvature = box_sum(curvature[None])[0]
-        step_size = norm_now / curvature
+            curvature = box_sum(jnp.sum(direction * image_vec).reshape(1))
+        step_size = (norm_now / curvature).reshape(1, 1)
         weights = weights + step_size * direction
         residual = residual - step_size * image_vec
         if iteration + 1 < ITERS:
-            norm_next = box_sum(jnp.sum(residual * residual)[None])[0]
-            direction = residual + norm_next / norm_now * direction
+            norm_next = box_sum(jnp.sum(residual * residual).reshape(1))
+            direction = residual + (norm_next / norm_now).reshape(1, 1) * direction
             norm_now = norm_next
     return (weights, residual)
 

time: 117 us -> 105 us (0.90)
  starting transfers between devices: 16.3 us -> 25.4 us
  between operations: 13.4 us -> 5.32 us
  waiting for transfers between devices: 17.3 us -> 11.2 us
  other arithmetic: 11.2 us -> 7.35 us
  local copies, waits for them, and re-layouts: 12.9 us -> 9.78 us
  blocking collectives: 26.8 us -> 29.2 us
  matrix products: 18 us -> 16 us
    all_to_all x2, waiting for transfers between devices: 14.2 us -> 4.1 us  [local(): lax.all_to_all(far_send.reshape(box_devices, far_size), 'box', 0, 0, tile...]
    ppermute x6 -> x8, starting transfers between devices: 5.54 us -> 15 us  [the longest x2 9.43 us: local(): lax.ppermute(landed[box_count:], 'box', [(i, i + 1) for i in range(box_de...]
    ppermute x6 -> x8, waiting for transfers between devices: 3.14 us -> 7.15 us  [the longest x4 7.13 us: rep_sum(): vector = vector + lax.ppermute(vector, 'rep', pairs)]
    all_to_all x3, blocking collectives: 26.8 us -> 29.2 us  [box_sum(): got = lax.all_to_all(sent, 'box', 0, 0, tiled=True)]
    all_to_all x2 -> x0, local copies, waits for them, and re-layouts: 1.68 us -> none  [local(): got = lax.all_to_all(send, 'box', 0, 0, tiled=True)]
    another operation x3 -> x1, other arithmetic: 1.54 us -> 0.01 us  [local(): jnp.stack([direction * image_vec, targets * targets])]
    select_n x0 -> x2, local copies, waits for them, and re-layouts: none -> 1.31 us  [local(): far_send = jnp.where(below, coef_wide[None], spread)]
    slice x5 -> x3, local copies, waits for them, and re-layouts: 1.81 us -> 0.59 us  [the longest x1 0.58 us: local(): curvature, norm_now = (sums[0:1], sums[1:2])]
  transfers between devices with their start and end apart: 8 -> 10, of which waited for: 7 -> 6; matrix products, arithmetic and copies ran while one was open for 1% -> 17% of each run, Pallas kernels for 0% -> 0%
where the time goes in v2:
time: 105 us; the launch traced here: 104 us
  blocking collectives  29.2 us (28%)
  starting transfers between devices  25.4 us (24%)
  matrix products  16 us (15%)
  waiting for transfers between devices  11.2 us (11%)
  local copies, waits for them, and re-layouts  9.78 us (9%)
  other arithmetic  7.35 us (7%)
  between operations  5.32 us (5%)
    all_to_all x3, blocking collectives, box_sum(): got = lax.all_to_all(sent, 'box', 0, 0, tiled=True)  29.2 us
    all_to_all x2, starting transfers between devices, local(): lax.all_to_all(far_send.reshape(box_devices, far_size), 'box', 0, 0, tile...  10.4 us
    ppermute x2, starting transfers between devices, local(): lax.ppermute(landed[box_count:], 'box', [(i, i + 1) for i in range(box_de...  9.43 us
    ppermute x4, waiting for transfers between devices, rep_sum(): vector = vector + lax.ppermute(vector, 'rep', pairs)  7.13 us
    dot_general x2, matrix products, local(): jnp.einsum('bsij,bsj->bi', near_tiles, near_in, preferred_element_type=jn...  6.73 us
    dot_general x2, matrix products, local(): jnp.einsum('bsij,bi->bsj', near_tiles, rounded, preferred_element_type=jn...  5.66 us
    all_to_all x2, waiting for transfers between devices, local(): lax.all_to_all(far_send.reshape(box_devices, far_size), 'box', 0, 0, tile...  4.1 us
    ppermute x4, starting transfers between devices, rep_sum(): vector = vector + lax.ppermute(vector, 'rep', pairs)  2.96 us
  transfers between devices with their start and end apart: 10, of which 6 were waited for; matrix products, arithmetic and copies ran while one was open for 17% of the time, Pallas kernels for 0%

profile of v2, /device:TPU:0, one launch (start us, length us, event | category | flops | bytes accessed | tf_op | source)
XLA Modules:
  0.0 104.3 jit_solution(5816131924027822569)
XLA Ops:
  0.7 0.9 convert_bitcast_fusion.5
  1.6 2.8 %fusion.26 = f32[16,1,2,256]{3,1,2,0:T(1,128)S(1)} fusion(bf16[16,2,256,256]{3,2,1,0:T(8,128)(2,1)} %param.11, bf16[16,256,1,1]{1,0,2,3:T(8,128)(2,1)S(1)} %convert_bitcast_fusion.5), kind=kOutput, calls=%fused_computation.57 | convolution fusion | flops 4194304 | bytes 4235264 | tf_op jit(solution)/shard_map/bsij,bi->bsj/dot_general | solution.py:77
  5.0 4.9 %collective-permute-start.1 = (f32[16,256]{1,0:T(8,128)S(1)}, f32[16,256]{1,0:T(8,128)S(1)}, u32[]{:S(2)}, u32[]{:S(2)}) collective-permute-start(f32[16,256]{1,0:T(8,128)S(1)} %slice.141), channel_id=1, source_target_pairs={{0,4},{4,8},{8,12},{12,16},{16,20},{20,24},{24,28},{1,5},{5,9},{9,... | collective-permute-start | bytes 49160 | tf_op jit(solution)/shard_map/ppermute | solution.py:103
  9.9 1.3 %collective-permute-start = (bf16[16,256]{1,0:T(8,128)(2,1)S(1)}, bf16[16,256]{1,0:T(8,128)(2,1)S(1)}, u32[]{:S(2)}, u32[]{:S(2)}) collective-permute-start(bf16[16,256]{1,0:T(8,128)(2,1)S(1)} %convert_element_type.73), channel_id=1, source_target_pairs={{4,0},{8,4},{12,8},{16,12},{20,16},{24,20},{28,24},{5,1},{9,5},{13... | collective-permute-start | bytes 24584 | tf_op jit(solution)/shard_map/ppermute | solution.py:100
  12.6 0.9 scatter_custom_fusion
  14.4 7.0 %all-to-all-start = ((f32[8,1,1280]{2,1,0:T(1,128)}), f32[8,1,1280]{2,1,0:T(1,128)S(1)}, u32[]{:S(2)}, u32[]{:S(2)}) async-start(f32[8,1,1280]{2,1,0:T(1,128)} %copy.54), calls=%async_computation | async-start | bytes 81920 | tf_op jit(solution)/shard_map/all_to_all | solution.py:108
  23.1 3.4 %fusion.12 = f32[16,1,256,1]{2,1,3,0:T(1,128)S(1)} fusion(bf16[16,2,256,256]{3,2,1,0:T(8,128)(2,1)} %param.11, bf16[16,2,256,1]{2,1,0,3:T(2,128)(2,1)S(1)} %fusion.14), kind=kOutput, calls=%fused_computation.29 | convolution fusion | flops 4194304 | bytes 4227072 | tf_op jit(solution)/shard_map/bsij,bsj->bi/dot_general | solution.py:118
  26.5 1.7 %all-to-all-done = f32[8,1,1280]{2,1,0:T(1,128)S(1)} async-done(((f32[8,1,1280]{2,1,0:T(1,128)}), f32[8,1,1280]{2,1,0:T(1,128)S(1)}, u32[]{:S(2)}, u32[]{:S(2)}) %all-to-all-start) | async-done | bytes 40992 | tf_op jit(solution)/shard_map/all_to_all | solution.py:108
  30.0 1.2 %collective-permute-done.2 = f32[5376]{0:T(1024)S(1)} collective-permute-done((f32[5376]{0:T(1024)S(1)}, f32[5376]{0:T(1024)S(1)}, u32[]{:S(2)}, u32[]{:S(2)}) %collective-permute-start.2) | collective-permute-done | bytes 21536 | tf_op jit(solution)/shard_map/ppermute | solution.py:15
  31.2 1.4 %collective-permute-start.3 = (f32[5376]{0:T(1024)S(1)}, f32[5376]{0:T(1024)S(1)}, u32[]{:S(2)}, u32[]{:S(2)}) collective-permute-start(f32[5376]{0:T(1024)S(1)} %add.99), channel_id=1, source_target_pairs={{0,2},{1,3},{2,0},{3,1},{4,6},{5,7},{6,4},{7,5},{8,10},{9,11},{10,... | collective-permute-start | bytes 64520 | tf_op jit(solution)/shard_map/ppermute | solution.py:15
  32.6 2.4 %collective-permute-done.3 = f32[5376]{0:T(1024)S(1)} collective-permute-done((f32[5376]{0:T(1024)S(1)}, f32[5376]{0:T(1024)S(1)}, u32[]{:S(2)}, u32[]{:S(2)}) %collective-permute-start.3) | collective-permute-done | bytes 21536 | tf_op jit(solution)/shard_map/ppermute | solution.py:15
  36.3 10.6 %all_to_all.36 = f32[8,1,2]{2,1,0:T(1,128)S(1)} all-to-all(f32[8,1,2]{2,1,0:T(1,128)S(1)} %broadcast_in_dim.192), channel_id=1, replica_groups=mesh['box'=8,'rep'=4] {'box'}, dimensions={0} | all-to-all | bytes 128 | tf_op jit(solution)/shard_map/all_to_all | solution.py:30
  50.1 8.8 %all_to_all.37 = f32[8,1,1]{2,1,0:T(1,128)S(1)} all-to-all(f32[8,1,1]{2,1,0:T(1,128)S(1)} %broadcast_in_dim.193), channel_id=1, replica_groups=mesh['box'=8,'rep'=4] {'box'}, dimensions={0} | all-to-all | bytes 64 | tf_op jit(solution)/shard_map/all_to_all | solution.py:30
  60.9 1.3 %collective-permute-start.4 = (bf16[16,256]{1,0:T(8,128)(2,1)S(1)}, bf16[16,256]{1,0:T(8,128)(2,1)S(1)}, u32[]{:S(2)}, u32[]{:S(2)}) collective-permute-start(bf16[16,256]{1,0:T(8,128)(2,1)S(1)} %fusion.61), channel_id=1, source_target_pairs={{4,0},{8,4},{12,8},{16,12},{20,16},{24,20},{28,24},{5,1},{9,5},{13... | collective-permute-start | bytes 24584 | tf_op jit(solution)/shard_map/ppermute | solution.py:100
  63.2 0.9 scatter_custom_fusion.1
  64.2 2.8 %fusion.22 = f32[16,1,2,256]{3,1,2,0:T(1,128)S(1)} fusion(bf16[16,2,256,256]{3,2,1,0:T(8,128)(2,1)} %param.11, bf16[16,256,1,1]{1,0,2,3:T(8,128)(2,1)S(1)} %bitcast.137), kind=kOutput, calls=%fused_computation.53 | convolution fusion | flops 4194304 | bytes 4235264 | tf_op jit(solution)/shard_map/bsij,bi->bsj/dot_general | solution.py:77
  67.2 4.6 %collective-permute-start.5 = (f32[16,256]{1,0:T(8,128)S(1)}, f32[16,256]{1,0:T(8,128)S(1)}, u32[]{:S(2)}, u32[]{:S(2)}) collective-permute-start(f32[16,256]{1,0:T(8,128)S(1)} %slice.146), channel_id=1, source_target_pairs={{0,4},{4,8},{8,12},{12,16},{16,20},{20,24},{24,28},{1,5},{5,9},{9,... | collective-permute-start | bytes 49160 | tf_op jit(solution)/shard_map/ppermute | solution.py:103
  72.6 3.3 %all-to-all-start.3 = ((f32[8,1,1280]{2,1,0:T(1,128)}), f32[8,1,1280]{2,1,0:T(1,128)S(1)}, u32[]{:S(2)}, u32[]{:S(2)}) async-start(f32[8,1,1280]{2,1,0:T(1,128)} %copy.58), calls=%async_computation.3 | async-start | bytes 81920 | tf_op jit(solution)/shard_map/all_to_all | solution.py:108
  76.8 3.4 %fusion.10 = f32[16,1,256,1]{2,1,3,0:T(1,128)S(1)} fusion(bf16[16,2,256,256]{3,2,1,0:T(8,128)(2,1)} %param.11, bf16[16,2,256,1]{2,1,0,3:T(2,128)(2,1)S(1)} %fusion.15), kind=kOutput, calls=%fused_computation.26 | convolution fusion | flops 4194304 | bytes 4227072 | tf_op jit(solution)/shard_map/bsij,bsj->bi/dot_general | solution.py:118
  80.2 2.4 %all-to-all-done.3 = f32[8,1,1280]{2,1,0:T(1,128)S(1)} async-done(((f32[8,1,1280]{2,1,0:T(1,128)}), f32[8,1,1280]{2,1,0:T(1,128)S(1)}, u32[]{:S(2)}, u32[]{:S(2)}) %all-to-all-start.3) | async-done | bytes 40992 | tf_op jit(solution)/shard_map/all_to_all | solution.py:108
  84.5 1.2 %collective-permute-done.6 = f32[5376]{0:T(1024)S(1)} collective-permute-done((f32[5376]{0:T(1024)S(1)}, f32[5376]{0:T(1024)S(1)}, u32[]{:S(2)}, u32[]{:S(2)}) %collective-permute-start.6) | collective-permute-done | bytes 21536 | tf_op jit(solution)/shard_map/ppermute | solution.py:15
  85.6 1.4 %collective-permute-start.7 = (f32[5376]{0:T(1024)S(1)}, f32[5376]{0:T(1024)S(1)}, u32[]{:S(2)}, u32[]{:S(2)}) collective-permute-start(f32[5376]{0:T(1024)S(1)} %add.110), channel_id=1, source_target_pairs={{0,2},{1,3},{2,0},{3,1},{4,6},{5,7},{6,4},{7,5},{8,10},{9,11},{10,... | collective-permute-start | bytes 64520 | tf_op jit(solution)/shard_map/ppermute | solution.py:15
  87.1 2.4 %collective-permute-done.7 = f32[5376]{0:T(1024)S(1)} collective-permute-done((f32[5376]{0:T(1024)S(1)}, f32[5376]{0:T(1024)S(1)}, u32[]{:S(2)}, u32[]{:S(2)}) %collective-permute-start.7) | collective-permute-done | bytes 21536 | tf_op jit(solution)/shard_map/ppermute | solution.py:15
  91.9 9.8 %all_to_all.38 = f32[8,1,1]{2,1,0:T(1,128)S(1)} all-to-all(f32[8,1,1]{2,1,0:T(1,128)S(1)} %broadcast_in_dim.197), channel_id=1, replica_groups=mesh['box'=8,'rep'=4] {'box'}, dimensions={0} | all-to-all | bytes 64 | tf_op jit(solution)/shard_map/all_to_all | solution.py:30
  (165 shorter events, 18.2 us)
Async XLA Ops:
  0.6 11.6 %copy-start = (bf16[20,4,64,64]{3,2,1,0:T(8,128)(2,1)S(1)}, bf16[20,4,64,64]{3,2,1,0:T(8,128)(2,1)}, u32[]{:S(2)}) copy-start(bf16[20,4,64,64]{3,2,1,0:T(8,128)(2,1)} %param.16) | copy-start | bytes 1966084
  0.6 9.3 %copy-start.2 = (f32[16,256]{1,0:T(8,128)S(1)}, f32[16,256]{1,0:T(8,128)}, u32[]{:S(2)}) copy-start(f32[16,256]{1,0:T(8,128)} %param.9) | copy-start | bytes 49156
  0.7 3.8 %copy-start.5 = (s32[16,2]{0,1:T(2,128)S(1)}, s32[16,2]{0,1:T(2,128)}, u32[]{:S(2)}) copy-start(s32[16,2]{0,1:T(2,128)} %param.12) | copy-start | bytes 388
  0.7 10.6 %copy-start.1 = (bf16[16,64,256]{2,1,0:T(8,128)(2,1)S(1)}, bf16[16,64,256]{2,1,0:T(8,128)(2,1)}, u32[]{:S(2)}) copy-start(bf16[16,64,256]{2,1,0:T(8,128)(2,1)} %param.13) | copy-start | bytes 1572868
  0.7 10.9 %copy-start.4 = (s32[20,4]{0,1:T(4,128)S(1)}, s32[20,4]{0,1:T(4,128)}, u32[]{:S(2)}) copy-start(s32[20,4]{0,1:T(4,128)} %param.17) | copy-start | bytes 964
  0.7 11.2 %copy-start.7 = (bf16[16,64,64]{2,1,0:T(8,128)(2,1)S(1)}, bf16[16,64,64]{2,1,0:T(8,128)(2,1)}, u32[]{:S(2)}) copy-start(bf16[16,64,64]{2,1,0:T(8,128)(2,1)} %param.14) | copy-start | bytes 393220
  0.7 11.4 %copy-start.6 = (s32[16]{0:T(128)S(1)}, s32[16]{0:T(128)}, u32[]{:S(2)}) copy-start(s32[16]{0:T(128)} %param.15) | copy-start | bytes 196
  5.0 21.4 %collective-permute-start.1 = (f32[16,256]{1,0:T(8,128)S(1)}, f32[16,256]{1,0:T(8,128)S(1)}, u32[]{:S(2)}, u32[]{:S(2)}) collective-permute-start(f32[16,256]{1,0:T(8,128)S(1)} %slice.141), channel_id=1, source_target_pairs={{0,4},{4,8},{8,12},{12,16},{16,20},{20,24},{24,28},{1,5},{5,9},{9,... | collective-permute-start | bytes 49160 | tf_op jit(solution)/shard_map/ppermute | solution.py:103
  9.9 12.4 %collective-permute-start = (bf16[16,256]{1,0:T(8,128)(2,1)S(1)}, bf16[16,256]{1,0:T(8,128)(2,1)S(1)}, u32[]{:S(2)}, u32[]{:S(2)}) collective-permute-start(bf16[16,256]{1,0:T(8,128)(2,1)S(1)} %convert_element_type.73), channel_id=1, source_target_pairs={{4,0},{8,4},{12,8},{16,12},{20,16},{24,20},{28,24},{5,1},{9,5},{13... | collective-permute-start | bytes 24584 | tf_op jit(solution)/shard_map/ppermute | solution.py:100
  13.7 22.5 %copy-start.3 = (f32[16,256]{1,0:T(8,128)S(1)}, f32[16,256]{1,0:T(8,128)}, u32[]{:S(2)}) copy-start(f32[16,256]{1,0:T(8,128)} %param.10) | copy-start | bytes 49156
  14.4 13.8 %all-to-all-start = ((f32[8,1,1280]{2,1,0:T(1,128)}), f32[8,1,1280]{2,1,0:T(1,128)S(1)}, u32[]{:S(2)}, u32[]{:S(2)}) async-start(f32[8,1,1280]{2,1,0:T(1,128)} %copy.54), calls=%async_computation | async-start | bytes 81920 | tf_op jit(solution)/shard_map/all_to_all | solution.py:108
  29.9 1.2 %collective-permute-start.2 = (f32[5376]{0:T(1024)S(1)}, f32[5376]{0:T(1024)S(1)}, u32[]{:S(2)}, u32[]{:S(2)}) collective-permute-start(f32[5376]{0:T(1024)S(1)} %constant_dynamic-update-slice_fusion), channel_id=1, source_target_pairs={{0,1},{1,0},{2,3},{3,2},{4,5},{5,4},{6,7},{7,6},{8,9},{9,8},{10,11... | collective-permute-start | bytes 64520 | tf_op jit(solution)/shard_map/ppermute | solution.py:15
  31.2 3.8 %collective-permute-start.3 = (f32[5376]{0:T(1024)S(1)}, f32[5376]{0:T(1024)S(1)}, u32[]{:S(2)}, u32[]{:S(2)}) collective-permute-start(f32[5376]{0:T(1024)S(1)} %add.99), channel_id=1, source_target_pairs={{0,2},{1,3},{2,0},{3,1},{4,6},{5,7},{6,4},{7,5},{8,10},{9,11},{10,... | collective-permute-start | bytes 64520 | tf_op jit(solution)/shard_map/ppermute | solution.py:15
  60.9 15.1 %collective-permute-start.4 = (bf16[16,256]{1,0:T(8,128)(2,1)S(1)}, bf16[16,256]{1,0:T(8,128)(2,1)S(1)}, u32[]{:S(2)}, u32[]{:S(2)}) collective-permute-start(bf16[16,256]{1,0:T(8,128)(2,1)S(1)} %fusion.61), channel_id=1, source_target_pairs={{4,0},{8,4},{12,8},{16,12},{20,16},{24,20},{28,24},{5,1},{9,5},{13... | collective-permute-start | bytes 24584 | tf_op jit(solution)/shard_map/ppermute | solution.py:100
  67.2 12.9 %collective-permute-start.5 = (f32[16,256]{1,0:T(8,128)S(1)}, f32[16,256]{1,0:T(8,128)S(1)}, u32[]{:S(2)}, u32[]{:S(2)}) collective-permute-start(f32[16,256]{1,0:T(8,128)S(1)} %slice.146), channel_id=1, source_target_pairs={{0,4},{4,8},{8,12},{12,16},{16,20},{20,24},{24,28},{1,5},{5,9},{9,... | collective-permute-start | bytes 49160 | tf_op jit(solution)/shard_map/ppermute | solution.py:103
  72.6 10.0 %all-to-all-start.3 = ((f32[8,1,1280]{2,1,0:T(1,128)}), f32[8,1,1280]{2,1,0:T(1,128)S(1)}, u32[]{:S(2)}, u32[]{:S(2)}) async-start(f32[8,1,1280]{2,1,0:T(1,128)} %copy.58), calls=%async_computation.3 | async-start | bytes 81920 | tf_op jit(solution)/shard_map/all_to_all | solution.py:108
  84.4 1.2 %collective-permute-start.6 = (f32[5376]{0:T(1024)S(1)}, f32[5376]{0:T(1024)S(1)}, u32[]{:S(2)}, u32[]{:S(2)}) collective-permute-start(f32[5376]{0:T(1024)S(1)} %constant_dynamic-update-slice_fusion.1), channel_id=1, source_target_pairs={{0,1},{1,0},{2,3},{3,2},{4,5},{5,4},{6,7},{7,6},{8,9},{9,8},{10,11... | collective-permute-start | bytes 64520 | tf_op jit(solution)/shard_map/ppermute | solution.py:15
  85.6 3.8 %collective-permute-start.7 = (f32[5376]{0:T(1024)S(1)}, f32[5376]{0:T(1024)S(1)}, u32[]{:S(2)}, u32[]{:S(2)}) collective-permute-start(f32[5376]{0:T(1024)S(1)} %add.110), channel_id=1, source_target_pairs={{0,2},{1,3},{2,0},{3,1},{4,6},{5,7},{6,4},{7,5},{8,10},{9,11},{10,... | collective-permute-start | bytes 64520 | tf_op jit(solution)/shard_map/ppermute | solution.py:15

commit v3 on v2

--- a/solution.py
+++ b/solution.py
@@ -136,16 +136,21 @@
             "brl,br->bl", leaf_bases, downward, preferred_element_type=jnp.float32
         )
         image_vec = noise_var * direction + near_total + far_field
+        partials = [direction * image_vec]
         if norm_now is None:
-            sums = box_sum(jnp.sum(jnp.stack([direction * image_vec, targets * targets]), axis=(1, 2)))
-            curvature, norm_now = sums[0:1], sums[1:2]
-        else:
-            curvature = box_sum(jnp.sum(direction * image_vec).reshape(1))
-        step_size = (norm_now / curvature).reshape(1, 1)
-        weights = weights + step_size * direction
-        residual = residual - step_size * image_vec
+            partials.append(targets * targets)
         if iteration + 1 < ITERS:
-            norm_next = box_sum(jnp.sum(residual * residual).reshape(1))
+            partials += [residual * image_vec, image_vec * image_vec]
+        sums = box_sum(jnp.sum(jnp.stack(partials), axis=(1, 2)))
+        curvature = sums[0:1]
+        if norm_now is None:
+            norm_now = sums[1:2]
+        step_size = norm_now / curvature
+        weights = weights + step_size.reshape(1, 1) * direction
+        residual = residual - step_size.reshape(1, 1) * image_vec
+        if iteration + 1 < ITERS:
+            cross, image_square = sums[-2:-1], sums[-1:]
+            norm_next = norm_now - 2.0 * step_size * cross + step_size * step_size * image_square
             direction = residual + (norm_next / norm_now).reshape(1, 1) * direction
             norm_now = norm_next
     return (weights, residual)

time: 105 us -> 94.7 us (0.902)
  blocking collectives: 29.2 us -> 20.4 us
  other arithmetic: 7.35 us -> 6.16 us
    all_to_all x3 -> x2, blocking collectives: 29.2 us -> 20.4 us  [box_sum(): got = lax.all_to_all(sent, 'box', 0, 0, tiled=True)]
  transfers between devices with their start and end apart: 10 -> 10, of which waited for: 6 -> 6; matrix products, arithmetic and copies ran while one was open for 17% -> 19% of each run, Pallas kernels for 0% -> 0%
where the time goes in v3:
time: 94.7 us; the launch traced here: 94 us
  starting transfers between devices  25.4 us (27%)
  blocking collectives  20.4 us (22%)
  matrix products  16 us (17%)
  waiting for transfers between devices  11.2 us (12%)
  local copies, waits for them, and re-layouts  9.17 us (10%)
  other arithmetic  6.16 us (7%)
  between operations  5.69 us (6%)
    all_to_all x2, blocking collectives, box_sum(): got = lax.all_to_all(sent, 'box', 0, 0, tiled=True)  20.4 us
    all_to_all x2, starting transfers between devices, local(): lax.all_to_all(far_send.reshape(box_devices, far_size), 'box', 0, 0, tile...  10.4 us
    ppermute x2, starting transfers between devices, local(): lax.ppermute(landed[box_count:], 'box', [(i, i + 1) for i in range(box_de...  9.4 us
    ppermute x4, waiting for transfers between devices, rep_sum(): vector = vector + lax.ppermute(vector, 'rep', pairs)  7.1 us
    dot_general x2, matrix products, local(): jnp.einsum('bsij,bsj->bi', near_tiles, near_in, preferred_element_type=jn...  6.73 us
    dot_general x2, matrix products, local(): jnp.einsum('bsij,bi->bsj', near_tiles, rounded, preferred_element_type=jn...  5.66 us
    all_to_all x2, waiting for transfers between devices, local(): lax.all_to_all(far_send.reshape(box_devices, far_size), 'box', 0, 0, tile...  4.1 us
    ppermute x4, starting transfers between devices, rep_sum(): vector = vector + lax.ppermute(vector, 'rep', pairs)  3 us
  transfers between devices with their start and end apart: 10, of which 6 were waited for; matrix products, arithmetic and copies ran while one was open for 19% of the time, Pallas kernels for 0%

profile of v3, /device:TPU:0, one launch (start us, length us, event | category | flops | bytes accessed | tf_op | source)
XLA Modules:
  0.0 94.0 jit_solution(14868930265305449170)
XLA Ops:
  0.7 0.9 convert_bitcast_fusion.5
  1.6 2.8 %fusion.26 = f32[16,1,2,256]{3,1,2,0:T(1,128)S(1)} fusion(bf16[16,2,256,256]{3,2,1,0:T(8,128)(2,1)} %param.11, bf16[16,256,1,1]{1,0,2,3:T(8,128)(2,1)S(1)} %convert_bitcast_fusion.5), kind=kOutput, calls=%fused_computation.57 | convolution fusion | flops 4194304 | bytes 4235264 | tf_op jit(solution)/shard_map/bsij,bi->bsj/dot_general | solution.py:77
  5.0 4.9 %collective-permute-start.1 = (f32[16,256]{1,0:T(8,128)S(1)}, f32[16,256]{1,0:T(8,128)S(1)}, u32[]{:S(2)}, u32[]{:S(2)}) collective-permute-start(f32[16,256]{1,0:T(8,128)S(1)} %slice.149), channel_id=1, source_target_pairs={{0,4},{4,8},{8,12},{12,16},{16,20},{20,24},{24,28},{1,5},{5,9},{9,... | collective-permute-start | bytes 49160 | tf_op jit(solution)/shard_map/ppermute | solution.py:103
  9.9 1.3 %collective-permute-start = (bf16[16,256]{1,0:T(8,128)(2,1)S(1)}, bf16[16,256]{1,0:T(8,128)(2,1)S(1)}, u32[]{:S(2)}, u32[]{:S(2)}) collective-permute-start(bf16[16,256]{1,0:T(8,128)(2,1)S(1)} %convert_element_type.73), channel_id=1, source_target_pairs={{4,0},{8,4},{12,8},{16,12},{20,16},{24,20},{28,24},{5,1},{9,5},{13... | collective-permute-start | bytes 24584 | tf_op jit(solution)/shard_map/ppermute | solution.py:100
  12.6 0.9 scatter_custom_fusion
  13.7 0.7 copy.54
  14.4 7.1 %all-to-all-start = ((f32[8,1,1280]{2,1,0:T(1,128)}), f32[8,1,1280]{2,1,0:T(1,128)S(1)}, u32[]{:S(2)}, u32[]{:S(2)}) async-start(f32[8,1,1280]{2,1,0:T(1,128)} %copy.54), calls=%async_computation | async-start | bytes 81920 | tf_op jit(solution)/shard_map/all_to_all | solution.py:108
  23.1 3.4 %fusion.12 = f32[16,1,256,1]{2,1,3,0:T(1,128)S(1)} fusion(bf16[16,2,256,256]{3,2,1,0:T(8,128)(2,1)} %param.11, bf16[16,2,256,1]{2,1,0,3:T(2,128)(2,1)S(1)} %fusion.14), kind=kOutput, calls=%fused_computation.29 | convolution fusion | flops 4194304 | bytes 4227072 | tf_op jit(solution)/shard_map/bsij,bsj->bi/dot_general | solution.py:118
  26.5 1.7 %all-to-all-done = f32[8,1,1280]{2,1,0:T(1,128)S(1)} async-done(((f32[8,1,1280]{2,1,0:T(1,128)}), f32[8,1,1280]{2,1,0:T(1,128)S(1)}, u32[]{:S(2)}, u32[]{:S(2)}) %all-to-all-start) | async-done | bytes 40992 | tf_op jit(solution)/shard_map/all_to_all | solution.py:108
  30.0 1.2 %collective-permute-done.2 = f32[5376]{0:T(1024)S(1)} collective-permute-done((f32[5376]{0:T(1024)S(1)}, f32[5376]{0:T(1024)S(1)}, u32[]{:S(2)}, u32[]{:S(2)}) %collective-permute-start.2) | collective-permute-done | bytes 21536 | tf_op jit(solution)/shard_map/ppermute | solution.py:15
  31.2 1.5 %collective-permute-start.3 = (f32[5376]{0:T(1024)S(1)}, f32[5376]{0:T(1024)S(1)}, u32[]{:S(2)}, u32[]{:S(2)}) collective-permute-start(f32[5376]{0:T(1024)S(1)} %add.102), channel_id=1, source_target_pairs={{0,2},{1,3},{2,0},{3,1},{4,6},{5,7},{6,4},{7,5},{8,10},{9,11},{10,... | collective-permute-start | bytes 64520 | tf_op jit(solution)/shard_map/ppermute | solution.py:15
  32.6 2.4 %collective-permute-done.3 = f32[5376]{0:T(1024)S(1)} collective-permute-done((f32[5376]{0:T(1024)S(1)}, f32[5376]{0:T(1024)S(1)}, u32[]{:S(2)}, u32[]{:S(2)}) %collective-permute-start.3) | collective-permute-done | bytes 21536 | tf_op jit(solution)/shard_map/ppermute | solution.py:15
  36.4 10.6 %all_to_all.30 = f32[8,1,4]{2,1,0:T(1,128)S(1)} all-to-all(f32[8,1,4]{2,1,0:T(1,128)S(1)} %broadcast_in_dim.188), channel_id=1, replica_groups=mesh['box'=8,'rep'=4] {'box'}, dimensions={0} | all-to-all | bytes 256 | tf_op jit(solution)/shard_map/all_to_all | solution.py:30
  51.4 1.3 %collective-permute-start.4 = (bf16[16,256]{1,0:T(8,128)(2,1)S(1)}, bf16[16,256]{1,0:T(8,128)(2,1)S(1)}, u32[]{:S(2)}, u32[]{:S(2)}) collective-permute-start(bf16[16,256]{1,0:T(8,128)(2,1)S(1)} %fusion.61), channel_id=1, source_target_pairs={{4,0},{8,4},{12,8},{16,12},{20,16},{24,20},{28,24},{5,1},{9,5},{13... | collective-permute-start | bytes 24584 | tf_op jit(solution)/shard_map/ppermute | solution.py:100
  53.6 0.9 scatter_custom_fusion.1
  54.6 2.8 %fusion.22 = f32[16,1,2,256]{3,1,2,0:T(1,128)S(1)} fusion(bf16[16,2,256,256]{3,2,1,0:T(8,128)(2,1)} %param.11, bf16[16,256,1,1]{1,0,2,3:T(8,128)(2,1)S(1)} %bitcast.134), kind=kOutput, calls=%fused_computation.53 | convolution fusion | flops 4194304 | bytes 4235264 | tf_op jit(solution)/shard_map/bsij,bi->bsj/dot_general | solution.py:77
  57.7 4.5 %collective-permute-start.5 = (f32[16,256]{1,0:T(8,128)S(1)}, f32[16,256]{1,0:T(8,128)S(1)}, u32[]{:S(2)}, u32[]{:S(2)}) collective-permute-start(f32[16,256]{1,0:T(8,128)S(1)} %slice.154), channel_id=1, source_target_pairs={{0,4},{4,8},{8,12},{12,16},{16,20},{20,24},{24,28},{1,5},{5,9},{9,... | collective-permute-start | bytes 49160 | tf_op jit(solution)/shard_map/ppermute | solution.py:103
  63.0 3.3 %all-to-all-start.2 = ((f32[8,1,1280]{2,1,0:T(1,128)}), f32[8,1,1280]{2,1,0:T(1,128)S(1)}, u32[]{:S(2)}, u32[]{:S(2)}) async-start(f32[8,1,1280]{2,1,0:T(1,128)} %copy.57), calls=%async_computation.2 | async-start | bytes 81920 | tf_op jit(solution)/shard_map/all_to_all | solution.py:108
  67.2 3.4 %fusion.10 = f32[16,1,256,1]{2,1,3,0:T(1,128)S(1)} fusion(bf16[16,2,256,256]{3,2,1,0:T(8,128)(2,1)} %param.11, bf16[16,2,256,1]{2,1,0,3:T(2,128)(2,1)S(1)} %fusion.15), kind=kOutput, calls=%fused_computation.26 | convolution fusion | flops 4194304 | bytes 4227072 | tf_op jit(solution)/shard_map/bsij,bsj->bi/dot_general | solution.py:118
  70.6 2.4 %all-to-all-done.2 = f32[8,1,1280]{2,1,0:T(1,128)S(1)} async-done(((f32[8,1,1280]{2,1,0:T(1,128)}), f32[8,1,1280]{2,1,0:T(1,128)S(1)}, u32[]{:S(2)}, u32[]{:S(2)}) %all-to-all-start.2) | async-done | bytes 40992 | tf_op jit(solution)/shard_map/all_to_all | solution.py:108
  74.9 1.2 %collective-permute-done.6 = f32[5376]{0:T(1024)S(1)} collective-permute-done((f32[5376]{0:T(1024)S(1)}, f32[5376]{0:T(1024)S(1)}, u32[]{:S(2)}, u32[]{:S(2)}) %collective-permute-start.6) | collective-permute-done | bytes 21536 | tf_op jit(solution)/shard_map/ppermute | solution.py:15
  76.0 1.5 %collective-permute-start.7 = (f32[5376]{0:T(1024)S(1)}, f32[5376]{0:T(1024)S(1)}, u32[]{:S(2)}, u32[]{:S(2)}) collective-permute-start(f32[5376]{0:T(1024)S(1)} %add.114), channel_id=1, source_target_pairs={{0,2},{1,3},{2,0},{3,1},{4,6},{5,7},{6,4},{7,5},{8,10},{9,11},{10,... | collective-permute-start | bytes 64520 | tf_op jit(solution)/shard_map/ppermute | solution.py:15
  77.5 2.4 %collective-permute-done.7 = f32[5376]{0:T(1024)S(1)} collective-permute-done((f32[5376]{0:T(1024)S(1)}, f32[5376]{0:T(1024)S(1)}, u32[]{:S(2)}, u32[]{:S(2)}) %collective-permute-start.7) | collective-permute-done | bytes 21536 | tf_op jit(solution)/shard_map/ppermute | solution.py:15
  82.3 9.8 %all_to_all.31 = f32[8,1,1]{2,1,0:T(1,128)S(1)} all-to-all(f32[8,1,1]{2,1,0:T(1,128)S(1)} %broadcast_in_dim.192), channel_id=1, replica_groups=mesh['box'=8,'rep'=4] {'box'}, dimensions={0} | all-to-all | bytes 64 | tf_op jit(solution)/shard_map/all_to_all | solution.py:30
  (162 shorter events, 15.8 us)
Async XLA Ops:
  0.6 11.6 %copy-start = (bf16[20,4,64,64]{3,2,1,0:T(8,128)(2,1)S(1)}, bf16[20,4,64,64]{3,2,1,0:T(8,128)(2,1)}, u32[]{:S(2)}) copy-start(bf16[20,4,64,64]{3,2,1,0:T(8,128)(2,1)} %param.16) | copy-start | bytes 1966084
  0.6 9.3 %copy-start.2 = (f32[16,256]{1,0:T(8,128)S(1)}, f32[16,256]{1,0:T(8,128)}, u32[]{:S(2)}) copy-start(f32[16,256]{1,0:T(8,128)} %param.9) | copy-start | bytes 49156
  0.7 3.8 %copy-start.5 = (s32[16,2]{0,1:T(2,128)S(1)}, s32[16,2]{0,1:T(2,128)}, u32[]{:S(2)}) copy-start(s32[16,2]{0,1:T(2,128)} %param.12) | copy-start | bytes 388
  0.7 10.6 %copy-start.1 = (bf16[16,64,256]{2,1,0:T(8,128)(2,1)S(1)}, bf16[16,64,256]{2,1,0:T(8,128)(2,1)}, u32[]{:S(2)}) copy-start(bf16[16,64,256]{2,1,0:T(8,128)(2,1)} %param.13) | copy-start | bytes 1572868
  0.7 10.9 %copy-start.4 = (s32[20,4]{0,1:T(4,128)S(1)}, s32[20,4]{0,1:T(4,128)}, u32[]{:S(2)}) copy-start(s32[20,4]{0,1:T(4,128)} %param.17) | copy-start | bytes 964
  0.7 11.2 %copy-start.7 = (bf16[16,64,64]{2,1,0:T(8,128)(2,1)S(1)}, bf16[16,64,64]{2,1,0:T(8,128)(2,1)}, u32[]{:S(2)}) copy-start(bf16[16,64,64]{2,1,0:T(8,128)(2,1)} %param.14) | copy-start | bytes 393220
  0.7 11.4 %copy-start.6 = (s32[16]{0:T(128)S(1)}, s32[16]{0:T(128)}, u32[]{:S(2)}) copy-start(s32[16]{0:T(128)} %param.15) | copy-start | bytes 196
  5.0 21.4 %collective-permute-start.1 = (f32[16,256]{1,0:T(8,128)S(1)}, f32[16,256]{1,0:T(8,128)S(1)}, u32[]{:S(2)}, u32[]{:S(2)}) collective-permute-start(f32[16,256]{1,0:T(8,128)S(1)} %slice.149), channel_id=1, source_target_pairs={{0,4},{4,8},{8,12},{12,16},{16,20},{20,24},{24,28},{1,5},{5,9},{9,... | collective-permute-start | bytes 49160 | tf_op jit(solution)/shard_map/ppermute | solution.py:103
  9.9 12.4 %collective-permute-start = (bf16[16,256]{1,0:T(8,128)(2,1)S(1)}, bf16[16,256]{1,0:T(8,128)(2,1)S(1)}, u32[]{:S(2)}, u32[]{:S(2)}) collective-permute-start(bf16[16,256]{1,0:T(8,128)(2,1)S(1)} %convert_element_type.73), channel_id=1, source_target_pairs={{4,0},{8,4},{12,8},{16,12},{20,16},{24,20},{28,24},{5,1},{9,5},{13... | collective-permute-start | bytes 24584 | tf_op jit(solution)/shard_map/ppermute | solution.py:100
  13.7 22.5 %copy-start.3 = (f32[16,256]{1,0:T(8,128)S(1)}, f32[16,256]{1,0:T(8,128)}, u32[]{:S(2)}) copy-start(f32[16,256]{1,0:T(8,128)} %param.10) | copy-start | bytes 49156
  14.4 13.8 %all-to-all-start = ((f32[8,1,1280]{2,1,0:T(1,128)}), f32[8,1,1280]{2,1,0:T(1,128)S(1)}, u32[]{:S(2)}, u32[]{:S(2)}) async-start(f32[8,1,1280]{2,1,0:T(1,128)} %copy.54), calls=%async_computation | async-start | bytes 81920 | tf_op jit(solution)/shard_map/all_to_all | solution.py:108
  30.0 1.2 %collective-permute-start.2 = (f32[5376]{0:T(1024)S(1)}, f32[5376]{0:T(1024)S(1)}, u32[]{:S(2)}, u32[]{:S(2)}) collective-permute-start(f32[5376]{0:T(1024)S(1)} %constant_dynamic-update-slice_fusion), channel_id=1, source_target_pairs={{0,1},{1,0},{2,3},{3,2},{4,5},{5,4},{6,7},{7,6},{8,9},{9,8},{10,11... | collective-permute-start | bytes 64520 | tf_op jit(solution)/shard_map/ppermute | solution.py:15
  31.2 3.8 %collective-permute-start.3 = (f32[5376]{0:T(1024)S(1)}, f32[5376]{0:T(1024)S(1)}, u32[]{:S(2)}, u32[]{:S(2)}) collective-permute-start(f32[5376]{0:T(1024)S(1)} %add.102), channel_id=1, source_target_pairs={{0,2},{1,3},{2,0},{3,1},{4,6},{5,7},{6,4},{7,5},{8,10},{9,11},{10,... | collective-permute-start | bytes 64520 | tf_op jit(solution)/shard_map/ppermute | solution.py:15
  51.4 15.1 %collective-permute-start.4 = (bf16[16,256]{1,0:T(8,128)(2,1)S(1)}, bf16[16,256]{1,0:T(8,128)(2,1)S(1)}, u32[]{:S(2)}, u32[]{:S(2)}) collective-permute-start(bf16[16,256]{1,0:T(8,128)(2,1)S(1)} %fusion.61), channel_id=1, source_target_pairs={{4,0},{8,4},{12,8},{16,12},{20,16},{24,20},{28,24},{5,1},{9,5},{13... | collective-permute-start | bytes 24584 | tf_op jit(solution)/shard_map/ppermute | solution.py:100
  57.7 12.9 %collective-permute-start.5 = (f32[16,256]{1,0:T(8,128)S(1)}, f32[16,256]{1,0:T(8,128)S(1)}, u32[]{:S(2)}, u32[]{:S(2)}) collective-permute-start(f32[16,256]{1,0:T(8,128)S(1)} %slice.154), channel_id=1, source_target_pairs={{0,4},{4,8},{8,12},{12,16},{16,20},{20,24},{24,28},{1,5},{5,9},{9,... | collective-permute-start | bytes 49160 | tf_op jit(solution)/shard_map/ppermute | solution.py:103
  63.0 10.0 %all-to-all-start.2 = ((f32[8,1,1280]{2,1,0:T(1,128)}), f32[8,1,1280]{2,1,0:T(1,128)S(1)}, u32[]{:S(2)}, u32[]{:S(2)}) async-start(f32[8,1,1280]{2,1,0:T(1,128)} %copy.57), calls=%async_computation.2 | async-start | bytes 81920 | tf_op jit(solution)/shard_map/all_to_all | solution.py:108
  74.8 1.2 %collective-permute-start.6 = (f32[5376]{0:T(1024)S(1)}, f32[5376]{0:T(1024)S(1)}, u32[]{:S(2)}, u32[]{:S(2)}) collective-permute-start(f32[5376]{0:T(1024)S(1)} %constant_dynamic-update-slice_fusion.1), channel_id=1, source_target_pairs={{0,1},{1,0},{2,3},{3,2},{4,5},{5,4},{6,7},{7,6},{8,9},{9,8},{10,11... | collective-permute-start | bytes 64520 | tf_op jit(solution)/shard_map/ppermute | solution.py:15
  76.0 3.8 %collective-permute-start.7 = (f32[5376]{0:T(1024)S(1)}, f32[5376]{0:T(1024)S(1)}, u32[]{:S(2)}, u32[]{:S(2)}) collective-permute-start(f32[5376]{0:T(1024)S(1)} %add.114), channel_id=1, source_target_pairs={{0,2},{1,3},{2,0},{3,1},{4,6},{5,7},{6,4},{7,5},{8,10},{9,11},{10,... | collective-permute-start | bytes 64520 | tf_op jit(solution)/shard_map/ppermute | solution.py:15

commit v4 on v3

--- a/solution.py
+++ b/solution.py
@@ -24,11 +24,12 @@
     return jnp.sum(ordered, axis=0)
 
 
-def box_sum(values):
+def box_sum(values, width):
     count = lax.axis_size("box")
     sent = jnp.broadcast_to(values[None, :], (count, values.shape[0]))
     got = lax.all_to_all(sent, "box", 0, 0, tiled=True)
-    return jnp.sum(got, axis=0)
+    wide = lax.optimization_barrier(jnp.broadcast_to(got[:, :, None], got.shape + (width,)))
+    return jnp.sum(wide, axis=0)
 
 
 def local(
@@ -141,17 +142,17 @@
             partials.append(targets * targets)
         if iteration + 1 < ITERS:
             partials += [residual * image_vec, image_vec * image_vec]
-        sums = box_sum(jnp.sum(jnp.stack(partials), axis=(1, 2)))
+        sums = box_sum(jnp.sum(jnp.stack(partials), axis=(1, 2)), leaf)
         curvature = sums[0:1]
         if norm_now is None:
             norm_now = sums[1:2]
         step_size = norm_now / curvature
-        weights = weights + step_size.reshape(1, 1) * direction
-        residual = residual - step_size.reshape(1, 1) * image_vec
+        weights = weights + step_size * direction
+        residual = residual - step_size * image_vec
         if iteration + 1 < ITERS:
             cross, image_square = sums[-2:-1], sums[-1:]
             norm_next = norm_now - 2.0 * step_size * cross + step_size * step_size * image_square
-            direction = residual + (norm_next / norm_now).reshape(1, 1) * direction
+            direction = residual + (norm_next / norm_now) * direction
             norm_now = norm_next
     return (weights, residual)
 

time: 94.7 us -> 89.3 us (0.943)
  between operations: 5.69 us -> 1.32 us
  transfers between devices with their start and end apart: 10 -> 10, of which waited for: 6 -> 6; matrix products, arithmetic and copies ran while one was open for 19% -> 20% of each run, Pallas kernels for 0% -> 0%
where the time goes in v4:
time: 89.3 us; the launch traced here: 88.8 us
  starting transfers between devices  25.6 us (29%)
  blocking collectives  20.4 us (23%)
  matrix products  16 us (18%)
  waiting for transfers between devices  11 us (12%)
  local copies, waits for them, and re-layouts  8.69 us (10%)
  other arithmetic  5.73 us (6%)
  between operations  1.32 us (1%)
    all_to_all x2, blocking collectives, box_sum(): got = lax.all_to_all(sent, 'box', 0, 0, tiled=True)  20.4 us
    all_to_all x2, starting transfers between devices, local(): lax.all_to_all(far_send.reshape(box_devices, far_size), 'box', 0, 0, tile...  10.4 us
    ppermute x2, starting transfers between devices, local(): lax.ppermute(landed[box_count:], 'box', [(i, i + 1) for i in range(box_de...  9.45 us
    ppermute x4, waiting for transfers between devices, rep_sum(): vector = vector + lax.ppermute(vector, 'rep', pairs)  6.93 us
    dot_general x2, matrix products, local(): jnp.einsum('bsij,bsj->bi', near_tiles, near_in, preferred_element_type=jn...  6.73 us
    dot_general x2, matrix products, local(): jnp.einsum('bsij,bi->bsj', near_tiles, rounded, preferred_element_type=jn...  5.66 us
    all_to_all x2, waiting for transfers between devices, local(): lax.all_to_all(far_send.reshape(box_devices, far_size), 'box', 0, 0, tile...  4.1 us
    ppermute x4, starting transfers between devices, rep_sum(): vector = vector + lax.ppermute(vector, 'rep', pairs)  3.17 us
  transfers between devices with their start and end apart: 10, of which 6 were waited for; matrix products, arithmetic and copies ran while one was open for 20% of the time, Pallas kernels for 0%

profile of v4, /device:TPU:0, one launch (start us, length us, event | category | flops | bytes accessed | tf_op | source)
XLA Modules:
  0.0 88.8 jit_solution(354044366526189851)
XLA Ops:
  0.7 0.9 convert_bitcast_fusion.5
  1.6 2.8 %fusion.26 = f32[16,1,2,256]{3,1,2,0:T(1,128)S(1)} fusion(bf16[16,2,256,256]{3,2,1,0:T(8,128)(2,1)} %param.11, bf16[16,256,1,1]{1,0,2,3:T(8,128)(2,1)S(1)} %convert_bitcast_fusion.5), kind=kOutput, calls=%fused_computation.57 | convolution fusion | flops 4194304 | bytes 4235264 | tf_op jit(solution)/shard_map/bsij,bi->bsj/dot_general | solution.py:78
  5.0 4.9 %collective-permute-start.1 = (f32[16,256]{1,0:T(8,128)S(1)}, f32[16,256]{1,0:T(8,128)S(1)}, u32[]{:S(2)}, u32[]{:S(2)}) collective-permute-start(f32[16,256]{1,0:T(8,128)S(1)} %slice.149), channel_id=1, source_target_pairs={{0,4},{4,8},{8,12},{12,16},{16,20},{20,24},{24,28},{1,5},{5,9},{9,... | collective-permute-start | bytes 49160 | tf_op jit(solution)/shard_map/ppermute | solution.py:104
  9.9 1.3 %collective-permute-start = (bf16[16,256]{1,0:T(8,128)(2,1)S(1)}, bf16[16,256]{1,0:T(8,128)(2,1)S(1)}, u32[]{:S(2)}, u32[]{:S(2)}) collective-permute-start(bf16[16,256]{1,0:T(8,128)(2,1)S(1)} %convert_element_type.73), channel_id=1, source_target_pairs={{4,0},{8,4},{12,8},{16,12},{20,16},{24,20},{28,24},{5,1},{9,5},{13... | collective-permute-start | bytes 24584 | tf_op jit(solution)/shard_map/ppermute | solution.py:101
  12.6 0.9 scatter_custom_fusion
  13.7 0.7 copy.48
  14.4 7.1 %all-to-all-start = ((f32[8,1,1280]{2,1,0:T(1,128)}), f32[8,1,1280]{2,1,0:T(1,128)S(1)}, u32[]{:S(2)}, u32[]{:S(2)}) async-start(f32[8,1,1280]{2,1,0:T(1,128)} %copy.48), calls=%async_computation | async-start | bytes 81920 | tf_op jit(solution)/shard_map/all_to_all | solution.py:109
  23.1 3.4 %fusion.12 = f32[16,1,256,1]{2,1,3,0:T(1,128)S(1)} fusion(bf16[16,2,256,256]{3,2,1,0:T(8,128)(2,1)} %param.11, bf16[16,2,256,1]{2,1,0,3:T(2,128)(2,1)S(1)} %fusion.14), kind=kOutput, calls=%fused_computation.29 | convolution fusion | flops 4194304 | bytes 4227072 | tf_op jit(solution)/shard_map/bsij,bsj->bi/dot_general | solution.py:119
  26.5 1.7 %all-to-all-done = f32[8,1,1280]{2,1,0:T(1,128)S(1)} async-done(((f32[8,1,1280]{2,1,0:T(1,128)}), f32[8,1,1280]{2,1,0:T(1,128)S(1)}, u32[]{:S(2)}, u32[]{:S(2)}) %all-to-all-start) | async-done | bytes 40992 | tf_op jit(solution)/shard_map/all_to_all | solution.py:109
  30.0 1.2 %collective-permute-done.2 = f32[5376]{0:T(1024)S(1)} collective-permute-done((f32[5376]{0:T(1024)S(1)}, f32[5376]{0:T(1024)S(1)}, u32[]{:S(2)}, u32[]{:S(2)}) %collective-permute-start.2) | collective-permute-done | bytes 21536 | tf_op jit(solution)/shard_map/ppermute | solution.py:15
  31.2 1.6 %collective-permute-start.3 = (f32[5376]{0:T(1024)S(1)}, f32[5376]{0:T(1024)S(1)}, u32[]{:S(2)}, u32[]{:S(2)}) collective-permute-start(f32[5376]{0:T(1024)S(1)} %add.102), channel_id=1, source_target_pairs={{0,2},{1,3},{2,0},{3,1},{4,6},{5,7},{6,4},{7,5},{8,10},{9,11},{10,... | collective-permute-start | bytes 64520 | tf_op jit(solution)/shard_map/ppermute | solution.py:15
  32.7 2.3 %collective-permute-done.3 = f32[5376]{0:T(1024)S(1)} collective-permute-done((f32[5376]{0:T(1024)S(1)}, f32[5376]{0:T(1024)S(1)}, u32[]{:S(2)}, u32[]{:S(2)}) %collective-permute-start.3) | collective-permute-done | bytes 21536 | tf_op jit(solution)/shard_map/ppermute | solution.py:15
  36.4 10.6 %all_to_all.30 = f32[8,1,4]{2,1,0:T(1,128)S(1)} all-to-all(f32[8,1,4]{2,1,0:T(1,128)S(1)} %broadcast_in_dim.204), channel_id=1, replica_groups=mesh['box'=8,'rep'=4] {'box'}, dimensions={0} | all-to-all | bytes 256 | tf_op jit(solution)/shard_map/all_to_all | solution.py:30
  47.1 1.3 %collective-permute-start.4 = (bf16[16,256]{1,0:T(8,128)(2,1)S(1)}, bf16[16,256]{1,0:T(8,128)(2,1)S(1)}, u32[]{:S(2)}, u32[]{:S(2)}) collective-permute-start(bf16[16,256]{1,0:T(8,128)(2,1)S(1)} %fusion.61), channel_id=1, source_target_pairs={{4,0},{8,4},{12,8},{16,12},{20,16},{24,20},{28,24},{5,1},{9,5},{13... | collective-permute-start | bytes 24584 | tf_op jit(solution)/shard_map/ppermute | solution.py:101
  49.4 0.9 scatter_custom_fusion.1
  50.3 2.8 %fusion.22 = f32[16,1,2,256]{3,1,2,0:T(1,128)S(1)} fusion(bf16[16,2,256,256]{3,2,1,0:T(8,128)(2,1)} %param.11, bf16[16,256,1,1]{1,0,2,3:T(8,128)(2,1)S(1)} %bitcast.135), kind=kOutput, calls=%fused_computation.53 | convolution fusion | flops 4194304 | bytes 4235264 | tf_op jit(solution)/shard_map/bsij,bi->bsj/dot_general | solution.py:78
  53.4 4.6 %collective-permute-start.5 = (f32[16,256]{1,0:T(8,128)S(1)}, f32[16,256]{1,0:T(8,128)S(1)}, u32[]{:S(2)}, u32[]{:S(2)}) collective-permute-start(f32[16,256]{1,0:T(8,128)S(1)} %slice.158), channel_id=1, source_target_pairs={{0,4},{4,8},{8,12},{12,16},{16,20},{20,24},{24,28},{1,5},{5,9},{9,... | collective-permute-start | bytes 49160 | tf_op jit(solution)/shard_map/ppermute | solution.py:104
  58.8 3.3 %all-to-all-start.2 = ((f32[8,1,1280]{2,1,0:T(1,128)}), f32[8,1,1280]{2,1,0:T(1,128)S(1)}, u32[]{:S(2)}, u32[]{:S(2)}) async-start(f32[8,1,1280]{2,1,0:T(1,128)} %copy.52), calls=%async_computation.2 | async-start | bytes 81920 | tf_op jit(solution)/shard_map/all_to_all | solution.py:109
  63.0 3.4 %fusion.10 = f32[16,1,256,1]{2,1,3,0:T(1,128)S(1)} fusion(bf16[16,2,256,256]{3,2,1,0:T(8,128)(2,1)} %param.11, bf16[16,2,256,1]{2,1,0,3:T(2,128)(2,1)S(1)} %fusion.15), kind=kOutput, calls=%fused_computation.26 | convolution fusion | flops 4194304 | bytes 4227072 | tf_op jit(solution)/shard_map/bsij,bsj->bi/dot_general | solution.py:119
  66.4 2.4 %all-to-all-done.2 = f32[8,1,1280]{2,1,0:T(1,128)S(1)} async-done(((f32[8,1,1280]{2,1,0:T(1,128)}), f32[8,1,1280]{2,1,0:T(1,128)S(1)}, u32[]{:S(2)}, u32[]{:S(2)}) %all-to-all-start.2) | async-done | bytes 40992 | tf_op jit(solution)/shard_map/all_to_all | solution.py:109
  70.6 1.2 %collective-permute-done.6 = f32[5376]{0:T(1024)S(1)} collective-permute-done((f32[5376]{0:T(1024)S(1)}, f32[5376]{0:T(1024)S(1)}, u32[]{:S(2)}, u32[]{:S(2)}) %collective-permute-start.6) | collective-permute-done | bytes 21536 | tf_op jit(solution)/shard_map/ppermute | solution.py:15
  71.8 1.5 %collective-permute-start.7 = (f32[5376]{0:T(1024)S(1)}, f32[5376]{0:T(1024)S(1)}, u32[]{:S(2)}, u32[]{:S(2)}) collective-permute-start(f32[5376]{0:T(1024)S(1)} %add.114), channel_id=1, source_target_pairs={{0,2},{1,3},{2,0},{3,1},{4,6},{5,7},{6,4},{7,5},{8,10},{9,11},{10,... | collective-permute-start | bytes 64520 | tf_op jit(solution)/shard_map/ppermute | solution.py:15
  73.4 2.3 %collective-permute-done.7 = f32[5376]{0:T(1024)S(1)} collective-permute-done((f32[5376]{0:T(1024)S(1)}, f32[5376]{0:T(1024)S(1)}, u32[]{:S(2)}, u32[]{:S(2)}) %collective-permute-start.7) | collective-permute-done | bytes 21536 | tf_op jit(solution)/shard_map/ppermute | solution.py:15
  78.1 9.8 %all_to_all.31 = f32[8,1,1]{2,1,0:T(1,128)S(1)} all-to-all(f32[8,1,1]{2,1,0:T(1,128)S(1)} %broadcast_in_dim.210), channel_id=1, replica_groups=mesh['box'=8,'rep'=4] {'box'}, dimensions={0} | all-to-all | bytes 64 | tf_op jit(solution)/shard_map/all_to_all | solution.py:30
  (166 shorter events, 14.9 us)
Async XLA Ops:
  0.6 11.6 %copy-start = (bf16[20,4,64,64]{3,2,1,0:T(8,128)(2,1)S(1)}, bf16[20,4,64,64]{3,2,1,0:T(8,128)(2,1)}, u32[]{:S(2)}) copy-start(bf16[20,4,64,64]{3,2,1,0:T(8,128)(2,1)} %param.16) | copy-start | bytes 1966084
  0.6 9.3 %copy-start.2 = (f32[16,256]{1,0:T(8,128)S(1)}, f32[16,256]{1,0:T(8,128)}, u32[]{:S(2)}) copy-start(f32[16,256]{1,0:T(8,128)} %param.9) | copy-start | bytes 49156
  0.7 3.8 %copy-start.5 = (s32[16,2]{0,1:T(2,128)S(1)}, s32[16,2]{0,1:T(2,128)}, u32[]{:S(2)}) copy-start(s32[16,2]{0,1:T(2,128)} %param.12) | copy-start | bytes 388
  0.7 10.6 %copy-start.1 = (bf16[16,64,256]{2,1,0:T(8,128)(2,1)S(1)}, bf16[16,64,256]{2,1,0:T(8,128)(2,1)}, u32[]{:S(2)}) copy-start(bf16[16,64,256]{2,1,0:T(8,128)(2,1)} %param.13) | copy-start | bytes 1572868
  0.7 10.9 %copy-start.4 = (s32[20,4]{0,1:T(4,128)S(1)}, s32[20,4]{0,1:T(4,128)}, u32[]{:S(2)}) copy-start(s32[20,4]{0,1:T(4,128)} %param.17) | copy-start | bytes 964
  0.7 11.2 %copy-start.7 = (bf16[16,64,64]{2,1,0:T(8,128)(2,1)S(1)}, bf16[16,64,64]{2,1,0:T(8,128)(2,1)}, u32[]{:S(2)}) copy-start(bf16[16,64,64]{2,1,0:T(8,128)(2,1)} %param.14) | copy-start | bytes 393220
  0.7 11.4 %copy-start.6 = (s32[16]{0:T(128)S(1)}, s32[16]{0:T(128)}, u32[]{:S(2)}) copy-start(s32[16]{0:T(128)} %param.15) | copy-start | bytes 196
  5.0 21.4 %collective-permute-start.1 = (f32[16,256]{1,0:T(8,128)S(1)}, f32[16,256]{1,0:T(8,128)S(1)}, u32[]{:S(2)}, u32[]{:S(2)}) collective-permute-start(f32[16,256]{1,0:T(8,128)S(1)} %slice.149), channel_id=1, source_target_pairs={{0,4},{4,8},{8,12},{12,16},{16,20},{20,24},{24,28},{1,5},{5,9},{9,... | collective-permute-start | bytes 49160 | tf_op jit(solution)/shard_map/ppermute | solution.py:104
  9.9 12.4 %collective-permute-start = (bf16[16,256]{1,0:T(8,128)(2,1)S(1)}, bf16[16,256]{1,0:T(8,128)(2,1)S(1)}, u32[]{:S(2)}, u32[]{:S(2)}) collective-permute-start(bf16[16,256]{1,0:T(8,128)(2,1)S(1)} %convert_element_type.73), channel_id=1, source_target_pairs={{4,0},{8,4},{12,8},{16,12},{20,16},{24,20},{28,24},{5,1},{9,5},{13... | collective-permute-start | bytes 24584 | tf_op jit(solution)/shard_map/ppermute | solution.py:101
  13.7 22.5 %copy-start.3 = (f32[16,256]{1,0:T(8,128)S(1)}, f32[16,256]{1,0:T(8,128)}, u32[]{:S(2)}) copy-start(f32[16,256]{1,0:T(8,128)} %param.10) | copy-start | bytes 49156
  14.4 13.8 %all-to-all-start = ((f32[8,1,1280]{2,1,0:T(1,128)}), f32[8,1,1280]{2,1,0:T(1,128)S(1)}, u32[]{:S(2)}, u32[]{:S(2)}) async-start(f32[8,1,1280]{2,1,0:T(1,128)} %copy.48), calls=%async_computation | async-start | bytes 81920 | tf_op jit(solution)/shard_map/all_to_all | solution.py:109
  29.9 1.2 %collective-permute-start.2 = (f32[5376]{0:T(1024)S(1)}, f32[5376]{0:T(1024)S(1)}, u32[]{:S(2)}, u32[]{:S(2)}) collective-permute-start(f32[5376]{0:T(1024)S(1)} %constant_dynamic-update-slice_fusion), channel_id=1, source_target_pairs={{0,1},{1,0},{2,3},{3,2},{4,5},{5,4},{6,7},{7,6},{8,9},{9,8},{10,11... | collective-permute-start | bytes 64520 | tf_op jit(solution)/shard_map/ppermute | solution.py:15
  31.2 3.8 %collective-permute-start.3 = (f32[5376]{0:T(1024)S(1)}, f32[5376]{0:T(1024)S(1)}, u32[]{:S(2)}, u32[]{:S(2)}) collective-permute-start(f32[5376]{0:T(1024)S(1)} %add.102), channel_id=1, source_target_pairs={{0,2},{1,3},{2,0},{3,1},{4,6},{5,7},{6,4},{7,5},{8,10},{9,11},{10,... | collective-permute-start | bytes 64520 | tf_op jit(solution)/shard_map/ppermute | solution.py:15
  47.1 15.1 %collective-permute-start.4 = (bf16[16,256]{1,0:T(8,128)(2,1)S(1)}, bf16[16,256]{1,0:T(8,128)(2,1)S(1)}, u32[]{:S(2)}, u32[]{:S(2)}) collective-permute-start(bf16[16,256]{1,0:T(8,128)(2,1)S(1)} %fusion.61), channel_id=1, source_target_pairs={{4,0},{8,4},{12,8},{16,12},{20,16},{24,20},{28,24},{5,1},{9,5},{13... | collective-permute-start | bytes 24584 | tf_op jit(solution)/shard_map/ppermute | solution.py:101
  53.4 12.9 %collective-permute-start.5 = (f32[16,256]{1,0:T(8,128)S(1)}, f32[16,256]{1,0:T(8,128)S(1)}, u32[]{:S(2)}, u32[]{:S(2)}) collective-permute-start(f32[16,256]{1,0:T(8,128)S(1)} %slice.158), channel_id=1, source_target_pairs={{0,4},{4,8},{8,12},{12,16},{16,20},{20,24},{24,28},{1,5},{5,9},{9,... | collective-permute-start | bytes 49160 | tf_op jit(solution)/shard_map/ppermute | solution.py:104
  58.8 10.0 %all-to-all-start.2 = ((f32[8,1,1280]{2,1,0:T(1,128)}), f32[8,1,1280]{2,1,0:T(1,128)S(1)}, u32[]{:S(2)}, u32[]{:S(2)}) async-start(f32[8,1,1280]{2,1,0:T(1,128)} %copy.52), calls=%async_computation.2 | async-start | bytes 81920 | tf_op jit(solution)/shard_map/all_to_all | solution.py:109
  70.6 1.2 %collective-permute-start.6 = (f32[5376]{0:T(1024)S(1)}, f32[5376]{0:T(1024)S(1)}, u32[]{:S(2)}, u32[]{:S(2)}) collective-permute-start(f32[5376]{0:T(1024)S(1)} %constant_dynamic-update-slice_fusion.1), channel_id=1, source_target_pairs={{0,1},{1,0},{2,3},{3,2},{4,5},{5,4},{6,7},{7,6},{8,9},{9,8},{10,11... | collective-permute-start | bytes 64520 | tf_op jit(solution)/shard_map/ppermute | solution.py:15
  71.8 3.8 %collective-permute-start.7 = (f32[5376]{0:T(1024)S(1)}, f32[5376]{0:T(1024)S(1)}, u32[]{:S(2)}, u32[]{:S(2)}) collective-permute-start(f32[5376]{0:T(1024)S(1)} %add.114), channel_id=1, source_target_pairs={{0,2},{1,3},{2,0},{3,1},{4,6},{5,7},{6,4},{7,5},{8,10},{9,11},{10,... | collective-permute-start | bytes 64520 | tf_op jit(solution)/shard_map/ppermute | solution.py:15

commit v5 on v4

--- a/solution.py
+++ b/solution.py
@@ -75,12 +75,6 @@
     norm_now = None
     for iteration in range(ITERS):
         rounded = direction.astype(jnp.bfloat16)
-        mirrored = jnp.einsum(
-            "bsij,bi->bsj", near_tiles, rounded, preferred_element_type=jnp.float32
-        )
-        landed = jnp.dot(
-            near_onehot, mirrored.reshape(-1, mirrored.shape[2]), precision=lax.Precision.HIGHEST
-        )
         leaf_coef = jnp.einsum(
             "brl,bl->br", leaf_bases, rounded, preferred_element_type=jnp.float32
         ).astype(jnp.bfloat16)
@@ -101,11 +95,18 @@
         following = lax.ppermute(
             rounded, "box", [(i, i - 1) for i in range(1, box_devices)]
         )
+        coef_wide = node_coef.astype(jnp.float32)
+        far_send = jnp.where(below, coef_wide[None], spread)
+        far_send, mirror_field = lax.optimization_barrier((far_send, rounded))
+        mirrored = jnp.einsum(
+            "bsij,bi->bsj", near_tiles, mirror_field, preferred_element_type=jnp.float32
+        )
+        landed = jnp.dot(
+            near_onehot, mirrored.reshape(-1, mirrored.shape[2]), precision=lax.Precision.HIGHEST
+        )
         arrived = lax.ppermute(
             landed[box_count:], "box", [(i, i + 1) for i in range(box_devices - 1)]
         )
-        coef_wide = node_coef.astype(jnp.float32)
-        far_send = jnp.where(below, coef_wide[None], spread)
         got_far = lax.all_to_all(
             far_send.reshape(box_devices, far_size), "box", 0, 0, tiled=True
         ).reshape(box_devices, node_count, rank_width)

time: 89.3 us -> 90.9 us (1.018)
  waiting for transfers between devices: 11 us -> 6.92 us
  other arithmetic: 5.73 us -> 7.8 us
  matrix products: 16 us -> 18 us
  blocking collectives: 20.4 us -> 21.6 us
    all_to_all x2, waiting for transfers between devices: 4.1 us -> 0.01 us  [local(): lax.all_to_all(far_send.reshape(box_devices, far_size), 'box', 0, 0, tile...]
    all_to_all x2, starting transfers between devices: 10.4 us -> 12.5 us  [local(): lax.all_to_all(far_send.reshape(box_devices, far_size), 'box', 0, 0, tile...]
    ppermute x2, starting transfers between devices: 9.45 us -> 7.85 us  [local(): lax.ppermute(landed[box_count:], 'box', [(i, i + 1) for i in range(box_de...]
    all_to_all x0 -> x2, local copies, waits for them, and re-layouts: none -> 1.44 us  [local(): lax.all_to_all(far_send.reshape(box_devices, far_size), 'box', 0, 0, tile...]
    select_n x2 -> x0, local copies, waits for them, and re-layouts: 1.31 us -> none  [local(): far_send = jnp.where(below, coef_wide[None], spread)]
    all_to_all x2, blocking collectives: 20.4 us -> 21.6 us  [box_sum(): got = lax.all_to_all(sent, 'box', 0, 0, tiled=True)]
    dot_general x2, matrix products: 0.47 us -> 1.51 us  [local(): jnp.einsum('brl,bl->br', leaf_bases, rounded, preferred_element_type=jnp....]
    dot_general x2, matrix products: 0.36 us -> 1.3 us  [local(): jnp.einsum('brq,br->bq', transfer, leaf_coef, preferred_element_type=jnp....]
  transfers between devices with their start and end apart: 10 -> 10, of which waited for: 6 -> 4; matrix products, arithmetic and copies ran while one was open for 20% -> 26% of each run, Pallas kernels for 0% -> 0%
where the time goes in v5:
time: 90.9 us; the launch traced here: 90.2 us
  starting transfers between devices  26.1 us (29%)
  blocking collectives  21.6 us (24%)
  matrix products  18 us (20%)
  local copies, waits for them, and re-layouts  8.5 us (9%)
  other arithmetic  7.8 us (9%)
  waiting for transfers between devices  6.92 us (8%)
  between operations  1.25 us (1%)
    all_to_all x2, blocking collectives, box_sum(): got = lax.all_to_all(sent, 'box', 0, 0, tiled=True)  21.6 us
    all_to_all x2, starting transfers between devices, local(): lax.all_to_all(far_send.reshape(box_devices, far_size), 'box', 0, 0, tile...  12.5 us
    ppermute x2, starting transfers between devices, local(): lax.ppermute(landed[box_count:], 'box', [(i, i + 1) for i in range(box_de...  7.85 us
    ppermute x4, waiting for transfers between devices, rep_sum(): vector = vector + lax.ppermute(vector, 'rep', pairs)  6.9 us
    dot_general x2, matrix products, local(): jnp.einsum('bsij,bsj->bi', near_tiles, near_in, preferred_element_type=jn...  6.73 us
    dot_general x2, matrix products, local(): jnp.einsum('bsij,bi->bsj', near_tiles, mirror_field, preferred_element_ty...  5.67 us
    ppermute x4, starting transfers between devices, rep_sum(): vector = vector + lax.ppermute(vector, 'rep', pairs)  3.13 us
    ppermute x2, starting transfers between devices, local(): lax.ppermute(rounded, 'box', [(i, i - 1) for i in range(1, box_devices)])  2.58 us
  transfers between devices with their start and end apart: 10, of which 4 were waited for; matrix products, arithmetic and copies ran while one was open for 26% of the time, Pallas kernels for 0%

profile of v5, /device:TPU:0, one launch (start us, length us, event | category | flops | bytes accessed | tf_op | source)
XLA Modules:
  0.0 90.2 jit_solution(8381937095139467104)
XLA Ops:
  0.7 0.8 convert_element_type.61
  1.5 1.3 %collective-permute-start = (bf16[16,256]{1,0:T(8,128)(2,1)S(1)}, bf16[16,256]{1,0:T(8,128)(2,1)S(1)}, u32[]{:S(2)}, u32[]{:S(2)}) collective-permute-start(bf16[16,256]{1,0:T(8,128)(2,1)S(1)} %convert_element_type.61), channel_id=1, source_target_pairs={{4,0},{8,4},{12,8},{16,12},{20,16},{24,20},{28,24},{5,1},{9,5},{13... | collective-permute-start | bytes 24584 | tf_op jit(solution)/shard_map/ppermute | solution.py:95
  2.8 0.7 convert_bitcast_fusion.2
  3.5 1.3 %fusion.26 = f32[16,1,64]{2,1,0:T(1,128)S(1)} fusion(bf16[16,64,256]{2,1,0:T(8,128)(2,1)} %param.13, bf16[16,256,1]{1,0,2:T(8,128)(2,1)S(1)} %convert_bitcast_fusion.2), kind=kOutput, calls=%fused_computation.57 | convolution fusion | flops 524288 | bytes 536576 | tf_op jit(solution)/shard_map/brl,bl->br/dot_general | solution.py:78
  6.5 1.1 %fusion.49 = f32[16,1,64]{2,1,0:T(1,128)S(1)} fusion(bf16[16,64,64]{2,1,0:T(8,128)(2,1)} %param.14, bf16[16,64,1]{1,0,2:T(8,128)(2,1)S(1)} %convert_bitcast_fusion.1), kind=kOutput, calls=%fused_computation.89 | convolution fusion | flops 131072 | bytes 137216 | tf_op jit(solution)/shard_map/brq,br->bq/dot_general | solution.py:81
  8.1 0.9 scatter_custom_fusion
  9.8 8.5 %all-to-all-start = ((f32[8,1,1280]{2,1,0:T(1,128)}), f32[8,1,1280]{2,1,0:T(1,128)S(1)}, u32[]{:S(2)}, u32[]{:S(2)}) async-start(f32[8,1,1280]{2,1,0:T(1,128)} %all_to_all.32), calls=%async_computation | async-start | bytes 81920 | tf_op jit(solution)/shard_map/all_to_all | solution.py:110
  18.3 2.8 %fusion.24 = f32[16,1,2,256]{3,1,2,0:T(1,128)S(1)} fusion(bf16[16,2,256,256]{3,2,1,0:T(8,128)(2,1)} %param.11, bf16[16,256,1,1]{1,0,2,3:T(8,128)(2,1)S(1)} %bitcast.127), kind=kOutput, calls=%fused_computation.55 | convolution fusion | flops 4194304 | bytes 4235264 | tf_op jit(solution)/shard_map/bsij,bi->bsj/dot_general | solution.py:101
  21.8 3.9 %collective-permute-start.1 = (f32[16,256]{1,0:T(8,128)S(1)}, f32[16,256]{1,0:T(8,128)S(1)}, u32[]{:S(2)}, u32[]{:S(2)}) collective-permute-start(f32[16,256]{1,0:T(8,128)S(1)} %slice.149), channel_id=1, source_target_pairs={{0,4},{4,8},{8,12},{12,16},{16,20},{20,24},{24,28},{1,5},{5,9},{9,... | collective-permute-start | bytes 49160 | tf_op jit(solution)/shard_map/ppermute | solution.py:107
  27.4 3.4 %fusion.12 = f32[16,1,256,1]{2,1,3,0:T(1,128)S(1)} fusion(bf16[16,2,256,256]{3,2,1,0:T(8,128)(2,1)} %param.11, bf16[16,2,256,1]{2,1,0,3:T(2,128)(2,1)S(1)} %fusion.14), kind=kOutput, calls=%fused_computation.31 | convolution fusion | flops 4194304 | bytes 4227072 | tf_op jit(solution)/shard_map/bsij,bsj->bi/dot_general | solution.py:120
  32.6 1.2 %collective-permute-done.2 = f32[5376]{0:T(1024)S(1)} collective-permute-done((f32[5376]{0:T(1024)S(1)}, f32[5376]{0:T(1024)S(1)}, u32[]{:S(2)}, u32[]{:S(2)}) %collective-permute-start.2) | collective-permute-done | bytes 21536 | tf_op jit(solution)/shard_map/ppermute | solution.py:15
  33.8 1.5 %collective-permute-start.3 = (f32[5376]{0:T(1024)S(1)}, f32[5376]{0:T(1024)S(1)}, u32[]{:S(2)}, u32[]{:S(2)}) collective-permute-start(f32[5376]{0:T(1024)S(1)} %add.102), channel_id=1, source_target_pairs={{0,2},{1,3},{2,0},{3,1},{4,6},{5,7},{6,4},{7,5},{8,10},{9,11},{10,... | collective-permute-start | bytes 64520 | tf_op jit(solution)/shard_map/ppermute | solution.py:15
  35.4 2.3 %collective-permute-done.3 = f32[5376]{0:T(1024)S(1)} collective-permute-done((f32[5376]{0:T(1024)S(1)}, f32[5376]{0:T(1024)S(1)}, u32[]{:S(2)}, u32[]{:S(2)}) %collective-permute-start.3) | collective-permute-done | bytes 21536 | tf_op jit(solution)/shard_map/ppermute | solution.py:15
  39.0 10.8 %all_to_all.38 = f32[8,1,4]{2,1,0:T(1,128)S(1)} all-to-all(f32[8,1,4]{2,1,0:T(1,128)S(1)} %broadcast_in_dim.199), channel_id=1, replica_groups=mesh['box'=8,'rep'=4] {'box'}, dimensions={0} | all-to-all | bytes 256 | tf_op jit(solution)/shard_map/all_to_all | solution.py:30
  50.2 1.3 %collective-permute-start.4 = (bf16[16,256]{1,0:T(8,128)(2,1)S(1)}, bf16[16,256]{1,0:T(8,128)(2,1)S(1)}, u32[]{:S(2)}, u32[]{:S(2)}) collective-permute-start(bf16[16,256]{1,0:T(8,128)(2,1)S(1)} %fusion.61), channel_id=1, source_target_pairs={{4,0},{8,4},{12,8},{16,12},{20,16},{24,20},{28,24},{5,1},{9,5},{13... | collective-permute-start | bytes 24584 | tf_op jit(solution)/shard_map/ppermute | solution.py:95
  52.2 0.9 scatter_custom_fusion.1
  53.9 4.0 %all-to-all-start.2 = ((f32[8,1,1280]{2,1,0:T(1,128)}), f32[8,1,1280]{2,1,0:T(1,128)S(1)}, u32[]{:S(2)}, u32[]{:S(2)}) async-start(f32[8,1,1280]{2,1,0:T(1,128)} %all_to_all.33), calls=%async_computation.2 | async-start | bytes 81920 | tf_op jit(solution)/shard_map/all_to_all | solution.py:110
  57.9 2.8 %fusion.20 = f32[16,1,2,256]{3,1,2,0:T(1,128)S(1)} fusion(bf16[16,2,256,256]{3,2,1,0:T(8,128)(2,1)} %param.11, bf16[16,256,1,1]{1,0,2,3:T(8,128)(2,1)S(1)} %bitcast.129), kind=kOutput, calls=%fused_computation.51 | convolution fusion | flops 4194304 | bytes 4235264 | tf_op jit(solution)/shard_map/bsij,bi->bsj/dot_general | solution.py:101
  61.0 3.9 %collective-permute-start.5 = (f32[16,256]{1,0:T(8,128)S(1)}, f32[16,256]{1,0:T(8,128)S(1)}, u32[]{:S(2)}, u32[]{:S(2)}) collective-permute-start(f32[16,256]{1,0:T(8,128)S(1)} %slice.158), channel_id=1, source_target_pairs={{0,4},{4,8},{8,12},{12,16},{16,20},{20,24},{24,28},{1,5},{5,9},{9,... | collective-permute-start | bytes 49160 | tf_op jit(solution)/shard_map/ppermute | solution.py:107
  65.7 3.4 %fusion.10 = f32[16,1,256,1]{2,1,3,0:T(1,128)S(1)} fusion(bf16[16,2,256,256]{3,2,1,0:T(8,128)(2,1)} %param.11, bf16[16,2,256,1]{2,1,0,3:T(2,128)(2,1)S(1)} %fusion.15), kind=kOutput, calls=%fused_computation.28 | convolution fusion | flops 4194304 | bytes 4227072 | tf_op jit(solution)/shard_map/bsij,bsj->bi/dot_general | solution.py:120
  71.0 1.2 %collective-permute-done.6 = f32[5376]{0:T(1024)S(1)} collective-permute-done((f32[5376]{0:T(1024)S(1)}, f32[5376]{0:T(1024)S(1)}, u32[]{:S(2)}, u32[]{:S(2)}) %collective-permute-start.6) | collective-permute-done | bytes 21536 | tf_op jit(solution)/shard_map/ppermute | solution.py:15
  72.1 1.6 %collective-permute-start.7 = (f32[5376]{0:T(1024)S(1)}, f32[5376]{0:T(1024)S(1)}, u32[]{:S(2)}, u32[]{:S(2)}) collective-permute-start(f32[5376]{0:T(1024)S(1)} %add.114), channel_id=1, source_target_pairs={{0,2},{1,3},{2,0},{3,1},{4,6},{5,7},{6,4},{7,5},{8,10},{9,11},{10,... | collective-permute-start | bytes 64520 | tf_op jit(solution)/shard_map/ppermute | solution.py:15
  73.7 2.2 %collective-permute-done.7 = f32[5376]{0:T(1024)S(1)} collective-permute-done((f32[5376]{0:T(1024)S(1)}, f32[5376]{0:T(1024)S(1)}, u32[]{:S(2)}, u32[]{:S(2)}) %collective-permute-start.7) | collective-permute-done | bytes 21536 | tf_op jit(solution)/shard_map/ppermute | solution.py:15
  78.5 10.8 %all_to_all.39 = f32[8,1,1]{2,1,0:T(1,128)S(1)} all-to-all(f32[8,1,1]{2,1,0:T(1,128)S(1)} %broadcast_in_dim.204), channel_id=1, replica_groups=mesh['box'=8,'rep'=4] {'box'}, dimensions={0} | all-to-all | bytes 64 | tf_op jit(solution)/shard_map/all_to_all | solution.py:30
  (153 shorter events, 16.3 us)
Async XLA Ops:
  0.6 7.1 %copy-start = (bf16[20,4,64,64]{3,2,1,0:T(8,128)(2,1)S(1)}, bf16[20,4,64,64]{3,2,1,0:T(8,128)(2,1)}, u32[]{:S(2)}) copy-start(bf16[20,4,64,64]{3,2,1,0:T(8,128)(2,1)} %param.16) | copy-start | bytes 1966084
  0.6 20.6 %copy-start.4 = (s32[16,2]{0,1:T(2,128)S(1)}, s32[16,2]{0,1:T(2,128)}, u32[]{:S(2)}) copy-start(s32[16,2]{0,1:T(2,128)} %param.12) | copy-start | bytes 388
  1.5 25.1 %collective-permute-start = (bf16[16,256]{1,0:T(8,128)(2,1)S(1)}, bf16[16,256]{1,0:T(8,128)(2,1)S(1)}, u32[]{:S(2)}, u32[]{:S(2)}) collective-permute-start(bf16[16,256]{1,0:T(8,128)(2,1)S(1)} %convert_element_type.61), channel_id=1, source_target_pairs={{4,0},{8,4},{12,8},{16,12},{20,16},{24,20},{28,24},{5,1},{9,5},{13... | collective-permute-start | bytes 24584 | tf_op jit(solution)/shard_map/ppermute | solution.py:95
  9.8 21.0 %all-to-all-start = ((f32[8,1,1280]{2,1,0:T(1,128)}), f32[8,1,1280]{2,1,0:T(1,128)S(1)}, u32[]{:S(2)}, u32[]{:S(2)}) async-start(f32[8,1,1280]{2,1,0:T(1,128)} %all_to_all.32), calls=%async_computation | async-start | bytes 81920 | tf_op jit(solution)/shard_map/all_to_all | solution.py:110
  21.1 17.2 %copy-start.5 = (bf16[16,64,64]{2,1,0:T(8,128)(2,1)S(1)}, bf16[16,64,64]{2,1,0:T(8,128)(2,1)}, u32[]{:S(2)}) copy-start(bf16[16,64,64]{2,1,0:T(8,128)(2,1)} %param.14) | copy-start | bytes 393220
  21.1 17.5 %copy-start.1 = (bf16[16,64,256]{2,1,0:T(8,128)(2,1)S(1)}, bf16[16,64,256]{2,1,0:T(8,128)(2,1)}, u32[]{:S(2)}) copy-start(bf16[16,64,256]{2,1,0:T(8,128)(2,1)} %param.13) | copy-start | bytes 1572868
  21.1 17.7 %copy-start.2 = (f32[16,256]{1,0:T(8,128)S(1)}, f32[16,256]{1,0:T(8,128)}, u32[]{:S(2)}) copy-start(f32[16,256]{1,0:T(8,128)} %param.9) | copy-start | bytes 49156
  21.2 17.7 %copy-start.3 = (f32[16,256]{1,0:T(8,128)S(1)}, f32[16,256]{1,0:T(8,128)}, u32[]{:S(2)}) copy-start(f32[16,256]{1,0:T(8,128)} %param.10) | copy-start | bytes 49156
  21.8 9.0 %collective-permute-start.1 = (f32[16,256]{1,0:T(8,128)S(1)}, f32[16,256]{1,0:T(8,128)S(1)}, u32[]{:S(2)}, u32[]{:S(2)}) collective-permute-start(f32[16,256]{1,0:T(8,128)S(1)} %slice.149), channel_id=1, source_target_pairs={{0,4},{4,8},{8,12},{12,16},{16,20},{20,24},{24,28},{1,5},{5,9},{9,... | collective-permute-start | bytes 49160 | tf_op jit(solution)/shard_map/ppermute | solution.py:107
  32.6 1.2 %collective-permute-start.2 = (f32[5376]{0:T(1024)S(1)}, f32[5376]{0:T(1024)S(1)}, u32[]{:S(2)}, u32[]{:S(2)}) collective-permute-start(f32[5376]{0:T(1024)S(1)} %constant_dynamic-update-slice_fusion), channel_id=1, source_target_pairs={{0,1},{1,0},{2,3},{3,2},{4,5},{5,4},{6,7},{7,6},{8,9},{9,8},{10,11... | collective-permute-start | bytes 64520 | tf_op jit(solution)/shard_map/ppermute | solution.py:15
  33.8 3.8 %collective-permute-start.3 = (f32[5376]{0:T(1024)S(1)}, f32[5376]{0:T(1024)S(1)}, u32[]{:S(2)}, u32[]{:S(2)}) collective-permute-start(f32[5376]{0:T(1024)S(1)} %add.102), channel_id=1, source_target_pairs={{0,2},{1,3},{2,0},{3,1},{4,6},{5,7},{6,4},{7,5},{8,10},{9,11},{10,... | collective-permute-start | bytes 64520 | tf_op jit(solution)/shard_map/ppermute | solution.py:15
  50.2 14.7 %collective-permute-start.4 = (bf16[16,256]{1,0:T(8,128)(2,1)S(1)}, bf16[16,256]{1,0:T(8,128)(2,1)S(1)}, u32[]{:S(2)}, u32[]{:S(2)}) collective-permute-start(bf16[16,256]{1,0:T(8,128)(2,1)S(1)} %fusion.61), channel_id=1, source_target_pairs={{4,0},{8,4},{12,8},{16,12},{20,16},{24,20},{28,24},{5,1},{9,5},{13... | collective-permute-start | bytes 24584 | tf_op jit(solution)/shard_map/ppermute | solution.py:95
  53.9 15.2 %all-to-all-start.2 = ((f32[8,1,1280]{2,1,0:T(1,128)}), f32[8,1,1280]{2,1,0:T(1,128)S(1)}, u32[]{:S(2)}, u32[]{:S(2)}) async-start(f32[8,1,1280]{2,1,0:T(1,128)} %all_to_all.33), calls=%async_computation.2 | async-start | bytes 81920 | tf_op jit(solution)/shard_map/all_to_all | solution.py:110
  61.0 8.1 %collective-permute-start.5 = (f32[16,256]{1,0:T(8,128)S(1)}, f32[16,256]{1,0:T(8,128)S(1)}, u32[]{:S(2)}, u32[]{:S(2)}) collective-permute-start(f32[16,256]{1,0:T(8,128)S(1)} %slice.158), channel_id=1, source_target_pairs={{0,4},{4,8},{8,12},{12,16},{16,20},{20,24},{24,28},{1,5},{5,9},{9,... | collective-permute-start | bytes 49160 | tf_op jit(solution)/shard_map/ppermute | solution.py:107
  70.9 1.2 %collective-permute-start.6 = (f32[5376]{0:T(1024)S(1)}, f32[5376]{0:T(1024)S(1)}, u32[]{:S(2)}, u32[]{:S(2)}) collective-permute-start(f32[5376]{0:T(1024)S(1)} %constant_dynamic-update-slice_fusion.1), channel_id=1, source_target_pairs={{0,1},{1,0},{2,3},{3,2},{4,5},{5,4},{6,7},{7,6},{8,9},{9,8},{10,11... | collective-permute-start | bytes 64520 | tf_op jit(solution)/shard_map/ppermute | solution.py:15
  72.1 3.8 %collective-permute-start.7 = (f32[5376]{0:T(1024)S(1)}, f32[5376]{0:T(1024)S(1)}, u32[]{:S(2)}, u32[]{:S(2)}) collective-permute-start(f32[5376]{0:T(1024)S(1)} %add.114), channel_id=1, source_target_pairs={{0,2},{1,3},{2,0},{3,1},{4,6},{5,7},{6,4},{7,5},{8,10},{9,11},{10,... | collective-permute-start | bytes 64520 | tf_op jit(solution)/shard_map/ppermute | solution.py:15

commit v6 on v5

--- a/solution.py
+++ b/solution.py
@@ -97,7 +97,9 @@
         )
         coef_wide = node_coef.astype(jnp.float32)
         far_send = jnp.where(below, coef_wide[None], spread)
-        far_send, mirror_field = lax.optimization_barrier((far_send, rounded))
+        mirror_field = rounded
+        if iteration > 0:
+            far_send, mirror_field = lax.optimization_barrier((far_send, rounded))
         mirrored = jnp.einsum(
             "bsij,bi->bsj", near_tiles, mirror_field, preferred_element_type=jnp.float32
         )

time: 90.9 us -> 95.6 us (1.052)
  waiting for transfers between devices: 6.92 us -> 10.4 us
  other arithmetic: 7.8 us -> 9.16 us
  starting transfers between devices: 26.1 us -> 25 us
    ppermute x2, waiting for transfers between devices: 0.01 us -> 3.36 us  [local(): lax.ppermute(rounded, 'box', [(i, i - 1) for i in range(1, box_devices)])]
    all_to_all x2, starting transfers between devices: 12.5 us -> 11.4 us  [local(): lax.all_to_all(far_send.reshape(box_devices, far_size), 'box', 0, 0, tile...]
  transfers between devices with their start and end apart: 10 -> 10, of which waited for: 4 -> 5; matrix products, arithmetic and copies ran while one was open for 26% -> 20% of each run, Pallas kernels for 0% -> 0%
where the time goes in v6:
time: 95.6 us; the launch traced here: 94.8 us
  starting transfers between devices  25 us (26%)
  blocking collectives  22.5 us (24%)
  matrix products  18 us (19%)
  waiting for transfers between devices  10.4 us (11%)
  other arithmetic  9.16 us (10%)
  local copies, waits for them, and re-layouts  8.6 us (9%)
  between operations  1.23 us (1%)
    all_to_all x2, blocking collectives, box_sum(): got = lax.all_to_all(sent, 'box', 0, 0, tiled=True)  22.5 us
    all_to_all x2, starting transfers between devices, local(): lax.all_to_all(far_send.reshape(box_devices, far_size), 'box', 0, 0, tile...  11.4 us
    ppermute x2, starting transfers between devices, local(): lax.ppermute(landed[box_count:], 'box', [(i, i + 1) for i in range(box_de...  7.98 us
    ppermute x4, waiting for transfers between devices, rep_sum(): vector = vector + lax.ppermute(vector, 'rep', pairs)  7 us
    dot_general x2, matrix products, local(): jnp.einsum('bsij,bsj->bi', near_tiles, near_in, preferred_element_type=jn...  6.73 us
    dot_general x2, matrix products, local(): jnp.einsum('bsij,bi->bsj', near_tiles, mirror_field, preferred_element_ty...  5.67 us
    ppermute x2, waiting for transfers between devices, local(): lax.ppermute(rounded, 'box', [(i, i - 1) for i in range(1, box_devices)])  3.36 us
    ppermute x4, starting transfers between devices, rep_sum(): vector = vector + lax.ppermute(vector, 'rep', pairs)  3.04 us
  transfers between devices with their start and end apart: 10, of which 5 were waited for; matrix products, arithmetic and copies ran while one was open for 20% of the time, Pallas kernels for 0%

profile of v6, /device:TPU:0, one launch (start us, length us, event | category | flops | bytes accessed | tf_op | source)
XLA Modules:
  0.0 94.8 jit_solution(17017527825283932770)
XLA Ops:
  0.7 0.8 convert_bitcast_fusion.3
  1.5 1.3 %fusion.24 = f32[16,1,64]{2,1,0:T(1,128)S(1)} fusion(bf16[16,64,256]{2,1,0:T(8,128)(2,1)} %param.13, bf16[16,256,1]{1,0,2:T(8,128)(2,1)S(1)} %convert_bitcast_fusion.3), kind=kOutput, calls=%fused_computation.55 | convolution fusion | flops 524288 | bytes 536576 | tf_op jit(solution)/shard_map/brl,bl->br/dot_general | solution.py:78
  4.5 1.1 %fusion.49 = f32[16,1,64]{2,1,0:T(1,128)S(1)} fusion(bf16[16,64,64]{2,1,0:T(8,128)(2,1)} %param.14, bf16[16,64,1]{1,0,2:T(8,128)(2,1)S(1)} %convert_bitcast_fusion.2), kind=kOutput, calls=%fused_computation.89 | convolution fusion | flops 131072 | bytes 137216 | tf_op jit(solution)/shard_map/brq,br->bq/dot_general | solution.py:81
  6.1 0.9 scatter_custom_fusion
  7.9 7.4 %all-to-all-start = ((f32[8,1,1280]{2,1,0:T(1,128)}), f32[8,1,1280]{2,1,0:T(1,128)S(1)}, u32[]{:S(2)}, u32[]{:S(2)}) async-start(f32[8,1,1280]{2,1,0:T(1,128)} %copy.48), calls=%async_computation | async-start | bytes 81920 | tf_op jit(solution)/shard_map/all_to_all | solution.py:112
  17.7 2.8 %fusion.26 = f32[16,1,2,256]{3,1,2,0:T(1,128)S(1)} fusion(bf16[16,2,256,256]{3,2,1,0:T(8,128)(2,1)} %param.11, bf16[16,256,1,1]{1,0,2,3:T(8,128)(2,1)S(1)} %convert_bitcast_fusion.4), kind=kOutput, calls=%fused_computation.57 | convolution fusion | flops 4194304 | bytes 4235264 | tf_op jit(solution)/shard_map/bsij,bi->bsj/dot_general | solution.py:103
  20.8 4.1 %collective-permute-start.1 = (f32[16,256]{1,0:T(8,128)S(1)}, f32[16,256]{1,0:T(8,128)S(1)}, u32[]{:S(2)}, u32[]{:S(2)}) collective-permute-start(f32[16,256]{1,0:T(8,128)S(1)} %slice.149), channel_id=1, source_target_pairs={{0,4},{4,8},{8,12},{12,16},{16,20},{20,24},{24,28},{1,5},{5,9},{9,... | collective-permute-start | bytes 49160 | tf_op jit(solution)/shard_map/ppermute | solution.py:109
  24.9 1.3 %collective-permute-start = (bf16[16,256]{1,0:T(8,128)(2,1)S(1)}, bf16[16,256]{1,0:T(8,128)(2,1)S(1)}, u32[]{:S(2)}, u32[]{:S(2)}) collective-permute-start(bf16[16,256]{1,0:T(8,128)(2,1)S(1)} %convert_element_type.67), channel_id=1, source_target_pairs={{4,0},{8,4},{12,8},{16,12},{20,16},{24,20},{28,24},{5,1},{9,5},{13... | collective-permute-start | bytes 24584 | tf_op jit(solution)/shard_map/ppermute | solution.py:95
  27.1 3.4 %collective-permute-done = bf16[16,256]{1,0:T(8,128)(2,1)S(1)} collective-permute-done((bf16[16,256]{1,0:T(8,128)(2,1)S(1)}, bf16[16,256]{1,0:T(8,128)(2,1)S(1)}, u32[]{:S(2)}, u32[]{:S(2)}) %collective-permute-start) | collective-permute-done | bytes 8224 | tf_op jit(solution)/shard_map/ppermute | solution.py:95
  31.2 3.4 %fusion.12 = f32[16,1,256,1]{2,1,3,0:T(1,128)S(1)} fusion(bf16[16,2,256,256]{3,2,1,0:T(8,128)(2,1)} %param.11, bf16[16,2,256,1]{2,1,0,3:T(2,128)(2,1)S(1)} %fusion.14), kind=kOutput, calls=%fused_computation.30 | convolution fusion | flops 4194304 | bytes 4227072 | tf_op jit(solution)/shard_map/bsij,bsj->bi/dot_general | solution.py:122
  36.4 1.2 %collective-permute-done.2 = f32[5376]{0:T(1024)S(1)} collective-permute-done((f32[5376]{0:T(1024)S(1)}, f32[5376]{0:T(1024)S(1)}, u32[]{:S(2)}, u32[]{:S(2)}) %collective-permute-start.2) | collective-permute-done | bytes 21536 | tf_op jit(solution)/shard_map/ppermute | solution.py:15
  37.6 1.5 %collective-permute-start.3 = (f32[5376]{0:T(1024)S(1)}, f32[5376]{0:T(1024)S(1)}, u32[]{:S(2)}, u32[]{:S(2)}) collective-permute-start(f32[5376]{0:T(1024)S(1)} %add.102), channel_id=1, source_target_pairs={{0,2},{1,3},{2,0},{3,1},{4,6},{5,7},{6,4},{7,5},{8,10},{9,11},{10,... | collective-permute-start | bytes 64520 | tf_op jit(solution)/shard_map/ppermute | solution.py:15
  39.1 2.3 %collective-permute-done.3 = f32[5376]{0:T(1024)S(1)} collective-permute-done((f32[5376]{0:T(1024)S(1)}, f32[5376]{0:T(1024)S(1)}, u32[]{:S(2)}, u32[]{:S(2)}) %collective-permute-start.3) | collective-permute-done | bytes 21536 | tf_op jit(solution)/shard_map/ppermute | solution.py:15
  42.8 11.7 %all_to_all.34 = f32[8,1,4]{2,1,0:T(1,128)S(1)} all-to-all(f32[8,1,4]{2,1,0:T(1,128)S(1)} %broadcast_in_dim.204), channel_id=1, replica_groups=mesh['box'=8,'rep'=4] {'box'}, dimensions={0} | all-to-all | bytes 256 | tf_op jit(solution)/shard_map/all_to_all | solution.py:30
  54.9 1.3 %collective-permute-start.4 = (bf16[16,256]{1,0:T(8,128)(2,1)S(1)}, bf16[16,256]{1,0:T(8,128)(2,1)S(1)}, u32[]{:S(2)}, u32[]{:S(2)}) collective-permute-start(bf16[16,256]{1,0:T(8,128)(2,1)S(1)} %fusion.61), channel_id=1, source_target_pairs={{4,0},{8,4},{12,8},{16,12},{20,16},{24,20},{28,24},{5,1},{9,5},{13... | collective-permute-start | bytes 24584 | tf_op jit(solution)/shard_map/ppermute | solution.py:95
  56.9 0.9 scatter_custom_fusion.1
  58.6 4.0 %all-to-all-start.2 = ((f32[8,1,1280]{2,1,0:T(1,128)}), f32[8,1,1280]{2,1,0:T(1,128)S(1)}, u32[]{:S(2)}, u32[]{:S(2)}) async-start(f32[8,1,1280]{2,1,0:T(1,128)} %all_to_all.29), calls=%async_computation.2 | async-start | bytes 81920 | tf_op jit(solution)/shard_map/all_to_all | solution.py:112
  62.6 2.8 %fusion.20 = f32[16,1,2,256]{3,1,2,0:T(1,128)S(1)} fusion(bf16[16,2,256,256]{3,2,1,0:T(8,128)(2,1)} %param.11, bf16[16,256,1,1]{1,0,2,3:T(8,128)(2,1)S(1)} %bitcast.132), kind=kOutput, calls=%fused_computation.51 | convolution fusion | flops 4194304 | bytes 4235264 | tf_op jit(solution)/shard_map/bsij,bi->bsj/dot_general | solution.py:103
  65.7 3.9 %collective-permute-start.5 = (f32[16,256]{1,0:T(8,128)S(1)}, f32[16,256]{1,0:T(8,128)S(1)}, u32[]{:S(2)}, u32[]{:S(2)}) collective-permute-start(f32[16,256]{1,0:T(8,128)S(1)} %slice.158), channel_id=1, source_target_pairs={{0,4},{4,8},{8,12},{12,16},{16,20},{20,24},{24,28},{1,5},{5,9},{9,... | collective-permute-start | bytes 49160 | tf_op jit(solution)/shard_map/ppermute | solution.py:109
  70.4 3.4 %fusion.10 = f32[16,1,256,1]{2,1,3,0:T(1,128)S(1)} fusion(bf16[16,2,256,256]{3,2,1,0:T(8,128)(2,1)} %param.11, bf16[16,2,256,1]{2,1,0,3:T(2,128)(2,1)S(1)} %fusion.15), kind=kOutput, calls=%fused_computation.27 | convolution fusion | flops 4194304 | bytes 4227072 | tf_op jit(solution)/shard_map/bsij,bsj->bi/dot_general | solution.py:122
  75.6 1.2 %collective-permute-done.6 = f32[5376]{0:T(1024)S(1)} collective-permute-done((f32[5376]{0:T(1024)S(1)}, f32[5376]{0:T(1024)S(1)}, u32[]{:S(2)}, u32[]{:S(2)}) %collective-permute-start.6) | collective-permute-done | bytes 21536 | tf_op jit(solution)/shard_map/ppermute | solution.py:15
  76.8 1.5 %collective-permute-start.7 = (f32[5376]{0:T(1024)S(1)}, f32[5376]{0:T(1024)S(1)}, u32[]{:S(2)}, u32[]{:S(2)}) collective-permute-start(f32[5376]{0:T(1024)S(1)} %add.114), channel_id=1, source_target_pairs={{0,2},{1,3},{2,0},{3,1},{4,6},{5,7},{6,4},{7,5},{8,10},{9,11},{10,... | collective-permute-start | bytes 64520 | tf_op jit(solution)/shard_map/ppermute | solution.py:15
  78.3 2.3 %collective-permute-done.7 = f32[5376]{0:T(1024)S(1)} collective-permute-done((f32[5376]{0:T(1024)S(1)}, f32[5376]{0:T(1024)S(1)}, u32[]{:S(2)}, u32[]{:S(2)}) %collective-permute-start.7) | collective-permute-done | bytes 21536 | tf_op jit(solution)/shard_map/ppermute | solution.py:15
  83.1 10.8 %all_to_all.35 = f32[8,1,1]{2,1,0:T(1,128)S(1)} all-to-all(f32[8,1,1]{2,1,0:T(1,128)S(1)} %broadcast_in_dim.210), channel_id=1, replica_groups=mesh['box'=8,'rep'=4] {'box'}, dimensions={0} | all-to-all | bytes 64 | tf_op jit(solution)/shard_map/all_to_all | solution.py:30
  (156 shorter events, 18.4 us)
Async XLA Ops:
  0.6 5.1 %copy-start = (bf16[20,4,64,64]{3,2,1,0:T(8,128)(2,1)S(1)}, bf16[20,4,64,64]{3,2,1,0:T(8,128)(2,1)}, u32[]{:S(2)}) copy-start(bf16[20,4,64,64]{3,2,1,0:T(8,128)(2,1)} %param.16) | copy-start | bytes 1966084
  0.6 24.2 %copy-start.2 = (f32[16,256]{1,0:T(8,128)S(1)}, f32[16,256]{1,0:T(8,128)}, u32[]{:S(2)}) copy-start(f32[16,256]{1,0:T(8,128)} %param.9) | copy-start | bytes 49156
  7.9 26.7 %all-to-all-start = ((f32[8,1,1280]{2,1,0:T(1,128)}), f32[8,1,1280]{2,1,0:T(1,128)S(1)}, u32[]{:S(2)}, u32[]{:S(2)}) async-start(f32[8,1,1280]{2,1,0:T(1,128)} %copy.48), calls=%async_computation | async-start | bytes 81920 | tf_op jit(solution)/shard_map/all_to_all | solution.py:112
  20.6 21.6 %copy-start.4 = (bf16[16,64,64]{2,1,0:T(8,128)(2,1)S(1)}, bf16[16,64,64]{2,1,0:T(8,128)(2,1)}, u32[]{:S(2)}) copy-start(bf16[16,64,64]{2,1,0:T(8,128)(2,1)} %param.14) | copy-start | bytes 393220
  20.6 21.9 %copy-start.1 = (bf16[16,64,256]{2,1,0:T(8,128)(2,1)S(1)}, bf16[16,64,256]{2,1,0:T(8,128)(2,1)}, u32[]{:S(2)}) copy-start(bf16[16,64,256]{2,1,0:T(8,128)(2,1)} %param.13) | copy-start | bytes 1572868
  20.6 22.1 %copy-start.3 = (f32[16,256]{1,0:T(8,128)S(1)}, f32[16,256]{1,0:T(8,128)}, u32[]{:S(2)}) copy-start(f32[16,256]{1,0:T(8,128)} %param.10) | copy-start | bytes 49156
  20.8 13.7 %collective-permute-start.1 = (f32[16,256]{1,0:T(8,128)S(1)}, f32[16,256]{1,0:T(8,128)S(1)}, u32[]{:S(2)}, u32[]{:S(2)}) collective-permute-start(f32[16,256]{1,0:T(8,128)S(1)} %slice.149), channel_id=1, source_target_pairs={{0,4},{4,8},{8,12},{12,16},{16,20},{20,24},{24,28},{1,5},{5,9},{9,... | collective-permute-start | bytes 49160 | tf_op jit(solution)/shard_map/ppermute | solution.py:109
  24.9 5.5 %collective-permute-start = (bf16[16,256]{1,0:T(8,128)(2,1)S(1)}, bf16[16,256]{1,0:T(8,128)(2,1)S(1)}, u32[]{:S(2)}, u32[]{:S(2)}) collective-permute-start(bf16[16,256]{1,0:T(8,128)(2,1)S(1)} %convert_element_type.67), channel_id=1, source_target_pairs={{4,0},{8,4},{12,8},{16,12},{20,16},{24,20},{28,24},{5,1},{9,5},{13... | collective-permute-start | bytes 24584 | tf_op jit(solution)/shard_map/ppermute | solution.py:95
  36.4 1.2 %collective-permute-start.2 = (f32[5376]{0:T(1024)S(1)}, f32[5376]{0:T(1024)S(1)}, u32[]{:S(2)}, u32[]{:S(2)}) collective-permute-start(f32[5376]{0:T(1024)S(1)} %constant_dynamic-update-slice_fusion), channel_id=1, source_target_pairs={{0,1},{1,0},{2,3},{3,2},{4,5},{5,4},{6,7},{7,6},{8,9},{9,8},{10,11... | collective-permute-start | bytes 64520 | tf_op jit(solution)/shard_map/ppermute | solution.py:15
  37.6 3.8 %collective-permute-start.3 = (f32[5376]{0:T(1024)S(1)}, f32[5376]{0:T(1024)S(1)}, u32[]{:S(2)}, u32[]{:S(2)}) collective-permute-start(f32[5376]{0:T(1024)S(1)} %add.102), channel_id=1, source_target_pairs={{0,2},{1,3},{2,0},{3,1},{4,6},{5,7},{6,4},{7,5},{8,10},{9,11},{10,... | collective-permute-start | bytes 64520 | tf_op jit(solution)/shard_map/ppermute | solution.py:15
  54.9 14.7 %collective-permute-start.4 = (bf16[16,256]{1,0:T(8,128)(2,1)S(1)}, bf16[16,256]{1,0:T(8,128)(2,1)S(1)}, u32[]{:S(2)}, u32[]{:S(2)}) collective-permute-start(bf16[16,256]{1,0:T(8,128)(2,1)S(1)} %fusion.61), channel_id=1, source_target_pairs={{4,0},{8,4},{12,8},{16,12},{20,16},{24,20},{28,24},{5,1},{9,5},{13... | collective-permute-start | bytes 24584 | tf_op jit(solution)/shard_map/ppermute | solution.py:95
  58.6 15.2 %all-to-all-start.2 = ((f32[8,1,1280]{2,1,0:T(1,128)}), f32[8,1,1280]{2,1,0:T(1,128)S(1)}, u32[]{:S(2)}, u32[]{:S(2)}) async-start(f32[8,1,1280]{2,1,0:T(1,128)} %all_to_all.29), calls=%async_computation.2 | async-start | bytes 81920 | tf_op jit(solution)/shard_map/all_to_all | solution.py:112
  65.7 8.1 %collective-permute-start.5 = (f32[16,256]{1,0:T(8,128)S(1)}, f32[16,256]{1,0:T(8,128)S(1)}, u32[]{:S(2)}, u32[]{:S(2)}) collective-permute-start(f32[16,256]{1,0:T(8,128)S(1)} %slice.158), channel_id=1, source_target_pairs={{0,4},{4,8},{8,12},{12,16},{16,20},{20,24},{24,28},{1,5},{5,9},{9,... | collective-permute-start | bytes 49160 | tf_op jit(solution)/shard_map/ppermute | solution.py:109
  75.6 1.2 %collective-permute-start.6 = (f32[5376]{0:T(1024)S(1)}, f32[5376]{0:T(1024)S(1)}, u32[]{:S(2)}, u32[]{:S(2)}) collective-permute-start(f32[5376]{0:T(1024)S(1)} %constant_dynamic-update-slice_fusion.1), channel_id=1, source_target_pairs={{0,1},{1,0},{2,3},{3,2},{4,5},{5,4},{6,7},{7,6},{8,9},{9,8},{10,11... | collective-permute-start | bytes 64520 | tf_op jit(solution)/shard_map/ppermute | solution.py:15
  76.8 3.8 %collective-permute-start.7 = (f32[5376]{0:T(1024)S(1)}, f32[5376]{0:T(1024)S(1)}, u32[]{:S(2)}, u32[]{:S(2)}) collective-permute-start(f32[5376]{0:T(1024)S(1)} %add.114), channel_id=1, source_target_pairs={{0,2},{1,3},{2,0},{3,1},{4,6},{5,7},{6,4},{7,5},{8,10},{9,11},{10,... | collective-permute-start | bytes 64520 | tf_op jit(solution)/shard_map/ppermute | solution.py:15

commit v7 on v4

--- a/solution.py
+++ b/solution.py
@@ -8,6 +8,12 @@
 
 def rep_sum(vector):
     count = lax.axis_size("rep")
+    if count == 4:
+        got = [
+            lax.ppermute(vector, "rep", [(i, i ^ mask) for i in range(count)])
+            for mask in (1, 2, 3)
+        ]
+        return (vector + got[0]) + (got[1] + got[2])
     if count & (count - 1) == 0:
         stride = 1
         while stride < count:

time: 89.3 us -> 88.3 us (0.989)
  waiting for transfers between devices: 11 us -> 8.88 us
  starting transfers between devices: 25.6 us -> 26.7 us
    ppermute x4 -> x6, waiting for transfers between devices: 6.93 us -> 4.76 us  [rep_sum(): lax.ppermute(vector, 'rep', [(i, i ^ mask) for i in range(count)])]
    ppermute x4 -> x6, starting transfers between devices: 3.17 us -> 4.35 us  [rep_sum(): lax.ppermute(vector, 'rep', [(i, i ^ mask) for i in range(count)])]
  transfers between devices with their start and end apart: 10 -> 12, of which waited for: 6 -> 6; matrix products, arithmetic and copies ran while one was open for 20% -> 20% of each run, Pallas kernels for 0% -> 0%
where the time goes in v7:
time: 88.3 us; the launch traced here: 87.8 us
  starting transfers between devices  26.7 us (30%)
  blocking collectives  20.4 us (23%)
  matrix products  16 us (18%)
  waiting for transfers between devices  8.88 us (10%)
  local copies, waits for them, and re-layouts  8.69 us (10%)
  other arithmetic  5.72 us (6%)
  between operations  1.34 us (2%)
    all_to_all x2, blocking collectives, box_sum(): got = lax.all_to_all(sent, 'box', 0, 0, tiled=True)  20.4 us
    all_to_all x2, starting transfers between devices, local(): lax.all_to_all(far_send.reshape(box_devices, far_size), 'box', 0, 0, tile...  10.4 us
    ppermute x2, starting transfers between devices, local(): lax.ppermute(landed[box_count:], 'box', [(i, i + 1) for i in range(box_de...  9.43 us
    dot_general x2, matrix products, local(): jnp.einsum('bsij,bsj->bi', near_tiles, near_in, preferred_element_type=jn...  6.73 us
    dot_general x2, matrix products, local(): jnp.einsum('bsij,bi->bsj', near_tiles, rounded, preferred_element_type=jn...  5.66 us
    ppermute x6, waiting for transfers between devices, rep_sum(): lax.ppermute(vector, 'rep', [(i, i ^ mask) for i in range(count)])  4.76 us
    ppermute x6, starting transfers between devices, rep_sum(): lax.ppermute(vector, 'rep', [(i, i ^ mask) for i in range(count)])  4.35 us
    all_to_all x2, waiting for transfers between devices, local(): lax.all_to_all(far_send.reshape(box_devices, far_size), 'box', 0, 0, tile...  4.1 us
  transfers between devices with their start and end apart: 12, of which 6 were waited for; matrix products, arithmetic and copies ran while one was open for 20% of the time, Pallas kernels for 0%

profile of v7, /device:TPU:0, one launch (start us, length us, event | category | flops | bytes accessed | tf_op | source)
XLA Modules:
  0.0 87.8 jit_solution(2823330570712078022)
XLA Ops:
  0.7 0.9 convert_bitcast_fusion.5
  1.6 2.8 %fusion.26 = f32[16,1,2,256]{3,1,2,0:T(1,128)S(1)} fusion(bf16[16,2,256,256]{3,2,1,0:T(8,128)(2,1)} %param.11, bf16[16,256,1,1]{1,0,2,3:T(8,128)(2,1)S(1)} %convert_bitcast_fusion.5), kind=kOutput, calls=%fused_computation.59 | convolution fusion | flops 4194304 | bytes 4235264 | tf_op jit(solution)/shard_map/bsij,bi->bsj/dot_general | solution.py:84
  5.0 4.9 %collective-permute-start.1 = (f32[16,256]{1,0:T(8,128)S(1)}, f32[16,256]{1,0:T(8,128)S(1)}, u32[]{:S(2)}, u32[]{:S(2)}) collective-permute-start(f32[16,256]{1,0:T(8,128)S(1)} %slice.149), channel_id=1, source_target_pairs={{0,4},{4,8},{8,12},{12,16},{16,20},{20,24},{24,28},{1,5},{5,9},{9,... | collective-permute-start | bytes 49160 | tf_op jit(solution)/shard_map/ppermute | solution.py:110
  9.9 1.3 %collective-permute-start = (bf16[16,256]{1,0:T(8,128)(2,1)S(1)}, bf16[16,256]{1,0:T(8,128)(2,1)S(1)}, u32[]{:S(2)}, u32[]{:S(2)}) collective-permute-start(bf16[16,256]{1,0:T(8,128)(2,1)S(1)} %convert_element_type.73), channel_id=1, source_target_pairs={{4,0},{8,4},{12,8},{16,12},{20,16},{24,20},{28,24},{5,1},{9,5},{13... | collective-permute-start | bytes 24584 | tf_op jit(solution)/shard_map/ppermute | solution.py:107
  12.6 0.9 scatter_custom_fusion
  13.7 0.7 copy.48
  14.4 7.0 %all-to-all-start = ((f32[8,1,1280]{2,1,0:T(1,128)}), f32[8,1,1280]{2,1,0:T(1,128)S(1)}, u32[]{:S(2)}, u32[]{:S(2)}) async-start(f32[8,1,1280]{2,1,0:T(1,128)} %copy.48), calls=%async_computation | async-start | bytes 81920 | tf_op jit(solution)/shard_map/all_to_all | solution.py:115
  23.1 3.4 %fusion.12 = f32[16,1,256,1]{2,1,3,0:T(1,128)S(1)} fusion(bf16[16,2,256,256]{3,2,1,0:T(8,128)(2,1)} %param.11, bf16[16,2,256,1]{2,1,0,3:T(2,128)(2,1)S(1)} %fusion.14), kind=kOutput, calls=%fused_computation.29 | convolution fusion | flops 4194304 | bytes 4227072 | tf_op jit(solution)/shard_map/bsij,bsj->bi/dot_general | solution.py:125
  26.5 1.7 %all-to-all-done = f32[8,1,1280]{2,1,0:T(1,128)S(1)} async-done(((f32[8,1,1280]{2,1,0:T(1,128)}), f32[8,1,1280]{2,1,0:T(1,128)S(1)}, u32[]{:S(2)}, u32[]{:S(2)}) %all-to-all-start) | async-done | bytes 40992 | tf_op jit(solution)/shard_map/all_to_all | solution.py:115
  29.9 1.5 %collective-permute-start.3 = (f32[5376]{0:T(1024)S(1)}, f32[5376]{0:T(1024)S(1)}, u32[]{:S(2)}, u32[]{:S(2)}) collective-permute-start(f32[5376]{0:T(1024)S(1)} %constant_dynamic-update-slice_fusion), channel_id=1, source_target_pairs={{0,2},{1,3},{2,0},{3,1},{4,6},{5,7},{6,4},{7,5},{8,10},{9,11},{10,... | collective-permute-start | bytes 64520 | tf_op jit(solution)/shard_map/ppermute | solution.py:13
  32.1 1.7 %collective-permute-done.3 = f32[5376]{0:T(1024)S(1)} collective-permute-done((f32[5376]{0:T(1024)S(1)}, f32[5376]{0:T(1024)S(1)}, u32[]{:S(2)}, u32[]{:S(2)}) %collective-permute-start.3) | collective-permute-done | bytes 21536 | tf_op jit(solution)/shard_map/ppermute | solution.py:13
  33.8 0.9 %collective-permute-done.4 = f32[5376]{0:T(1024)S(1)} collective-permute-done((f32[5376]{0:T(1024)S(1)}, f32[5376]{0:T(1024)S(1)}, u32[]{:S(2)}, u32[]{:S(2)}) %collective-permute-start.4) | collective-permute-done | bytes 21536 | tf_op jit(solution)/shard_map/ppermute | solution.py:13
  36.1 10.6 %all_to_all.30 = f32[8,1,4]{2,1,0:T(1,128)S(1)} all-to-all(f32[8,1,4]{2,1,0:T(1,128)S(1)} %broadcast_in_dim.204), channel_id=1, replica_groups=mesh['box'=8,'rep'=4] {'box'}, dimensions={0} | all-to-all | bytes 256 | tf_op jit(solution)/shard_map/all_to_all | solution.py:36
  46.8 1.3 %collective-permute-start.5 = (bf16[16,256]{1,0:T(8,128)(2,1)S(1)}, bf16[16,256]{1,0:T(8,128)(2,1)S(1)}, u32[]{:S(2)}, u32[]{:S(2)}) collective-permute-start(bf16[16,256]{1,0:T(8,128)(2,1)S(1)} %fusion.61), channel_id=1, source_target_pairs={{4,0},{8,4},{12,8},{16,12},{20,16},{24,20},{28,24},{5,1},{9,5},{13... | collective-permute-start | bytes 24584 | tf_op jit(solution)/shard_map/ppermute | solution.py:107
  49.1 0.9 scatter_custom_fusion.1
  50.1 2.8 %fusion.22 = f32[16,1,2,256]{3,1,2,0:T(1,128)S(1)} fusion(bf16[16,2,256,256]{3,2,1,0:T(8,128)(2,1)} %param.11, bf16[16,256,1,1]{1,0,2,3:T(8,128)(2,1)S(1)} %bitcast.135), kind=kOutput, calls=%fused_computation.55 | convolution fusion | flops 4194304 | bytes 4235264 | tf_op jit(solution)/shard_map/bsij,bi->bsj/dot_general | solution.py:84
  53.1 4.6 %collective-permute-start.6 = (f32[16,256]{1,0:T(8,128)S(1)}, f32[16,256]{1,0:T(8,128)S(1)}, u32[]{:S(2)}, u32[]{:S(2)}) collective-permute-start(f32[16,256]{1,0:T(8,128)S(1)} %slice.158), channel_id=1, source_target_pairs={{0,4},{4,8},{8,12},{12,16},{16,20},{20,24},{24,28},{1,5},{5,9},{9,... | collective-permute-start | bytes 49160 | tf_op jit(solution)/shard_map/ppermute | solution.py:110
  58.5 3.3 %all-to-all-start.2 = ((f32[8,1,1280]{2,1,0:T(1,128)}), f32[8,1,1280]{2,1,0:T(1,128)S(1)}, u32[]{:S(2)}, u32[]{:S(2)}) async-start(f32[8,1,1280]{2,1,0:T(1,128)} %copy.52), calls=%async_computation.2 | async-start | bytes 81920 | tf_op jit(solution)/shard_map/all_to_all | solution.py:115
  62.7 3.4 %fusion.10 = f32[16,1,256,1]{2,1,3,0:T(1,128)S(1)} fusion(bf16[16,2,256,256]{3,2,1,0:T(8,128)(2,1)} %param.11, bf16[16,2,256,1]{2,1,0,3:T(2,128)(2,1)S(1)} %fusion.15), kind=kOutput, calls=%fused_computation.26 | convolution fusion | flops 4194304 | bytes 4227072 | tf_op jit(solution)/shard_map/bsij,bsj->bi/dot_general | solution.py:125
  66.1 2.4 %all-to-all-done.2 = f32[8,1,1280]{2,1,0:T(1,128)S(1)} async-done(((f32[8,1,1280]{2,1,0:T(1,128)}), f32[8,1,1280]{2,1,0:T(1,128)S(1)}, u32[]{:S(2)}, u32[]{:S(2)}) %all-to-all-start.2) | async-done | bytes 40992 | tf_op jit(solution)/shard_map/all_to_all | solution.py:115
  70.3 0.8 collective-permute-start.8
  71.1 1.4 %collective-permute-start.7 = (f32[5376]{0:T(1024)S(1)}, f32[5376]{0:T(1024)S(1)}, u32[]{:S(2)}, u32[]{:S(2)}) collective-permute-start(f32[5376]{0:T(1024)S(1)} %constant_dynamic-update-slice_fusion.1), channel_id=1, source_target_pairs={{0,1},{1,0},{2,3},{3,2},{4,5},{5,4},{6,7},{7,6},{8,9},{9,8},{10,11... | collective-permute-start | bytes 64520 | tf_op jit(solution)/shard_map/ppermute | solution.py:13
  72.5 1.7 %collective-permute-done.8 = f32[5376]{0:T(1024)S(1)} collective-permute-done((f32[5376]{0:T(1024)S(1)}, f32[5376]{0:T(1024)S(1)}, u32[]{:S(2)}, u32[]{:S(2)}) %collective-permute-start.8) | collective-permute-done | bytes 21536 | tf_op jit(solution)/shard_map/ppermute | solution.py:13
  77.1 9.8 %all_to_all.31 = f32[8,1,1]{2,1,0:T(1,128)S(1)} all-to-all(f32[8,1,1]{2,1,0:T(1,128)S(1)} %broadcast_in_dim.210), channel_id=1, replica_groups=mesh['box'=8,'rep'=4] {'box'}, dimensions={0} | all-to-all | bytes 64 | tf_op jit(solution)/shard_map/all_to_all | solution.py:36
  (168 shorter events, 15.9 us)
Async XLA Ops:
  0.6 11.6 %copy-start = (bf16[20,4,64,64]{3,2,1,0:T(8,128)(2,1)S(1)}, bf16[20,4,64,64]{3,2,1,0:T(8,128)(2,1)}, u32[]{:S(2)}) copy-start(bf16[20,4,64,64]{3,2,1,0:T(8,128)(2,1)} %param.16) | copy-start | bytes 1966084
  0.6 9.3 %copy-start.2 = (f32[16,256]{1,0:T(8,128)S(1)}, f32[16,256]{1,0:T(8,128)}, u32[]{:S(2)}) copy-start(f32[16,256]{1,0:T(8,128)} %param.9) | copy-start | bytes 49156
  0.7 3.8 %copy-start.5 = (s32[16,2]{0,1:T(2,128)S(1)}, s32[16,2]{0,1:T(2,128)}, u32[]{:S(2)}) copy-start(s32[16,2]{0,1:T(2,128)} %param.12) | copy-start | bytes 388
  0.7 10.6 %copy-start.1 = (bf16[16,64,256]{2,1,0:T(8,128)(2,1)S(1)}, bf16[16,64,256]{2,1,0:T(8,128)(2,1)}, u32[]{:S(2)}) copy-start(bf16[16,64,256]{2,1,0:T(8,128)(2,1)} %param.13) | copy-start | bytes 1572868
  0.7 10.9 %copy-start.4 = (s32[20,4]{0,1:T(4,128)S(1)}, s32[20,4]{0,1:T(4,128)}, u32[]{:S(2)}) copy-start(s32[20,4]{0,1:T(4,128)} %param.17) | copy-start | bytes 964
  0.7 11.2 %copy-start.7 = (bf16[16,64,64]{2,1,0:T(8,128)(2,1)S(1)}, bf16[16,64,64]{2,1,0:T(8,128)(2,1)}, u32[]{:S(2)}) copy-start(bf16[16,64,64]{2,1,0:T(8,128)(2,1)} %param.14) | copy-start | bytes 393220
  0.7 11.4 %copy-start.6 = (s32[16]{0:T(128)S(1)}, s32[16]{0:T(128)}, u32[]{:S(2)}) copy-start(s32[16]{0:T(128)} %param.15) | copy-start | bytes 196
  5.0 21.4 %collective-permute-start.1 = (f32[16,256]{1,0:T(8,128)S(1)}, f32[16,256]{1,0:T(8,128)S(1)}, u32[]{:S(2)}, u32[]{:S(2)}) collective-permute-start(f32[16,256]{1,0:T(8,128)S(1)} %slice.149), channel_id=1, source_target_pairs={{0,4},{4,8},{8,12},{12,16},{16,20},{20,24},{24,28},{1,5},{5,9},{9,... | collective-permute-start | bytes 49160 | tf_op jit(solution)/shard_map/ppermute | solution.py:110
  9.9 12.4 %collective-permute-start = (bf16[16,256]{1,0:T(8,128)(2,1)S(1)}, bf16[16,256]{1,0:T(8,128)(2,1)S(1)}, u32[]{:S(2)}, u32[]{:S(2)}) collective-permute-start(bf16[16,256]{1,0:T(8,128)(2,1)S(1)} %convert_element_type.73), channel_id=1, source_target_pairs={{4,0},{8,4},{12,8},{16,12},{20,16},{24,20},{28,24},{5,1},{9,5},{13... | collective-permute-start | bytes 24584 | tf_op jit(solution)/shard_map/ppermute | solution.py:107
  13.7 22.2 %copy-start.3 = (f32[16,256]{1,0:T(8,128)S(1)}, f32[16,256]{1,0:T(8,128)}, u32[]{:S(2)}) copy-start(f32[16,256]{1,0:T(8,128)} %param.10) | copy-start | bytes 49156
  14.4 13.8 %all-to-all-start = ((f32[8,1,1280]{2,1,0:T(1,128)}), f32[8,1,1280]{2,1,0:T(1,128)S(1)}, u32[]{:S(2)}, u32[]{:S(2)}) async-start(f32[8,1,1280]{2,1,0:T(1,128)} %copy.48), calls=%async_computation | async-start | bytes 81920 | tf_op jit(solution)/shard_map/all_to_all | solution.py:115
  29.9 3.9 %collective-permute-start.3 = (f32[5376]{0:T(1024)S(1)}, f32[5376]{0:T(1024)S(1)}, u32[]{:S(2)}, u32[]{:S(2)}) collective-permute-start(f32[5376]{0:T(1024)S(1)} %constant_dynamic-update-slice_fusion), channel_id=1, source_target_pairs={{0,2},{1,3},{2,0},{3,1},{4,6},{5,7},{6,4},{7,5},{8,10},{9,11},{10,... | collective-permute-start | bytes 64520 | tf_op jit(solution)/shard_map/ppermute | solution.py:13
  31.4 3.3 %collective-permute-start.4 = (f32[5376]{0:T(1024)S(1)}, f32[5376]{0:T(1024)S(1)}, u32[]{:S(2)}, u32[]{:S(2)}) collective-permute-start(f32[5376]{0:T(1024)S(1)} %constant_dynamic-update-slice_fusion), channel_id=1, source_target_pairs={{0,3},{1,2},{2,1},{3,0},{4,7},{5,6},{6,5},{7,4},{8,11},{9,10},{10,... | collective-permute-start | bytes 64520 | tf_op jit(solution)/shard_map/ppermute | solution.py:13
  31.4 3.3 %collective-permute-start.2 = (f32[5376]{0:T(1024)S(1)}, f32[5376]{0:T(1024)S(1)}, u32[]{:S(2)}, u32[]{:S(2)}) collective-permute-start(f32[5376]{0:T(1024)S(1)} %constant_dynamic-update-slice_fusion), channel_id=1, source_target_pairs={{0,1},{1,0},{2,3},{3,2},{4,5},{5,4},{6,7},{7,6},{8,9},{9,8},{10,11... | collective-permute-start | bytes 64520 | tf_op jit(solution)/shard_map/ppermute | solution.py:13
  46.8 15.1 %collective-permute-start.5 = (bf16[16,256]{1,0:T(8,128)(2,1)S(1)}, bf16[16,256]{1,0:T(8,128)(2,1)S(1)}, u32[]{:S(2)}, u32[]{:S(2)}) collective-permute-start(bf16[16,256]{1,0:T(8,128)(2,1)S(1)} %fusion.61), channel_id=1, source_target_pairs={{4,0},{8,4},{12,8},{16,12},{20,16},{24,20},{28,24},{5,1},{9,5},{13... | collective-permute-start | bytes 24584 | tf_op jit(solution)/shard_map/ppermute | solution.py:107
  53.1 12.9 %collective-permute-start.6 = (f32[16,256]{1,0:T(8,128)S(1)}, f32[16,256]{1,0:T(8,128)S(1)}, u32[]{:S(2)}, u32[]{:S(2)}) collective-permute-start(f32[16,256]{1,0:T(8,128)S(1)} %slice.158), channel_id=1, source_target_pairs={{0,4},{4,8},{8,12},{12,16},{16,20},{20,24},{24,28},{1,5},{5,9},{9,... | collective-permute-start | bytes 49160 | tf_op jit(solution)/shard_map/ppermute | solution.py:110
  58.5 10.0 %all-to-all-start.2 = ((f32[8,1,1280]{2,1,0:T(1,128)}), f32[8,1,1280]{2,1,0:T(1,128)S(1)}, u32[]{:S(2)}, u32[]{:S(2)}) async-start(f32[8,1,1280]{2,1,0:T(1,128)} %copy.52), calls=%async_computation.2 | async-start | bytes 81920 | tf_op jit(solution)/shard_map/all_to_all | solution.py:115
  70.3 3.9 %collective-permute-start.8 = (f32[5376]{0:T(1024)S(1)}, f32[5376]{0:T(1024)S(1)}, u32[]{:S(2)}, u32[]{:S(2)}) collective-permute-start(f32[5376]{0:T(1024)S(1)} %constant_dynamic-update-slice_fusion.1), channel_id=1, source_target_pairs={{0,2},{1,3},{2,0},{3,1},{4,6},{5,7},{6,4},{7,5},{8,10},{9,11},{10,... | collective-permute-start | bytes 64520 | tf_op jit(solution)/shard_map/ppermute | solution.py:13
  71.1 3.5 %collective-permute-start.9 = (f32[5376]{0:T(1024)S(1)}, f32[5376]{0:T(1024)S(1)}, u32[]{:S(2)}, u32[]{:S(2)}) collective-permute-start(f32[5376]{0:T(1024)S(1)} %constant_dynamic-update-slice_fusion.1), channel_id=1, source_target_pairs={{0,3},{1,2},{2,1},{3,0},{4,7},{5,6},{6,5},{7,4},{8,11},{9,10},{10,... | collective-permute-start | bytes 64520 | tf_op jit(solution)/shard_map/ppermute | solution.py:13
  71.1 3.5 %collective-permute-start.7 = (f32[5376]{0:T(1024)S(1)}, f32[5376]{0:T(1024)S(1)}, u32[]{:S(2)}, u32[]{:S(2)}) collective-permute-start(f32[5376]{0:T(1024)S(1)} %constant_dynamic-update-slice_fusion.1), channel_id=1, source_target_pairs={{0,1},{1,0},{2,3},{3,2},{4,5},{5,4},{6,7},{7,6},{8,9},{9,8},{10,11... | collective-permute-start | bytes 64520 | tf_op jit(solution)/shard_map/ppermute | solution.py:13

commit v8 on v7

--- a/solution.py
+++ b/solution.py
@@ -68,6 +68,10 @@
     ).astype(jnp.float32)
     far_valid = coupling_partners >= 0
     far_index = jnp.where(far_valid, coupling_partners, 0)
+    far_pick = (
+        (jnp.arange(all_nodes, dtype=jnp.int32)[:, None] == far_index.reshape(1, -1))
+        & far_valid.reshape(1, -1)
+    )
     bf_zero = jnp.zeros((), jnp.bfloat16)
     devices = jnp.arange(box_devices, dtype=jnp.int32)
     below = (devices < box_rank)[:, None, None]
@@ -99,10 +103,9 @@
             "nsab,na->nsb", coupling, node_coef, preferred_element_type=jnp.float32
         )
         far_mirror = far_mirror * far_valid[:, :, None].astype(jnp.float32)
-        spread = (
-            jnp.zeros((all_nodes, rank_width), jnp.float32)
-            .at[far_index.reshape(-1)]
-            .add(far_mirror.reshape(-1, rank_width))
+        spread = jnp.dot(
+            far_pick.astype(jnp.float32), far_mirror.reshape(-1, rank_width),
+            precision=lax.Precision.HIGHEST,
         ).reshape(box_devices, node_count, rank_width)
         following = lax.ppermute(
             rounded, "box", [(i, i - 1) for i in range(1, box_devices)]
@@ -112,9 +115,7 @@
         )
         coef_wide = node_coef.astype(jnp.float32)
         far_send = jnp.where(below, coef_wide[None], spread)
-        got_far = lax.all_to_all(
-            far_send.reshape(box_devices, far_size), "box", 0, 0, tiled=True
-        ).reshape(box_devices, node_count, rank_width)
+        got_far = lax.all_to_all(far_send, "box", 0, 0, tiled=True)
         mirror_in = jnp.sum(jnp.where(below, got_far, 0.0), axis=0)
         every_coef = jnp.where(
             above, got_far, jnp.where(devices[:, None, None] == box_rank, coef_wide[None], 0.0)
@@ -126,7 +127,9 @@
             "bsij,bsj->bi", near_tiles, near_in, preferred_element_type=jnp.float32
         )
         near_part = forward + landed[:box_count] + arrived
-        partner_coef = jnp.where(far_valid[:, :, None], every_coef[far_index], bf_zero)
+        partner_coef = jnp.dot(
+            far_pick.T.astype(jnp.bfloat16), every_coef, preferred_element_type=jnp.float32
+        ).astype(jnp.bfloat16).reshape(node_count, -1, rank_width)
         far_forward = jnp.einsum(
             "nsab,nsb->na", coupling, partner_coef, preferred_element_type=jnp.float32
         )
@@ -135,8 +138,11 @@
         near_total = both[:near_size].reshape(box_count, leaf)
         far_total = both[near_size:].reshape(node_count, rank_width)
         group_out = far_total[box_count:].astype(jnp.bfloat16)
+        parent_pick = jnp.zeros((box_count, rank_width), jnp.bfloat16)
+        for group in range(group_count):
+            parent_pick = jnp.where((parent_local == group)[:, None], group_out[group][None], parent_pick)
         from_parent = jnp.einsum(
-            "brq,bq->br", transfer, group_out[parent_local], preferred_element_type=jnp.float32
+            "brq,bq->br", transfer, parent_pick, preferred_element_type=jnp.float32
         )
         downward = (far_total[:box_count] + from_parent).astype(jnp.bfloat16)
         far_field = jnp.einsum(

time: 88.3 us -> 85.8 us (0.972)
  local copies, waits for them, and re-layouts: 8.69 us -> 6.1 us
  matrix products: 16 us -> 16.9 us
    gather x4 -> x0, local copies, waits for them, and re-layouts: 2.46 us -> none  [the longest x2 1.31 us: local(): every_coef[far_index]]
    scatter-add x2 -> x0, other arithmetic: 1.73 us -> none  [local(): spread = jnp.zeros((all_nodes, rank_width), jnp.float32).at[far_index.res...]
    unnamed x20 -> x24, local copies, waits for them, and re-layouts: 0.06 us -> 1.66 us
    select_n x3 -> x0, local copies, waits for them, and re-layouts: 1.41 us -> none  [the longest x2 1.31 us: local(): far_send = jnp.where(below, coef_wide[None], spread)]
    all_to_all x2, other arithmetic: 0.21 us -> 1.48 us  [local(): got_far = lax.all_to_all(far_send, 'box', 0, 0, tiled=True)]
  transfers between devices with their start and end apart: 12 -> 12, of which waited for: 6 -> 6; matrix products, arithmetic and copies ran while one was open for 20% -> 19% of each run, Pallas kernels for 0% -> 0%
where the time goes in v8:
time: 85.8 us; the launch traced here: 85.2 us
  starting transfers between devices  26.6 us (31%)
  blocking collectives  19.6 us (23%)
  matrix products  16.9 us (20%)
  waiting for transfers between devices  9.61 us (11%)
  local copies, waits for them, and re-layouts  6.1 us (7%)
  other arithmetic  5.01 us (6%)
  between operations  1.31 us (2%)
    all_to_all x2, blocking collectives, box_sum(): got = lax.all_to_all(sent, 'box', 0, 0, tiled=True)  19.6 us
    all_to_all x2, starting transfers between devices, local(): got_far = lax.all_to_all(far_send, 'box', 0, 0, tiled=True)  10.3 us
    ppermute x2, starting transfers between devices, local(): lax.ppermute(landed[box_count:], 'box', [(i, i + 1) for i in range(box_de...  9.42 us
    dot_general x2, matrix products, local(): jnp.einsum('bsij,bsj->bi', near_tiles, near_in, preferred_element_type=jn...  6.73 us
    dot_general x2, matrix products, local(): jnp.einsum('bsij,bi->bsj', near_tiles, rounded, preferred_element_type=jn...  5.68 us
    all_to_all x2, waiting for transfers between devices, local(): got_far = lax.all_to_all(far_send, 'box', 0, 0, tiled=True)  4.83 us
    ppermute x6, waiting for transfers between devices, rep_sum(): lax.ppermute(vector, 'rep', [(i, i ^ mask) for i in range(count)])  4.77 us
    ppermute x6, starting transfers between devices, rep_sum(): lax.ppermute(vector, 'rep', [(i, i ^ mask) for i in range(count)])  4.35 us
  transfers between devices with their start and end apart: 12, of which 6 were waited for; matrix products, arithmetic and copies ran while one was open for 19% of the time, Pallas kernels for 0%

profile of v8, /device:TPU:0, one launch (start us, length us, event | category | flops | bytes accessed | tf_op | source)
XLA Modules:
  0.0 85.2 jit_solution(3865133145106176840)
XLA Ops:
  0.7 0.9 %convert_bitcast_fusion.3 = bf16[16,256,1,1]{1,0,2,3:T(8,128)(2,1)S(1)} fusion(f32[16,256]{1,0:T(8,128)} %param.9), kind=kLoop, calls=%fused_computation.148 | loop fusion | flops 4096 | bytes 24576 | tf_op jit(solution)/shard_map/convert_element_type | solution.py:87
  1.6 2.8 %fusion.35 = f32[16,1,2,256]{3,1,2,0:T(1,128)S(1)} fusion(bf16[16,2,256,256]{3,2,1,0:T(8,128)(2,1)} %param.11, bf16[16,256,1,1]{1,0,2,3:T(8,128)(2,1)S(1)} %convert_bitcast_fusion.3), kind=kOutput, calls=%fused_computation.62 | convolution fusion | flops 4194304 | bytes 4235264 | tf_op jit(solution)/shard_map/bsij,bi->bsj/dot_general | solution.py:88
  5.0 4.9 %collective-permute-start.1 = (f32[16,256]{1,0:T(8,128)S(1)}, f32[16,256]{1,0:T(8,128)S(1)}, u32[]{:S(2)}, u32[]{:S(2)}) collective-permute-start(f32[16,256]{1,0:T(8,128)S(1)} %slice.183), channel_id=1, source_target_pairs={{0,4},{4,8},{8,12},{12,16},{16,20},{20,24},{24,28},{1,5},{5,9},{9,... | collective-permute-start | bytes 49160 | tf_op jit(solution)/shard_map/ppermute | solution.py:113
  9.9 1.3 %collective-permute-start = (bf16[16,256]{1,0:T(8,128)(2,1)S(1)}, bf16[16,256]{1,0:T(8,128)(2,1)S(1)}, u32[]{:S(2)}, u32[]{:S(2)}) collective-permute-start(bf16[16,256]{1,0:T(8,128)(2,1)S(1)} %convert_element_type.65), channel_id=1, source_target_pairs={{4,0},{8,4},{12,8},{16,12},{20,16},{24,20},{28,24},{5,1},{9,5},{13... | collective-permute-start | bytes 24584 | tf_op jit(solution)/shard_map/ppermute | solution.py:110
  13.1 0.7 reshape.310
  13.8 7.0 %all-to-all-start = ((f32[8,1,1280]{2,1,0:T(1,128)}), f32[8,1,1280]{2,1,0:T(1,128)S(1)}, u32[]{:S(2)}, u32[]{:S(2)}) async-start(f32[8,1,1280]{2,1,0:T(1,128)} %reshape.310), calls=%async_computation | async-start | bytes 81920 | tf_op jit(solution)/shard_map/all_to_all | solution.py:118
  21.7 3.4 %fusion.21 = f32[16,1,256,1]{2,1,3,0:T(1,128)S(1)} fusion(bf16[16,2,256,256]{3,2,1,0:T(8,128)(2,1)} %param.11, bf16[16,2,256,1]{2,1,0,3:T(2,128)(2,1)S(1)} %fusion.23), kind=kOutput, calls=%fused_computation.36 | convolution fusion | flops 4194304 | bytes 4227072 | tf_op jit(solution)/shard_map/bsij,bsj->bi/dot_general | solution.py:126
  25.1 2.3 %all-to-all-done = f32[8,1,1280]{2,1,0:T(1,128)S(1)} async-done(((f32[8,1,1280]{2,1,0:T(1,128)}), f32[8,1,1280]{2,1,0:T(1,128)S(1)}, u32[]{:S(2)}, u32[]{:S(2)}) %all-to-all-start) | async-done | bytes 40992 | tf_op jit(solution)/shard_map/all_to_all | solution.py:118
  28.0 0.7 reduce.4
  29.9 1.5 %collective-permute-start.3 = (f32[5376]{0:T(1024)S(1)}, f32[5376]{0:T(1024)S(1)}, u32[]{:S(2)}, u32[]{:S(2)}) collective-permute-start(f32[5376]{0:T(1024)S(1)} %constant_dynamic-update-slice_fusion), channel_id=1, source_target_pairs={{0,2},{1,3},{2,0},{3,1},{4,6},{5,7},{6,4},{7,5},{8,10},{9,11},{10,... | collective-permute-start | bytes 64520 | tf_op jit(solution)/shard_map/ppermute | solution.py:13
  32.0 1.7 %collective-permute-done.3 = f32[5376]{0:T(1024)S(1)} collective-permute-done((f32[5376]{0:T(1024)S(1)}, f32[5376]{0:T(1024)S(1)}, u32[]{:S(2)}, u32[]{:S(2)}) %collective-permute-start.3) | collective-permute-done | bytes 21536 | tf_op jit(solution)/shard_map/ppermute | solution.py:13
  33.7 0.9 %collective-permute-done.4 = f32[5376]{0:T(1024)S(1)} collective-permute-done((f32[5376]{0:T(1024)S(1)}, f32[5376]{0:T(1024)S(1)}, u32[]{:S(2)}, u32[]{:S(2)}) %collective-permute-start.4) | collective-permute-done | bytes 21536 | tf_op jit(solution)/shard_map/ppermute | solution.py:13
  35.5 9.9 %all_to_all.22 = f32[8,1,4]{2,1,0:T(1,128)S(1)} all-to-all(f32[8,1,4]{2,1,0:T(1,128)S(1)} %broadcast_in_dim.242), channel_id=1, replica_groups=mesh['box'=8,'rep'=4] {'box'}, dimensions={0} | all-to-all | bytes 256 | tf_op jit(solution)/shard_map/all_to_all | solution.py:36
  45.6 1.3 %collective-permute-start.5 = (bf16[16,256]{1,0:T(8,128)(2,1)S(1)}, bf16[16,256]{1,0:T(8,128)(2,1)S(1)}, u32[]{:S(2)}, u32[]{:S(2)}) collective-permute-start(bf16[16,256]{1,0:T(8,128)(2,1)S(1)} %fusion.70), channel_id=1, source_target_pairs={{4,0},{8,4},{12,8},{16,12},{20,16},{24,20},{28,24},{5,1},{9,5},{13... | collective-permute-start | bytes 24584 | tf_op jit(solution)/shard_map/ppermute | solution.py:110
  47.1 2.9 %fusion.31 = f32[16,1,2,256]{3,1,2,0:T(1,128)S(1)} fusion(bf16[16,2,256,256]{3,2,1,0:T(8,128)(2,1)} %param.11, bf16[16,256,1,1]{1,0,2,3:T(8,128)(2,1)S(1)} %bitcast.131), kind=kOutput, calls=%fused_computation.58 | convolution fusion | flops 4194304 | bytes 4235264 | tf_op jit(solution)/shard_map/bsij,bi->bsj/dot_general | solution.py:88
  50.2 4.5 %collective-permute-start.6 = (f32[16,256]{1,0:T(8,128)S(1)}, f32[16,256]{1,0:T(8,128)S(1)}, u32[]{:S(2)}, u32[]{:S(2)}) collective-permute-start(f32[16,256]{1,0:T(8,128)S(1)} %slice.195), channel_id=1, source_target_pairs={{0,4},{4,8},{8,12},{12,16},{16,20},{20,24},{24,28},{1,5},{5,9},{9,... | collective-permute-start | bytes 49160 | tf_op jit(solution)/shard_map/ppermute | solution.py:113
  56.4 3.3 %all-to-all-start.2 = ((f32[8,1,1280]{2,1,0:T(1,128)}), f32[8,1,1280]{2,1,0:T(1,128)S(1)}, u32[]{:S(2)}, u32[]{:S(2)}) async-start(f32[8,1,1280]{2,1,0:T(1,128)} %reshape.312), calls=%async_computation.2 | async-start | bytes 81920 | tf_op jit(solution)/shard_map/all_to_all | solution.py:118
  60.5 3.4 %fusion.19 = f32[16,1,256,1]{2,1,3,0:T(1,128)S(1)} fusion(bf16[16,2,256,256]{3,2,1,0:T(8,128)(2,1)} %param.11, bf16[16,2,256,1]{2,1,0,3:T(2,128)(2,1)S(1)} %fusion.24), kind=kOutput, calls=%fused_computation.33 | convolution fusion | flops 4194304 | bytes 4227072 | tf_op jit(solution)/shard_map/bsij,bsj->bi/dot_general | solution.py:126
  64.0 2.5 %all-to-all-done.2 = f32[8,1,1280]{2,1,0:T(1,128)S(1)} async-done(((f32[8,1,1280]{2,1,0:T(1,128)}), f32[8,1,1280]{2,1,0:T(1,128)S(1)}, u32[]{:S(2)}, u32[]{:S(2)}) %all-to-all-start.2) | async-done | bytes 40992 | tf_op jit(solution)/shard_map/all_to_all | solution.py:118
  66.4 0.7 reduce.5
  68.3 0.8 collective-permute-start.8
  69.1 1.3 %collective-permute-start.7 = (f32[5376]{0:T(1024)S(1)}, f32[5376]{0:T(1024)S(1)}, u32[]{:S(2)}, u32[]{:S(2)}) collective-permute-start(f32[5376]{0:T(1024)S(1)} %constant_dynamic-update-slice_fusion.1), channel_id=1, source_target_pairs={{0,1},{1,0},{2,3},{3,2},{4,5},{5,4},{6,7},{7,6},{8,9},{9,8},{10,11... | collective-permute-start | bytes 64520 | tf_op jit(solution)/shard_map/ppermute | solution.py:13
  70.5 1.7 %collective-permute-done.8 = f32[5376]{0:T(1024)S(1)} collective-permute-done((f32[5376]{0:T(1024)S(1)}, f32[5376]{0:T(1024)S(1)}, u32[]{:S(2)}, u32[]{:S(2)}) %collective-permute-start.8) | collective-permute-done | bytes 21536 | tf_op jit(solution)/shard_map/ppermute | solution.py:13
  74.6 9.7 %all_to_all.23 = f32[8,1,1]{2,1,0:T(1,128)S(1)} all-to-all(f32[8,1,1]{2,1,0:T(1,128)S(1)} %broadcast_in_dim.250), channel_id=1, replica_groups=mesh['box'=8,'rep'=4] {'box'}, dimensions={0} | all-to-all | bytes 64 | tf_op jit(solution)/shard_map/all_to_all | solution.py:36
  (146 shorter events, 13.7 us)
Async XLA Ops:
  0.6 11.8 %copy-start = (bf16[20,4,64,64]{3,2,1,0:T(8,128)(2,1)S(1)}, bf16[20,4,64,64]{3,2,1,0:T(8,128)(2,1)}, u32[]{:S(2)}) copy-start(bf16[20,4,64,64]{3,2,1,0:T(8,128)(2,1)} %param.16) | copy-start | bytes 1966084
  0.6 9.3 %copy-start.2 = (f32[16,256]{1,0:T(8,128)S(1)}, f32[16,256]{1,0:T(8,128)}, u32[]{:S(2)}) copy-start(f32[16,256]{1,0:T(8,128)} %param.9) | copy-start | bytes 49156
  0.7 3.8 %copy-start.5 = (s32[16,2]{0,1:T(2,128)S(1)}, s32[16,2]{0,1:T(2,128)}, u32[]{:S(2)}) copy-start(s32[16,2]{0,1:T(2,128)} %param.12) | copy-start | bytes 388
  0.7 10.6 %copy-start.1 = (bf16[16,64,256]{2,1,0:T(8,128)(2,1)S(1)}, bf16[16,64,256]{2,1,0:T(8,128)(2,1)}, u32[]{:S(2)}) copy-start(bf16[16,64,256]{2,1,0:T(8,128)(2,1)} %param.13) | copy-start | bytes 1572868
  0.7 10.9 %copy-start.4 = (s32[20,4]{0,1:T(4,128)S(1)}, s32[20,4]{0,1:T(4,128)}, u32[]{:S(2)}) copy-start(s32[20,4]{0,1:T(4,128)} %param.17) | copy-start | bytes 964
  0.7 11.4 %copy-start.7 = (bf16[16,64,64]{2,1,0:T(8,128)(2,1)S(1)}, bf16[16,64,64]{2,1,0:T(8,128)(2,1)}, u32[]{:S(2)}) copy-start(bf16[16,64,64]{2,1,0:T(8,128)(2,1)} %param.14) | copy-start | bytes 393220
  0.7 11.6 %copy-start.6 = (s32[16]{0:T(128)S(1)}, s32[16]{0:T(128)}, u32[]{:S(2)}) copy-start(s32[16]{0:T(128)} %param.15) | copy-start | bytes 196
  5.0 20.0 %collective-permute-start.1 = (f32[16,256]{1,0:T(8,128)S(1)}, f32[16,256]{1,0:T(8,128)S(1)}, u32[]{:S(2)}, u32[]{:S(2)}) collective-permute-start(f32[16,256]{1,0:T(8,128)S(1)} %slice.183), channel_id=1, source_target_pairs={{0,4},{4,8},{8,12},{12,16},{16,20},{20,24},{24,28},{1,5},{5,9},{9,... | collective-permute-start | bytes 49160 | tf_op jit(solution)/shard_map/ppermute | solution.py:113
  9.9 11.0 %collective-permute-start = (bf16[16,256]{1,0:T(8,128)(2,1)S(1)}, bf16[16,256]{1,0:T(8,128)(2,1)S(1)}, u32[]{:S(2)}, u32[]{:S(2)}) collective-permute-start(bf16[16,256]{1,0:T(8,128)(2,1)S(1)} %convert_element_type.65), channel_id=1, source_target_pairs={{4,0},{8,4},{12,8},{16,12},{20,16},{24,20},{28,24},{5,1},{9,5},{13... | collective-permute-start | bytes 24584 | tf_op jit(solution)/shard_map/ppermute | solution.py:110
  12.8 22.5 %copy-start.3 = (f32[16,256]{1,0:T(8,128)S(1)}, f32[16,256]{1,0:T(8,128)}, u32[]{:S(2)}) copy-start(f32[16,256]{1,0:T(8,128)} %param.10) | copy-start | bytes 49156
  13.8 13.7 %all-to-all-start = ((f32[8,1,1280]{2,1,0:T(1,128)}), f32[8,1,1280]{2,1,0:T(1,128)S(1)}, u32[]{:S(2)}, u32[]{:S(2)}) async-start(f32[8,1,1280]{2,1,0:T(1,128)} %reshape.310), calls=%async_computation | async-start | bytes 81920 | tf_op jit(solution)/shard_map/all_to_all | solution.py:118
  29.9 3.9 %collective-permute-start.3 = (f32[5376]{0:T(1024)S(1)}, f32[5376]{0:T(1024)S(1)}, u32[]{:S(2)}, u32[]{:S(2)}) collective-permute-start(f32[5376]{0:T(1024)S(1)} %constant_dynamic-update-slice_fusion), channel_id=1, source_target_pairs={{0,2},{1,3},{2,0},{3,1},{4,6},{5,7},{6,4},{7,5},{8,10},{9,11},{10,... | collective-permute-start | bytes 64520 | tf_op jit(solution)/shard_map/ppermute | solution.py:13
  31.4 3.3 %collective-permute-start.4 = (f32[5376]{0:T(1024)S(1)}, f32[5376]{0:T(1024)S(1)}, u32[]{:S(2)}, u32[]{:S(2)}) collective-permute-start(f32[5376]{0:T(1024)S(1)} %constant_dynamic-update-slice_fusion), channel_id=1, source_target_pairs={{0,3},{1,2},{2,1},{3,0},{4,7},{5,6},{6,5},{7,4},{8,11},{9,10},{10,... | collective-permute-start | bytes 64520 | tf_op jit(solution)/shard_map/ppermute | solution.py:13
  31.4 3.3 %collective-permute-start.2 = (f32[5376]{0:T(1024)S(1)}, f32[5376]{0:T(1024)S(1)}, u32[]{:S(2)}, u32[]{:S(2)}) collective-permute-start(f32[5376]{0:T(1024)S(1)} %constant_dynamic-update-slice_fusion), channel_id=1, source_target_pairs={{0,1},{1,0},{2,3},{3,2},{4,5},{5,4},{6,7},{7,6},{8,9},{9,8},{10,11... | collective-permute-start | bytes 64520 | tf_op jit(solution)/shard_map/ppermute | solution.py:13
  45.6 14.2 %collective-permute-start.5 = (bf16[16,256]{1,0:T(8,128)(2,1)S(1)}, bf16[16,256]{1,0:T(8,128)(2,1)S(1)}, u32[]{:S(2)}, u32[]{:S(2)}) collective-permute-start(bf16[16,256]{1,0:T(8,128)(2,1)S(1)} %fusion.70), channel_id=1, source_target_pairs={{4,0},{8,4},{12,8},{16,12},{20,16},{24,20},{28,24},{5,1},{9,5},{13... | collective-permute-start | bytes 24584 | tf_op jit(solution)/shard_map/ppermute | solution.py:110
  50.2 13.7 %collective-permute-start.6 = (f32[16,256]{1,0:T(8,128)S(1)}, f32[16,256]{1,0:T(8,128)S(1)}, u32[]{:S(2)}, u32[]{:S(2)}) collective-permute-start(f32[16,256]{1,0:T(8,128)S(1)} %slice.195), channel_id=1, source_target_pairs={{0,4},{4,8},{8,12},{12,16},{16,20},{20,24},{24,28},{1,5},{5,9},{9,... | collective-permute-start | bytes 49160 | tf_op jit(solution)/shard_map/ppermute | solution.py:113
  56.4 10.0 %all-to-all-start.2 = ((f32[8,1,1280]{2,1,0:T(1,128)}), f32[8,1,1280]{2,1,0:T(1,128)S(1)}, u32[]{:S(2)}, u32[]{:S(2)}) async-start(f32[8,1,1280]{2,1,0:T(1,128)} %reshape.312), calls=%async_computation.2 | async-start | bytes 81920 | tf_op jit(solution)/shard_map/all_to_all | solution.py:118
  68.3 3.9 %collective-permute-start.8 = (f32[5376]{0:T(1024)S(1)}, f32[5376]{0:T(1024)S(1)}, u32[]{:S(2)}, u32[]{:S(2)}) collective-permute-start(f32[5376]{0:T(1024)S(1)} %constant_dynamic-update-slice_fusion.1), channel_id=1, source_target_pairs={{0,2},{1,3},{2,0},{3,1},{4,6},{5,7},{6,4},{7,5},{8,10},{9,11},{10,... | collective-permute-start | bytes 64520 | tf_op jit(solution)/shard_map/ppermute | solution.py:13
  69.1 3.5 %collective-permute-start.9 = (f32[5376]{0:T(1024)S(1)}, f32[5376]{0:T(1024)S(1)}, u32[]{:S(2)}, u32[]{:S(2)}) collective-permute-start(f32[5376]{0:T(1024)S(1)} %constant_dynamic-update-slice_fusion.1), channel_id=1, source_target_pairs={{0,3},{1,2},{2,1},{3,0},{4,7},{5,6},{6,5},{7,4},{8,11},{9,10},{10,... | collective-permute-start | bytes 64520 | tf_op jit(solution)/shard_map/ppermute | solution.py:13
  69.1 3.5 %collective-permute-start.7 = (f32[5376]{0:T(1024)S(1)}, f32[5376]{0:T(1024)S(1)}, u32[]{:S(2)}, u32[]{:S(2)}) collective-permute-start(f32[5376]{0:T(1024)S(1)} %constant_dynamic-update-slice_fusion.1), channel_id=1, source_target_pairs={{0,1},{1,0},{2,3},{3,2},{4,5},{5,4},{6,7},{7,6},{8,9},{9,8},{10,11... | collective-permute-start | bytes 64520 | tf_op jit(solution)/shard_map/ppermute | solution.py:13

commit v9 on v8

--- a/solution.py
+++ b/solution.py
@@ -110,12 +110,13 @@
         following = lax.ppermute(
             rounded, "box", [(i, i - 1) for i in range(1, box_devices)]
         )
-        arrived = lax.ppermute(
-            landed[box_count:], "box", [(i, i + 1) for i in range(box_devices - 1)]
-        )
         coef_wide = node_coef.astype(jnp.float32)
         far_send = jnp.where(below, coef_wide[None], spread)
         got_far = lax.all_to_all(far_send, "box", 0, 0, tiled=True)
+        landed_next, got_far = lax.optimization_barrier((landed[box_count:], got_far))
+        arrived = lax.ppermute(
+            landed_next, "box", [(i, i + 1) for i in range(box_devices - 1)]
+        )
         mirror_in = jnp.sum(jnp.where(below, got_far, 0.0), axis=0)
         every_coef = jnp.where(
             above, got_far, jnp.where(devices[:, None, None] == box_rank, coef_wide[None], 0.0)

time: 85.8 us -> 93.7 us (1.092)
  blocking collectives: 19.6 us -> 25.4 us
  other arithmetic: 5.01 us -> 7.73 us
  matrix products: 16.9 us -> 18.9 us
  starting transfers between devices: 26.6 us -> 25.2 us
  waiting for transfers between devices: 9.61 us -> 8.37 us
    all_to_all x2, blocking collectives: 19.6 us -> 25.4 us  [box_sum(): got = lax.all_to_all(sent, 'box', 0, 0, tiled=True)]
    ppermute x2, starting transfers between devices: 9.42 us -> 6.99 us  [local(): lax.ppermute(landed_next, 'box', [(i, i + 1) for i in range(box_devices -...]
    all_to_all x2, waiting for transfers between devices: 4.83 us -> 2.61 us  [local(): got_far = lax.all_to_all(far_send, 'box', 0, 0, tiled=True)]
    convert_element_type x4, other arithmetic: 0.87 us -> 2.27 us  [local(): rounded = direction.astype(jnp.bfloat16)]
    dot_general x2, matrix products: 0.47 us -> 1.51 us  [local(): jnp.einsum('brl,bl->br', leaf_bases, rounded, preferred_element_type=jnp....]
    ppermute x2, waiting for transfers between devices: 0.01 us -> 0.97 us  [local(): lax.ppermute(landed_next, 'box', [(i, i + 1) for i in range(box_devices -...]
    dot_general x2, matrix products: 0.36 us -> 1.3 us  [local(): jnp.einsum('brq,br->bq', transfer, leaf_coef, preferred_element_type=jnp....]
  transfers between devices with their start and end apart: 12 -> 12, of which waited for: 6 -> 7; matrix products, arithmetic and copies ran while one was open for 19% -> 21% of each run, Pallas kernels for 0% -> 0%
where the time goes in v9:
time: 93.7 us; the launch traced here: 92.9 us
  blocking collectives  25.4 us (27%)
  starting transfers between devices  25.2 us (27%)
  matrix products  18.9 us (20%)
  waiting for transfers between devices  8.37 us (9%)
  other arithmetic  7.73 us (8%)
  local copies, waits for them, and re-layouts  6.12 us (7%)
  between operations  1.18 us (1%)
    all_to_all x2, blocking collectives, box_sum(): got = lax.all_to_all(sent, 'box', 0, 0, tiled=True)  25.4 us
    all_to_all x2, starting transfers between devices, local(): got_far = lax.all_to_all(far_send, 'box', 0, 0, tiled=True)  11.2 us
    ppermute x2, starting transfers between devices, local(): lax.ppermute(landed_next, 'box', [(i, i + 1) for i in range(box_devices -...  6.99 us
    dot_general x2, matrix products, local(): jnp.einsum('bsij,bsj->bi', near_tiles, near_in, preferred_element_type=jn...  6.73 us
    dot_general x2, matrix products, local(): jnp.einsum('bsij,bi->bsj', near_tiles, rounded, preferred_element_type=jn...  5.66 us
    ppermute x6, waiting for transfers between devices, rep_sum(): lax.ppermute(vector, 'rep', [(i, i ^ mask) for i in range(count)])  4.77 us
    ppermute x6, starting transfers between devices, rep_sum(): lax.ppermute(vector, 'rep', [(i, i ^ mask) for i in range(count)])  4.41 us
    all_to_all x2, waiting for transfers between devices, local(): got_far = lax.all_to_all(far_send, 'box', 0, 0, tiled=True)  2.61 us
  transfers between devices with their start and end apart: 12, of which 7 were waited for; matrix products, arithmetic and copies ran while one was open for 21% of the time, Pallas kernels for 0%

profile of v9, /device:TPU:0, one launch (start us, length us, event | category | flops | bytes accessed | tf_op | source)
XLA Modules:
  0.0 92.9 jit_solution(7497137980555635627)
XLA Ops:
  0.7 0.8 convert_bitcast_fusion.2
  1.5 1.3 %fusion.33 = f32[16,1,64]{2,1,0:T(1,128)S(1)} fusion(bf16[16,64,256]{2,1,0:T(8,128)(2,1)} %param.13, bf16[16,256,1]{1,0,2:T(8,128)(2,1)S(1)} %convert_bitcast_fusion.2), kind=kOutput, calls=%fused_computation.60 | convolution fusion | flops 524288 | bytes 536576 | tf_op jit(solution)/shard_map/brl,bl->br/dot_general | solution.py:94
  4.0 1.1 %fusion.58 = f32[16,1,64]{2,1,0:T(1,128)S(1)} fusion(bf16[16,64,64]{2,1,0:T(8,128)(2,1)} %param.14, bf16[16,64,1]{1,0,2:T(8,128)(2,1)S(1)} %convert_bitcast_fusion.1), kind=kOutput, calls=%fused_computation.94 | convolution fusion | flops 131072 | bytes 137216 | tf_op jit(solution)/shard_map/brq,br->bq/dot_general | solution.py:97
  7.3 7.3 %all-to-all-start = ((f32[8,1,1280]{2,1,0:T(1,128)}), f32[8,1,1280]{2,1,0:T(1,128)S(1)}, u32[]{:S(2)}, u32[]{:S(2)}) async-start(f32[8,1,1280]{2,1,0:T(1,128)} %reshape.310), calls=%async_computation | async-start | bytes 81920 | tf_op jit(solution)/shard_map/all_to_all | solution.py:115
  15.3 1.3 %collective-permute-start = (bf16[16,256]{1,0:T(8,128)(2,1)S(1)}, bf16[16,256]{1,0:T(8,128)(2,1)S(1)}, u32[]{:S(2)}, u32[]{:S(2)}) collective-permute-start(bf16[16,256]{1,0:T(8,128)(2,1)S(1)} %convert_element_type.65), channel_id=1, source_target_pairs={{4,0},{8,4},{12,8},{16,12},{20,16},{24,20},{28,24},{5,1},{9,5},{13... | collective-permute-start | bytes 24584 | tf_op jit(solution)/shard_map/ppermute | solution.py:110
  17.3 2.8 %fusion.35 = f32[16,1,2,256]{3,1,2,0:T(1,128)S(1)} fusion(bf16[16,2,256,256]{3,2,1,0:T(8,128)(2,1)} %param.11, bf16[16,256,1,1]{1,0,2,3:T(8,128)(2,1)S(1)} %convert_bitcast_fusion.3), kind=kOutput, calls=%fused_computation.62 | convolution fusion | flops 4194304 | bytes 4235264 | tf_op jit(solution)/shard_map/bsij,bi->bsj/dot_general | solution.py:88
  21.7 3.4 %fusion.21 = f32[16,1,256,1]{2,1,3,0:T(1,128)S(1)} fusion(bf16[16,2,256,256]{3,2,1,0:T(8,128)(2,1)} %param.11, bf16[16,2,256,1]{2,1,0,3:T(2,128)(2,1)S(1)} %fusion.23), kind=kOutput, calls=%fused_computation.36 | convolution fusion | flops 4194304 | bytes 4227072 | tf_op jit(solution)/shard_map/bsij,bsj->bi/dot_general | solution.py:127
  25.6 0.7 reduce.4
  26.5 4.6 %collective-permute-start.1 = (f32[16,256]{1,0:T(8,128)S(1)}, f32[16,256]{1,0:T(8,128)S(1)}, u32[]{:S(2)}, u32[]{:S(2)}) collective-permute-start(f32[16,256]{1,0:T(8,128)S(1)} %slice.183), channel_id=1, source_target_pairs={{0,4},{4,8},{8,12},{12,16},{16,20},{20,24},{24,28},{1,5},{5,9},{9,... | collective-permute-start | bytes 49160 | tf_op jit(solution)/shard_map/ppermute | solution.py:117
  32.6 1.6 %collective-permute-start.3 = (f32[5376]{0:T(1024)S(1)}, f32[5376]{0:T(1024)S(1)}, u32[]{:S(2)}, u32[]{:S(2)}) collective-permute-start(f32[5376]{0:T(1024)S(1)} %constant_dynamic-update-slice_fusion), channel_id=1, source_target_pairs={{0,2},{1,3},{2,0},{3,1},{4,6},{5,7},{6,4},{7,5},{8,10},{9,11},{10,... | collective-permute-start | bytes 64520 | tf_op jit(solution)/shard_map/ppermute | solution.py:13
  34.8 1.7 %collective-permute-done.3 = f32[5376]{0:T(1024)S(1)} collective-permute-done((f32[5376]{0:T(1024)S(1)}, f32[5376]{0:T(1024)S(1)}, u32[]{:S(2)}, u32[]{:S(2)}) %collective-permute-start.3) | collective-permute-done | bytes 21536 | tf_op jit(solution)/shard_map/ppermute | solution.py:13
  36.5 0.9 collective-permute-done.4
  38.3 13.9 %all_to_all.22 = f32[8,1,4]{2,1,0:T(1,128)S(1)} all-to-all(f32[8,1,4]{2,1,0:T(1,128)S(1)} %broadcast_in_dim.242), channel_id=1, replica_groups=mesh['box'=8,'rep'=4] {'box'}, dimensions={0} | all-to-all | bytes 256 | tf_op jit(solution)/shard_map/all_to_all | solution.py:36
  52.6 1.3 %collective-permute-start.5 = (bf16[16,256]{1,0:T(8,128)(2,1)S(1)}, bf16[16,256]{1,0:T(8,128)(2,1)S(1)}, u32[]{:S(2)}, u32[]{:S(2)}) collective-permute-start(bf16[16,256]{1,0:T(8,128)(2,1)S(1)} %fusion.70), channel_id=1, source_target_pairs={{4,0},{8,4},{12,8},{16,12},{20,16},{24,20},{28,24},{5,1},{9,5},{13... | collective-permute-start | bytes 24584 | tf_op jit(solution)/shard_map/ppermute | solution.py:110
  53.9 2.8 %fusion.31 = f32[16,1,2,256]{3,1,2,0:T(1,128)S(1)} fusion(bf16[16,2,256,256]{3,2,1,0:T(8,128)(2,1)} %param.11, bf16[16,256,1,1]{1,0,2,3:T(8,128)(2,1)S(1)} %bitcast.131), kind=kOutput, calls=%fused_computation.58 | convolution fusion | flops 4194304 | bytes 4235264 | tf_op jit(solution)/shard_map/bsij,bi->bsj/dot_general | solution.py:88
  58.6 3.9 %all-to-all-start.2 = ((f32[8,1,1280]{2,1,0:T(1,128)}), f32[8,1,1280]{2,1,0:T(1,128)S(1)}, u32[]{:S(2)}, u32[]{:S(2)}) async-start(f32[8,1,1280]{2,1,0:T(1,128)} %reshape.312), calls=%async_computation.2 | async-start | bytes 81920 | tf_op jit(solution)/shard_map/all_to_all | solution.py:115
  63.3 3.4 %fusion.19 = f32[16,1,256,1]{2,1,3,0:T(1,128)S(1)} fusion(bf16[16,2,256,256]{3,2,1,0:T(8,128)(2,1)} %param.11, bf16[16,2,256,1]{2,1,0,3:T(2,128)(2,1)S(1)} %fusion.24), kind=kOutput, calls=%fused_computation.33 | convolution fusion | flops 4194304 | bytes 4227072 | tf_op jit(solution)/shard_map/bsij,bsj->bi/dot_general | solution.py:127
  66.6 2.6 %all-to-all-done.2 = f32[8,1,1280]{2,1,0:T(1,128)S(1)} async-done(((f32[8,1,1280]{2,1,0:T(1,128)}), f32[8,1,1280]{2,1,0:T(1,128)S(1)}, u32[]{:S(2)}, u32[]{:S(2)}) %all-to-all-start.2) | async-done | bytes 40992 | tf_op jit(solution)/shard_map/all_to_all | solution.py:115
  69.3 0.7 reduce.5
  70.3 2.4 %collective-permute-start.6 = (f32[16,256]{1,0:T(8,128)S(1)}, f32[16,256]{1,0:T(8,128)S(1)}, u32[]{:S(2)}, u32[]{:S(2)}) collective-permute-start(f32[16,256]{1,0:T(8,128)S(1)} %slice.195), channel_id=1, source_target_pairs={{0,4},{4,8},{8,12},{12,16},{16,20},{20,24},{24,28},{1,5},{5,9},{9,... | collective-permute-start | bytes 49160 | tf_op jit(solution)/shard_map/ppermute | solution.py:117
  74.1 0.9 collective-permute-start.8
  75.0 1.3 %collective-permute-start.7 = (f32[5376]{0:T(1024)S(1)}, f32[5376]{0:T(1024)S(1)}, u32[]{:S(2)}, u32[]{:S(2)}) collective-permute-start(f32[5376]{0:T(1024)S(1)} %constant_dynamic-update-slice_fusion.1), channel_id=1, source_target_pairs={{0,1},{1,0},{2,3},{3,2},{4,5},{5,4},{6,7},{7,6},{8,9},{9,8},{10,11... | collective-permute-start | bytes 64520 | tf_op jit(solution)/shard_map/ppermute | solution.py:13
  76.3 1.7 %collective-permute-done.8 = f32[5376]{0:T(1024)S(1)} collective-permute-done((f32[5376]{0:T(1024)S(1)}, f32[5376]{0:T(1024)S(1)}, u32[]{:S(2)}, u32[]{:S(2)}) %collective-permute-start.8) | collective-permute-done | bytes 21536 | tf_op jit(solution)/shard_map/ppermute | solution.py:13
  80.5 11.5 %all_to_all.23 = f32[8,1,1]{2,1,0:T(1,128)S(1)} all-to-all(f32[8,1,1]{2,1,0:T(1,128)S(1)} %broadcast_in_dim.250), channel_id=1, replica_groups=mesh['box'=8,'rep'=4] {'box'}, dimensions={0} | all-to-all | bytes 64 | tf_op jit(solution)/shard_map/all_to_all | solution.py:36
  (142 shorter events, 17.7 us)
Async XLA Ops:
  0.6 5.3 %copy-start = (bf16[20,4,64,64]{3,2,1,0:T(8,128)(2,1)S(1)}, bf16[20,4,64,64]{3,2,1,0:T(8,128)(2,1)}, u32[]{:S(2)}) copy-start(bf16[20,4,64,64]{3,2,1,0:T(8,128)(2,1)} %param.16) | copy-start | bytes 1966084
  0.6 19.6 %copy-start.4 = (s32[16,2]{0,1:T(2,128)S(1)}, s32[16,2]{0,1:T(2,128)}, u32[]{:S(2)}) copy-start(s32[16,2]{0,1:T(2,128)} %param.12) | copy-start | bytes 388
  7.3 17.8 %all-to-all-start = ((f32[8,1,1280]{2,1,0:T(1,128)}), f32[8,1,1280]{2,1,0:T(1,128)S(1)}, u32[]{:S(2)}, u32[]{:S(2)}) async-start(f32[8,1,1280]{2,1,0:T(1,128)} %reshape.310), calls=%async_computation | async-start | bytes 81920 | tf_op jit(solution)/shard_map/all_to_all | solution.py:115
  15.3 5.7 %collective-permute-start = (bf16[16,256]{1,0:T(8,128)(2,1)S(1)}, bf16[16,256]{1,0:T(8,128)(2,1)S(1)}, u32[]{:S(2)}, u32[]{:S(2)}) collective-permute-start(bf16[16,256]{1,0:T(8,128)(2,1)S(1)} %convert_element_type.65), channel_id=1, source_target_pairs={{4,0},{8,4},{12,8},{16,12},{20,16},{24,20},{28,24},{5,1},{9,5},{13... | collective-permute-start | bytes 24584 | tf_op jit(solution)/shard_map/ppermute | solution.py:110
  20.1 17.5 %copy-start.5 = (bf16[16,64,64]{2,1,0:T(8,128)(2,1)S(1)}, bf16[16,64,64]{2,1,0:T(8,128)(2,1)}, u32[]{:S(2)}) copy-start(bf16[16,64,64]{2,1,0:T(8,128)(2,1)} %param.14) | copy-start | bytes 393220
  20.1 17.8 %copy-start.1 = (bf16[16,64,256]{2,1,0:T(8,128)(2,1)S(1)}, bf16[16,64,256]{2,1,0:T(8,128)(2,1)}, u32[]{:S(2)}) copy-start(bf16[16,64,256]{2,1,0:T(8,128)(2,1)} %param.13) | copy-start | bytes 1572868
  20.1 18.0 %copy-start.2 = (f32[16,256]{1,0:T(8,128)S(1)}, f32[16,256]{1,0:T(8,128)}, u32[]{:S(2)}) copy-start(f32[16,256]{1,0:T(8,128)} %param.9) | copy-start | bytes 49156
  20.1 18.0 %copy-start.3 = (f32[16,256]{1,0:T(8,128)S(1)}, f32[16,256]{1,0:T(8,128)}, u32[]{:S(2)}) copy-start(f32[16,256]{1,0:T(8,128)} %param.10) | copy-start | bytes 49156
  26.5 6.1 %collective-permute-start.1 = (f32[16,256]{1,0:T(8,128)S(1)}, f32[16,256]{1,0:T(8,128)S(1)}, u32[]{:S(2)}, u32[]{:S(2)}) collective-permute-start(f32[16,256]{1,0:T(8,128)S(1)} %slice.183), channel_id=1, source_target_pairs={{0,4},{4,8},{8,12},{12,16},{16,20},{20,24},{24,28},{1,5},{5,9},{9,... | collective-permute-start | bytes 49160 | tf_op jit(solution)/shard_map/ppermute | solution.py:117
  32.6 3.9 %collective-permute-start.3 = (f32[5376]{0:T(1024)S(1)}, f32[5376]{0:T(1024)S(1)}, u32[]{:S(2)}, u32[]{:S(2)}) collective-permute-start(f32[5376]{0:T(1024)S(1)} %constant_dynamic-update-slice_fusion), channel_id=1, source_target_pairs={{0,2},{1,3},{2,0},{3,1},{4,6},{5,7},{6,4},{7,5},{8,10},{9,11},{10,... | collective-permute-start | bytes 64520 | tf_op jit(solution)/shard_map/ppermute | solution.py:13
  34.1 3.3 %collective-permute-start.4 = (f32[5376]{0:T(1024)S(1)}, f32[5376]{0:T(1024)S(1)}, u32[]{:S(2)}, u32[]{:S(2)}) collective-permute-start(f32[5376]{0:T(1024)S(1)} %constant_dynamic-update-slice_fusion), channel_id=1, source_target_pairs={{0,3},{1,2},{2,1},{3,0},{4,7},{5,6},{6,5},{7,4},{8,11},{9,10},{10,... | collective-permute-start | bytes 64520 | tf_op jit(solution)/shard_map/ppermute | solution.py:13
  34.1 3.3 %collective-permute-start.2 = (f32[5376]{0:T(1024)S(1)}, f32[5376]{0:T(1024)S(1)}, u32[]{:S(2)}, u32[]{:S(2)}) collective-permute-start(f32[5376]{0:T(1024)S(1)} %constant_dynamic-update-slice_fusion), channel_id=1, source_target_pairs={{0,1},{1,0},{2,3},{3,2},{4,5},{5,4},{6,7},{7,6},{8,9},{9,8},{10,11... | collective-permute-start | bytes 64520 | tf_op jit(solution)/shard_map/ppermute | solution.py:13
  52.6 10.0 %collective-permute-start.5 = (bf16[16,256]{1,0:T(8,128)(2,1)S(1)}, bf16[16,256]{1,0:T(8,128)(2,1)S(1)}, u32[]{:S(2)}, u32[]{:S(2)}) collective-permute-start(bf16[16,256]{1,0:T(8,128)(2,1)S(1)} %fusion.70), channel_id=1, source_target_pairs={{4,0},{8,4},{12,8},{16,12},{20,16},{24,20},{28,24},{5,1},{9,5},{13... | collective-permute-start | bytes 24584 | tf_op jit(solution)/shard_map/ppermute | solution.py:110
  58.6 10.7 %all-to-all-start.2 = ((f32[8,1,1280]{2,1,0:T(1,128)}), f32[8,1,1280]{2,1,0:T(1,128)S(1)}, u32[]{:S(2)}, u32[]{:S(2)}) async-start(f32[8,1,1280]{2,1,0:T(1,128)} %reshape.312), calls=%async_computation.2 | async-start | bytes 81920 | tf_op jit(solution)/shard_map/all_to_all | solution.py:115
  70.3 3.8 %collective-permute-start.6 = (f32[16,256]{1,0:T(8,128)S(1)}, f32[16,256]{1,0:T(8,128)S(1)}, u32[]{:S(2)}, u32[]{:S(2)}) collective-permute-start(f32[16,256]{1,0:T(8,128)S(1)} %slice.195), channel_id=1, source_target_pairs={{0,4},{4,8},{8,12},{12,16},{16,20},{20,24},{24,28},{1,5},{5,9},{9,... | collective-permute-start | bytes 49160 | tf_op jit(solution)/shard_map/ppermute | solution.py:117
  74.1 3.9 %collective-permute-start.8 = (f32[5376]{0:T(1024)S(1)}, f32[5376]{0:T(1024)S(1)}, u32[]{:S(2)}, u32[]{:S(2)}) collective-permute-start(f32[5376]{0:T(1024)S(1)} %constant_dynamic-update-slice_fusion.1), channel_id=1, source_target_pairs={{0,2},{1,3},{2,0},{3,1},{4,6},{5,7},{6,4},{7,5},{8,10},{9,11},{10,... | collective-permute-start | bytes 64520 | tf_op jit(solution)/shard_map/ppermute | solution.py:13
  75.0 3.5 %collective-permute-start.9 = (f32[5376]{0:T(1024)S(1)}, f32[5376]{0:T(1024)S(1)}, u32[]{:S(2)}, u32[]{:S(2)}) collective-permute-start(f32[5376]{0:T(1024)S(1)} %constant_dynamic-update-slice_fusion.1), channel_id=1, source_target_pairs={{0,3},{1,2},{2,1},{3,0},{4,7},{5,6},{6,5},{7,4},{8,11},{9,10},{10,... | collective-permute-start | bytes 64520 | tf_op jit(solution)/shard_map/ppermute | solution.py:13
  75.0 3.5 %collective-permute-start.7 = (f32[5376]{0:T(1024)S(1)}, f32[5376]{0:T(1024)S(1)}, u32[]{:S(2)}, u32[]{:S(2)}) collective-permute-start(f32[5376]{0:T(1024)S(1)} %constant_dynamic-update-slice_fusion.1), channel_id=1, source_target_pairs={{0,1},{1,0},{2,3},{3,2},{4,5},{5,4},{6,7},{7,6},{8,9},{9,8},{10,11... | collective-permute-start | bytes 64520 | tf_op jit(solution)/shard_map/ppermute | solution.py:13

commit v10 on v9

--- a/solution.py
+++ b/solution.py
@@ -112,11 +112,15 @@
         )
         coef_wide = node_coef.astype(jnp.float32)
         far_send = jnp.where(below, coef_wide[None], spread)
-        got_far = lax.all_to_all(far_send, "box", 0, 0, tiled=True)
-        landed_next, got_far = lax.optimization_barrier((landed[box_count:], got_far))
-        arrived = lax.ppermute(
-            landed_next, "box", [(i, i + 1) for i in range(box_devices - 1)]
+        is_next = (devices == box_rank + 1)[:, None]
+        near_send = jnp.where(is_next, landed[box_count:].reshape(1, -1), 0.0)
+        got = lax.all_to_all(
+            jnp.concatenate([far_send.reshape(box_devices, far_size), near_send], axis=1),
+            "box", 0, 0, tiled=True,
         )
+        got_far = got[:, :far_size].reshape(box_devices, node_count, rank_width)
+        is_prev = (devices == box_rank - 1)[:, None]
+        arrived = jnp.sum(jnp.where(is_prev, got[:, far_size:], 0.0), axis=0).reshape(box_count, leaf)
         mirror_in = jnp.sum(jnp.where(below, got_far, 0.0), axis=0)
         every_coef = jnp.where(
             above, got_far, jnp.where(devices[:, None, None] == box_rank, coef_wide[None], 0.0)

time: 93.7 us -> 82.9 us (0.88)
  starting transfers between devices: 25.2 us -> 18.1 us
  blocking collectives: 25.4 us -> 21.1 us
  waiting for transfers between devices: 8.37 us -> 11.9 us
  other arithmetic: 7.73 us -> 5.15 us
    ppermute x2 -> x0, starting transfers between devices: 6.99 us -> none  [local(): lax.ppermute(landed_next, 'box', [(i, i + 1) for i in range(box_devices -...]
    all_to_all x2, blocking collectives: 25.4 us -> 21.1 us  [box_sum(): got = lax.all_to_all(sent, 'box', 0, 0, tiled=True)]
    ppermute x2, waiting for transfers between devices: 0.01 us -> 3.67 us  [local(): lax.ppermute(rounded, 'box', [(i, i - 1) for i in range(1, box_devices)])]
    all_to_all x2 -> x1, other arithmetic: 1.48 us -> 0.01 us  [local(): lax.all_to_all(jnp.concatenate([far_send.reshape(box_devices, far_size),...]
    unnamed x18 -> x24, local copies, waits for them, and re-layouts: 1.51 us -> 0.13 us
    all_to_all x1 -> x2, local copies, waits for them, and re-layouts: 0.53 us -> 1.6 us  [local(): lax.all_to_all(jnp.concatenate([far_send.reshape(box_devices, far_size),...]
    ppermute x2 -> x0, waiting for transfers between devices: 0.97 us -> none  [local(): lax.ppermute(landed_next, 'box', [(i, i + 1) for i in range(box_devices -...]
    dot_general x2, matrix products: 1.3 us -> 0.36 us  [local(): jnp.einsum('brq,br->bq', transfer, leaf_coef, preferred_element_type=jnp....]
  transfers between devices with their start and end apart: 12 -> 10, of which waited for: 7 -> 6; matrix products, arithmetic and copies ran while one was open for 21% -> 17% of each run, Pallas kernels for 0% -> 0%
where the time goes in v10:
time: 82.9 us; the launch traced here: 82.2 us
  blocking collectives  21.1 us (25%)
  matrix products  18.1 us (22%)
  starting transfers between devices  18.1 us (22%)
  waiting for transfers between devices  11.9 us (14%)
  local copies, waits for them, and re-layouts  6.51 us (8%)
  other arithmetic  5.15 us (6%)
  between operations  1.3 us (2%)
    all_to_all x2, blocking collectives, box_sum(): got = lax.all_to_all(sent, 'box', 0, 0, tiled=True)  21.1 us
    all_to_all x2, starting transfers between devices, local(): lax.all_to_all(jnp.concatenate([far_send.reshape(box_devices, far_size),...  11.2 us
    dot_general x2, matrix products, local(): jnp.einsum('bsij,bsj->bi', near_tiles, near_in, preferred_element_type=jn...  6.73 us
    dot_general x2, matrix products, local(): jnp.einsum('bsij,bi->bsj', near_tiles, rounded, preferred_element_type=jn...  5.66 us
    ppermute x6, waiting for transfers between devices, rep_sum(): lax.ppermute(vector, 'rep', [(i, i ^ mask) for i in range(count)])  4.77 us
    ppermute x6, starting transfers between devices, rep_sum(): lax.ppermute(vector, 'rep', [(i, i ^ mask) for i in range(count)])  4.35 us
    ppermute x2, waiting for transfers between devices, local(): lax.ppermute(rounded, 'box', [(i, i - 1) for i in range(1, box_devices)])  3.67 us
    all_to_all x2, waiting for transfers between devices, local(): lax.all_to_all(jnp.concatenate([far_send.reshape(box_devices, far_size),...  3.45 us
  transfers between devices with their start and end apart: 10, of which 6 were waited for; matrix products, arithmetic and copies ran while one was open for 17% of the time, Pallas kernels for 0%

profile of v10, /device:TPU:0, one launch (start us, length us, event | category | flops | bytes accessed | tf_op | source)
XLA Modules:
  0.0 82.2 jit_solution(3824165918286731879)
XLA Ops:
  0.7 0.8 %convert_bitcast_fusion.3 = bf16[16,256,1,1]{1,0,2,3:T(8,128)(2,1)S(1)} fusion(f32[16,256]{1,0:T(8,128)} %param.9), kind=kLoop, calls=%fused_computation.170 | loop fusion | flops 4096 | bytes 24576 | tf_op jit(solution)/shard_map/convert_element_type | solution.py:87
  1.5 0.7 convert_bitcast_fusion.2
  2.2 1.3 %fusion.41 = f32[16,1,64]{2,1,0:T(1,128)S(1)} fusion(bf16[16,64,256]{2,1,0:T(8,128)(2,1)} %param.13, bf16[16,256,1]{1,0,2:T(8,128)(2,1)S(1)} %convert_bitcast_fusion.2), kind=kOutput, calls=%fused_computation.78 | convolution fusion | flops 524288 | bytes 536576 | tf_op jit(solution)/shard_map/brl,bl->br/dot_general | solution.py:94
  3.6 0.7 broadcast_select_fusion.6
  4.4 2.8 %fusion.43 = f32[16,1,2,256]{3,1,2,0:T(1,128)S(1)} fusion(bf16[16,2,256,256]{3,2,1,0:T(8,128)(2,1)} %param.11, bf16[16,256,1,1]{1,0,2,3:T(8,128)(2,1)S(1)} %convert_bitcast_fusion.3), kind=kOutput, calls=%fused_computation.80 | convolution fusion | flops 4194304 | bytes 4235264 | tf_op jit(solution)/shard_map/bsij,bi->bsj/dot_general | solution.py:88
  9.5 0.8 all_to_all.24
  10.2 7.3 %all-to-all-start = ((f32[8,1,5376]{2,1,0:T(1,128)}), f32[8,1,5376]{2,1,0:T(1,128)S(1)}, u32[]{:S(2)}, u32[]{:S(2)}) async-start(f32[8,1,5376]{2,1,0:T(1,128)} %all_to_all.24), calls=%async_computation | async-start | bytes 344064 | tf_op jit(solution)/shard_map/all_to_all | solution.py:117
  17.5 1.3 %collective-permute-start = (bf16[16,256]{1,0:T(8,128)(2,1)S(1)}, bf16[16,256]{1,0:T(8,128)(2,1)S(1)}, u32[]{:S(2)}, u32[]{:S(2)}) collective-permute-start(bf16[16,256]{1,0:T(8,128)(2,1)S(1)} %convert_element_type.67), channel_id=1, source_target_pairs={{4,0},{8,4},{12,8},{16,12},{20,16},{24,20},{28,24},{5,1},{9,5},{13... | collective-permute-start | bytes 24584 | tf_op jit(solution)/shard_map/ppermute | solution.py:110
  19.4 3.7 %collective-permute-done = bf16[16,256]{1,0:T(8,128)(2,1)S(1)} collective-permute-done((bf16[16,256]{1,0:T(8,128)(2,1)S(1)}, bf16[16,256]{1,0:T(8,128)(2,1)S(1)}, u32[]{:S(2)}, u32[]{:S(2)}) %collective-permute-start) | collective-permute-done | bytes 8224 | tf_op jit(solution)/shard_map/ppermute | solution.py:110
  23.8 3.4 %fusion.29 = f32[16,1,256,1]{2,1,3,0:T(1,128)S(1)} fusion(bf16[16,2,256,256]{3,2,1,0:T(8,128)(2,1)} %param.11, bf16[16,2,256,1]{2,1,0,3:T(2,128)(2,1)S(1)} %fusion.31), kind=kOutput, calls=%fused_computation.52 | convolution fusion | flops 4194304 | bytes 4227072 | tf_op jit(solution)/shard_map/bsij,bsj->bi/dot_general | solution.py:131
  28.6 1.5 %collective-permute-start.2 = (f32[5376]{0:T(1024)S(1)}, f32[5376]{0:T(1024)S(1)}, u32[]{:S(2)}, u32[]{:S(2)}) collective-permute-start(f32[5376]{0:T(1024)S(1)} %constant_dynamic-update-slice_fusion), channel_id=1, source_target_pairs={{0,2},{1,3},{2,0},{3,1},{4,6},{5,7},{6,4},{7,5},{8,10},{9,11},{10,... | collective-permute-start | bytes 64520 | tf_op jit(solution)/shard_map/ppermute | solution.py:13
  30.8 1.7 %collective-permute-done.2 = f32[5376]{0:T(1024)S(1)} collective-permute-done((f32[5376]{0:T(1024)S(1)}, f32[5376]{0:T(1024)S(1)}, u32[]{:S(2)}, u32[]{:S(2)}) %collective-permute-start.2) | collective-permute-done | bytes 21536 | tf_op jit(solution)/shard_map/ppermute | solution.py:13
  32.4 0.9 %collective-permute-done.3 = f32[5376]{0:T(1024)S(1)} collective-permute-done((f32[5376]{0:T(1024)S(1)}, f32[5376]{0:T(1024)S(1)}, u32[]{:S(2)}, u32[]{:S(2)}) %collective-permute-start.3) | collective-permute-done | bytes 21536 | tf_op jit(solution)/shard_map/ppermute | solution.py:13
  34.2 12.2 %all_to_all.36 = f32[8,1,4]{2,1,0:T(1,128)S(1)} all-to-all(f32[8,1,4]{2,1,0:T(1,128)S(1)} %broadcast_in_dim.321), channel_id=1, replica_groups=mesh['box'=8,'rep'=4] {'box'}, dimensions={0} | all-to-all | bytes 256 | tf_op jit(solution)/shard_map/all_to_all | solution.py:36
  46.9 1.3 %collective-permute-start.4 = (bf16[16,256]{1,0:T(8,128)(2,1)S(1)}, bf16[16,256]{1,0:T(8,128)(2,1)S(1)}, u32[]{:S(2)}, u32[]{:S(2)}) collective-permute-start(bf16[16,256]{1,0:T(8,128)(2,1)S(1)} %fusion.78), channel_id=1, source_target_pairs={{4,0},{8,4},{12,8},{16,12},{20,16},{24,20},{28,24},{5,1},{9,5},{13... | collective-permute-start | bytes 24584 | tf_op jit(solution)/shard_map/ppermute | solution.py:110
  48.2 2.8 %fusion.39 = f32[16,1,2,256]{3,1,2,0:T(1,128)S(1)} fusion(bf16[16,2,256,256]{3,2,1,0:T(8,128)(2,1)} %param.11, bf16[16,256,1,1]{1,0,2,3:T(8,128)(2,1)S(1)} %bitcast.149), kind=kOutput, calls=%fused_computation.76 | convolution fusion | flops 4194304 | bytes 4235264 | tf_op jit(solution)/shard_map/bsij,bi->bsj/dot_general | solution.py:88
  52.4 0.8 %copy.57 = f32[8,1,5376]{2,1,0:T(1,128)} copy(f32[8,1,5376]{2,0,1:T(8,128)S(1)} %maximum_bitcast_fusion) | data formatting | bytes 344064 | tf_op jit(solution)/shard_map/all_to_all | solution.py:117
  53.2 3.9 %all-to-all-start.2 = ((f32[8,1,5376]{2,1,0:T(1,128)}), f32[8,1,5376]{2,1,0:T(1,128)S(1)}, u32[]{:S(2)}, u32[]{:S(2)}) async-start(f32[8,1,5376]{2,1,0:T(1,128)} %copy.57), calls=%async_computation.2 | async-start | bytes 344064 | tf_op jit(solution)/shard_map/all_to_all | solution.py:117
  57.9 3.4 %fusion.27 = f32[16,1,256,1]{2,1,3,0:T(1,128)S(1)} fusion(bf16[16,2,256,256]{3,2,1,0:T(8,128)(2,1)} %param.11, bf16[16,2,256,1]{2,1,0,3:T(2,128)(2,1)S(1)} %fusion.32), kind=kOutput, calls=%fused_computation.49 | convolution fusion | flops 4194304 | bytes 4227072 | tf_op jit(solution)/shard_map/bsij,bsj->bi/dot_general | solution.py:131
  61.3 3.4 %all-to-all-done.2 = f32[8,1,5376]{2,1,0:T(1,128)S(1)} async-done(((f32[8,1,5376]{2,1,0:T(1,128)}), f32[8,1,5376]{2,1,0:T(1,128)S(1)}, u32[]{:S(2)}, u32[]{:S(2)}) %all-to-all-start.2) | async-done | bytes 172064 | tf_op jit(solution)/shard_map/all_to_all | solution.py:117
  66.1 0.8 %collective-permute-start.6 = (f32[5376]{0:T(1024)S(1)}, f32[5376]{0:T(1024)S(1)}, u32[]{:S(2)}, u32[]{:S(2)}) collective-permute-start(f32[5376]{0:T(1024)S(1)} %constant_dynamic-update-slice_fusion.1), channel_id=1, source_target_pairs={{0,2},{1,3},{2,0},{3,1},{4,6},{5,7},{6,4},{7,5},{8,10},{9,11},{10,... | collective-permute-start | bytes 64520 | tf_op jit(solution)/shard_map/ppermute | solution.py:13
  67.0 1.3 %collective-permute-start.5 = (f32[5376]{0:T(1024)S(1)}, f32[5376]{0:T(1024)S(1)}, u32[]{:S(2)}, u32[]{:S(2)}) collective-permute-start(f32[5376]{0:T(1024)S(1)} %constant_dynamic-update-slice_fusion.1), channel_id=1, source_target_pairs={{0,1},{1,0},{2,3},{3,2},{4,5},{5,4},{6,7},{7,6},{8,9},{9,8},{10,11... | collective-permute-start | bytes 64520 | tf_op jit(solution)/shard_map/ppermute | solution.py:13
  68.3 1.7 %collective-permute-done.6 = f32[5376]{0:T(1024)S(1)} collective-permute-done((f32[5376]{0:T(1024)S(1)}, f32[5376]{0:T(1024)S(1)}, u32[]{:S(2)}, u32[]{:S(2)}) %collective-permute-start.6) | collective-permute-done | bytes 21536 | tf_op jit(solution)/shard_map/ppermute | solution.py:13
  72.5 8.8 %all_to_all.37 = f32[8,1,1]{2,1,0:T(1,128)S(1)} all-to-all(f32[8,1,1]{2,1,0:T(1,128)S(1)} %broadcast_in_dim.332), channel_id=1, replica_groups=mesh['box'=8,'rep'=4] {'box'}, dimensions={0} | all-to-all | bytes 64 | tf_op jit(solution)/shard_map/all_to_all | solution.py:36
  (161 shorter events, 13.4 us)
Async XLA Ops:
  0.6 8.0 %copy-start = (bf16[20,4,64,64]{3,2,1,0:T(8,128)(2,1)S(1)}, bf16[20,4,64,64]{3,2,1,0:T(8,128)(2,1)}, u32[]{:S(2)}) copy-start(bf16[20,4,64,64]{3,2,1,0:T(8,128)(2,1)} %param.16) | copy-start | bytes 1966084
  0.6 6.6 %copy-start.4 = (s32[16,2]{0,1:T(2,128)S(1)}, s32[16,2]{0,1:T(2,128)}, u32[]{:S(2)}) copy-start(s32[16,2]{0,1:T(2,128)} %param.12) | copy-start | bytes 388
  0.7 7.6 %copy-start.6 = (bf16[16,64,64]{2,1,0:T(8,128)(2,1)S(1)}, bf16[16,64,64]{2,1,0:T(8,128)(2,1)}, u32[]{:S(2)}) copy-start(bf16[16,64,64]{2,1,0:T(8,128)(2,1)} %param.14) | copy-start | bytes 393220
  0.7 7.8 %copy-start.5 = (s32[16]{0:T(128)S(1)}, s32[16]{0:T(128)}, u32[]{:S(2)}) copy-start(s32[16]{0:T(128)} %param.15) | copy-start | bytes 196
  2.2 15.3 %copy-start.2 = (f32[16,256]{1,0:T(8,128)S(1)}, f32[16,256]{1,0:T(8,128)}, u32[]{:S(2)}) copy-start(f32[16,256]{1,0:T(8,128)} %param.9) | copy-start | bytes 49156
  9.4 24.4 %copy-start.1 = (bf16[16,64,256]{2,1,0:T(8,128)(2,1)S(1)}, bf16[16,64,256]{2,1,0:T(8,128)(2,1)}, u32[]{:S(2)}) copy-start(bf16[16,64,256]{2,1,0:T(8,128)(2,1)} %param.13) | copy-start | bytes 1572868
  10.2 17.0 %all-to-all-start = ((f32[8,1,5376]{2,1,0:T(1,128)}), f32[8,1,5376]{2,1,0:T(1,128)S(1)}, u32[]{:S(2)}, u32[]{:S(2)}) async-start(f32[8,1,5376]{2,1,0:T(1,128)} %all_to_all.24), calls=%async_computation | async-start | bytes 344064 | tf_op jit(solution)/shard_map/all_to_all | solution.py:117
  17.5 16.6 %copy-start.3 = (f32[16,256]{1,0:T(8,128)S(1)}, f32[16,256]{1,0:T(8,128)}, u32[]{:S(2)}) copy-start(f32[16,256]{1,0:T(8,128)} %param.10) | copy-start | bytes 49156
  17.5 5.5 %collective-permute-start = (bf16[16,256]{1,0:T(8,128)(2,1)S(1)}, bf16[16,256]{1,0:T(8,128)(2,1)S(1)}, u32[]{:S(2)}, u32[]{:S(2)}) collective-permute-start(bf16[16,256]{1,0:T(8,128)(2,1)S(1)} %convert_element_type.67), channel_id=1, source_target_pairs={{4,0},{8,4},{12,8},{16,12},{20,16},{24,20},{28,24},{5,1},{9,5},{13... | collective-permute-start | bytes 24584 | tf_op jit(solution)/shard_map/ppermute | solution.py:110
  28.6 3.9 %collective-permute-start.2 = (f32[5376]{0:T(1024)S(1)}, f32[5376]{0:T(1024)S(1)}, u32[]{:S(2)}, u32[]{:S(2)}) collective-permute-start(f32[5376]{0:T(1024)S(1)} %constant_dynamic-update-slice_fusion), channel_id=1, source_target_pairs={{0,2},{1,3},{2,0},{3,1},{4,6},{5,7},{6,4},{7,5},{8,10},{9,11},{10,... | collective-permute-start | bytes 64520 | tf_op jit(solution)/shard_map/ppermute | solution.py:13
  30.1 3.3 %collective-permute-start.3 = (f32[5376]{0:T(1024)S(1)}, f32[5376]{0:T(1024)S(1)}, u32[]{:S(2)}, u32[]{:S(2)}) collective-permute-start(f32[5376]{0:T(1024)S(1)} %constant_dynamic-update-slice_fusion), channel_id=1, source_target_pairs={{0,3},{1,2},{2,1},{3,0},{4,7},{5,6},{6,5},{7,4},{8,11},{9,10},{10,... | collective-permute-start | bytes 64520 | tf_op jit(solution)/shard_map/ppermute | solution.py:13
  30.1 3.3 %collective-permute-start.1 = (f32[5376]{0:T(1024)S(1)}, f32[5376]{0:T(1024)S(1)}, u32[]{:S(2)}, u32[]{:S(2)}) collective-permute-start(f32[5376]{0:T(1024)S(1)} %constant_dynamic-update-slice_fusion), channel_id=1, source_target_pairs={{0,1},{1,0},{2,3},{3,2},{4,5},{5,4},{6,7},{7,6},{8,9},{9,8},{10,11... | collective-permute-start | bytes 64520 | tf_op jit(solution)/shard_map/ppermute | solution.py:13
  46.9 10.3 %collective-permute-start.4 = (bf16[16,256]{1,0:T(8,128)(2,1)S(1)}, bf16[16,256]{1,0:T(8,128)(2,1)S(1)}, u32[]{:S(2)}, u32[]{:S(2)}) collective-permute-start(bf16[16,256]{1,0:T(8,128)(2,1)S(1)} %fusion.78), channel_id=1, source_target_pairs={{4,0},{8,4},{12,8},{16,12},{20,16},{24,20},{28,24},{5,1},{9,5},{13... | collective-permute-start | bytes 24584 | tf_op jit(solution)/shard_map/ppermute | solution.py:110
  53.2 11.5 %all-to-all-start.2 = ((f32[8,1,5376]{2,1,0:T(1,128)}), f32[8,1,5376]{2,1,0:T(1,128)S(1)}, u32[]{:S(2)}, u32[]{:S(2)}) async-start(f32[8,1,5376]{2,1,0:T(1,128)} %copy.57), calls=%async_computation.2 | async-start | bytes 344064 | tf_op jit(solution)/shard_map/all_to_all | solution.py:117
  66.1 3.9 %collective-permute-start.6 = (f32[5376]{0:T(1024)S(1)}, f32[5376]{0:T(1024)S(1)}, u32[]{:S(2)}, u32[]{:S(2)}) collective-permute-start(f32[5376]{0:T(1024)S(1)} %constant_dynamic-update-slice_fusion.1), channel_id=1, source_target_pairs={{0,2},{1,3},{2,0},{3,1},{4,6},{5,7},{6,4},{7,5},{8,10},{9,11},{10,... | collective-permute-start | bytes 64520 | tf_op jit(solution)/shard_map/ppermute | solution.py:13
  67.0 3.5 %collective-permute-start.7 = (f32[5376]{0:T(1024)S(1)}, f32[5376]{0:T(1024)S(1)}, u32[]{:S(2)}, u32[]{:S(2)}) collective-permute-start(f32[5376]{0:T(1024)S(1)} %constant_dynamic-update-slice_fusion.1), channel_id=1, source_target_pairs={{0,3},{1,2},{2,1},{3,0},{4,7},{5,6},{6,5},{7,4},{8,11},{9,10},{10,... | collective-permute-start | bytes 64520 | tf_op jit(solution)/shard_map/ppermute | solution.py:13
  67.0 3.5 %collective-permute-start.5 = (f32[5376]{0:T(1024)S(1)}, f32[5376]{0:T(1024)S(1)}, u32[]{:S(2)}, u32[]{:S(2)}) collective-permute-start(f32[5376]{0:T(1024)S(1)} %constant_dynamic-update-slice_fusion.1), channel_id=1, source_target_pairs={{0,1},{1,0},{2,3},{3,2},{4,5},{5,4},{6,7},{7,6},{8,9},{9,8},{10,11... | collective-permute-start | bytes 64520 | tf_op jit(solution)/shard_map/ppermute | solution.py:13

commit v11 on v10

--- a/solution.py
+++ b/solution.py
@@ -1,9 +1,36 @@
 import jax
 import jax.numpy as jnp
 from jax import lax
+from jax.experimental import pallas as pl
 from jax.sharding import PartitionSpec as P
 
 ITERS = 2
+
+
+def _mirror_kernel(tiles_ref, column_ref, out_ref):
+    for b in range(tiles_ref.shape[0]):
+        column = column_ref[b]
+        for s in range(tiles_ref.shape[1]):
+            tile = tiles_ref[b, s].astype(jnp.float32)
+            out_ref[b, s:s + 1, :] = jnp.sum(tile * column, axis=0, keepdims=True)
+
+
+def near_mirror(tiles, rounded):
+    boxes, slots, leaf, _ = tiles.shape
+    per_step = 4 if boxes % 4 == 0 else 1
+    column = rounded.astype(jnp.float32)[:, :, None]
+    return pl.pallas_call(
+        _mirror_kernel,
+        grid=(boxes // per_step,),
+        in_specs=[
+            pl.BlockSpec((per_step, slots, leaf, leaf), lambda i: (i, 0, 0, 0)),
+            pl.BlockSpec((per_step, leaf, 1), lambda i: (i, 0, 0)),
+        ],
+        out_specs=pl.BlockSpec((per_step, slots, leaf), lambda i: (i, 0, 0)),
+        out_shape=jax.ShapeDtypeStruct((boxes, slots, leaf), jnp.float32),
+        cost_estimate=pl.CostEstimate(flops=2 * tiles.size, transcendentals=0,
+                                      bytes_accessed=tiles.size * 2 + boxes * slots * leaf * 4),
+    )(tiles, column)
 
 
 def rep_sum(vector):
@@ -85,9 +112,7 @@
     norm_now = None
     for iteration in range(ITERS):
         rounded = direction.astype(jnp.bfloat16)
-        mirrored = jnp.einsum(
-            "bsij,bi->bsj", near_tiles, rounded, preferred_element_type=jnp.float32
-        )
+        mirrored = near_mirror(near_tiles, rounded)
         landed = jnp.dot(
             near_onehot, mirrored.reshape(-1, mirrored.shape[2]), precision=lax.Precision.HIGHEST
         )

time: 82.9 us -> 88.7 us (1.070)
  Pallas kernels: 0 us -> 9.25 us
  matrix products: 18.1 us -> 12.5 us
  local copies, waits for them, and re-layouts: 6.51 us -> 12 us
  blocking collectives: 21.1 us -> 18.2 us
  starting transfers between devices: 18.1 us -> 19.2 us
    pallas_call x0 -> x2, Pallas kernels: none -> 9.25 us  [near_mirror(): pl.pallas_call(_mirror_kernel, grid=(boxes // per_step,), in_specs=[pl.Bl...]
    dot_general x2 -> x0, matrix products: 5.66 us -> none  [local(): jnp.einsum('bsij,bi->bsj', near_tiles, rounded, preferred_element_type=jn...]
    broadcast_in_dim x0 -> x2, local copies, waits for them, and re-layouts: none -> 3.97 us  [near_mirror(): column = rounded.astype(jnp.float32)[:, :, None]]
    ppermute x2, waiting for transfers between devices: 3.67 us -> 0.01 us  [local(): lax.ppermute(rounded, 'box', [(i, i - 1) for i in range(1, box_devices)])]
    all_to_all x2, waiting for transfers between devices: 3.45 us -> 6.36 us  [local(): lax.all_to_all(jnp.concatenate([far_send.reshape(box_devices, far_size),...]
    all_to_all x2, blocking collectives: 21.1 us -> 18.2 us  [box_sum(): got = lax.all_to_all(sent, 'box', 0, 0, tiled=True)]
    convert_element_type x4 -> x0, other arithmetic: 1.57 us -> none  [local(): rounded = direction.astype(jnp.bfloat16)]
    reshape x2, local copies, waits for them, and re-layouts: 0.05 us -> 1.56 us  [local(): mirrored.reshape(-1, mirrored.shape[2])]
  transfers between devices with their start and end apart: 10 -> 10, of which waited for: 6 -> 6; matrix products, arithmetic and copies ran while one was open for 17% -> 23% of each run, Pallas kernels for 0% -> 11%
where the time goes in v11:
time: 88.7 us; the launch traced here: 87.9 us
  starting transfers between devices  19.2 us (22%)
  blocking collectives  18.2 us (21%)
  matrix products  12.5 us (14%)
  local copies, waits for them, and re-layouts  12 us (14%)
  waiting for transfers between devices  11.1 us (13%)
  Pallas kernels  9.25 us (10%)
  other arithmetic  4.41 us (5%)
  between operations  1.26 us (1%)
    all_to_all x2, blocking collectives, box_sum(): got = lax.all_to_all(sent, 'box', 0, 0, tiled=True)  18.2 us
    all_to_all x2, starting transfers between devices, local(): lax.all_to_all(jnp.concatenate([far_send.reshape(box_devices, far_size),...  12.3 us
    pallas_call x2, Pallas kernels, near_mirror(): pl.pallas_call(_mirror_kernel, grid=(boxes // per_step,), in_specs=[pl.Bl...  9.25 us
    dot_general x2, matrix products, local(): jnp.einsum('bsij,bsj->bi', near_tiles, near_in, preferred_element_type=jn...  6.73 us
    all_to_all x2, waiting for transfers between devices, local(): lax.all_to_all(jnp.concatenate([far_send.reshape(box_devices, far_size),...  6.36 us
    ppermute x6, waiting for transfers between devices, rep_sum(): lax.ppermute(vector, 'rep', [(i, i ^ mask) for i in range(count)])  4.77 us
    ppermute x6, starting transfers between devices, rep_sum(): lax.ppermute(vector, 'rep', [(i, i ^ mask) for i in range(count)])  4.35 us
    broadcast_in_dim x2, local copies, waits for them, and re-layouts, near_mirror(): column = rounded.astype(jnp.float32)[:, :, None]  3.97 us
  transfers between devices with their start and end apart: 10, of which 6 were waited for; matrix products, arithmetic and copies ran while one was open for 23% of the time, Pallas kernels for 11%

profile of v11, /device:TPU:0, one launch (start us, length us, event | category | flops | bytes accessed | tf_op | source)
XLA Modules:
  0.0 87.9 jit_solution(14043658444322111875)
XLA Ops:
  0.6 0.8 bitcast_convert_fusion.1
  1.5 1.3 %collective-permute-start = (bf16[16,256]{1,0:T(8,128)(2,1)S(1)}, bf16[16,256]{1,0:T(8,128)(2,1)S(1)}, u32[]{:S(2)}, u32[]{:S(2)}) collective-permute-start(bf16[16,256]{1,0:T(8,128)(2,1)S(1)} %get-tuple-element.20), channel_id=1, source_target_pairs={{4,0},{8,4},{12,8},{16,12},{20,16},{24,20},{28,24},{5,1},{9,5},{13... | collective-permute-start | bytes 24584 | tf_op jit(solution)/shard_map/ppermute | solution.py:135
  2.8 1.3 %fusion.39 = f32[16,1,64]{2,1,0:T(1,128)S(1)} fusion(bf16[16,64,256]{2,1,0:T(8,128)(2,1)} %param.13, bf16[16,256,1]{1,0,2:T(8,128)(2,1)S(1)} %bitcast.150), kind=kOutput, calls=%fused_computation.74 | convolution fusion | flops 524288 | bytes 536576 | tf_op jit(solution)/shard_map/brl,bl->br/dot_general | solution.py:119
  4.9 2.0 %copy.53.column_ref = f32[16,256,1]{2,1,0:T(8,128)} copy(f32[16,256,1]{1,0,2:T(8,128)S(1)} %get-tuple-element.19) | data formatting | bytes 32768 | tf_op jit(solution)/shard_map/broadcast_in_dim | solution.py:21
  6.9 4.6 %shard_map.104 = f32[16,2,256]{2,1,0:T(2,128)} custom-call(bf16[16,2,256,256]{3,2,1,0:T(8,128)(2,1)} %tiles_ref.3, f32[16,256,1]{2,1,0:T(8,128)} %copy.53.column_ref), custom_call_target="tpu_custom_call" | custom-call | flops 4194304 | bytes 4227072 | tf_op jit(solution)/shard_map/pallas_call | solution.py:22
  14.5 0.8 all_to_all.24
  15.3 8.4 %all-to-all-start = ((f32[8,1,5376]{2,1,0:T(1,128)}), f32[8,1,5376]{2,1,0:T(1,128)S(1)}, u32[]{:S(2)}, u32[]{:S(2)}) async-start(f32[8,1,5376]{2,1,0:T(1,128)} %all_to_all.24), calls=%async_computation | async-start | bytes 344064 | tf_op jit(solution)/shard_map/all_to_all | solution.py:142
  25.0 3.4 %fusion.29 = f32[16,1,256,1]{2,1,3,0:T(1,128)S(1)} fusion(bf16[16,2,256,256]{3,2,1,0:T(8,128)(2,1)} %tiles_ref.3, bf16[16,2,256,1]{2,1,0,3:T(2,128)(2,1)S(1)} %fusion.31), kind=kOutput, calls=%fused_computation.50 | convolution fusion | flops 4194304 | bytes 4227072 | tf_op jit(solution)/shard_map/bsij,bsj->bi/dot_general | solution.py:156
  28.4 2.9 %all-to-all-done = f32[8,1,5376]{2,1,0:T(1,128)S(1)} async-done(((f32[8,1,5376]{2,1,0:T(1,128)}), f32[8,1,5376]{2,1,0:T(1,128)S(1)}, u32[]{:S(2)}, u32[]{:S(2)}) %all-to-all-start) | async-done | bytes 172064 | tf_op jit(solution)/shard_map/all_to_all | solution.py:142
  32.7 1.5 %collective-permute-start.2 = (f32[5376]{0:T(1024)S(1)}, f32[5376]{0:T(1024)S(1)}, u32[]{:S(2)}, u32[]{:S(2)}) collective-permute-start(f32[5376]{0:T(1024)S(1)} %constant_dynamic-update-slice_fusion), channel_id=1, source_target_pairs={{0,2},{1,3},{2,0},{3,1},{4,6},{5,7},{6,4},{7,5},{8,10},{9,11},{10,... | collective-permute-start | bytes 64520 | tf_op jit(solution)/shard_map/ppermute | solution.py:40
  34.9 1.7 %collective-permute-done.2 = f32[5376]{0:T(1024)S(1)} collective-permute-done((f32[5376]{0:T(1024)S(1)}, f32[5376]{0:T(1024)S(1)}, u32[]{:S(2)}, u32[]{:S(2)}) %collective-permute-start.2) | collective-permute-done | bytes 21536 | tf_op jit(solution)/shard_map/ppermute | solution.py:40
  36.6 0.9 %collective-permute-done.3 = f32[5376]{0:T(1024)S(1)} collective-permute-done((f32[5376]{0:T(1024)S(1)}, f32[5376]{0:T(1024)S(1)}, u32[]{:S(2)}, u32[]{:S(2)}) %collective-permute-start.3) | collective-permute-done | bytes 21536 | tf_op jit(solution)/shard_map/ppermute | solution.py:40
  38.4 9.4 %all_to_all.36 = f32[8,1,4]{2,1,0:T(1,128)S(1)} all-to-all(f32[8,1,4]{2,1,0:T(1,128)S(1)} %broadcast_in_dim.333), channel_id=1, replica_groups=mesh['box'=8,'rep'=4] {'box'}, dimensions={0} | all-to-all | bytes 256 | tf_op jit(solution)/shard_map/all_to_all | solution.py:63
  48.1 1.3 %collective-permute-start.4 = (bf16[16,256]{1,0:T(8,128)(2,1)S(1)}, bf16[16,256]{1,0:T(8,128)(2,1)S(1)}, u32[]{:S(2)}, u32[]{:S(2)}) collective-permute-start(bf16[16,256]{1,0:T(8,128)(2,1)S(1)} %get-tuple-element.5), channel_id=1, source_target_pairs={{4,0},{8,4},{12,8},{16,12},{20,16},{24,20},{28,24},{5,1},{9,5},{13... | collective-permute-start | bytes 24584 | tf_op jit(solution)/shard_map/ppermute | solution.py:135
  49.4 2.0 %copy.61.column_ref = f32[16,256,1]{2,1,0:T(8,128)} copy(f32[16,256,1]{1,0,2:T(8,128)S(1)} %get-tuple-element.4) | data formatting | bytes 32768 | tf_op jit(solution)/shard_map/broadcast_in_dim | solution.py:21
  51.4 4.6 %shard_map.105 = f32[16,2,256]{2,1,0:T(2,128)} custom-call(bf16[16,2,256,256]{3,2,1,0:T(8,128)(2,1)} %tiles_ref.3, f32[16,256,1]{2,1,0:T(8,128)} %copy.61.column_ref), custom_call_target="tpu_custom_call" | custom-call | flops 4194304 | bytes 4227072 | tf_op jit(solution)/shard_map/pallas_call | solution.py:22
  58.1 0.8 copy.63
  59.0 3.9 %all-to-all-start.2 = ((f32[8,1,5376]{2,1,0:T(1,128)}), f32[8,1,5376]{2,1,0:T(1,128)S(1)}, u32[]{:S(2)}, u32[]{:S(2)}) async-start(f32[8,1,5376]{2,1,0:T(1,128)} %copy.63), calls=%async_computation.2 | async-start | bytes 344064 | tf_op jit(solution)/shard_map/all_to_all | solution.py:142
  63.7 3.4 %fusion.27 = f32[16,1,256,1]{2,1,3,0:T(1,128)S(1)} fusion(bf16[16,2,256,256]{3,2,1,0:T(8,128)(2,1)} %tiles_ref.3, bf16[16,2,256,1]{2,1,0,3:T(2,128)(2,1)S(1)} %fusion.32), kind=kOutput, calls=%fused_computation.48 | convolution fusion | flops 4194304 | bytes 4227072 | tf_op jit(solution)/shard_map/bsij,bsj->bi/dot_general | solution.py:156
  67.1 3.4 %all-to-all-done.2 = f32[8,1,5376]{2,1,0:T(1,128)S(1)} async-done(((f32[8,1,5376]{2,1,0:T(1,128)}), f32[8,1,5376]{2,1,0:T(1,128)S(1)}, u32[]{:S(2)}, u32[]{:S(2)}) %all-to-all-start.2) | async-done | bytes 172064 | tf_op jit(solution)/shard_map/all_to_all | solution.py:142
  71.9 0.8 collective-permute-start.6
  72.7 1.3 %collective-permute-start.5 = (f32[5376]{0:T(1024)S(1)}, f32[5376]{0:T(1024)S(1)}, u32[]{:S(2)}, u32[]{:S(2)}) collective-permute-start(f32[5376]{0:T(1024)S(1)} %constant_dynamic-update-slice_fusion.1), channel_id=1, source_target_pairs={{0,1},{1,0},{2,3},{3,2},{4,5},{5,4},{6,7},{7,6},{8,9},{9,8},{10,11... | collective-permute-start | bytes 64520 | tf_op jit(solution)/shard_map/ppermute | solution.py:40
  74.0 1.7 %collective-permute-done.6 = f32[5376]{0:T(1024)S(1)} collective-permute-done((f32[5376]{0:T(1024)S(1)}, f32[5376]{0:T(1024)S(1)}, u32[]{:S(2)}, u32[]{:S(2)}) %collective-permute-start.6) | collective-permute-done | bytes 21536 | tf_op jit(solution)/shard_map/ppermute | solution.py:40
  78.2 8.8 %all_to_all.37 = f32[8,1,1]{2,1,0:T(1,128)S(1)} all-to-all(f32[8,1,1]{2,1,0:T(1,128)S(1)} %broadcast_in_dim.346), channel_id=1, replica_groups=mesh['box'=8,'rep'=4] {'box'}, dimensions={0} | all-to-all | bytes 64 | tf_op jit(solution)/shard_map/all_to_all | solution.py:63
  (159 shorter events, 15.5 us)
Async XLA Ops:
  0.6 13.0 %copy-start = (bf16[20,4,64,64]{3,2,1,0:T(8,128)(2,1)S(1)}, bf16[20,4,64,64]{3,2,1,0:T(8,128)(2,1)}, u32[]{:S(2)}) copy-start(bf16[20,4,64,64]{3,2,1,0:T(8,128)(2,1)} %param.16) | copy-start | bytes 1966084
  1.5 22.8 %collective-permute-start = (bf16[16,256]{1,0:T(8,128)(2,1)S(1)}, bf16[16,256]{1,0:T(8,128)(2,1)S(1)}, u32[]{:S(2)}, u32[]{:S(2)}) collective-permute-start(bf16[16,256]{1,0:T(8,128)(2,1)S(1)} %get-tuple-element.20), channel_id=1, source_target_pairs={{4,0},{8,4},{12,8},{16,12},{20,16},{24,20},{28,24},{5,1},{9,5},{13... | collective-permute-start | bytes 24584 | tf_op jit(solution)/shard_map/ppermute | solution.py:135
  6.9 5.5 %copy-start.4 = (s32[16,2]{0,1:T(2,128)S(1)}, s32[16,2]{0,1:T(2,128)}, u32[]{:S(2)}) copy-start(s32[16,2]{0,1:T(2,128)} %param.12) | copy-start | bytes 388
  6.9 6.5 %copy-start.6 = (bf16[16,64,64]{2,1,0:T(8,128)(2,1)S(1)}, bf16[16,64,64]{2,1,0:T(8,128)(2,1)}, u32[]{:S(2)}) copy-start(bf16[16,64,64]{2,1,0:T(8,128)(2,1)} %param.14) | copy-start | bytes 393220
  6.9 6.6 %copy-start.5 = (s32[16]{0:T(128)S(1)}, s32[16]{0:T(128)}, u32[]{:S(2)}) copy-start(s32[16]{0:T(128)} %param.15) | copy-start | bytes 196
  15.3 16.0 %all-to-all-start = ((f32[8,1,5376]{2,1,0:T(1,128)}), f32[8,1,5376]{2,1,0:T(1,128)S(1)}, u32[]{:S(2)}, u32[]{:S(2)}) async-start(f32[8,1,5376]{2,1,0:T(1,128)} %all_to_all.24), calls=%async_computation | async-start | bytes 344064 | tf_op jit(solution)/shard_map/all_to_all | solution.py:142
  31.4 6.6 %copy-start.1 = (bf16[16,64,256]{2,1,0:T(8,128)(2,1)S(1)}, bf16[16,64,256]{2,1,0:T(8,128)(2,1)}, u32[]{:S(2)}) copy-start(bf16[16,64,256]{2,1,0:T(8,128)(2,1)} %param.13) | copy-start | bytes 1572868
  32.1 6.1 %copy-start.2 = (f32[16,256]{1,0:T(8,128)S(1)}, f32[16,256]{1,0:T(8,128)}, u32[]{:S(2)}) copy-start(f32[16,256]{1,0:T(8,128)} %param.9) | copy-start | bytes 49156
  32.1 6.1 %copy-start.3 = (f32[16,256]{1,0:T(8,128)S(1)}, f32[16,256]{1,0:T(8,128)}, u32[]{:S(2)}) copy-start(f32[16,256]{1,0:T(8,128)} %param.10) | copy-start | bytes 49156
  32.7 3.9 %collective-permute-start.2 = (f32[5376]{0:T(1024)S(1)}, f32[5376]{0:T(1024)S(1)}, u32[]{:S(2)}, u32[]{:S(2)}) collective-permute-start(f32[5376]{0:T(1024)S(1)} %constant_dynamic-update-slice_fusion), channel_id=1, source_target_pairs={{0,2},{1,3},{2,0},{3,1},{4,6},{5,7},{6,4},{7,5},{8,10},{9,11},{10,... | collective-permute-start | bytes 64520 | tf_op jit(solution)/shard_map/ppermute | solution.py:40
  34.2 3.3 %collective-permute-start.3 = (f32[5376]{0:T(1024)S(1)}, f32[5376]{0:T(1024)S(1)}, u32[]{:S(2)}, u32[]{:S(2)}) collective-permute-start(f32[5376]{0:T(1024)S(1)} %constant_dynamic-update-slice_fusion), channel_id=1, source_target_pairs={{0,3},{1,2},{2,1},{3,0},{4,7},{5,6},{6,5},{7,4},{8,11},{9,10},{10,... | collective-permute-start | bytes 64520 | tf_op jit(solution)/shard_map/ppermute | solution.py:40
  34.2 3.3 %collective-permute-start.1 = (f32[5376]{0:T(1024)S(1)}, f32[5376]{0:T(1024)S(1)}, u32[]{:S(2)}, u32[]{:S(2)}) collective-permute-start(f32[5376]{0:T(1024)S(1)} %constant_dynamic-update-slice_fusion), channel_id=1, source_target_pairs={{0,1},{1,0},{2,3},{3,2},{4,5},{5,4},{6,7},{7,6},{8,9},{9,8},{10,11... | collective-permute-start | bytes 64520 | tf_op jit(solution)/shard_map/ppermute | solution.py:40
  48.1 14.8 %collective-permute-start.4 = (bf16[16,256]{1,0:T(8,128)(2,1)S(1)}, bf16[16,256]{1,0:T(8,128)(2,1)S(1)}, u32[]{:S(2)}, u32[]{:S(2)}) collective-permute-start(bf16[16,256]{1,0:T(8,128)(2,1)S(1)} %get-tuple-element.5), channel_id=1, source_target_pairs={{4,0},{8,4},{12,8},{16,12},{20,16},{24,20},{28,24},{5,1},{9,5},{13... | collective-permute-start | bytes 24584 | tf_op jit(solution)/shard_map/ppermute | solution.py:135
  59.0 11.5 %all-to-all-start.2 = ((f32[8,1,5376]{2,1,0:T(1,128)}), f32[8,1,5376]{2,1,0:T(1,128)S(1)}, u32[]{:S(2)}, u32[]{:S(2)}) async-start(f32[8,1,5376]{2,1,0:T(1,128)} %copy.63), calls=%async_computation.2 | async-start | bytes 344064 | tf_op jit(solution)/shard_map/all_to_all | solution.py:142
  71.9 3.9 %collective-permute-start.6 = (f32[5376]{0:T(1024)S(1)}, f32[5376]{0:T(1024)S(1)}, u32[]{:S(2)}, u32[]{:S(2)}) collective-permute-start(f32[5376]{0:T(1024)S(1)} %constant_dynamic-update-slice_fusion.1), channel_id=1, source_target_pairs={{0,2},{1,3},{2,0},{3,1},{4,6},{5,7},{6,4},{7,5},{8,10},{9,11},{10,... | collective-permute-start | bytes 64520 | tf_op jit(solution)/shard_map/ppermute | solution.py:40
  72.7 3.5 %collective-permute-start.7 = (f32[5376]{0:T(1024)S(1)}, f32[5376]{0:T(1024)S(1)}, u32[]{:S(2)}, u32[]{:S(2)}) collective-permute-start(f32[5376]{0:T(1024)S(1)} %constant_dynamic-update-slice_fusion.1), channel_id=1, source_target_pairs={{0,3},{1,2},{2,1},{3,0},{4,7},{5,6},{6,5},{7,4},{8,11},{9,10},{10,... | collective-permute-start | bytes 64520 | tf_op jit(solution)/shard_map/ppermute | solution.py:40
  72.7 3.5 %collective-permute-start.5 = (f32[5376]{0:T(1024)S(1)}, f32[5376]{0:T(1024)S(1)}, u32[]{:S(2)}, u32[]{:S(2)}) collective-permute-start(f32[5376]{0:T(1024)S(1)} %constant_dynamic-update-slice_fusion.1), channel_id=1, source_target_pairs={{0,1},{1,0},{2,3},{3,2},{4,5},{5,4},{6,7},{7,6},{8,9},{9,8},{10,11... | collective-permute-start | bytes 64520 | tf_op jit(solution)/shard_map/ppermute | solution.py:40

commit v12 on v10

--- a/solution.py
+++ b/solution.py
@@ -113,14 +113,14 @@
         coef_wide = node_coef.astype(jnp.float32)
         far_send = jnp.where(below, coef_wide[None], spread)
         is_next = (devices == box_rank + 1)[:, None]
-        near_send = jnp.where(is_next, landed[box_count:].reshape(1, -1), 0.0)
+        near_send = jnp.where(is_next[:, None], landed[box_count:].reshape(1, 1, -1), 0.0)
         got = lax.all_to_all(
-            jnp.concatenate([far_send.reshape(box_devices, far_size), near_send], axis=1),
+            jnp.concatenate([far_send.reshape(box_devices, 1, far_size), near_send], axis=2),
             "box", 0, 0, tiled=True,
         )
-        got_far = got[:, :far_size].reshape(box_devices, node_count, rank_width)
+        got_far = got[:, 0, :far_size].reshape(box_devices, node_count, rank_width)
         is_prev = (devices == box_rank - 1)[:, None]
-        arrived = jnp.sum(jnp.where(is_prev, got[:, far_size:], 0.0), axis=0).reshape(box_count, leaf)
+        arrived = jnp.sum(jnp.where(is_prev, got[:, 0, far_size:], 0.0), axis=0).reshape(box_count, leaf)
         mirror_in = jnp.sum(jnp.where(below, got_far, 0.0), axis=0)
         every_coef = jnp.where(
             above, got_far, jnp.where(devices[:, None, None] == box_rank, coef_wide[None], 0.0)

time: 82.9 us -> 83.2 us (level)
  other arithmetic: 5.15 us -> 7.01 us
  local copies, waits for them, and re-layouts: 6.51 us -> 4.95 us
    concatenate x1 -> x2, other arithmetic: 0.01 us -> 1.62 us  [local(): jnp.concatenate([far_send.reshape(box_devices, 1, far_size), near_send],...]
    all_to_all x2 -> x0, local copies, waits for them, and re-layouts: 1.6 us -> none  [local(): lax.all_to_all(jnp.concatenate([far_send.reshape(box_devices, far_size),...]
where the time goes in v12:
time: 83.2 us; the launch traced here: 82.5 us
  blocking collectives  21.1 us (25%)
  matrix products  18.1 us (22%)
  starting transfers between devices  18.1 us (22%)
  waiting for transfers between devices  11.9 us (14%)
  other arithmetic  7.01 us (8%)
  local copies, waits for them, and re-layouts  4.95 us (6%)
  between operations  1.28 us (2%)
    all_to_all x2, blocking collectives, box_sum(): got = lax.all_to_all(sent, 'box', 0, 0, tiled=True)  21.1 us
    all_to_all x2, starting transfers between devices, local(): lax.all_to_all(jnp.concatenate([far_send.reshape(box_devices, 1, far_size...  11.2 us
    dot_general x2, matrix products, local(): jnp.einsum('bsij,bsj->bi', near_tiles, near_in, preferred_element_type=jn...  6.73 us
    dot_general x2, matrix products, local(): jnp.einsum('bsij,bi->bsj', near_tiles, rounded, preferred_element_type=jn...  5.67 us
    ppermute x6, waiting for transfers between devices, rep_sum(): lax.ppermute(vector, 'rep', [(i, i ^ mask) for i in range(count)])  4.77 us
    ppermute x6, starting transfers between devices, rep_sum(): lax.ppermute(vector, 'rep', [(i, i ^ mask) for i in range(count)])  4.35 us
    ppermute x2, waiting for transfers between devices, local(): lax.ppermute(rounded, 'box', [(i, i - 1) for i in range(1, box_devices)])  3.67 us
    all_to_all x2, waiting for transfers between devices, local(): lax.all_to_all(jnp.concatenate([far_send.reshape(box_devices, 1, far_size...  3.45 us
  transfers between devices with their start and end apart: 10, of which 6 were waited for; matrix products, arithmetic and copies ran while one was open for 17% of the time, Pallas kernels for 0%

profile of v12, /device:TPU:0, one launch (start us, length us, event | category | flops | bytes accessed | tf_op | source)
XLA Modules:
  0.0 82.5 jit_solution(2511481124864335888)
XLA Ops:
  0.7 0.8 %convert_bitcast_fusion.3 = bf16[16,256,1,1]{1,0,2,3:T(8,128)(2,1)S(1)} fusion(f32[16,256]{1,0:T(8,128)} %param.9), kind=kLoop, calls=%fused_computation.173 | loop fusion | flops 4096 | bytes 24576 | tf_op jit(solution)/shard_map/convert_element_type | solution.py:87
  1.5 0.7 convert_bitcast_fusion.2
  2.2 1.3 %fusion.44 = f32[16,1,64]{2,1,0:T(1,128)S(1)} fusion(bf16[16,64,256]{2,1,0:T(8,128)(2,1)} %param.13, bf16[16,256,1]{1,0,2:T(8,128)(2,1)S(1)} %convert_bitcast_fusion.2), kind=kOutput, calls=%fused_computation.81 | convolution fusion | flops 524288 | bytes 536576 | tf_op jit(solution)/shard_map/brl,bl->br/dot_general | solution.py:94
  3.5 0.7 broadcast_select_fusion.8
  4.4 2.8 %fusion.46 = f32[16,1,2,256]{3,1,2,0:T(1,128)S(1)} fusion(bf16[16,2,256,256]{3,2,1,0:T(8,128)(2,1)} %param.11, bf16[16,256,1,1]{1,0,2,3:T(8,128)(2,1)S(1)} %convert_bitcast_fusion.3), kind=kOutput, calls=%fused_computation.83 | convolution fusion | flops 4194304 | bytes 4235264 | tf_op jit(solution)/shard_map/bsij,bi->bsj/dot_general | solution.py:88
  9.5 0.8 pad_maximum_fusion
  10.3 7.3 %all-to-all-start = ((f32[8,1,5376]{2,1,0:T(1,128)}), f32[8,1,5376]{2,1,0:T(1,128)S(1)}, u32[]{:S(2)}, u32[]{:S(2)}) async-start(f32[8,1,5376]{2,1,0:T(1,128)} %pad_maximum_fusion), calls=%async_computation | async-start | bytes 344064 | tf_op jit(solution)/shard_map/all_to_all | solution.py:117
  17.6 1.3 %collective-permute-start = (bf16[16,256]{1,0:T(8,128)(2,1)S(1)}, bf16[16,256]{1,0:T(8,128)(2,1)S(1)}, u32[]{:S(2)}, u32[]{:S(2)}) collective-permute-start(bf16[16,256]{1,0:T(8,128)(2,1)S(1)} %convert_element_type.67), channel_id=1, source_target_pairs={{4,0},{8,4},{12,8},{16,12},{20,16},{24,20},{28,24},{5,1},{9,5},{13... | collective-permute-start | bytes 24584 | tf_op jit(solution)/shard_map/ppermute | solution.py:110
  19.5 3.7 %collective-permute-done = bf16[16,256]{1,0:T(8,128)(2,1)S(1)} collective-permute-done((bf16[16,256]{1,0:T(8,128)(2,1)S(1)}, bf16[16,256]{1,0:T(8,128)(2,1)S(1)}, u32[]{:S(2)}, u32[]{:S(2)}) %collective-permute-start) | collective-permute-done | bytes 8224 | tf_op jit(solution)/shard_map/ppermute | solution.py:110
  23.9 3.4 %fusion.32 = f32[16,1,256,1]{2,1,3,0:T(1,128)S(1)} fusion(bf16[16,2,256,256]{3,2,1,0:T(8,128)(2,1)} %param.11, bf16[16,2,256,1]{2,1,0,3:T(2,128)(2,1)S(1)} %fusion.34), kind=kOutput, calls=%fused_computation.53 | convolution fusion | flops 4194304 | bytes 4227072 | tf_op jit(solution)/shard_map/bsij,bsj->bi/dot_general | solution.py:131
  28.7 1.5 %collective-permute-start.2 = (f32[5376]{0:T(1024)S(1)}, f32[5376]{0:T(1024)S(1)}, u32[]{:S(2)}, u32[]{:S(2)}) collective-permute-start(f32[5376]{0:T(1024)S(1)} %constant_dynamic-update-slice_fusion), channel_id=1, source_target_pairs={{0,2},{1,3},{2,0},{3,1},{4,6},{5,7},{6,4},{7,5},{8,10},{9,11},{10,... | collective-permute-start | bytes 64520 | tf_op jit(solution)/shard_map/ppermute | solution.py:13
  30.9 1.7 %collective-permute-done.2 = f32[5376]{0:T(1024)S(1)} collective-permute-done((f32[5376]{0:T(1024)S(1)}, f32[5376]{0:T(1024)S(1)}, u32[]{:S(2)}, u32[]{:S(2)}) %collective-permute-start.2) | collective-permute-done | bytes 21536 | tf_op jit(solution)/shard_map/ppermute | solution.py:13
  32.6 0.9 %collective-permute-done.3 = f32[5376]{0:T(1024)S(1)} collective-permute-done((f32[5376]{0:T(1024)S(1)}, f32[5376]{0:T(1024)S(1)}, u32[]{:S(2)}, u32[]{:S(2)}) %collective-permute-start.3) | collective-permute-done | bytes 21536 | tf_op jit(solution)/shard_map/ppermute | solution.py:13
  34.4 12.2 %all_to_all.22 = f32[8,1,4]{2,1,0:T(1,128)S(1)} all-to-all(f32[8,1,4]{2,1,0:T(1,128)S(1)} %broadcast_in_dim.322), channel_id=1, replica_groups=mesh['box'=8,'rep'=4] {'box'}, dimensions={0} | all-to-all | bytes 256 | tf_op jit(solution)/shard_map/all_to_all | solution.py:36
  47.0 1.3 %collective-permute-start.4 = (bf16[16,256]{1,0:T(8,128)(2,1)S(1)}, bf16[16,256]{1,0:T(8,128)(2,1)S(1)}, u32[]{:S(2)}, u32[]{:S(2)}) collective-permute-start(bf16[16,256]{1,0:T(8,128)(2,1)S(1)} %fusion.81), channel_id=1, source_target_pairs={{4,0},{8,4},{12,8},{16,12},{20,16},{24,20},{28,24},{5,1},{9,5},{13... | collective-permute-start | bytes 24584 | tf_op jit(solution)/shard_map/ppermute | solution.py:110
  48.3 2.8 %fusion.42 = f32[16,1,2,256]{3,1,2,0:T(1,128)S(1)} fusion(bf16[16,2,256,256]{3,2,1,0:T(8,128)(2,1)} %param.11, bf16[16,256,1,1]{1,0,2,3:T(8,128)(2,1)S(1)} %bitcast.145), kind=kOutput, calls=%fused_computation.79 | convolution fusion | flops 4194304 | bytes 4235264 | tf_op jit(solution)/shard_map/bsij,bi->bsj/dot_general | solution.py:88
  52.6 0.8 pad_maximum_fusion.1
  53.4 3.9 %all-to-all-start.2 = ((f32[8,1,5376]{2,1,0:T(1,128)}), f32[8,1,5376]{2,1,0:T(1,128)S(1)}, u32[]{:S(2)}, u32[]{:S(2)}) async-start(f32[8,1,5376]{2,1,0:T(1,128)} %pad_maximum_fusion.1), calls=%async_computation.2 | async-start | bytes 344064 | tf_op jit(solution)/shard_map/all_to_all | solution.py:117
  58.1 3.4 %fusion.30 = f32[16,1,256,1]{2,1,3,0:T(1,128)S(1)} fusion(bf16[16,2,256,256]{3,2,1,0:T(8,128)(2,1)} %param.11, bf16[16,2,256,1]{2,1,0,3:T(2,128)(2,1)S(1)} %fusion.35), kind=kOutput, calls=%fused_computation.50 | convolution fusion | flops 4194304 | bytes 4227072 | tf_op jit(solution)/shard_map/bsij,bsj->bi/dot_general | solution.py:131
  61.5 3.4 %all-to-all-done.2 = f32[8,1,5376]{2,1,0:T(1,128)S(1)} async-done(((f32[8,1,5376]{2,1,0:T(1,128)}), f32[8,1,5376]{2,1,0:T(1,128)S(1)}, u32[]{:S(2)}, u32[]{:S(2)}) %all-to-all-start.2) | async-done | bytes 172064 | tf_op jit(solution)/shard_map/all_to_all | solution.py:117
  66.4 0.8 %collective-permute-start.6 = (f32[5376]{0:T(1024)S(1)}, f32[5376]{0:T(1024)S(1)}, u32[]{:S(2)}, u32[]{:S(2)}) collective-permute-start(f32[5376]{0:T(1024)S(1)} %constant_dynamic-update-slice_fusion.1), channel_id=1, source_target_pairs={{0,2},{1,3},{2,0},{3,1},{4,6},{5,7},{6,4},{7,5},{8,10},{9,11},{10,... | collective-permute-start | bytes 64520 | tf_op jit(solution)/shard_map/ppermute | solution.py:13
  67.2 1.3 %collective-permute-start.5 = (f32[5376]{0:T(1024)S(1)}, f32[5376]{0:T(1024)S(1)}, u32[]{:S(2)}, u32[]{:S(2)}) collective-permute-start(f32[5376]{0:T(1024)S(1)} %constant_dynamic-update-slice_fusion.1), channel_id=1, source_target_pairs={{0,1},{1,0},{2,3},{3,2},{4,5},{5,4},{6,7},{7,6},{8,9},{9,8},{10,11... | collective-permute-start | bytes 64520 | tf_op jit(solution)/shard_map/ppermute | solution.py:13
  68.6 1.7 %collective-permute-done.6 = f32[5376]{0:T(1024)S(1)} collective-permute-done((f32[5376]{0:T(1024)S(1)}, f32[5376]{0:T(1024)S(1)}, u32[]{:S(2)}, u32[]{:S(2)}) %collective-permute-start.6) | collective-permute-done | bytes 21536 | tf_op jit(solution)/shard_map/ppermute | solution.py:13
  72.7 8.8 %all_to_all.23 = f32[8,1,1]{2,1,0:T(1,128)S(1)} all-to-all(f32[8,1,1]{2,1,0:T(1,128)S(1)} %broadcast_in_dim.333), channel_id=1, replica_groups=mesh['box'=8,'rep'=4] {'box'}, dimensions={0} | all-to-all | bytes 64 | tf_op jit(solution)/shard_map/all_to_all | solution.py:36
  (157 shorter events, 13.7 us)
Async XLA Ops:
  0.6 8.0 %copy-start = (bf16[20,4,64,64]{3,2,1,0:T(8,128)(2,1)S(1)}, bf16[20,4,64,64]{3,2,1,0:T(8,128)(2,1)}, u32[]{:S(2)}) copy-start(bf16[20,4,64,64]{3,2,1,0:T(8,128)(2,1)} %param.16) | copy-start | bytes 1966084
  0.6 17.0 %copy-start.2 = (f32[16,256]{1,0:T(8,128)S(1)}, f32[16,256]{1,0:T(8,128)}, u32[]{:S(2)}) copy-start(f32[16,256]{1,0:T(8,128)} %param.9) | copy-start | bytes 49156
  0.7 6.6 %copy-start.4 = (s32[16,2]{0,1:T(2,128)S(1)}, s32[16,2]{0,1:T(2,128)}, u32[]{:S(2)}) copy-start(s32[16,2]{0,1:T(2,128)} %param.12) | copy-start | bytes 388
  0.7 7.6 %copy-start.6 = (bf16[16,64,64]{2,1,0:T(8,128)(2,1)S(1)}, bf16[16,64,64]{2,1,0:T(8,128)(2,1)}, u32[]{:S(2)}) copy-start(bf16[16,64,64]{2,1,0:T(8,128)(2,1)} %param.14) | copy-start | bytes 393220
  0.7 7.8 %copy-start.5 = (s32[16]{0:T(128)S(1)}, s32[16]{0:T(128)}, u32[]{:S(2)}) copy-start(s32[16]{0:T(128)} %param.15) | copy-start | bytes 196
  9.5 24.5 %copy-start.1 = (bf16[16,64,256]{2,1,0:T(8,128)(2,1)S(1)}, bf16[16,64,256]{2,1,0:T(8,128)(2,1)}, u32[]{:S(2)}) copy-start(bf16[16,64,256]{2,1,0:T(8,128)(2,1)} %param.13) | copy-start | bytes 1572868
  10.3 17.0 %all-to-all-start = ((f32[8,1,5376]{2,1,0:T(1,128)}), f32[8,1,5376]{2,1,0:T(1,128)S(1)}, u32[]{:S(2)}, u32[]{:S(2)}) async-start(f32[8,1,5376]{2,1,0:T(1,128)} %pad_maximum_fusion), calls=%async_computation | async-start | bytes 344064 | tf_op jit(solution)/shard_map/all_to_all | solution.py:117
  17.6 16.6 %copy-start.3 = (f32[16,256]{1,0:T(8,128)S(1)}, f32[16,256]{1,0:T(8,128)}, u32[]{:S(2)}) copy-start(f32[16,256]{1,0:T(8,128)} %param.10) | copy-start | bytes 49156
  17.6 5.5 %collective-permute-start = (bf16[16,256]{1,0:T(8,128)(2,1)S(1)}, bf16[16,256]{1,0:T(8,128)(2,1)S(1)}, u32[]{:S(2)}, u32[]{:S(2)}) collective-permute-start(bf16[16,256]{1,0:T(8,128)(2,1)S(1)} %convert_element_type.67), channel_id=1, source_target_pairs={{4,0},{8,4},{12,8},{16,12},{20,16},{24,20},{28,24},{5,1},{9,5},{13... | collective-permute-start | bytes 24584 | tf_op jit(solution)/shard_map/ppermute | solution.py:110
  28.7 3.9 %collective-permute-start.2 = (f32[5376]{0:T(1024)S(1)}, f32[5376]{0:T(1024)S(1)}, u32[]{:S(2)}, u32[]{:S(2)}) collective-permute-start(f32[5376]{0:T(1024)S(1)} %constant_dynamic-update-slice_fusion), channel_id=1, source_target_pairs={{0,2},{1,3},{2,0},{3,1},{4,6},{5,7},{6,4},{7,5},{8,10},{9,11},{10,... | collective-permute-start | bytes 64520 | tf_op jit(solution)/shard_map/ppermute | solution.py:13
  30.3 3.3 %collective-permute-start.3 = (f32[5376]{0:T(1024)S(1)}, f32[5376]{0:T(1024)S(1)}, u32[]{:S(2)}, u32[]{:S(2)}) collective-permute-start(f32[5376]{0:T(1024)S(1)} %constant_dynamic-update-slice_fusion), channel_id=1, source_target_pairs={{0,3},{1,2},{2,1},{3,0},{4,7},{5,6},{6,5},{7,4},{8,11},{9,10},{10,... | collective-permute-start | bytes 64520 | tf_op jit(solution)/shard_map/ppermute | solution.py:13
  30.3 3.3 %collective-permute-start.1 = (f32[5376]{0:T(1024)S(1)}, f32[5376]{0:T(1024)S(1)}, u32[]{:S(2)}, u32[]{:S(2)}) collective-permute-start(f32[5376]{0:T(1024)S(1)} %constant_dynamic-update-slice_fusion), channel_id=1, source_target_pairs={{0,1},{1,0},{2,3},{3,2},{4,5},{5,4},{6,7},{7,6},{8,9},{9,8},{10,11... | collective-permute-start | bytes 64520 | tf_op jit(solution)/shard_map/ppermute | solution.py:13
  47.0 10.4 %collective-permute-start.4 = (bf16[16,256]{1,0:T(8,128)(2,1)S(1)}, bf16[16,256]{1,0:T(8,128)(2,1)S(1)}, u32[]{:S(2)}, u32[]{:S(2)}) collective-permute-start(bf16[16,256]{1,0:T(8,128)(2,1)S(1)} %fusion.81), channel_id=1, source_target_pairs={{4,0},{8,4},{12,8},{16,12},{20,16},{24,20},{28,24},{5,1},{9,5},{13... | collective-permute-start | bytes 24584 | tf_op jit(solution)/shard_map/ppermute | solution.py:110
  53.4 11.5 %all-to-all-start.2 = ((f32[8,1,5376]{2,1,0:T(1,128)}), f32[8,1,5376]{2,1,0:T(1,128)S(1)}, u32[]{:S(2)}, u32[]{:S(2)}) async-start(f32[8,1,5376]{2,1,0:T(1,128)} %pad_maximum_fusion.1), calls=%async_computation.2 | async-start | bytes 344064 | tf_op jit(solution)/shard_map/all_to_all | solution.py:117
  66.4 3.9 %collective-permute-start.6 = (f32[5376]{0:T(1024)S(1)}, f32[5376]{0:T(1024)S(1)}, u32[]{:S(2)}, u32[]{:S(2)}) collective-permute-start(f32[5376]{0:T(1024)S(1)} %constant_dynamic-update-slice_fusion.1), channel_id=1, source_target_pairs={{0,2},{1,3},{2,0},{3,1},{4,6},{5,7},{6,4},{7,5},{8,10},{9,11},{10,... | collective-permute-start | bytes 64520 | tf_op jit(solution)/shard_map/ppermute | solution.py:13
  67.2 3.5 %collective-permute-start.7 = (f32[5376]{0:T(1024)S(1)}, f32[5376]{0:T(1024)S(1)}, u32[]{:S(2)}, u32[]{:S(2)}) collective-permute-start(f32[5376]{0:T(1024)S(1)} %constant_dynamic-update-slice_fusion.1), channel_id=1, source_target_pairs={{0,3},{1,2},{2,1},{3,0},{4,7},{5,6},{6,5},{7,4},{8,11},{9,10},{10,... | collective-permute-start | bytes 64520 | tf_op jit(solution)/shard_map/ppermute | solution.py:13
  67.2 3.5 %collective-permute-start.5 = (f32[5376]{0:T(1024)S(1)}, f32[5376]{0:T(1024)S(1)}, u32[]{:S(2)}, u32[]{:S(2)}) collective-permute-start(f32[5376]{0:T(1024)S(1)} %constant_dynamic-update-slice_fusion.1), channel_id=1, source_target_pairs={{0,1},{1,0},{2,3},{3,2},{4,5},{5,4},{6,7},{7,6},{8,9},{9,8},{10,11... | collective-permute-start | bytes 64520 | tf_op jit(solution)/shard_map/ppermute | solution.py:13

commit v13 on v12

--- a/solution.py
+++ b/solution.py
@@ -85,8 +85,14 @@
     norm_now = None
     for iteration in range(ITERS):
         rounded = direction.astype(jnp.bfloat16)
+        following = lax.ppermute(
+            rounded, "box", [(i, i - 1) for i in range(1, box_devices)]
+        )
+        mirror_field = rounded
+        if iteration == 0:
+            following, mirror_field = lax.optimization_barrier((following, rounded))
         mirrored = jnp.einsum(
-            "bsij,bi->bsj", near_tiles, rounded, preferred_element_type=jnp.float32
+            "bsij,bi->bsj", near_tiles, mirror_field, preferred_element_type=jnp.float32
         )
         landed = jnp.dot(
             near_onehot, mirrored.reshape(-1, mirrored.shape[2]), precision=lax.Precision.HIGHEST
@@ -107,9 +113,6 @@
             far_pick.astype(jnp.float32), far_mirror.reshape(-1, rank_width),
             precision=lax.Precision.HIGHEST,
         ).reshape(box_devices, node_count, rank_width)
-        following = lax.ppermute(
-            rounded, "box", [(i, i - 1) for i in range(1, box_devices)]
-        )
         coef_wide = node_coef.astype(jnp.float32)
         far_send = jnp.where(below, coef_wide[None], spread)
         is_next = (devices == box_rank + 1)[:, None]

time: 83.2 us -> 84 us (level)
  blocking collectives: 21.1 us -> 17.8 us
  other arithmetic: 7.01 us -> 9.03 us
  matrix products: 18.1 us -> 19.1 us
    ppermute x2, waiting for transfers between devices: 3.67 us -> 0.01 us  [local(): lax.ppermute(rounded, 'box', [(i, i - 1) for i in range(1, box_devices)])]
    all_to_all x2, waiting for transfers between devices: 3.45 us -> 6.95 us  [local(): lax.all_to_all(jnp.concatenate([far_send.reshape(box_devices, 1, far_size...]
    all_to_all x2, blocking collectives: 21.1 us -> 17.8 us  [box_sum(): got = lax.all_to_all(sent, 'box', 0, 0, tiled=True)]
    all_to_all x2, starting transfers between devices: 11.2 us -> 12.5 us  [local(): lax.all_to_all(jnp.concatenate([far_send.reshape(box_devices, 1, far_size...]
    dot_general x2, matrix products: 0.35 us -> 1.3 us  [local(): jnp.einsum('brq,br->bq', transfer, leaf_coef, preferred_element_type=jnp....]
  transfers between devices with their start and end apart: 10 -> 10, of which waited for: 6 -> 6; matrix products, arithmetic and copies ran while one was open for 17% -> 26% of each run, Pallas kernels for 0% -> 0%
where the time goes in v13:
time: 84 us; the launch traced here: 83.2 us
  matrix products  19.1 us (23%)
  starting transfers between devices  18.9 us (22%)
  blocking collectives  17.8 us (21%)
  waiting for transfers between devices  12.2 us (15%)
  other arithmetic  9.03 us (11%)
  local copies, waits for them, and re-layouts  4.97 us (6%)
  between operations  1.25 us (1%)
    all_to_all x2, blocking collectives, box_sum(): got = lax.all_to_all(sent, 'box', 0, 0, tiled=True)  17.8 us
    all_to_all x2, starting transfers between devices, local(): lax.all_to_all(jnp.concatenate([far_send.reshape(box_devices, 1, far_size...  12.5 us
    all_to_all x2, waiting for transfers between devices, local(): lax.all_to_all(jnp.concatenate([far_send.reshape(box_devices, 1, far_size...  6.95 us
    dot_general x2, matrix products, local(): jnp.einsum('bsij,bsj->bi', near_tiles, near_in, preferred_element_type=jn...  6.73 us
    dot_general x2, matrix products, local(): jnp.einsum('bsij,bi->bsj', near_tiles, mirror_field, preferred_element_ty...  5.68 us
    ppermute x6, waiting for transfers between devices, rep_sum(): lax.ppermute(vector, 'rep', [(i, i ^ mask) for i in range(count)])  5.23 us
    ppermute x6, starting transfers between devices, rep_sum(): lax.ppermute(vector, 'rep', [(i, i ^ mask) for i in range(count)])  3.87 us
    ppermute x2, starting transfers between devices, local(): lax.ppermute(rounded, 'box', [(i, i - 1) for i in range(1, box_devices)])  2.58 us
  transfers between devices with their start and end apart: 10, of which 6 were waited for; matrix products, arithmetic and copies ran while one was open for 26% of the time, Pallas kernels for 0%

profile of v13, /device:TPU:0, one launch (start us, length us, event | category | flops | bytes accessed | tf_op | source)
XLA Modules:
  0.0 83.2 jit_solution(5541917972779047127)
XLA Ops:
  0.6 0.8 convert_element_type.67
  1.5 1.3 %collective-permute-start = (bf16[16,256]{1,0:T(8,128)(2,1)S(1)}, bf16[16,256]{1,0:T(8,128)(2,1)S(1)}, u32[]{:S(2)}, u32[]{:S(2)}) collective-permute-start(bf16[16,256]{1,0:T(8,128)(2,1)S(1)} %convert_element_type.67), channel_id=1, source_target_pairs={{4,0},{8,4},{12,8},{16,12},{20,16},{24,20},{28,24},{5,1},{9,5},{13... | collective-permute-start | bytes 24584 | tf_op jit(solution)/shard_map/ppermute | solution.py:88
  2.8 0.7 convert_bitcast_fusion.2
  3.5 1.3 %fusion.44 = f32[16,1,64]{2,1,0:T(1,128)S(1)} fusion(bf16[16,64,256]{2,1,0:T(8,128)(2,1)} %param.13, bf16[16,256,1]{1,0,2:T(8,128)(2,1)S(1)} %convert_bitcast_fusion.2), kind=kOutput, calls=%fused_computation.81 | convolution fusion | flops 524288 | bytes 536576 | tf_op jit(solution)/shard_map/brl,bl->br/dot_general | solution.py:100
  8.2 1.1 %fusion.69 = f32[16,1,64]{2,1,0:T(1,128)S(1)} fusion(bf16[16,64,64]{2,1,0:T(8,128)(2,1)} %param.14, bf16[16,64,1]{1,0,2:T(8,128)(2,1)S(1)} %convert_bitcast_fusion.1), kind=kOutput, calls=%fused_computation.115 | convolution fusion | flops 131072 | bytes 137216 | tf_op jit(solution)/shard_map/brq,br->bq/dot_general | solution.py:103
  11.0 2.8 %fusion.46 = f32[16,1,2,256]{3,1,2,0:T(1,128)S(1)} fusion(bf16[16,2,256,256]{3,2,1,0:T(8,128)(2,1)} %param.11, bf16[16,256,1,1]{1,0,2,3:T(8,128)(2,1)S(1)} %bitcast.143), kind=kOutput, calls=%fused_computation.83 | convolution fusion | flops 4194304 | bytes 4235264 | tf_op jit(solution)/shard_map/bsij,bi->bsj/dot_general | solution.py:94
  14.3 0.8 pad_maximum_fusion
  15.1 8.5 %all-to-all-start = ((f32[8,1,5376]{2,1,0:T(1,128)}), f32[8,1,5376]{2,1,0:T(1,128)S(1)}, u32[]{:S(2)}, u32[]{:S(2)}) async-start(f32[8,1,5376]{2,1,0:T(1,128)} %pad_maximum_fusion), calls=%async_computation | async-start | bytes 344064 | tf_op jit(solution)/shard_map/all_to_all | solution.py:120
  24.4 3.4 %fusion.32 = f32[16,1,256,1]{2,1,3,0:T(1,128)S(1)} fusion(bf16[16,2,256,256]{3,2,1,0:T(8,128)(2,1)} %param.11, bf16[16,2,256,1]{2,1,0,3:T(2,128)(2,1)S(1)} %fusion.34), kind=kOutput, calls=%fused_computation.53 | convolution fusion | flops 4194304 | bytes 4227072 | tf_op jit(solution)/shard_map/bsij,bsj->bi/dot_general | solution.py:134
  27.7 3.5 %all-to-all-done = f32[8,1,5376]{2,1,0:T(1,128)S(1)} async-done(((f32[8,1,5376]{2,1,0:T(1,128)}), f32[8,1,5376]{2,1,0:T(1,128)S(1)}, u32[]{:S(2)}, u32[]{:S(2)}) %all-to-all-start) | async-done | bytes 172064 | tf_op jit(solution)/shard_map/all_to_all | solution.py:120
  32.8 1.6 %collective-permute-start.2 = (f32[5376]{0:T(1024)S(1)}, f32[5376]{0:T(1024)S(1)}, u32[]{:S(2)}, u32[]{:S(2)}) collective-permute-start(f32[5376]{0:T(1024)S(1)} %constant_dynamic-update-slice_fusion), channel_id=1, source_target_pairs={{0,2},{1,3},{2,0},{3,1},{4,6},{5,7},{6,4},{7,5},{8,10},{9,11},{10,... | collective-permute-start | bytes 64520 | tf_op jit(solution)/shard_map/ppermute | solution.py:13
  34.7 2.0 %collective-permute-done.2 = f32[5376]{0:T(1024)S(1)} collective-permute-done((f32[5376]{0:T(1024)S(1)}, f32[5376]{0:T(1024)S(1)}, u32[]{:S(2)}, u32[]{:S(2)}) %collective-permute-start.2) | collective-permute-done | bytes 21536 | tf_op jit(solution)/shard_map/ppermute | solution.py:13
  36.7 0.9 %collective-permute-done.3 = f32[5376]{0:T(1024)S(1)} collective-permute-done((f32[5376]{0:T(1024)S(1)}, f32[5376]{0:T(1024)S(1)}, u32[]{:S(2)}, u32[]{:S(2)}) %collective-permute-start.3) | collective-permute-done | bytes 21536 | tf_op jit(solution)/shard_map/ppermute | solution.py:13
  38.5 8.9 %all_to_all.22 = f32[8,1,4]{2,1,0:T(1,128)S(1)} all-to-all(f32[8,1,4]{2,1,0:T(1,128)S(1)} %broadcast_in_dim.322), channel_id=1, replica_groups=mesh['box'=8,'rep'=4] {'box'}, dimensions={0} | all-to-all | bytes 256 | tf_op jit(solution)/shard_map/all_to_all | solution.py:36
  47.8 1.3 %collective-permute-start.4 = (bf16[16,256]{1,0:T(8,128)(2,1)S(1)}, bf16[16,256]{1,0:T(8,128)(2,1)S(1)}, u32[]{:S(2)}, u32[]{:S(2)}) collective-permute-start(bf16[16,256]{1,0:T(8,128)(2,1)S(1)} %fusion.81), channel_id=1, source_target_pairs={{4,0},{8,4},{12,8},{16,12},{20,16},{24,20},{28,24},{5,1},{9,5},{13... | collective-permute-start | bytes 24584 | tf_op jit(solution)/shard_map/ppermute | solution.py:88
  50.2 2.8 %fusion.42 = f32[16,1,2,256]{3,1,2,0:T(1,128)S(1)} fusion(bf16[16,2,256,256]{3,2,1,0:T(8,128)(2,1)} %param.11, bf16[16,256,1,1]{1,0,2,3:T(8,128)(2,1)S(1)} %bitcast.145), kind=kOutput, calls=%fused_computation.79 | convolution fusion | flops 4194304 | bytes 4235264 | tf_op jit(solution)/shard_map/bsij,bi->bsj/dot_general | solution.py:94
  53.4 0.8 pad_maximum_fusion.1
  54.2 3.9 %all-to-all-start.2 = ((f32[8,1,5376]{2,1,0:T(1,128)}), f32[8,1,5376]{2,1,0:T(1,128)S(1)}, u32[]{:S(2)}, u32[]{:S(2)}) async-start(f32[8,1,5376]{2,1,0:T(1,128)} %pad_maximum_fusion.1), calls=%async_computation.2 | async-start | bytes 344064 | tf_op jit(solution)/shard_map/all_to_all | solution.py:120
  58.9 3.4 %fusion.30 = f32[16,1,256,1]{2,1,3,0:T(1,128)S(1)} fusion(bf16[16,2,256,256]{3,2,1,0:T(8,128)(2,1)} %param.11, bf16[16,2,256,1]{2,1,0,3:T(2,128)(2,1)S(1)} %fusion.35), kind=kOutput, calls=%fused_computation.50 | convolution fusion | flops 4194304 | bytes 4227072 | tf_op jit(solution)/shard_map/bsij,bsj->bi/dot_general | solution.py:134
  62.3 3.4 %all-to-all-done.2 = f32[8,1,5376]{2,1,0:T(1,128)S(1)} async-done(((f32[8,1,5376]{2,1,0:T(1,128)}), f32[8,1,5376]{2,1,0:T(1,128)S(1)}, u32[]{:S(2)}, u32[]{:S(2)}) %all-to-all-start.2) | async-done | bytes 172064 | tf_op jit(solution)/shard_map/all_to_all | solution.py:120
  67.3 0.9 %collective-permute-start.6 = (f32[5376]{0:T(1024)S(1)}, f32[5376]{0:T(1024)S(1)}, u32[]{:S(2)}, u32[]{:S(2)}) collective-permute-start(f32[5376]{0:T(1024)S(1)} %constant_dynamic-update-slice_fusion.1), channel_id=1, source_target_pairs={{0,2},{1,3},{2,0},{3,1},{4,6},{5,7},{6,4},{7,5},{8,10},{9,11},{10,... | collective-permute-start | bytes 64520 | tf_op jit(solution)/shard_map/ppermute | solution.py:13
  68.2 1.0 %collective-permute-start.7 = (f32[5376]{0:T(1024)S(1)}, f32[5376]{0:T(1024)S(1)}, u32[]{:S(2)}, u32[]{:S(2)}) collective-permute-start(f32[5376]{0:T(1024)S(1)} %constant_dynamic-update-slice_fusion.1), channel_id=1, source_target_pairs={{0,3},{1,2},{2,1},{3,0},{4,7},{5,6},{6,5},{7,4},{8,11},{9,10},{10,... | collective-permute-start | bytes 64520 | tf_op jit(solution)/shard_map/ppermute | solution.py:13
  69.2 2.1 %collective-permute-done.6 = f32[5376]{0:T(1024)S(1)} collective-permute-done((f32[5376]{0:T(1024)S(1)}, f32[5376]{0:T(1024)S(1)}, u32[]{:S(2)}, u32[]{:S(2)}) %collective-permute-start.6) | collective-permute-done | bytes 21536 | tf_op jit(solution)/shard_map/ppermute | solution.py:13
  73.4 8.8 %all_to_all.23 = f32[8,1,1]{2,1,0:T(1,128)S(1)} all-to-all(f32[8,1,1]{2,1,0:T(1,128)S(1)} %broadcast_in_dim.333), channel_id=1, replica_groups=mesh['box'=8,'rep'=4] {'box'}, dimensions={0} | all-to-all | bytes 64 | tf_op jit(solution)/shard_map/all_to_all | solution.py:36
  (152 shorter events, 15.8 us)
Async XLA Ops:
  0.6 8.9 %copy-start = (bf16[20,4,64,64]{3,2,1,0:T(8,128)(2,1)S(1)}, bf16[20,4,64,64]{3,2,1,0:T(8,128)(2,1)}, u32[]{:S(2)}) copy-start(bf16[20,4,64,64]{3,2,1,0:T(8,128)(2,1)} %param.16) | copy-start | bytes 1966084
  1.5 9.6 %collective-permute-start = (bf16[16,256]{1,0:T(8,128)(2,1)S(1)}, bf16[16,256]{1,0:T(8,128)(2,1)S(1)}, u32[]{:S(2)}, u32[]{:S(2)}) collective-permute-start(bf16[16,256]{1,0:T(8,128)(2,1)S(1)} %convert_element_type.67), channel_id=1, source_target_pairs={{4,0},{8,4},{12,8},{16,12},{20,16},{24,20},{28,24},{5,1},{9,5},{13... | collective-permute-start | bytes 24584 | tf_op jit(solution)/shard_map/ppermute | solution.py:88
  13.9 23.9 %copy-start.4 = (bf16[16,64,64]{2,1,0:T(8,128)(2,1)S(1)}, bf16[16,64,64]{2,1,0:T(8,128)(2,1)}, u32[]{:S(2)}) copy-start(bf16[16,64,64]{2,1,0:T(8,128)(2,1)} %param.14) | copy-start | bytes 393220
  14.1 24.0 %copy-start.1 = (bf16[16,64,256]{2,1,0:T(8,128)(2,1)S(1)}, bf16[16,64,256]{2,1,0:T(8,128)(2,1)}, u32[]{:S(2)}) copy-start(bf16[16,64,256]{2,1,0:T(8,128)(2,1)} %param.13) | copy-start | bytes 1572868
  15.1 23.2 %copy-start.2 = (f32[16,256]{1,0:T(8,128)S(1)}, f32[16,256]{1,0:T(8,128)}, u32[]{:S(2)}) copy-start(f32[16,256]{1,0:T(8,128)} %param.9) | copy-start | bytes 49156
  15.1 23.2 %copy-start.3 = (f32[16,256]{1,0:T(8,128)S(1)}, f32[16,256]{1,0:T(8,128)}, u32[]{:S(2)}) copy-start(f32[16,256]{1,0:T(8,128)} %param.10) | copy-start | bytes 49156
  15.1 16.2 %all-to-all-start = ((f32[8,1,5376]{2,1,0:T(1,128)}), f32[8,1,5376]{2,1,0:T(1,128)S(1)}, u32[]{:S(2)}, u32[]{:S(2)}) async-start(f32[8,1,5376]{2,1,0:T(1,128)} %pad_maximum_fusion), calls=%async_computation | async-start | bytes 344064 | tf_op jit(solution)/shard_map/all_to_all | solution.py:120
  32.7 2.0 %collective-permute-start.1 = (f32[5376]{0:T(1024)S(1)}, f32[5376]{0:T(1024)S(1)}, u32[]{:S(2)}, u32[]{:S(2)}) collective-permute-start(f32[5376]{0:T(1024)S(1)} %constant_dynamic-update-slice_fusion), channel_id=1, source_target_pairs={{0,1},{1,0},{2,3},{3,2},{4,5},{5,4},{6,7},{7,6},{8,9},{9,8},{10,11... | collective-permute-start | bytes 64520 | tf_op jit(solution)/shard_map/ppermute | solution.py:13
  32.8 3.9 %collective-permute-start.2 = (f32[5376]{0:T(1024)S(1)}, f32[5376]{0:T(1024)S(1)}, u32[]{:S(2)}, u32[]{:S(2)}) collective-permute-start(f32[5376]{0:T(1024)S(1)} %constant_dynamic-update-slice_fusion), channel_id=1, source_target_pairs={{0,2},{1,3},{2,0},{3,1},{4,6},{5,7},{6,4},{7,5},{8,10},{9,11},{10,... | collective-permute-start | bytes 64520 | tf_op jit(solution)/shard_map/ppermute | solution.py:13
  34.3 3.3 %collective-permute-start.3 = (f32[5376]{0:T(1024)S(1)}, f32[5376]{0:T(1024)S(1)}, u32[]{:S(2)}, u32[]{:S(2)}) collective-permute-start(f32[5376]{0:T(1024)S(1)} %constant_dynamic-update-slice_fusion), channel_id=1, source_target_pairs={{0,3},{1,2},{2,1},{3,0},{4,7},{5,6},{6,5},{7,4},{8,11},{9,10},{10,... | collective-permute-start | bytes 64520 | tf_op jit(solution)/shard_map/ppermute | solution.py:13
  47.8 10.4 %collective-permute-start.4 = (bf16[16,256]{1,0:T(8,128)(2,1)S(1)}, bf16[16,256]{1,0:T(8,128)(2,1)S(1)}, u32[]{:S(2)}, u32[]{:S(2)}) collective-permute-start(bf16[16,256]{1,0:T(8,128)(2,1)S(1)} %fusion.81), channel_id=1, source_target_pairs={{4,0},{8,4},{12,8},{16,12},{20,16},{24,20},{28,24},{5,1},{9,5},{13... | collective-permute-start | bytes 24584 | tf_op jit(solution)/shard_map/ppermute | solution.py:88
  54.2 11.5 %all-to-all-start.2 = ((f32[8,1,5376]{2,1,0:T(1,128)}), f32[8,1,5376]{2,1,0:T(1,128)S(1)}, u32[]{:S(2)}, u32[]{:S(2)}) async-start(f32[8,1,5376]{2,1,0:T(1,128)} %pad_maximum_fusion.1), calls=%async_computation.2 | async-start | bytes 344064 | tf_op jit(solution)/shard_map/all_to_all | solution.py:120
  67.2 1.9 %collective-permute-start.5 = (f32[5376]{0:T(1024)S(1)}, f32[5376]{0:T(1024)S(1)}, u32[]{:S(2)}, u32[]{:S(2)}) collective-permute-start(f32[5376]{0:T(1024)S(1)} %constant_dynamic-update-slice_fusion.1), channel_id=1, source_target_pairs={{0,1},{1,0},{2,3},{3,2},{4,5},{5,4},{6,7},{7,6},{8,9},{9,8},{10,11... | collective-permute-start | bytes 64520 | tf_op jit(solution)/shard_map/ppermute | solution.py:13
  67.3 3.9 %collective-permute-start.6 = (f32[5376]{0:T(1024)S(1)}, f32[5376]{0:T(1024)S(1)}, u32[]{:S(2)}, u32[]{:S(2)}) collective-permute-start(f32[5376]{0:T(1024)S(1)} %constant_dynamic-update-slice_fusion.1), channel_id=1, source_target_pairs={{0,2},{1,3},{2,0},{3,1},{4,6},{5,7},{6,4},{7,5},{8,10},{9,11},{10,... | collective-permute-start | bytes 64520 | tf_op jit(solution)/shard_map/ppermute | solution.py:13
  68.2 3.3 %collective-permute-start.7 = (f32[5376]{0:T(1024)S(1)}, f32[5376]{0:T(1024)S(1)}, u32[]{:S(2)}, u32[]{:S(2)}) collective-permute-start(f32[5376]{0:T(1024)S(1)} %constant_dynamic-update-slice_fusion.1), channel_id=1, source_target_pairs={{0,3},{1,2},{2,1},{3,0},{4,7},{5,6},{6,5},{7,4},{8,11},{9,10},{10,... | collective-permute-start | bytes 64520 | tf_op jit(solution)/shard_map/ppermute | solution.py:13

commit v14 on v10

--- a/solution.py
+++ b/solution.py
@@ -139,9 +139,8 @@
             "nsab,nsb->na", coupling, partner_coef, preferred_element_type=jnp.float32
         )
         far_part = far_forward + spread[box_rank] + mirror_in
-        both = rep_sum(jnp.concatenate([near_part.reshape(-1), far_part.reshape(-1)]))
-        near_total = both[:near_size].reshape(box_count, leaf)
-        far_total = both[near_size:].reshape(node_count, rank_width)
+        far_total = rep_sum(far_part)
+        near_total = rep_sum(near_part)
         group_out = far_total[box_count:].astype(jnp.bfloat16)
         parent_pick = jnp.zeros((box_count, rank_width), jnp.bfloat16)
         for group in range(group_count):

time: 82.9 us -> 85.5 us (1.031)
  starting transfers between devices: 18.1 us -> 22.6 us
  waiting for transfers between devices: 11.9 us -> 10.5 us
    ppermute x6 -> x12, starting transfers between devices: 4.35 us -> 8.72 us  [rep_sum(): lax.ppermute(vector, 'rep', [(i, i ^ mask) for i in range(count)])]
    ppermute x6 -> x12, waiting for transfers between devices: 4.77 us -> 3.37 us  [rep_sum(): lax.ppermute(vector, 'rep', [(i, i ^ mask) for i in range(count)])]
  transfers between devices with their start and end apart: 10 -> 16, of which waited for: 6 -> 8; matrix products, arithmetic and copies ran while one was open for 17% -> 18% of each run, Pallas kernels for 0% -> 0%
where the time goes in v14:
time: 85.5 us; the launch traced here: 84.8 us
  starting transfers between devices  22.6 us (26%)
  blocking collectives  21.1 us (25%)
  matrix products  18.1 us (21%)
  waiting for transfers between devices  10.5 us (12%)
  local copies, waits for them, and re-layouts  6.08 us (7%)
  other arithmetic  5.15 us (6%)
  between operations  1.23 us (1%)
    all_to_all x2, blocking collectives, box_sum(): got = lax.all_to_all(sent, 'box', 0, 0, tiled=True)  21.1 us
    all_to_all x2, starting transfers between devices, local(): lax.all_to_all(jnp.concatenate([far_send.reshape(box_devices, far_size),...  11.3 us
    ppermute x12, starting transfers between devices, rep_sum(): lax.ppermute(vector, 'rep', [(i, i ^ mask) for i in range(count)])  8.72 us
    dot_general x2, matrix products, local(): jnp.einsum('bsij,bsj->bi', near_tiles, near_in, preferred_element_type=jn...  6.73 us
    dot_general x2, matrix products, local(): jnp.einsum('bsij,bi->bsj', near_tiles, rounded, preferred_element_type=jn...  5.66 us
    ppermute x2, waiting for transfers between devices, local(): lax.ppermute(rounded, 'box', [(i, i - 1) for i in range(1, box_devices)])  3.65 us
    all_to_all x2, waiting for transfers between devices, local(): lax.all_to_all(jnp.concatenate([far_send.reshape(box_devices, far_size),...  3.45 us
    ppermute x12, waiting for transfers between devices, rep_sum(): lax.ppermute(vector, 'rep', [(i, i ^ mask) for i in range(count)])  3.37 us
  transfers between devices with their start and end apart: 16, of which 8 were waited for; matrix products, arithmetic and copies ran while one was open for 18% of the time, Pallas kernels for 0%

profile of v14, /device:TPU:0, one launch (start us, length us, event | category | flops | bytes accessed | tf_op | source)
XLA Modules:
  0.0 84.8 jit_solution(6933946957171709995)
XLA Ops:
  0.7 0.8 convert_bitcast_fusion.3
  1.5 0.7 convert_bitcast_fusion.2
  2.2 1.3 %fusion.39 = f32[16,1,64]{2,1,0:T(1,128)S(1)} fusion(bf16[16,64,256]{2,1,0:T(8,128)(2,1)} %param.13, bf16[16,256,1]{1,0,2:T(8,128)(2,1)S(1)} %convert_bitcast_fusion.2), kind=kOutput, calls=%fused_computation.74 | convolution fusion | flops 524288 | bytes 536576 | tf_op jit(solution)/shard_map/brl,bl->br/dot_general | solution.py:94
  4.4 2.8 %fusion.41 = f32[16,1,2,256]{3,1,2,0:T(1,128)S(1)} fusion(bf16[16,2,256,256]{3,2,1,0:T(8,128)(2,1)} %param.11, bf16[16,256,1,1]{1,0,2,3:T(8,128)(2,1)S(1)} %convert_bitcast_fusion.3), kind=kOutput, calls=%fused_computation.76 | convolution fusion | flops 4194304 | bytes 4235264 | tf_op jit(solution)/shard_map/bsij,bi->bsj/dot_general | solution.py:88
  9.5 0.8 all_to_all.24
  10.3 7.4 %all-to-all-start = ((f32[8,1,5376]{2,1,0:T(1,128)}), f32[8,1,5376]{2,1,0:T(1,128)S(1)}, u32[]{:S(2)}, u32[]{:S(2)}) async-start(f32[8,1,5376]{2,1,0:T(1,128)} %all_to_all.24), calls=%async_computation | async-start | bytes 344064 | tf_op jit(solution)/shard_map/all_to_all | solution.py:117
  17.7 1.3 %collective-permute-start = (bf16[16,256]{1,0:T(8,128)(2,1)S(1)}, bf16[16,256]{1,0:T(8,128)(2,1)S(1)}, u32[]{:S(2)}, u32[]{:S(2)}) collective-permute-start(bf16[16,256]{1,0:T(8,128)(2,1)S(1)} %convert_element_type.65), channel_id=1, source_target_pairs={{4,0},{8,4},{12,8},{16,12},{20,16},{24,20},{28,24},{5,1},{9,5},{13... | collective-permute-start | bytes 24584 | tf_op jit(solution)/shard_map/ppermute | solution.py:110
  19.6 3.7 %collective-permute-done = bf16[16,256]{1,0:T(8,128)(2,1)S(1)} collective-permute-done((bf16[16,256]{1,0:T(8,128)(2,1)S(1)}, bf16[16,256]{1,0:T(8,128)(2,1)S(1)}, u32[]{:S(2)}, u32[]{:S(2)}) %collective-permute-start) | collective-permute-done | bytes 8224 | tf_op jit(solution)/shard_map/ppermute | solution.py:110
  24.0 3.4 %fusion.29 = f32[16,1,256,1]{2,1,3,0:T(1,128)S(1)} fusion(bf16[16,2,256,256]{3,2,1,0:T(8,128)(2,1)} %param.11, bf16[16,2,256,1]{2,1,0,3:T(2,128)(2,1)S(1)} %fusion.31), kind=kOutput, calls=%fused_computation.52 | convolution fusion | flops 4194304 | bytes 4227072 | tf_op jit(solution)/shard_map/bsij,bsj->bi/dot_general | solution.py:131
  28.5 1.5 %collective-permute-start.5 = (f32[20,64]{1,0:T(8,128)S(1)}, f32[20,64]{1,0:T(8,128)S(1)}, u32[]{:S(2)}, u32[]{:S(2)}) collective-permute-start(f32[20,64]{1,0:T(8,128)S(1)} %fusion.49), channel_id=1, source_target_pairs={{0,2},{1,3},{2,0},{3,1},{4,6},{5,7},{6,4},{7,5},{8,10},{9,11},{10,... | collective-permute-start | bytes 15368 | tf_op jit(solution)/shard_map/ppermute | solution.py:13
  30.8 1.6 %collective-permute-start.2 = (f32[16,256]{1,0:T(8,128)S(1)}, f32[16,256]{1,0:T(8,128)S(1)}, u32[]{:S(2)}, u32[]{:S(2)}) collective-permute-start(f32[16,256]{1,0:T(8,128)S(1)} %fusion.34), channel_id=1, source_target_pairs={{0,2},{1,3},{2,0},{3,1},{4,6},{5,7},{6,4},{7,5},{8,10},{9,11},{10,... | collective-permute-start | bytes 49160 | tf_op jit(solution)/shard_map/ppermute | solution.py:13
  33.7 0.9 %collective-permute-done.2 = f32[16,256]{1,0:T(8,128)S(1)} collective-permute-done((f32[16,256]{1,0:T(8,128)S(1)}, f32[16,256]{1,0:T(8,128)S(1)}, u32[]{:S(2)}, u32[]{:S(2)}) %collective-permute-start.2) | collective-permute-done | bytes 16416 | tf_op jit(solution)/shard_map/ppermute | solution.py:13
  34.6 1.0 %collective-permute-done.3 = f32[16,256]{1,0:T(8,128)S(1)} collective-permute-done((f32[16,256]{1,0:T(8,128)S(1)}, f32[16,256]{1,0:T(8,128)S(1)}, u32[]{:S(2)}, u32[]{:S(2)}) %collective-permute-start.3) | collective-permute-done | bytes 16416 | tf_op jit(solution)/shard_map/ppermute | solution.py:13
  35.8 12.2 %all_to_all.36 = f32[8,1,4]{2,1,0:T(1,128)S(1)} all-to-all(f32[8,1,4]{2,1,0:T(1,128)S(1)} %broadcast_in_dim.341), channel_id=1, replica_groups=mesh['box'=8,'rep'=4] {'box'}, dimensions={0} | all-to-all | bytes 256 | tf_op jit(solution)/shard_map/all_to_all | solution.py:36
  48.4 1.3 %collective-permute-start.7 = (bf16[16,256]{1,0:T(8,128)(2,1)S(1)}, bf16[16,256]{1,0:T(8,128)(2,1)S(1)}, u32[]{:S(2)}, u32[]{:S(2)}) collective-permute-start(bf16[16,256]{1,0:T(8,128)(2,1)S(1)} %get-tuple-element.6), channel_id=1, source_target_pairs={{4,0},{8,4},{12,8},{16,12},{20,16},{24,20},{28,24},{5,1},{9,5},{13... | collective-permute-start | bytes 24584 | tf_op jit(solution)/shard_map/ppermute | solution.py:110
  49.7 2.8 %fusion.37 = f32[16,1,2,256]{3,1,2,0:T(1,128)S(1)} fusion(bf16[16,2,256,256]{3,2,1,0:T(8,128)(2,1)} %param.11, bf16[16,256,1,1]{1,0,2,3:T(8,128)(2,1)S(1)} %bitcast.156), kind=kOutput, calls=%fused_computation.72 | convolution fusion | flops 4194304 | bytes 4235264 | tf_op jit(solution)/shard_map/bsij,bi->bsj/dot_general | solution.py:88
  53.9 0.9 %copy.57 = f32[8,1,5376]{2,1,0:T(1,128)} copy(f32[8,1,5376]{2,0,1:T(8,128)S(1)} %maximum_bitcast_fusion) | data formatting | bytes 344064 | tf_op jit(solution)/shard_map/all_to_all | solution.py:117
  54.8 3.9 %all-to-all-start.2 = ((f32[8,1,5376]{2,1,0:T(1,128)}), f32[8,1,5376]{2,1,0:T(1,128)S(1)}, u32[]{:S(2)}, u32[]{:S(2)}) async-start(f32[8,1,5376]{2,1,0:T(1,128)} %copy.57), calls=%async_computation.2 | async-start | bytes 344064 | tf_op jit(solution)/shard_map/all_to_all | solution.py:117
  59.5 3.4 %fusion.27 = f32[16,1,256,1]{2,1,3,0:T(1,128)S(1)} fusion(bf16[16,2,256,256]{3,2,1,0:T(8,128)(2,1)} %param.11, bf16[16,2,256,1]{2,1,0,3:T(2,128)(2,1)S(1)} %fusion.32), kind=kOutput, calls=%fused_computation.49 | convolution fusion | flops 4194304 | bytes 4227072 | tf_op jit(solution)/shard_map/bsij,bsj->bi/dot_general | solution.py:131
  62.9 3.4 %all-to-all-done.2 = f32[8,1,5376]{2,1,0:T(1,128)S(1)} async-done(((f32[8,1,5376]{2,1,0:T(1,128)}), f32[8,1,5376]{2,1,0:T(1,128)S(1)}, u32[]{:S(2)}, u32[]{:S(2)}) %all-to-all-start.2) | async-done | bytes 172064 | tf_op jit(solution)/shard_map/all_to_all | solution.py:117
  68.1 1.5 %collective-permute-start.11 = (f32[20,64]{1,0:T(8,128)S(1)}, f32[20,64]{1,0:T(8,128)S(1)}, u32[]{:S(2)}, u32[]{:S(2)}) collective-permute-start(f32[20,64]{1,0:T(8,128)S(1)} %fusion.48), channel_id=1, source_target_pairs={{0,1},{1,0},{2,3},{3,2},{4,5},{5,4},{6,7},{7,6},{8,9},{9,8},{10,11... | collective-permute-start | bytes 15368 | tf_op jit(solution)/shard_map/ppermute | solution.py:13
  71.2 0.8 collective-permute-start.8
  72.5 1.2 %collective-permute-done.9 = f32[16,256]{1,0:T(8,128)S(1)} collective-permute-done((f32[16,256]{1,0:T(8,128)S(1)}, f32[16,256]{1,0:T(8,128)S(1)}, u32[]{:S(2)}, u32[]{:S(2)}) %collective-permute-start.9) | collective-permute-done | bytes 16416 | tf_op jit(solution)/shard_map/ppermute | solution.py:13
  75.1 8.8 %all_to_all.37 = f32[8,1,1]{2,1,0:T(1,128)S(1)} all-to-all(f32[8,1,1]{2,1,0:T(1,128)S(1)} %broadcast_in_dim.356), channel_id=1, replica_groups=mesh['box'=8,'rep'=4] {'box'}, dimensions={0} | all-to-all | bytes 64 | tf_op jit(solution)/shard_map/all_to_all | solution.py:36
  (157 shorter events, 16.2 us)
Async XLA Ops:
  0.6 8.0 %copy-start = (bf16[20,4,64,64]{3,2,1,0:T(8,128)(2,1)S(1)}, bf16[20,4,64,64]{3,2,1,0:T(8,128)(2,1)}, u32[]{:S(2)}) copy-start(bf16[20,4,64,64]{3,2,1,0:T(8,128)(2,1)} %param.16) | copy-start | bytes 1966084
  0.6 6.6 %copy-start.4 = (s32[16,2]{0,1:T(2,128)S(1)}, s32[16,2]{0,1:T(2,128)}, u32[]{:S(2)}) copy-start(s32[16,2]{0,1:T(2,128)} %param.12) | copy-start | bytes 388
  0.7 7.6 %copy-start.5 = (s32[16]{0:T(128)S(1)}, s32[16]{0:T(128)}, u32[]{:S(2)}) copy-start(s32[16]{0:T(128)} %param.15) | copy-start | bytes 196
  0.7 7.6 %copy-start.6 = (bf16[16,64,64]{2,1,0:T(8,128)(2,1)S(1)}, bf16[16,64,64]{2,1,0:T(8,128)(2,1)}, u32[]{:S(2)}) copy-start(bf16[16,64,64]{2,1,0:T(8,128)(2,1)} %param.14) | copy-start | bytes 393220
  2.2 15.4 %copy-start.2 = (f32[16,256]{1,0:T(8,128)S(1)}, f32[16,256]{1,0:T(8,128)}, u32[]{:S(2)}) copy-start(f32[16,256]{1,0:T(8,128)} %param.9) | copy-start | bytes 49156
  9.5 24.0 %copy-start.1 = (bf16[16,64,256]{2,1,0:T(8,128)(2,1)S(1)}, bf16[16,64,256]{2,1,0:T(8,128)(2,1)}, u32[]{:S(2)}) copy-start(bf16[16,64,256]{2,1,0:T(8,128)(2,1)} %param.13) | copy-start | bytes 1572868
  10.3 25.3 %copy-start.3 = (f32[16,256]{1,0:T(8,128)S(1)}, f32[16,256]{1,0:T(8,128)}, u32[]{:S(2)}) copy-start(f32[16,256]{1,0:T(8,128)} %param.10) | copy-start | bytes 49156
  10.3 17.1 %all-to-all-start = ((f32[8,1,5376]{2,1,0:T(1,128)}), f32[8,1,5376]{2,1,0:T(1,128)S(1)}, u32[]{:S(2)}, u32[]{:S(2)}) async-start(f32[8,1,5376]{2,1,0:T(1,128)} %all_to_all.24), calls=%async_computation | async-start | bytes 344064 | tf_op jit(solution)/shard_map/all_to_all | solution.py:117
  17.7 5.5 %collective-permute-start = (bf16[16,256]{1,0:T(8,128)(2,1)S(1)}, bf16[16,256]{1,0:T(8,128)(2,1)S(1)}, u32[]{:S(2)}, u32[]{:S(2)}) collective-permute-start(bf16[16,256]{1,0:T(8,128)(2,1)S(1)} %convert_element_type.65), channel_id=1, source_target_pairs={{4,0},{8,4},{12,8},{16,12},{20,16},{24,20},{28,24},{5,1},{9,5},{13... | collective-permute-start | bytes 24584 | tf_op jit(solution)/shard_map/ppermute | solution.py:110
  28.5 3.9 %collective-permute-start.5 = (f32[20,64]{1,0:T(8,128)S(1)}, f32[20,64]{1,0:T(8,128)S(1)}, u32[]{:S(2)}, u32[]{:S(2)}) collective-permute-start(f32[20,64]{1,0:T(8,128)S(1)} %fusion.49), channel_id=1, source_target_pairs={{0,2},{1,3},{2,0},{3,1},{4,6},{5,7},{6,4},{7,5},{8,10},{9,11},{10,... | collective-permute-start | bytes 15368 | tf_op jit(solution)/shard_map/ppermute | solution.py:13
  30.0 3.1 %collective-permute-start.6 = (f32[20,64]{1,0:T(8,128)S(1)}, f32[20,64]{1,0:T(8,128)S(1)}, u32[]{:S(2)}, u32[]{:S(2)}) collective-permute-start(f32[20,64]{1,0:T(8,128)S(1)} %fusion.49), channel_id=1, source_target_pairs={{0,3},{1,2},{2,1},{3,0},{4,7},{5,6},{6,5},{7,4},{8,11},{9,10},{10,... | collective-permute-start | bytes 15368 | tf_op jit(solution)/shard_map/ppermute | solution.py:13
  30.0 3.1 %collective-permute-start.4 = (f32[20,64]{1,0:T(8,128)S(1)}, f32[20,64]{1,0:T(8,128)S(1)}, u32[]{:S(2)}, u32[]{:S(2)}) collective-permute-start(f32[20,64]{1,0:T(8,128)S(1)} %fusion.49), channel_id=1, source_target_pairs={{0,1},{1,0},{2,3},{3,2},{4,5},{5,4},{6,7},{7,6},{8,9},{9,8},{10,11... | collective-permute-start | bytes 15368 | tf_op jit(solution)/shard_map/ppermute | solution.py:13
  30.8 3.8 %collective-permute-start.2 = (f32[16,256]{1,0:T(8,128)S(1)}, f32[16,256]{1,0:T(8,128)S(1)}, u32[]{:S(2)}, u32[]{:S(2)}) collective-permute-start(f32[16,256]{1,0:T(8,128)S(1)} %fusion.34), channel_id=1, source_target_pairs={{0,2},{1,3},{2,0},{3,1},{4,6},{5,7},{6,4},{7,5},{8,10},{9,11},{10,... | collective-permute-start | bytes 49160 | tf_op jit(solution)/shard_map/ppermute | solution.py:13
  32.4 3.2 %collective-permute-start.3 = (f32[16,256]{1,0:T(8,128)S(1)}, f32[16,256]{1,0:T(8,128)S(1)}, u32[]{:S(2)}, u32[]{:S(2)}) collective-permute-start(f32[16,256]{1,0:T(8,128)S(1)} %fusion.34), channel_id=1, source_target_pairs={{0,3},{1,2},{2,1},{3,0},{4,7},{5,6},{6,5},{7,4},{8,11},{9,10},{10,... | collective-permute-start | bytes 49160 | tf_op jit(solution)/shard_map/ppermute | solution.py:13
  32.4 3.2 %collective-permute-start.1 = (f32[16,256]{1,0:T(8,128)S(1)}, f32[16,256]{1,0:T(8,128)S(1)}, u32[]{:S(2)}, u32[]{:S(2)}) collective-permute-start(f32[16,256]{1,0:T(8,128)S(1)} %fusion.34), channel_id=1, source_target_pairs={{0,1},{1,0},{2,3},{3,2},{4,5},{5,4},{6,7},{7,6},{8,9},{9,8},{10,11... | collective-permute-start | bytes 49160 | tf_op jit(solution)/shard_map/ppermute | solution.py:13
  48.4 10.3 %collective-permute-start.7 = (bf16[16,256]{1,0:T(8,128)(2,1)S(1)}, bf16[16,256]{1,0:T(8,128)(2,1)S(1)}, u32[]{:S(2)}, u32[]{:S(2)}) collective-permute-start(bf16[16,256]{1,0:T(8,128)(2,1)S(1)} %get-tuple-element.6), channel_id=1, source_target_pairs={{4,0},{8,4},{12,8},{16,12},{20,16},{24,20},{28,24},{5,1},{9,5},{13... | collective-permute-start | bytes 24584 | tf_op jit(solution)/shard_map/ppermute | solution.py:110
  54.8 11.5 %all-to-all-start.2 = ((f32[8,1,5376]{2,1,0:T(1,128)}), f32[8,1,5376]{2,1,0:T(1,128)S(1)}, u32[]{:S(2)}, u32[]{:S(2)}) async-start(f32[8,1,5376]{2,1,0:T(1,128)} %copy.57), calls=%async_computation.2 | async-start | bytes 344064 | tf_op jit(solution)/shard_map/all_to_all | solution.py:117
  67.4 3.8 %collective-permute-start.12 = (f32[20,64]{1,0:T(8,128)S(1)}, f32[20,64]{1,0:T(8,128)S(1)}, u32[]{:S(2)}, u32[]{:S(2)}) collective-permute-start(f32[20,64]{1,0:T(8,128)S(1)} %fusion.48), channel_id=1, source_target_pairs={{0,2},{1,3},{2,0},{3,1},{4,6},{5,7},{6,4},{7,5},{8,10},{9,11},{10,... | collective-permute-start | bytes 15368 | tf_op jit(solution)/shard_map/ppermute | solution.py:13
  68.1 3.9 %collective-permute-start.13 = (f32[20,64]{1,0:T(8,128)S(1)}, f32[20,64]{1,0:T(8,128)S(1)}, u32[]{:S(2)}, u32[]{:S(2)}) collective-permute-start(f32[20,64]{1,0:T(8,128)S(1)} %fusion.48), channel_id=1, source_target_pairs={{0,3},{1,2},{2,1},{3,0},{4,7},{5,6},{6,5},{7,4},{8,11},{9,10},{10,... | collective-permute-start | bytes 15368 | tf_op jit(solution)/shard_map/ppermute | solution.py:13
  68.1 3.9 %collective-permute-start.11 = (f32[20,64]{1,0:T(8,128)S(1)}, f32[20,64]{1,0:T(8,128)S(1)}, u32[]{:S(2)}, u32[]{:S(2)}) collective-permute-start(f32[20,64]{1,0:T(8,128)S(1)} %fusion.48), channel_id=1, source_target_pairs={{0,1},{1,0},{2,3},{3,2},{4,5},{5,4},{6,7},{7,6},{8,9},{9,8},{10,11... | collective-permute-start | bytes 15368 | tf_op jit(solution)/shard_map/ppermute | solution.py:13
  69.7 3.9 %collective-permute-start.9 = (f32[16,256]{1,0:T(8,128)S(1)}, f32[16,256]{1,0:T(8,128)S(1)}, u32[]{:S(2)}, u32[]{:S(2)}) collective-permute-start(f32[16,256]{1,0:T(8,128)S(1)} %fusion.33), channel_id=1, source_target_pairs={{0,2},{1,3},{2,0},{3,1},{4,6},{5,7},{6,4},{7,5},{8,10},{9,11},{10,... | collective-permute-start | bytes 49160 | tf_op jit(solution)/shard_map/ppermute | solution.py:13
  70.4 3.3 %collective-permute-start.10 = (f32[16,256]{1,0:T(8,128)S(1)}, f32[16,256]{1,0:T(8,128)S(1)}, u32[]{:S(2)}, u32[]{:S(2)}) collective-permute-start(f32[16,256]{1,0:T(8,128)S(1)} %fusion.33), channel_id=1, source_target_pairs={{0,3},{1,2},{2,1},{3,0},{4,7},{5,6},{6,5},{7,4},{8,11},{9,10},{10,... | collective-permute-start | bytes 49160 | tf_op jit(solution)/shard_map/ppermute | solution.py:13
  71.2 2.6 %collective-permute-start.8 = (f32[16,256]{1,0:T(8,128)S(1)}, f32[16,256]{1,0:T(8,128)S(1)}, u32[]{:S(2)}, u32[]{:S(2)}) collective-permute-start(f32[16,256]{1,0:T(8,128)S(1)} %fusion.33), channel_id=1, source_target_pairs={{0,1},{1,0},{2,3},{3,2},{4,5},{5,4},{6,7},{7,6},{8,9},{9,8},{10,11... | collective-permute-start | bytes 49160 | tf_op jit(solution)/shard_map/ppermute | solution.py:13

commit v15 on v10

--- a/solution.py
+++ b/solution.py
@@ -127,10 +127,10 @@
         ).astype(jnp.bfloat16).reshape(all_nodes, rank_width)
 
         extended = jnp.concatenate([rounded, following], axis=0)
-        near_in = jnp.where(near_valid[:, :, None], extended[near_local], bf_zero)
-        forward = jnp.einsum(
-            "bsij,bsj->bi", near_tiles, near_in, preferred_element_type=jnp.float32
-        )
+        near_in = jnp.dot(
+            near_onehot.T.astype(jnp.bfloat16), extended, preferred_element_type=jnp.float32
+        ).reshape(near_tiles.shape[0], near_tiles.shape[1], 1, leaf)
+        forward = jnp.sum(near_tiles.astype(jnp.float32) * near_in, axis=(1, 3))
         near_part = forward + landed[:box_count] + arrived
         partner_coef = jnp.dot(
             far_pick.T.astype(jnp.bfloat16), every_coef, preferred_element_type=jnp.float32

time: 82.9 us -> 82.1 us (level)
  matrix products: 18.1 us -> 11.8 us
  other arithmetic: 5.15 us -> 11.1 us
  local copies, waits for them, and re-layouts: 6.51 us -> 5.09 us
  waiting for transfers between devices: 11.9 us -> 12.9 us
    dot_general x2, matrix products: 6.73 us -> 0.38 us  [local(): jnp.dot(near_onehot.T.astype(jnp.bfloat16), extended, preferred_element_t...]
    reduce_sum x0 -> x2, other arithmetic: none -> 6.19 us  [local(): forward = jnp.sum(near_tiles.astype(jnp.float32) * near_in, axis=(1, 3))]
    gather x4 -> x0, local copies, waits for them, and re-layouts: 1.28 us -> none  [local(): near_in = jnp.where(near_valid[:, :, None], extended[near_local], bf_zero)]
  transfers between devices with their start and end apart: 10 -> 10, of which waited for: 6 -> 6; matrix products, arithmetic and copies ran while one was open for 17% -> 15% of each run, Pallas kernels for 0% -> 0%
where the time goes in v15:
time: 82.1 us; the launch traced here: 81.4 us
  blocking collectives  21.1 us (26%)
  starting transfers between devices  18.1 us (22%)
  waiting for transfers between devices  12.9 us (16%)
  matrix products  11.8 us (14%)
  other arithmetic  11.1 us (14%)
  local copies, waits for them, and re-layouts  5.09 us (6%)
  between operations  1.28 us (2%)
    all_to_all x2, blocking collectives, box_sum(): got = lax.all_to_all(sent, 'box', 0, 0, tiled=True)  21.1 us
    all_to_all x2, starting transfers between devices, local(): lax.all_to_all(jnp.concatenate([far_send.reshape(box_devices, far_size),...  11.2 us
    reduce_sum x2, other arithmetic, local(): forward = jnp.sum(near_tiles.astype(jnp.float32) * near_in, axis=(1, 3))  6.19 us
    dot_general x2, matrix products, local(): jnp.einsum('bsij,bi->bsj', near_tiles, rounded, preferred_element_type=jn...  5.66 us
    ppermute x6, waiting for transfers between devices, rep_sum(): lax.ppermute(vector, 'rep', [(i, i ^ mask) for i in range(count)])  4.77 us
    ppermute x6, starting transfers between devices, rep_sum(): lax.ppermute(vector, 'rep', [(i, i ^ mask) for i in range(count)])  4.35 us
    all_to_all x2, waiting for transfers between devices, local(): lax.all_to_all(jnp.concatenate([far_send.reshape(box_devices, far_size),...  4.25 us
    ppermute x2, waiting for transfers between devices, local(): lax.ppermute(rounded, 'box', [(i, i - 1) for i in range(1, box_devices)])  3.85 us
  transfers between devices with their start and end apart: 10, of which 6 were waited for; matrix products, arithmetic and copies ran while one was open for 15% of the time, Pallas kernels for 0%

profile of v15, /device:TPU:0, one launch (start us, length us, event | category | flops | bytes accessed | tf_op | source)
XLA Modules:
  0.0 81.4 jit_solution(2362061180040584598)
XLA Ops:
  0.7 0.8 %convert_bitcast_fusion.3 = bf16[16,256,1,1]{1,0,2,3:T(8,128)(2,1)S(1)} fusion(f32[16,256]{1,0:T(8,128)} %param.9), kind=kLoop, calls=%fused_computation.177 | loop fusion | flops 4096 | bytes 24576 | tf_op jit(solution)/shard_map/convert_element_type | solution.py:87
  1.5 0.7 convert_bitcast_fusion.2
  2.2 1.3 %fusion.45 = f32[16,1,64]{2,1,0:T(1,128)S(1)} fusion(bf16[16,64,256]{2,1,0:T(8,128)(2,1)} %param.13, bf16[16,256,1]{1,0,2:T(8,128)(2,1)S(1)} %convert_bitcast_fusion.2), kind=kOutput, calls=%fused_computation.78 | convolution fusion | flops 524288 | bytes 536576 | tf_op jit(solution)/shard_map/brl,bl->br/dot_general | solution.py:94
  3.6 0.7 broadcast_select_fusion.4
  4.4 2.8 %fusion.47 = f32[16,1,2,256]{3,1,2,0:T(1,128)S(1)} fusion(bf16[16,2,256,256]{3,2,1,0:T(8,128)(2,1)} %param.11, bf16[16,256,1,1]{1,0,2,3:T(8,128)(2,1)S(1)} %convert_bitcast_fusion.3), kind=kOutput, calls=%fused_computation.80 | convolution fusion | flops 4194304 | bytes 4235264 | tf_op jit(solution)/shard_map/bsij,bi->bsj/dot_general | solution.py:88
  9.5 0.8 all_to_all.24
  10.2 7.3 %all-to-all-start = ((f32[8,1,5376]{2,1,0:T(1,128)}), f32[8,1,5376]{2,1,0:T(1,128)S(1)}, u32[]{:S(2)}, u32[]{:S(2)}) async-start(f32[8,1,5376]{2,1,0:T(1,128)} %all_to_all.24), calls=%async_computation | async-start | bytes 344064 | tf_op jit(solution)/shard_map/all_to_all | solution.py:117
  17.5 1.3 %collective-permute-start = (bf16[16,256]{1,0:T(8,128)(2,1)S(1)}, bf16[16,256]{1,0:T(8,128)(2,1)S(1)}, u32[]{:S(2)}, u32[]{:S(2)}) collective-permute-start(bf16[16,256]{1,0:T(8,128)(2,1)S(1)} %convert_element_type.81), channel_id=1, source_target_pairs={{4,0},{8,4},{12,8},{16,12},{20,16},{24,20},{28,24},{5,1},{9,5},{13... | collective-permute-start | bytes 24584 | tf_op jit(solution)/shard_map/ppermute | solution.py:110
  19.2 3.9 %collective-permute-done = bf16[16,256]{1,0:T(8,128)(2,1)S(1)} collective-permute-done((bf16[16,256]{1,0:T(8,128)(2,1)S(1)}, bf16[16,256]{1,0:T(8,128)(2,1)S(1)}, u32[]{:S(2)}, u32[]{:S(2)}) %collective-permute-start) | collective-permute-done | bytes 8224 | tf_op jit(solution)/shard_map/ppermute | solution.py:110
  23.3 3.1 %fusion = f32[16,256]{1,0:T(8,128)S(1)} fusion(bf16[16,2,256,256]{3,2,1,0:T(8,128)(2,1)} %param.11, f32[16,2,256]{2,1,0:T(2,128)S(1)} %mul.118), kind=kLoop, calls=%fused_computation.2 | loop fusion | flops 6287360 | bytes 4243456 | tf_op jit(solution)/shard_map/reduce_sum | solution.py:133
  27.8 1.5 %collective-permute-start.2 = (f32[5376]{0:T(1024)S(1)}, f32[5376]{0:T(1024)S(1)}, u32[]{:S(2)}, u32[]{:S(2)}) collective-permute-start(f32[5376]{0:T(1024)S(1)} %constant_dynamic-update-slice_fusion), channel_id=1, source_target_pairs={{0,2},{1,3},{2,0},{3,1},{4,6},{5,7},{6,4},{7,5},{8,10},{9,11},{10,... | collective-permute-start | bytes 64520 | tf_op jit(solution)/shard_map/ppermute | solution.py:13
  30.0 1.7 %collective-permute-done.2 = f32[5376]{0:T(1024)S(1)} collective-permute-done((f32[5376]{0:T(1024)S(1)}, f32[5376]{0:T(1024)S(1)}, u32[]{:S(2)}, u32[]{:S(2)}) %collective-permute-start.2) | collective-permute-done | bytes 21536 | tf_op jit(solution)/shard_map/ppermute | solution.py:13
  31.6 0.9 %collective-permute-done.3 = f32[5376]{0:T(1024)S(1)} collective-permute-done((f32[5376]{0:T(1024)S(1)}, f32[5376]{0:T(1024)S(1)}, u32[]{:S(2)}, u32[]{:S(2)}) %collective-permute-start.3) | collective-permute-done | bytes 21536 | tf_op jit(solution)/shard_map/ppermute | solution.py:13
  33.4 12.2 %all_to_all.36 = f32[8,1,4]{2,1,0:T(1,128)S(1)} all-to-all(f32[8,1,4]{2,1,0:T(1,128)S(1)} %broadcast_in_dim.296), channel_id=1, replica_groups=mesh['box'=8,'rep'=4] {'box'}, dimensions={0} | all-to-all | bytes 256 | tf_op jit(solution)/shard_map/all_to_all | solution.py:36
  46.1 1.3 %collective-permute-start.4 = (bf16[16,256]{1,0:T(8,128)(2,1)S(1)}, bf16[16,256]{1,0:T(8,128)(2,1)S(1)}, u32[]{:S(2)}, u32[]{:S(2)}) collective-permute-start(bf16[16,256]{1,0:T(8,128)(2,1)S(1)} %fusion.87), channel_id=1, source_target_pairs={{4,0},{8,4},{12,8},{16,12},{20,16},{24,20},{28,24},{5,1},{9,5},{13... | collective-permute-start | bytes 24584 | tf_op jit(solution)/shard_map/ppermute | solution.py:110
  47.4 2.8 %fusion.43 = f32[16,1,2,256]{3,1,2,0:T(1,128)S(1)} fusion(bf16[16,2,256,256]{3,2,1,0:T(8,128)(2,1)} %param.11, bf16[16,256,1,1]{1,0,2,3:T(8,128)(2,1)S(1)} %bitcast.141), kind=kOutput, calls=%fused_computation.76 | convolution fusion | flops 4194304 | bytes 4235264 | tf_op jit(solution)/shard_map/bsij,bi->bsj/dot_general | solution.py:88
  51.6 0.8 %copy.49 = f32[8,1,5376]{2,1,0:T(1,128)} copy(f32[8,1,5376]{2,0,1:T(8,128)S(1)} %maximum_bitcast_fusion) | data formatting | bytes 344064 | tf_op jit(solution)/shard_map/all_to_all | solution.py:117
  52.4 3.9 %all-to-all-start.2 = ((f32[8,1,5376]{2,1,0:T(1,128)}), f32[8,1,5376]{2,1,0:T(1,128)S(1)}, u32[]{:S(2)}, u32[]{:S(2)}) async-start(f32[8,1,5376]{2,1,0:T(1,128)} %copy.49), calls=%async_computation.2 | async-start | bytes 344064 | tf_op jit(solution)/shard_map/all_to_all | solution.py:117
  56.6 3.1 %fusion.1 = f32[16,256]{1,0:T(8,128)S(1)} fusion(bf16[16,2,256,256]{3,2,1,0:T(8,128)(2,1)} %param.11, f32[16,2,256]{2,1,0:T(2,128)S(1)} %mul.140), kind=kLoop, calls=%fused_computation.3 | loop fusion | flops 6287360 | bytes 4243456 | tf_op jit(solution)/shard_map/reduce_sum | solution.py:133
  59.7 4.2 %all-to-all-done.2 = f32[8,1,5376]{2,1,0:T(1,128)S(1)} async-done(((f32[8,1,5376]{2,1,0:T(1,128)}), f32[8,1,5376]{2,1,0:T(1,128)S(1)}, u32[]{:S(2)}, u32[]{:S(2)}) %all-to-all-start.2) | async-done | bytes 172064 | tf_op jit(solution)/shard_map/all_to_all | solution.py:117
  65.3 0.8 %collective-permute-start.6 = (f32[5376]{0:T(1024)S(1)}, f32[5376]{0:T(1024)S(1)}, u32[]{:S(2)}, u32[]{:S(2)}) collective-permute-start(f32[5376]{0:T(1024)S(1)} %constant_dynamic-update-slice_fusion.1), channel_id=1, source_target_pairs={{0,2},{1,3},{2,0},{3,1},{4,6},{5,7},{6,4},{7,5},{8,10},{9,11},{10,... | collective-permute-start | bytes 64520 | tf_op jit(solution)/shard_map/ppermute | solution.py:13
  66.2 1.3 %collective-permute-start.5 = (f32[5376]{0:T(1024)S(1)}, f32[5376]{0:T(1024)S(1)}, u32[]{:S(2)}, u32[]{:S(2)}) collective-permute-start(f32[5376]{0:T(1024)S(1)} %constant_dynamic-update-slice_fusion.1), channel_id=1, source_target_pairs={{0,1},{1,0},{2,3},{3,2},{4,5},{5,4},{6,7},{7,6},{8,9},{9,8},{10,11... | collective-permute-start | bytes 64520 | tf_op jit(solution)/shard_map/ppermute | solution.py:13
  67.5 1.7 %collective-permute-done.6 = f32[5376]{0:T(1024)S(1)} collective-permute-done((f32[5376]{0:T(1024)S(1)}, f32[5376]{0:T(1024)S(1)}, u32[]{:S(2)}, u32[]{:S(2)}) %collective-permute-start.6) | collective-permute-done | bytes 21536 | tf_op jit(solution)/shard_map/ppermute | solution.py:13
  71.7 8.8 %all_to_all.37 = f32[8,1,1]{2,1,0:T(1,128)S(1)} all-to-all(f32[8,1,1]{2,1,0:T(1,128)S(1)} %broadcast_in_dim.307), channel_id=1, replica_groups=mesh['box'=8,'rep'=4] {'box'}, dimensions={0} | all-to-all | bytes 64 | tf_op jit(solution)/shard_map/all_to_all | solution.py:36
  (154 shorter events, 12.2 us)
Async XLA Ops:
  0.6 8.0 %copy-start = (bf16[20,4,64,64]{3,2,1,0:T(8,128)(2,1)S(1)}, bf16[20,4,64,64]{3,2,1,0:T(8,128)(2,1)}, u32[]{:S(2)}) copy-start(bf16[20,4,64,64]{3,2,1,0:T(8,128)(2,1)} %param.16) | copy-start | bytes 1966084
  0.6 6.6 %copy-start.4 = (s32[16,2]{0,1:T(2,128)S(1)}, s32[16,2]{0,1:T(2,128)}, u32[]{:S(2)}) copy-start(s32[16,2]{0,1:T(2,128)} %param.12) | copy-start | bytes 388
  0.7 7.6 %copy-start.6 = (bf16[16,64,64]{2,1,0:T(8,128)(2,1)S(1)}, bf16[16,64,64]{2,1,0:T(8,128)(2,1)}, u32[]{:S(2)}) copy-start(bf16[16,64,64]{2,1,0:T(8,128)(2,1)} %param.14) | copy-start | bytes 393220
  0.7 7.8 %copy-start.5 = (s32[16]{0:T(128)S(1)}, s32[16]{0:T(128)}, u32[]{:S(2)}) copy-start(s32[16]{0:T(128)} %param.15) | copy-start | bytes 196
  2.2 15.3 %copy-start.2 = (f32[16,256]{1,0:T(8,128)S(1)}, f32[16,256]{1,0:T(8,128)}, u32[]{:S(2)}) copy-start(f32[16,256]{1,0:T(8,128)} %param.9) | copy-start | bytes 49156
  9.4 23.6 %copy-start.1 = (bf16[16,64,256]{2,1,0:T(8,128)(2,1)S(1)}, bf16[16,64,256]{2,1,0:T(8,128)(2,1)}, u32[]{:S(2)}) copy-start(bf16[16,64,256]{2,1,0:T(8,128)(2,1)} %param.13) | copy-start | bytes 1572868
  10.2 16.2 %all-to-all-start = ((f32[8,1,5376]{2,1,0:T(1,128)}), f32[8,1,5376]{2,1,0:T(1,128)S(1)}, u32[]{:S(2)}, u32[]{:S(2)}) async-start(f32[8,1,5376]{2,1,0:T(1,128)} %all_to_all.24), calls=%async_computation | async-start | bytes 344064 | tf_op jit(solution)/shard_map/all_to_all | solution.py:117
  17.5 15.8 %copy-start.3 = (f32[16,256]{1,0:T(8,128)S(1)}, f32[16,256]{1,0:T(8,128)}, u32[]{:S(2)}) copy-start(f32[16,256]{1,0:T(8,128)} %param.10) | copy-start | bytes 49156
  17.5 5.5 %collective-permute-start = (bf16[16,256]{1,0:T(8,128)(2,1)S(1)}, bf16[16,256]{1,0:T(8,128)(2,1)S(1)}, u32[]{:S(2)}, u32[]{:S(2)}) collective-permute-start(bf16[16,256]{1,0:T(8,128)(2,1)S(1)} %convert_element_type.81), channel_id=1, source_target_pairs={{4,0},{8,4},{12,8},{16,12},{20,16},{24,20},{28,24},{5,1},{9,5},{13... | collective-permute-start | bytes 24584 | tf_op jit(solution)/shard_map/ppermute | solution.py:110
  27.8 3.9 %collective-permute-start.2 = (f32[5376]{0:T(1024)S(1)}, f32[5376]{0:T(1024)S(1)}, u32[]{:S(2)}, u32[]{:S(2)}) collective-permute-start(f32[5376]{0:T(1024)S(1)} %constant_dynamic-update-slice_fusion), channel_id=1, source_target_pairs={{0,2},{1,3},{2,0},{3,1},{4,6},{5,7},{6,4},{7,5},{8,10},{9,11},{10,... | collective-permute-start | bytes 64520 | tf_op jit(solution)/shard_map/ppermute | solution.py:13
  29.3 3.3 %collective-permute-start.3 = (f32[5376]{0:T(1024)S(1)}, f32[5376]{0:T(1024)S(1)}, u32[]{:S(2)}, u32[]{:S(2)}) collective-permute-start(f32[5376]{0:T(1024)S(1)} %constant_dynamic-update-slice_fusion), channel_id=1, source_target_pairs={{0,3},{1,2},{2,1},{3,0},{4,7},{5,6},{6,5},{7,4},{8,11},{9,10},{10,... | collective-permute-start | bytes 64520 | tf_op jit(solution)/shard_map/ppermute | solution.py:13
  29.3 3.3 %collective-permute-start.1 = (f32[5376]{0:T(1024)S(1)}, f32[5376]{0:T(1024)S(1)}, u32[]{:S(2)}, u32[]{:S(2)}) collective-permute-start(f32[5376]{0:T(1024)S(1)} %constant_dynamic-update-slice_fusion), channel_id=1, source_target_pairs={{0,1},{1,0},{2,3},{3,2},{4,5},{5,4},{6,7},{7,6},{8,9},{9,8},{10,11... | collective-permute-start | bytes 64520 | tf_op jit(solution)/shard_map/ppermute | solution.py:13
  46.1 10.3 %collective-permute-start.4 = (bf16[16,256]{1,0:T(8,128)(2,1)S(1)}, bf16[16,256]{1,0:T(8,128)(2,1)S(1)}, u32[]{:S(2)}, u32[]{:S(2)}) collective-permute-start(bf16[16,256]{1,0:T(8,128)(2,1)S(1)} %fusion.87), channel_id=1, source_target_pairs={{4,0},{8,4},{12,8},{16,12},{20,16},{24,20},{28,24},{5,1},{9,5},{13... | collective-permute-start | bytes 24584 | tf_op jit(solution)/shard_map/ppermute | solution.py:110
  52.4 11.5 %all-to-all-start.2 = ((f32[8,1,5376]{2,1,0:T(1,128)}), f32[8,1,5376]{2,1,0:T(1,128)S(1)}, u32[]{:S(2)}, u32[]{:S(2)}) async-start(f32[8,1,5376]{2,1,0:T(1,128)} %copy.49), calls=%async_computation.2 | async-start | bytes 344064 | tf_op jit(solution)/shard_map/all_to_all | solution.py:117
  65.3 3.9 %collective-permute-start.6 = (f32[5376]{0:T(1024)S(1)}, f32[5376]{0:T(1024)S(1)}, u32[]{:S(2)}, u32[]{:S(2)}) collective-permute-start(f32[5376]{0:T(1024)S(1)} %constant_dynamic-update-slice_fusion.1), channel_id=1, source_target_pairs={{0,2},{1,3},{2,0},{3,1},{4,6},{5,7},{6,4},{7,5},{8,10},{9,11},{10,... | collective-permute-start | bytes 64520 | tf_op jit(solution)/shard_map/ppermute | solution.py:13
  66.2 3.5 %collective-permute-start.7 = (f32[5376]{0:T(1024)S(1)}, f32[5376]{0:T(1024)S(1)}, u32[]{:S(2)}, u32[]{:S(2)}) collective-permute-start(f32[5376]{0:T(1024)S(1)} %constant_dynamic-update-slice_fusion.1), channel_id=1, source_target_pairs={{0,3},{1,2},{2,1},{3,0},{4,7},{5,6},{6,5},{7,4},{8,11},{9,10},{10,... | collective-permute-start | bytes 64520 | tf_op jit(solution)/shard_map/ppermute | solution.py:13
  66.2 3.5 %collective-permute-start.5 = (f32[5376]{0:T(1024)S(1)}, f32[5376]{0:T(1024)S(1)}, u32[]{:S(2)}, u32[]{:S(2)}) collective-permute-start(f32[5376]{0:T(1024)S(1)} %constant_dynamic-update-slice_fusion.1), channel_id=1, source_target_pairs={{0,1},{1,0},{2,3},{3,2},{4,5},{5,4},{6,7},{7,6},{8,9},{9,8},{10,11... | collective-permute-start | bytes 64520 | tf_op jit(solution)/shard_map/ppermute | solution.py:13

commit v16 on v15

--- a/solution.py
+++ b/solution.py
@@ -91,8 +91,8 @@
         landed = jnp.dot(
             near_onehot, mirrored.reshape(-1, mirrored.shape[2]), precision=lax.Precision.HIGHEST
         )
-        leaf_coef = jnp.einsum(
-            "brl,bl->br", leaf_bases, rounded, preferred_element_type=jnp.float32
+        leaf_coef = jnp.sum(
+            leaf_bases.astype(jnp.float32) * rounded.astype(jnp.float32)[:, None, :], axis=2
         ).astype(jnp.bfloat16)
         upward = jnp.einsum("brq,br->bq", transfer, leaf_coef, preferred_element_type=jnp.float32)
         group_coef = jnp.dot(parent_onehot, upward, precision=lax.Precision.HIGHEST).astype(

time: 82.1 us -> 78 us (0.950)
  blocking collectives: 21.1 us -> 17.8 us
  matrix products: 11.8 us -> 10.3 us
  starting transfers between devices: 18.1 us -> 19.2 us
    all_to_all x2, waiting for transfers between devices: 4.25 us -> 8.12 us  [local(): lax.all_to_all(jnp.concatenate([far_send.reshape(box_devices, far_size),...]
    ppermute x2, waiting for transfers between devices: 3.85 us -> 0.01 us  [local(): lax.ppermute(rounded, 'box', [(i, i - 1) for i in range(1, box_devices)])]
    all_to_all x2, blocking collectives: 21.1 us -> 17.8 us  [box_sum(): got = lax.all_to_all(sent, 'box', 0, 0, tiled=True)]
    dot_general x2 -> x0, matrix products: 1.52 us -> none  [local(): jnp.einsum('brl,bl->br', leaf_bases, rounded, preferred_element_type=jnp....]
    all_to_all x2, starting transfers between devices: 11.2 us -> 12.3 us  [local(): lax.all_to_all(jnp.concatenate([far_send.reshape(box_devices, far_size),...]
  transfers between devices with their start and end apart: 10 -> 10, of which waited for: 6 -> 6; matrix products, arithmetic and copies ran while one was open for 15% -> 23% of each run, Pallas kernels for 0% -> 0%
where the time goes in v16:
time: 78 us; the launch traced here: 77.4 us
  starting transfers between devices  19.2 us (25%)
  blocking collectives  17.8 us (23%)
  waiting for transfers between devices  12.9 us (17%)
  other arithmetic  10.9 us (14%)
  matrix products  10.3 us (13%)
  local copies, waits for them, and re-layouts  5.11 us (7%)
  between operations  1.29 us (2%)
    all_to_all x2, blocking collectives, box_sum(): got = lax.all_to_all(sent, 'box', 0, 0, tiled=True)  17.8 us
    all_to_all x2, starting transfers between devices, local(): lax.all_to_all(jnp.concatenate([far_send.reshape(box_devices, far_size),...  12.3 us
    all_to_all x2, waiting for transfers between devices, local(): lax.all_to_all(jnp.concatenate([far_send.reshape(box_devices, far_size),...  8.12 us
    reduce_sum x2, other arithmetic, local(): forward = jnp.sum(near_tiles.astype(jnp.float32) * near_in, axis=(1, 3))  6.19 us
    dot_general x2, matrix products, local(): jnp.einsum('bsij,bi->bsj', near_tiles, rounded, preferred_element_type=jn...  5.66 us
    ppermute x6, waiting for transfers between devices, rep_sum(): lax.ppermute(vector, 'rep', [(i, i ^ mask) for i in range(count)])  4.77 us
    ppermute x6, starting transfers between devices, rep_sum(): lax.ppermute(vector, 'rep', [(i, i ^ mask) for i in range(count)])  4.35 us
    ppermute x2, starting transfers between devices, local(): lax.ppermute(rounded, 'box', [(i, i - 1) for i in range(1, box_devices)])  2.57 us
  transfers between devices with their start and end apart: 10, of which 6 were waited for; matrix products, arithmetic and copies ran while one was open for 23% of the time, Pallas kernels for 0%

profile of v16, /device:TPU:0, one launch (start us, length us, event | category | flops | bytes accessed | tf_op | source)
XLA Modules:
  0.0 77.4 jit_solution(18172313510025028992)
XLA Ops:
  0.7 0.9 %fusion.99 = (f32[16,256]{1,0:T(8,128)S(1)}, bf16[16,256]{1,0:T(8,128)(2,1)S(1)}) fusion(f32[16,256]{1,0:T(8,128)} %param.9), kind=kLoop, calls=%fused_computation.173 | loop fusion | flops 8192 | bytes 40960 | tf_op jit(solution)/shard_map/convert_element_type | solution.py:95
  1.6 1.3 %collective-permute-start = (bf16[16,256]{1,0:T(8,128)(2,1)S(1)}, bf16[16,256]{1,0:T(8,128)(2,1)S(1)}, u32[]{:S(2)}, u32[]{:S(2)}) collective-permute-start(bf16[16,256]{1,0:T(8,128)(2,1)S(1)} %get-tuple-element.18), channel_id=1, source_target_pairs={{4,0},{8,4},{12,8},{16,12},{20,16},{24,20},{28,24},{5,1},{9,5},{13... | collective-permute-start | bytes 24584 | tf_op jit(solution)/shard_map/ppermute | solution.py:110
  2.9 0.7 broadcast_select_fusion.4
  3.7 2.8 %fusion.45 = f32[16,1,2,256]{3,1,2,0:T(1,128)S(1)} fusion(bf16[16,2,256,256]{3,2,1,0:T(8,128)(2,1)} %param.11, bf16[16,256,1,1]{1,0,2,3:T(8,128)(2,1)S(1)} %bitcast.128), kind=kOutput, calls=%fused_computation.80 | convolution fusion | flops 4194304 | bytes 4235264 | tf_op jit(solution)/shard_map/bsij,bi->bsj/dot_general | solution.py:88
  9.0 0.8 %all_to_all.24 = f32[8,1,5376]{2,1,0:T(1,128)} reshape(f32[8,5376]{1,0:T(8,128)S(1)} %pad_maximum_fusion) | data formatting | bytes 344064 | tf_op jit(solution)/shard_map/all_to_all | solution.py:117
  9.8 8.4 %all-to-all-start = ((f32[8,1,5376]{2,1,0:T(1,128)}), f32[8,1,5376]{2,1,0:T(1,128)S(1)}, u32[]{:S(2)}, u32[]{:S(2)}) async-start(f32[8,1,5376]{2,1,0:T(1,128)} %all_to_all.24), calls=%async_computation | async-start | bytes 344064 | tf_op jit(solution)/shard_map/all_to_all | solution.py:117
  18.8 3.1 %fusion = f32[16,256]{1,0:T(8,128)S(1)} fusion(bf16[16,2,256,256]{3,2,1,0:T(8,128)(2,1)} %param.11, f32[16,2,256]{2,1,0:T(2,128)S(1)} %mul.134), kind=kLoop, calls=%fused_computation.2 | loop fusion | flops 6287360 | bytes 4243456 | tf_op jit(solution)/shard_map/reduce_sum | solution.py:133
  21.9 3.9 %all-to-all-done = f32[8,1,5376]{2,1,0:T(1,128)S(1)} async-done(((f32[8,1,5376]{2,1,0:T(1,128)}), f32[8,1,5376]{2,1,0:T(1,128)S(1)}, u32[]{:S(2)}, u32[]{:S(2)}) %all-to-all-start) | async-done | bytes 172064 | tf_op jit(solution)/shard_map/all_to_all | solution.py:117
  27.2 1.5 %collective-permute-start.2 = (f32[5376]{0:T(1024)S(1)}, f32[5376]{0:T(1024)S(1)}, u32[]{:S(2)}, u32[]{:S(2)}) collective-permute-start(f32[5376]{0:T(1024)S(1)} %constant_dynamic-update-slice_fusion), channel_id=1, source_target_pairs={{0,2},{1,3},{2,0},{3,1},{4,6},{5,7},{6,4},{7,5},{8,10},{9,11},{10,... | collective-permute-start | bytes 64520 | tf_op jit(solution)/shard_map/ppermute | solution.py:13
  28.7 0.6 collective-permute-start.1
  29.3 1.7 %collective-permute-done.2 = f32[5376]{0:T(1024)S(1)} collective-permute-done((f32[5376]{0:T(1024)S(1)}, f32[5376]{0:T(1024)S(1)}, u32[]{:S(2)}, u32[]{:S(2)}) %collective-permute-start.2) | collective-permute-done | bytes 21536 | tf_op jit(solution)/shard_map/ppermute | solution.py:13
  31.0 0.9 %collective-permute-done.3 = f32[5376]{0:T(1024)S(1)} collective-permute-done((f32[5376]{0:T(1024)S(1)}, f32[5376]{0:T(1024)S(1)}, u32[]{:S(2)}, u32[]{:S(2)}) %collective-permute-start.3) | collective-permute-done | bytes 21536 | tf_op jit(solution)/shard_map/ppermute | solution.py:13
  32.8 8.9 %all_to_all.36 = f32[8,1,4]{2,1,0:T(1,128)S(1)} all-to-all(f32[8,1,4]{2,1,0:T(1,128)S(1)} %broadcast_in_dim.298), channel_id=1, replica_groups=mesh['box'=8,'rep'=4] {'box'}, dimensions={0} | all-to-all | bytes 256 | tf_op jit(solution)/shard_map/all_to_all | solution.py:36
  41.9 1.3 %collective-permute-start.4 = (bf16[16,256]{1,0:T(8,128)(2,1)S(1)}, bf16[16,256]{1,0:T(8,128)(2,1)S(1)}, u32[]{:S(2)}, u32[]{:S(2)}) collective-permute-start(bf16[16,256]{1,0:T(8,128)(2,1)S(1)} %get-tuple-element.5), channel_id=1, source_target_pairs={{4,0},{8,4},{12,8},{16,12},{20,16},{24,20},{28,24},{5,1},{9,5},{13... | collective-permute-start | bytes 24584 | tf_op jit(solution)/shard_map/ppermute | solution.py:110
  43.2 2.8 %fusion.43 = f32[16,1,2,256]{3,1,2,0:T(1,128)S(1)} fusion(bf16[16,2,256,256]{3,2,1,0:T(8,128)(2,1)} %param.11, bf16[16,256,1,1]{1,0,2,3:T(8,128)(2,1)S(1)} %bitcast.129), kind=kOutput, calls=%fused_computation.78 | convolution fusion | flops 4194304 | bytes 4235264 | tf_op jit(solution)/shard_map/bsij,bi->bsj/dot_general | solution.py:88
  47.6 0.8 %copy.49 = f32[8,1,5376]{2,1,0:T(1,128)} copy(f32[8,1,5376]{2,0,1:T(8,128)S(1)} %maximum_bitcast_fusion) | data formatting | bytes 344064 | tf_op jit(solution)/shard_map/all_to_all | solution.py:117
  48.5 3.9 %all-to-all-start.2 = ((f32[8,1,5376]{2,1,0:T(1,128)}), f32[8,1,5376]{2,1,0:T(1,128)S(1)}, u32[]{:S(2)}, u32[]{:S(2)}) async-start(f32[8,1,5376]{2,1,0:T(1,128)} %copy.49), calls=%async_computation.2 | async-start | bytes 344064 | tf_op jit(solution)/shard_map/all_to_all | solution.py:117
  52.7 3.1 %fusion.1 = f32[16,256]{1,0:T(8,128)S(1)} fusion(bf16[16,2,256,256]{3,2,1,0:T(8,128)(2,1)} %param.11, f32[16,2,256]{2,1,0:T(2,128)S(1)} %mul.158), kind=kLoop, calls=%fused_computation.3 | loop fusion | flops 6287360 | bytes 4243456 | tf_op jit(solution)/shard_map/reduce_sum | solution.py:133
  55.8 4.2 %all-to-all-done.2 = f32[8,1,5376]{2,1,0:T(1,128)S(1)} async-done(((f32[8,1,5376]{2,1,0:T(1,128)}), f32[8,1,5376]{2,1,0:T(1,128)S(1)}, u32[]{:S(2)}, u32[]{:S(2)}) %all-to-all-start.2) | async-done | bytes 172064 | tf_op jit(solution)/shard_map/all_to_all | solution.py:117
  61.4 0.8 %collective-permute-start.6 = (f32[5376]{0:T(1024)S(1)}, f32[5376]{0:T(1024)S(1)}, u32[]{:S(2)}, u32[]{:S(2)}) collective-permute-start(f32[5376]{0:T(1024)S(1)} %constant_dynamic-update-slice_fusion.1), channel_id=1, source_target_pairs={{0,2},{1,3},{2,0},{3,1},{4,6},{5,7},{6,4},{7,5},{8,10},{9,11},{10,... | collective-permute-start | bytes 64520 | tf_op jit(solution)/shard_map/ppermute | solution.py:13
  62.2 1.3 %collective-permute-start.5 = (f32[5376]{0:T(1024)S(1)}, f32[5376]{0:T(1024)S(1)}, u32[]{:S(2)}, u32[]{:S(2)}) collective-permute-start(f32[5376]{0:T(1024)S(1)} %constant_dynamic-update-slice_fusion.1), channel_id=1, source_target_pairs={{0,1},{1,0},{2,3},{3,2},{4,5},{5,4},{6,7},{7,6},{8,9},{9,8},{10,11... | collective-permute-start | bytes 64520 | tf_op jit(solution)/shard_map/ppermute | solution.py:13
  63.5 1.7 %collective-permute-done.6 = f32[5376]{0:T(1024)S(1)} collective-permute-done((f32[5376]{0:T(1024)S(1)}, f32[5376]{0:T(1024)S(1)}, u32[]{:S(2)}, u32[]{:S(2)}) %collective-permute-start.6) | collective-permute-done | bytes 21536 | tf_op jit(solution)/shard_map/ppermute | solution.py:13
  67.0 0.6 broadcast_in_dim.309
  67.7 8.8 %all_to_all.37 = f32[8,1,1]{2,1,0:T(1,128)S(1)} all-to-all(f32[8,1,1]{2,1,0:T(1,128)S(1)} %broadcast_in_dim.309), channel_id=1, replica_groups=mesh['box'=8,'rep'=4] {'box'}, dimensions={0} | all-to-all | bytes 64 | tf_op jit(solution)/shard_map/all_to_all | solution.py:36
  (148 shorter events, 11.0 us)
Async XLA Ops:
  0.6 7.5 %copy-start = (bf16[20,4,64,64]{3,2,1,0:T(8,128)(2,1)S(1)}, bf16[20,4,64,64]{3,2,1,0:T(8,128)(2,1)}, u32[]{:S(2)}) copy-start(bf16[20,4,64,64]{3,2,1,0:T(8,128)(2,1)} %param.16) | copy-start | bytes 1966084
  0.6 5.9 %copy-start.4 = (s32[16,2]{0,1:T(2,128)S(1)}, s32[16,2]{0,1:T(2,128)}, u32[]{:S(2)}) copy-start(s32[16,2]{0,1:T(2,128)} %param.12) | copy-start | bytes 388
  0.7 6.5 %copy-start.1 = (bf16[16,64,256]{2,1,0:T(8,128)(2,1)S(1)}, bf16[16,64,256]{2,1,0:T(8,128)(2,1)}, u32[]{:S(2)}) copy-start(bf16[16,64,256]{2,1,0:T(8,128)(2,1)} %param.13) | copy-start | bytes 1572868
  0.7 6.8 %copy-start.6 = (bf16[16,64,64]{2,1,0:T(8,128)(2,1)S(1)}, bf16[16,64,64]{2,1,0:T(8,128)(2,1)}, u32[]{:S(2)}) copy-start(bf16[16,64,64]{2,1,0:T(8,128)(2,1)} %param.14) | copy-start | bytes 393220
  0.7 6.9 %copy-start.5 = (s32[16]{0:T(128)S(1)}, s32[16]{0:T(128)}, u32[]{:S(2)}) copy-start(s32[16]{0:T(128)} %param.15) | copy-start | bytes 196
  1.6 17.0 %collective-permute-start = (bf16[16,256]{1,0:T(8,128)(2,1)S(1)}, bf16[16,256]{1,0:T(8,128)(2,1)S(1)}, u32[]{:S(2)}, u32[]{:S(2)}) collective-permute-start(bf16[16,256]{1,0:T(8,128)(2,1)S(1)} %get-tuple-element.18), channel_id=1, source_target_pairs={{4,0},{8,4},{12,8},{16,12},{20,16},{24,20},{28,24},{5,1},{9,5},{13... | collective-permute-start | bytes 24584 | tf_op jit(solution)/shard_map/ppermute | solution.py:110
  9.8 16.0 %all-to-all-start = ((f32[8,1,5376]{2,1,0:T(1,128)}), f32[8,1,5376]{2,1,0:T(1,128)S(1)}, u32[]{:S(2)}, u32[]{:S(2)}) async-start(f32[8,1,5376]{2,1,0:T(1,128)} %all_to_all.24), calls=%async_computation | async-start | bytes 344064 | tf_op jit(solution)/shard_map/all_to_all | solution.py:117
  18.2 14.5 %copy-start.2 = (f32[16,256]{1,0:T(8,128)S(1)}, f32[16,256]{1,0:T(8,128)}, u32[]{:S(2)}) copy-start(f32[16,256]{1,0:T(8,128)} %param.9) | copy-start | bytes 49156
  18.2 14.5 %copy-start.3 = (f32[16,256]{1,0:T(8,128)S(1)}, f32[16,256]{1,0:T(8,128)}, u32[]{:S(2)}) copy-start(f32[16,256]{1,0:T(8,128)} %param.10) | copy-start | bytes 49156
  27.2 3.9 %collective-permute-start.2 = (f32[5376]{0:T(1024)S(1)}, f32[5376]{0:T(1024)S(1)}, u32[]{:S(2)}, u32[]{:S(2)}) collective-permute-start(f32[5376]{0:T(1024)S(1)} %constant_dynamic-update-slice_fusion), channel_id=1, source_target_pairs={{0,2},{1,3},{2,0},{3,1},{4,6},{5,7},{6,4},{7,5},{8,10},{9,11},{10,... | collective-permute-start | bytes 64520 | tf_op jit(solution)/shard_map/ppermute | solution.py:13
  28.7 3.3 %collective-permute-start.3 = (f32[5376]{0:T(1024)S(1)}, f32[5376]{0:T(1024)S(1)}, u32[]{:S(2)}, u32[]{:S(2)}) collective-permute-start(f32[5376]{0:T(1024)S(1)} %constant_dynamic-update-slice_fusion), channel_id=1, source_target_pairs={{0,3},{1,2},{2,1},{3,0},{4,7},{5,6},{6,5},{7,4},{8,11},{9,10},{10,... | collective-permute-start | bytes 64520 | tf_op jit(solution)/shard_map/ppermute | solution.py:13
  28.7 3.3 %collective-permute-start.1 = (f32[5376]{0:T(1024)S(1)}, f32[5376]{0:T(1024)S(1)}, u32[]{:S(2)}, u32[]{:S(2)}) collective-permute-start(f32[5376]{0:T(1024)S(1)} %constant_dynamic-update-slice_fusion), channel_id=1, source_target_pairs={{0,1},{1,0},{2,3},{3,2},{4,5},{5,4},{6,7},{7,6},{8,9},{9,8},{10,11... | collective-permute-start | bytes 64520 | tf_op jit(solution)/shard_map/ppermute | solution.py:13
  41.9 10.5 %collective-permute-start.4 = (bf16[16,256]{1,0:T(8,128)(2,1)S(1)}, bf16[16,256]{1,0:T(8,128)(2,1)S(1)}, u32[]{:S(2)}, u32[]{:S(2)}) collective-permute-start(bf16[16,256]{1,0:T(8,128)(2,1)S(1)} %get-tuple-element.5), channel_id=1, source_target_pairs={{4,0},{8,4},{12,8},{16,12},{20,16},{24,20},{28,24},{5,1},{9,5},{13... | collective-permute-start | bytes 24584 | tf_op jit(solution)/shard_map/ppermute | solution.py:110
  48.5 11.5 %all-to-all-start.2 = ((f32[8,1,5376]{2,1,0:T(1,128)}), f32[8,1,5376]{2,1,0:T(1,128)S(1)}, u32[]{:S(2)}, u32[]{:S(2)}) async-start(f32[8,1,5376]{2,1,0:T(1,128)} %copy.49), calls=%async_computation.2 | async-start | bytes 344064 | tf_op jit(solution)/shard_map/all_to_all | solution.py:117
  61.4 3.9 %collective-permute-start.6 = (f32[5376]{0:T(1024)S(1)}, f32[5376]{0:T(1024)S(1)}, u32[]{:S(2)}, u32[]{:S(2)}) collective-permute-start(f32[5376]{0:T(1024)S(1)} %constant_dynamic-update-slice_fusion.1), channel_id=1, source_target_pairs={{0,2},{1,3},{2,0},{3,1},{4,6},{5,7},{6,4},{7,5},{8,10},{9,11},{10,... | collective-permute-start | bytes 64520 | tf_op jit(solution)/shard_map/ppermute | solution.py:13
  62.2 3.5 %collective-permute-start.7 = (f32[5376]{0:T(1024)S(1)}, f32[5376]{0:T(1024)S(1)}, u32[]{:S(2)}, u32[]{:S(2)}) collective-permute-start(f32[5376]{0:T(1024)S(1)} %constant_dynamic-update-slice_fusion.1), channel_id=1, source_target_pairs={{0,3},{1,2},{2,1},{3,0},{4,7},{5,6},{6,5},{7,4},{8,11},{9,10},{10,... | collective-permute-start | bytes 64520 | tf_op jit(solution)/shard_map/ppermute | solution.py:13
  62.2 3.5 %collective-permute-start.5 = (f32[5376]{0:T(1024)S(1)}, f32[5376]{0:T(1024)S(1)}, u32[]{:S(2)}, u32[]{:S(2)}) collective-permute-start(f32[5376]{0:T(1024)S(1)} %constant_dynamic-update-slice_fusion.1), channel_id=1, source_target_pairs={{0,1},{1,0},{2,3},{3,2},{4,5},{5,4},{6,7},{7,6},{8,9},{9,8},{10,11... | collective-permute-start | bytes 64520 | tf_op jit(solution)/shard_map/ppermute | solution.py:13

commit v17 on v16

--- a/solution.py
+++ b/solution.py
@@ -146,12 +146,12 @@
         parent_pick = jnp.zeros((box_count, rank_width), jnp.bfloat16)
         for group in range(group_count):
             parent_pick = jnp.where((parent_local == group)[:, None], group_out[group][None], parent_pick)
-        from_parent = jnp.einsum(
-            "brq,bq->br", transfer, parent_pick, preferred_element_type=jnp.float32
+        from_parent = jnp.sum(
+            transfer.astype(jnp.float32) * parent_pick.astype(jnp.float32)[:, None, :], axis=2
         )
         downward = (far_total[:box_count] + from_parent).astype(jnp.bfloat16)
-        far_field = jnp.einsum(
-            "brl,br->bl", leaf_bases, downward, preferred_element_type=jnp.float32
+        far_field = jnp.sum(
+            leaf_bases.astype(jnp.float32) * downward.astype(jnp.float32)[:, :, None], axis=1
         )
         image_vec = noise_var * direction + near_total + far_field
         partials = [direction * image_vec]

time: 78 us -> 78.1 us (level)
  matrix products: 10.3 us -> 9.4 us
  other arithmetic: 10.9 us -> 11.7 us
    reduce_sum x0 -> x4, other arithmetic: none -> 0.88 us  [the longest x2 0.46 us: local(): jnp.sum(leaf_bases.astype(jnp.float32) * downward.astype(jnp.float32)[:,...]
    dot_general x4 -> x0, matrix products: 0.86 us -> none  [the longest x2 0.45 us: local(): jnp.einsum('brq,bq->br', transfer, parent_pick, preferred_element_type=jn...]
where the time goes in v17:
time: 78.1 us; the launch traced here: 77.5 us
  starting transfers between devices  19.2 us (25%)
  blocking collectives  17.8 us (23%)
  waiting for transfers between devices  12.9 us (17%)
  other arithmetic  11.7 us (15%)
  matrix products  9.4 us (12%)
  local copies, waits for them, and re-layouts  5.11 us (7%)
  between operations  1.34 us (2%)
    all_to_all x2, blocking collectives, box_sum(): got = lax.all_to_all(sent, 'box', 0, 0, tiled=True)  17.8 us
    all_to_all x2, starting transfers between devices, local(): lax.all_to_all(jnp.concatenate([far_send.reshape(box_devices, far_size),...  12.3 us
    all_to_all x2, waiting for transfers between devices, local(): lax.all_to_all(jnp.concatenate([far_send.reshape(box_devices, far_size),...  8.12 us
    reduce_sum x2, other arithmetic, local(): forward = jnp.sum(near_tiles.astype(jnp.float32) * near_in, axis=(1, 3))  6.19 us
    dot_general x2, matrix products, local(): jnp.einsum('bsij,bi->bsj', near_tiles, rounded, preferred_element_type=jn...  5.66 us
    ppermute x6, waiting for transfers between devices, rep_sum(): lax.ppermute(vector, 'rep', [(i, i ^ mask) for i in range(count)])  4.77 us
    ppermute x6, starting transfers between devices, rep_sum(): lax.ppermute(vector, 'rep', [(i, i ^ mask) for i in range(count)])  4.35 us
    ppermute x2, starting transfers between devices, local(): lax.ppermute(rounded, 'box', [(i, i - 1) for i in range(1, box_devices)])  2.57 us
  transfers between devices with their start and end apart: 10, of which 6 were waited for; matrix products, arithmetic and copies ran while one was open for 23% of the time, Pallas kernels for 0%

profile of v17, /device:TPU:0, one launch (start us, length us, event | category | flops | bytes accessed | tf_op | source)
XLA Modules:
  0.0 77.5 jit_solution(624566831453694032)
XLA Ops:
  0.7 0.9 %fusion.95 = (f32[16,256]{1,0:T(8,128)S(1)}, bf16[16,256]{1,0:T(8,128)(2,1)S(1)}) fusion(f32[16,256]{1,0:T(8,128)} %param.9), kind=kLoop, calls=%fused_computation.173 | loop fusion | flops 8192 | bytes 40960 | tf_op jit(solution)/shard_map/convert_element_type | solution.py:95
  1.6 1.3 %collective-permute-start = (bf16[16,256]{1,0:T(8,128)(2,1)S(1)}, bf16[16,256]{1,0:T(8,128)(2,1)S(1)}, u32[]{:S(2)}, u32[]{:S(2)}) collective-permute-start(bf16[16,256]{1,0:T(8,128)(2,1)S(1)} %get-tuple-element.18), channel_id=1, source_target_pairs={{4,0},{8,4},{12,8},{16,12},{20,16},{24,20},{28,24},{5,1},{9,5},{13... | collective-permute-start | bytes 24584 | tf_op jit(solution)/shard_map/ppermute | solution.py:110
  2.9 0.7 broadcast_select_fusion.4
  3.7 2.8 %fusion.49 = f32[16,1,2,256]{3,1,2,0:T(1,128)S(1)} fusion(bf16[16,2,256,256]{3,2,1,0:T(8,128)(2,1)} %param.11, bf16[16,256,1,1]{1,0,2,3:T(8,128)(2,1)S(1)} %bitcast.103), kind=kOutput, calls=%fused_computation.86 | convolution fusion | flops 4194304 | bytes 4235264 | tf_op jit(solution)/shard_map/bsij,bi->bsj/dot_general | solution.py:88
  9.0 0.8 %all_to_all.24 = f32[8,1,5376]{2,1,0:T(1,128)} reshape(f32[8,5376]{1,0:T(8,128)S(1)} %pad_maximum_fusion) | data formatting | bytes 344064 | tf_op jit(solution)/shard_map/all_to_all | solution.py:117
  9.8 8.4 %all-to-all-start = ((f32[8,1,5376]{2,1,0:T(1,128)}), f32[8,1,5376]{2,1,0:T(1,128)S(1)}, u32[]{:S(2)}, u32[]{:S(2)}) async-start(f32[8,1,5376]{2,1,0:T(1,128)} %all_to_all.24), calls=%async_computation | async-start | bytes 344064 | tf_op jit(solution)/shard_map/all_to_all | solution.py:117
  18.8 3.1 %fusion = f32[16,256]{1,0:T(8,128)S(1)} fusion(bf16[16,2,256,256]{3,2,1,0:T(8,128)(2,1)} %param.11, f32[16,2,256]{2,1,0:T(2,128)S(1)} %mul.166), kind=kLoop, calls=%fused_computation.2 | loop fusion | flops 6287360 | bytes 4243456 | tf_op jit(solution)/shard_map/reduce_sum | solution.py:133
  21.9 3.9 %all-to-all-done = f32[8,1,5376]{2,1,0:T(1,128)S(1)} async-done(((f32[8,1,5376]{2,1,0:T(1,128)}), f32[8,1,5376]{2,1,0:T(1,128)S(1)}, u32[]{:S(2)}, u32[]{:S(2)}) %all-to-all-start) | async-done | bytes 172064 | tf_op jit(solution)/shard_map/all_to_all | solution.py:117
  27.2 1.5 %collective-permute-start.2 = (f32[5376]{0:T(1024)S(1)}, f32[5376]{0:T(1024)S(1)}, u32[]{:S(2)}, u32[]{:S(2)}) collective-permute-start(f32[5376]{0:T(1024)S(1)} %constant_dynamic-update-slice_fusion), channel_id=1, source_target_pairs={{0,2},{1,3},{2,0},{3,1},{4,6},{5,7},{6,4},{7,5},{8,10},{9,11},{10,... | collective-permute-start | bytes 64520 | tf_op jit(solution)/shard_map/ppermute | solution.py:13
  28.7 0.6 collective-permute-start.1
  29.3 1.7 %collective-permute-done.2 = f32[5376]{0:T(1024)S(1)} collective-permute-done((f32[5376]{0:T(1024)S(1)}, f32[5376]{0:T(1024)S(1)}, u32[]{:S(2)}, u32[]{:S(2)}) %collective-permute-start.2) | collective-permute-done | bytes 21536 | tf_op jit(solution)/shard_map/ppermute | solution.py:13
  31.0 0.9 %collective-permute-done.3 = f32[5376]{0:T(1024)S(1)} collective-permute-done((f32[5376]{0:T(1024)S(1)}, f32[5376]{0:T(1024)S(1)}, u32[]{:S(2)}, u32[]{:S(2)}) %collective-permute-start.3) | collective-permute-done | bytes 21536 | tf_op jit(solution)/shard_map/ppermute | solution.py:13
  32.9 8.9 %all_to_all.36 = f32[8,1,4]{2,1,0:T(1,128)S(1)} all-to-all(f32[8,1,4]{2,1,0:T(1,128)S(1)} %broadcast_in_dim.302), channel_id=1, replica_groups=mesh['box'=8,'rep'=4] {'box'}, dimensions={0} | all-to-all | bytes 256 | tf_op jit(solution)/shard_map/all_to_all | solution.py:36
  41.9 1.3 %collective-permute-start.4 = (bf16[16,256]{1,0:T(8,128)(2,1)S(1)}, bf16[16,256]{1,0:T(8,128)(2,1)S(1)}, u32[]{:S(2)}, u32[]{:S(2)}) collective-permute-start(bf16[16,256]{1,0:T(8,128)(2,1)S(1)} %get-tuple-element.5), channel_id=1, source_target_pairs={{4,0},{8,4},{12,8},{16,12},{20,16},{24,20},{28,24},{5,1},{9,5},{13... | collective-permute-start | bytes 24584 | tf_op jit(solution)/shard_map/ppermute | solution.py:110
  43.2 2.8 %fusion.47 = f32[16,1,2,256]{3,1,2,0:T(1,128)S(1)} fusion(bf16[16,2,256,256]{3,2,1,0:T(8,128)(2,1)} %param.11, bf16[16,256,1,1]{1,0,2,3:T(8,128)(2,1)S(1)} %bitcast.104), kind=kOutput, calls=%fused_computation.84 | convolution fusion | flops 4194304 | bytes 4235264 | tf_op jit(solution)/shard_map/bsij,bi->bsj/dot_general | solution.py:88
  47.7 0.8 %copy.49 = f32[8,1,5376]{2,1,0:T(1,128)} copy(f32[8,1,5376]{2,0,1:T(8,128)S(1)} %maximum_bitcast_fusion) | data formatting | bytes 344064 | tf_op jit(solution)/shard_map/all_to_all | solution.py:117
  48.5 3.9 %all-to-all-start.2 = ((f32[8,1,5376]{2,1,0:T(1,128)}), f32[8,1,5376]{2,1,0:T(1,128)S(1)}, u32[]{:S(2)}, u32[]{:S(2)}) async-start(f32[8,1,5376]{2,1,0:T(1,128)} %copy.49), calls=%async_computation.2 | async-start | bytes 344064 | tf_op jit(solution)/shard_map/all_to_all | solution.py:117
  52.7 3.1 %fusion.1 = f32[16,256]{1,0:T(8,128)S(1)} fusion(bf16[16,2,256,256]{3,2,1,0:T(8,128)(2,1)} %param.11, f32[16,2,256]{2,1,0:T(2,128)S(1)} %mul.194), kind=kLoop, calls=%fused_computation.3 | loop fusion | flops 6287360 | bytes 4243456 | tf_op jit(solution)/shard_map/reduce_sum | solution.py:133
  55.8 4.2 %all-to-all-done.2 = f32[8,1,5376]{2,1,0:T(1,128)S(1)} async-done(((f32[8,1,5376]{2,1,0:T(1,128)}), f32[8,1,5376]{2,1,0:T(1,128)S(1)}, u32[]{:S(2)}, u32[]{:S(2)}) %all-to-all-start.2) | async-done | bytes 172064 | tf_op jit(solution)/shard_map/all_to_all | solution.py:117
  61.4 0.8 %collective-permute-start.6 = (f32[5376]{0:T(1024)S(1)}, f32[5376]{0:T(1024)S(1)}, u32[]{:S(2)}, u32[]{:S(2)}) collective-permute-start(f32[5376]{0:T(1024)S(1)} %constant_dynamic-update-slice_fusion.1), channel_id=1, source_target_pairs={{0,2},{1,3},{2,0},{3,1},{4,6},{5,7},{6,4},{7,5},{8,10},{9,11},{10,... | collective-permute-start | bytes 64520 | tf_op jit(solution)/shard_map/ppermute | solution.py:13
  62.2 1.3 %collective-permute-start.5 = (f32[5376]{0:T(1024)S(1)}, f32[5376]{0:T(1024)S(1)}, u32[]{:S(2)}, u32[]{:S(2)}) collective-permute-start(f32[5376]{0:T(1024)S(1)} %constant_dynamic-update-slice_fusion.1), channel_id=1, source_target_pairs={{0,1},{1,0},{2,3},{3,2},{4,5},{5,4},{6,7},{7,6},{8,9},{9,8},{10,11... | collective-permute-start | bytes 64520 | tf_op jit(solution)/shard_map/ppermute | solution.py:13
  63.6 1.7 %collective-permute-done.6 = f32[5376]{0:T(1024)S(1)} collective-permute-done((f32[5376]{0:T(1024)S(1)}, f32[5376]{0:T(1024)S(1)}, u32[]{:S(2)}, u32[]{:S(2)}) %collective-permute-start.6) | collective-permute-done | bytes 21536 | tf_op jit(solution)/shard_map/ppermute | solution.py:13
  67.1 0.6 broadcast_in_dim.313
  67.8 8.8 %all_to_all.37 = f32[8,1,1]{2,1,0:T(1,128)S(1)} all-to-all(f32[8,1,1]{2,1,0:T(1,128)S(1)} %broadcast_in_dim.313), channel_id=1, replica_groups=mesh['box'=8,'rep'=4] {'box'}, dimensions={0} | all-to-all | bytes 64 | tf_op jit(solution)/shard_map/all_to_all | solution.py:36
  (148 shorter events, 11.1 us)
Async XLA Ops:
  0.6 7.5 %copy-start = (bf16[20,4,64,64]{3,2,1,0:T(8,128)(2,1)S(1)}, bf16[20,4,64,64]{3,2,1,0:T(8,128)(2,1)}, u32[]{:S(2)}) copy-start(bf16[20,4,64,64]{3,2,1,0:T(8,128)(2,1)} %param.16) | copy-start | bytes 1966084
  0.6 5.9 %copy-start.5 = (s32[16,2]{0,1:T(2,128)S(1)}, s32[16,2]{0,1:T(2,128)}, u32[]{:S(2)}) copy-start(s32[16,2]{0,1:T(2,128)} %param.12) | copy-start | bytes 388
  0.7 6.5 %copy-start.1 = (bf16[16,64,256]{2,1,0:T(8,128)(2,1)S(1)}, bf16[16,64,256]{2,1,0:T(8,128)(2,1)}, u32[]{:S(2)}) copy-start(bf16[16,64,256]{2,1,0:T(8,128)(2,1)} %param.13) | copy-start | bytes 1572868
  0.7 6.8 %copy-start.2 = (bf16[16,64,64]{2,1,0:T(8,128)(2,1)S(1)}, bf16[16,64,64]{2,1,0:T(8,128)(2,1)}, u32[]{:S(2)}) copy-start(bf16[16,64,64]{2,1,0:T(8,128)(2,1)} %param.14) | copy-start | bytes 393220
  0.7 6.9 %copy-start.6 = (s32[16]{0:T(128)S(1)}, s32[16]{0:T(128)}, u32[]{:S(2)}) copy-start(s32[16]{0:T(128)} %param.15) | copy-start | bytes 196
  1.6 17.0 %collective-permute-start = (bf16[16,256]{1,0:T(8,128)(2,1)S(1)}, bf16[16,256]{1,0:T(8,128)(2,1)S(1)}, u32[]{:S(2)}, u32[]{:S(2)}) collective-permute-start(bf16[16,256]{1,0:T(8,128)(2,1)S(1)} %get-tuple-element.18), channel_id=1, source_target_pairs={{4,0},{8,4},{12,8},{16,12},{20,16},{24,20},{28,24},{5,1},{9,5},{13... | collective-permute-start | bytes 24584 | tf_op jit(solution)/shard_map/ppermute | solution.py:110
  9.8 16.0 %all-to-all-start = ((f32[8,1,5376]{2,1,0:T(1,128)}), f32[8,1,5376]{2,1,0:T(1,128)S(1)}, u32[]{:S(2)}, u32[]{:S(2)}) async-start(f32[8,1,5376]{2,1,0:T(1,128)} %all_to_all.24), calls=%async_computation | async-start | bytes 344064 | tf_op jit(solution)/shard_map/all_to_all | solution.py:117
  18.2 14.5 %copy-start.3 = (f32[16,256]{1,0:T(8,128)S(1)}, f32[16,256]{1,0:T(8,128)}, u32[]{:S(2)}) copy-start(f32[16,256]{1,0:T(8,128)} %param.9) | copy-start | bytes 49156
  18.2 14.5 %copy-start.4 = (f32[16,256]{1,0:T(8,128)S(1)}, f32[16,256]{1,0:T(8,128)}, u32[]{:S(2)}) copy-start(f32[16,256]{1,0:T(8,128)} %param.10) | copy-start | bytes 49156
  27.2 3.9 %collective-permute-start.2 = (f32[5376]{0:T(1024)S(1)}, f32[5376]{0:T(1024)S(1)}, u32[]{:S(2)}, u32[]{:S(2)}) collective-permute-start(f32[5376]{0:T(1024)S(1)} %constant_dynamic-update-slice_fusion), channel_id=1, source_target_pairs={{0,2},{1,3},{2,0},{3,1},{4,6},{5,7},{6,4},{7,5},{8,10},{9,11},{10,... | collective-permute-start | bytes 64520 | tf_op jit(solution)/shard_map/ppermute | solution.py:13
  28.7 3.3 %collective-permute-start.3 = (f32[5376]{0:T(1024)S(1)}, f32[5376]{0:T(1024)S(1)}, u32[]{:S(2)}, u32[]{:S(2)}) collective-permute-start(f32[5376]{0:T(1024)S(1)} %constant_dynamic-update-slice_fusion), channel_id=1, source_target_pairs={{0,3},{1,2},{2,1},{3,0},{4,7},{5,6},{6,5},{7,4},{8,11},{9,10},{10,... | collective-permute-start | bytes 64520 | tf_op jit(solution)/shard_map/ppermute | solution.py:13
  28.7 3.3 %collective-permute-start.1 = (f32[5376]{0:T(1024)S(1)}, f32[5376]{0:T(1024)S(1)}, u32[]{:S(2)}, u32[]{:S(2)}) collective-permute-start(f32[5376]{0:T(1024)S(1)} %constant_dynamic-update-slice_fusion), channel_id=1, source_target_pairs={{0,1},{1,0},{2,3},{3,2},{4,5},{5,4},{6,7},{7,6},{8,9},{9,8},{10,11... | collective-permute-start | bytes 64520 | tf_op jit(solution)/shard_map/ppermute | solution.py:13
  41.9 10.5 %collective-permute-start.4 = (bf16[16,256]{1,0:T(8,128)(2,1)S(1)}, bf16[16,256]{1,0:T(8,128)(2,1)S(1)}, u32[]{:S(2)}, u32[]{:S(2)}) collective-permute-start(bf16[16,256]{1,0:T(8,128)(2,1)S(1)} %get-tuple-element.5), channel_id=1, source_target_pairs={{4,0},{8,4},{12,8},{16,12},{20,16},{24,20},{28,24},{5,1},{9,5},{13... | collective-permute-start | bytes 24584 | tf_op jit(solution)/shard_map/ppermute | solution.py:110
  48.5 11.5 %all-to-all-start.2 = ((f32[8,1,5376]{2,1,0:T(1,128)}), f32[8,1,5376]{2,1,0:T(1,128)S(1)}, u32[]{:S(2)}, u32[]{:S(2)}) async-start(f32[8,1,5376]{2,1,0:T(1,128)} %copy.49), calls=%async_computation.2 | async-start | bytes 344064 | tf_op jit(solution)/shard_map/all_to_all | solution.py:117
  61.4 3.9 %collective-permute-start.6 = (f32[5376]{0:T(1024)S(1)}, f32[5376]{0:T(1024)S(1)}, u32[]{:S(2)}, u32[]{:S(2)}) collective-permute-start(f32[5376]{0:T(1024)S(1)} %constant_dynamic-update-slice_fusion.1), channel_id=1, source_target_pairs={{0,2},{1,3},{2,0},{3,1},{4,6},{5,7},{6,4},{7,5},{8,10},{9,11},{10,... | collective-permute-start | bytes 64520 | tf_op jit(solution)/shard_map/ppermute | solution.py:13
  62.2 3.5 %collective-permute-start.7 = (f32[5376]{0:T(1024)S(1)}, f32[5376]{0:T(1024)S(1)}, u32[]{:S(2)}, u32[]{:S(2)}) collective-permute-start(f32[5376]{0:T(1024)S(1)} %constant_dynamic-update-slice_fusion.1), channel_id=1, source_target_pairs={{0,3},{1,2},{2,1},{3,0},{4,7},{5,6},{6,5},{7,4},{8,11},{9,10},{10,... | collective-permute-start | bytes 64520 | tf_op jit(solution)/shard_map/ppermute | solution.py:13
  62.2 3.5 %collective-permute-start.5 = (f32[5376]{0:T(1024)S(1)}, f32[5376]{0:T(1024)S(1)}, u32[]{:S(2)}, u32[]{:S(2)}) collective-permute-start(f32[5376]{0:T(1024)S(1)} %constant_dynamic-update-slice_fusion.1), channel_id=1, source_target_pairs={{0,1},{1,0},{2,3},{3,2},{4,5},{5,4},{6,7},{7,6},{8,9},{9,8},{10,11... | collective-permute-start | bytes 64520 | tf_op jit(solution)/shard_map/ppermute | solution.py:13

commit v18 on v16

--- a/solution.py
+++ b/solution.py
@@ -94,13 +94,15 @@
         leaf_coef = jnp.sum(
             leaf_bases.astype(jnp.float32) * rounded.astype(jnp.float32)[:, None, :], axis=2
         ).astype(jnp.bfloat16)
-        upward = jnp.einsum("brq,br->bq", transfer, leaf_coef, preferred_element_type=jnp.float32)
+        upward = jnp.sum(
+            transfer.astype(jnp.float32) * leaf_coef.astype(jnp.float32)[:, :, None], axis=1
+        )
         group_coef = jnp.dot(parent_onehot, upward, precision=lax.Precision.HIGHEST).astype(
             jnp.bfloat16
         )
         node_coef = jnp.concatenate([leaf_coef, group_coef], axis=0)
-        far_mirror = jnp.einsum(
-            "nsab,na->nsb", coupling, node_coef, preferred_element_type=jnp.float32
+        far_mirror = jnp.sum(
+            coupling.astype(jnp.float32) * node_coef.astype(jnp.float32)[:, None, :, None], axis=2
         )
         far_mirror = far_mirror * far_valid[:, :, None].astype(jnp.float32)
         spread = jnp.dot(
@@ -135,8 +137,9 @@
         partner_coef = jnp.dot(
             far_pick.T.astype(jnp.bfloat16), every_coef, preferred_element_type=jnp.float32
         ).astype(jnp.bfloat16).reshape(node_count, -1, rank_width)
-        far_forward = jnp.einsum(
-            "nsab,nsb->na", coupling, partner_coef, preferred_element_type=jnp.float32
+        far_forward = jnp.sum(
+            coupling.astype(jnp.float32) * partner_coef.astype(jnp.float32)[:, :, None, :],
+            axis=(1, 3),
         )
         far_part = far_forward + spread[box_rank] + mirror_in
         both = rep_sum(jnp.concatenate([near_part.reshape(-1), far_part.reshape(-1)]))

time: 78 us -> 79.1 us (1.014)
  other arithmetic: 10.9 us -> 13.8 us
  matrix products: 10.3 us -> 8.59 us
    reduce_sum x0 -> x6, other arithmetic: none -> 2.51 us  [the longest x2 1.25 us: local(): jnp.sum(coupling.astype(jnp.float32) * node_coef.astype(jnp.float32)[:, N...]
    dot_general x6 -> x0, matrix products: 1.79 us -> none  [the longest x2 0.87 us: local(): jnp.einsum('nsab,nsb->na', coupling, partner_coef, preferred_element_type...]
  transfers between devices with their start and end apart: 10 -> 10, of which waited for: 6 -> 6; matrix products, arithmetic and copies ran while one was open for 23% -> 25% of each run, Pallas kernels for 0% -> 0%
where the time goes in v18:
time: 79.1 us; the launch traced here: 78.5 us
  starting transfers between devices  19.3 us (24%)
  blocking collectives  17.8 us (23%)
  other arithmetic  13.8 us (17%)
  waiting for transfers between devices  12.7 us (16%)
  matrix products  8.59 us (11%)
  local copies, waits for them, and re-layouts  5 us (6%)
  between operations  1.3 us (2%)
    all_to_all x2, blocking collectives, box_sum(): got = lax.all_to_all(sent, 'box', 0, 0, tiled=True)  17.8 us
    all_to_all x2, starting transfers between devices, local(): lax.all_to_all(jnp.concatenate([far_send.reshape(box_devices, far_size),...  12.3 us
    all_to_all x2, waiting for transfers between devices, local(): lax.all_to_all(jnp.concatenate([far_send.reshape(box_devices, far_size),...  7.96 us
    reduce_sum x2, other arithmetic, local(): forward = jnp.sum(near_tiles.astype(jnp.float32) * near_in, axis=(1, 3))  6.19 us
    dot_general x2, matrix products, local(): jnp.einsum('bsij,bi->bsj', near_tiles, rounded, preferred_element_type=jn...  5.77 us
    ppermute x6, waiting for transfers between devices, rep_sum(): lax.ppermute(vector, 'rep', [(i, i ^ mask) for i in range(count)])  4.77 us
    ppermute x6, starting transfers between devices, rep_sum(): lax.ppermute(vector, 'rep', [(i, i ^ mask) for i in range(count)])  4.41 us
    ppermute x2, starting transfers between devices, local(): lax.ppermute(rounded, 'box', [(i, i - 1) for i in range(1, box_devices)])  2.57 us
  transfers between devices with their start and end apart: 10, of which 6 were waited for; matrix products, arithmetic and copies ran while one was open for 25% of the time, Pallas kernels for 0%

profile of v18, /device:TPU:0, one launch (start us, length us, event | category | flops | bytes accessed | tf_op | source)
XLA Modules:
  0.0 78.5 jit_solution(4534439120390492789)
XLA Ops:
  0.7 0.8 %fusion.95 = (f32[16,256]{1,0:T(8,128)S(1)}, bf16[16,256]{1,0:T(8,128)(2,1)S(1)}) fusion(f32[16,256]{1,0:T(8,128)} %param.9), kind=kLoop, calls=%fused_computation.173 | loop fusion | flops 8192 | bytes 40960 | tf_op jit(solution)/shard_map/convert_element_type | solution.py:95
  1.5 1.3 %collective-permute-start = (bf16[16,256]{1,0:T(8,128)(2,1)S(1)}, bf16[16,256]{1,0:T(8,128)(2,1)S(1)}, u32[]{:S(2)}, u32[]{:S(2)}) collective-permute-start(bf16[16,256]{1,0:T(8,128)(2,1)S(1)} %get-tuple-element.16), channel_id=1, source_target_pairs={{4,0},{8,4},{12,8},{16,12},{20,16},{24,20},{28,24},{5,1},{9,5},{13... | collective-permute-start | bytes 24584 | tf_op jit(solution)/shard_map/ppermute | solution.py:112
  2.7 0.7 broadcast_compare_fusion
  3.4 0.7 broadcast_select_fusion.4
  4.2 2.9 %fusion.55 = f32[16,1,2,256]{3,1,2,0:T(1,128)S(1)} fusion(bf16[16,2,256,256]{3,2,1,0:T(8,128)(2,1)} %param.11, bf16[16,256,1,1]{1,0,2,3:T(8,128)(2,1)S(1)} %bitcast.100), kind=kOutput, calls=%fused_computation.96 | convolution fusion | flops 4194304 | bytes 4235264 | tf_op jit(solution)/shard_map/bsij,bi->bsj/dot_general | solution.py:88
  9.9 0.8 all_to_all.24
  10.7 8.4 %all-to-all-start = ((f32[8,1,5376]{2,1,0:T(1,128)}), f32[8,1,5376]{2,1,0:T(1,128)S(1)}, u32[]{:S(2)}, u32[]{:S(2)}) async-start(f32[8,1,5376]{2,1,0:T(1,128)} %all_to_all.24), calls=%async_computation | async-start | bytes 344064 | tf_op jit(solution)/shard_map/all_to_all | solution.py:119
  19.8 3.1 %fusion = f32[16,256]{1,0:T(8,128)S(1)} fusion(bf16[16,2,256,256]{3,2,1,0:T(8,128)(2,1)} %param.11, f32[16,2,256]{2,1,0:T(2,128)S(1)} %mul.190), kind=kLoop, calls=%fused_computation.2 | loop fusion | flops 6287360 | bytes 4243456 | tf_op jit(solution)/shard_map/reduce_sum | solution.py:135
  22.9 3.8 %all-to-all-done = f32[8,1,5376]{2,1,0:T(1,128)S(1)} async-done(((f32[8,1,5376]{2,1,0:T(1,128)}), f32[8,1,5376]{2,1,0:T(1,128)S(1)}, u32[]{:S(2)}, u32[]{:S(2)}) %all-to-all-start) | async-done | bytes 172064 | tf_op jit(solution)/shard_map/all_to_all | solution.py:119
  28.0 1.6 %collective-permute-start.2 = (f32[5376]{0:T(1024)S(1)}, f32[5376]{0:T(1024)S(1)}, u32[]{:S(2)}, u32[]{:S(2)}) collective-permute-start(f32[5376]{0:T(1024)S(1)} %pad_maximum_fusion.1), channel_id=1, source_target_pairs={{0,2},{1,3},{2,0},{3,1},{4,6},{5,7},{6,4},{7,5},{8,10},{9,11},{10,... | collective-permute-start | bytes 64520 | tf_op jit(solution)/shard_map/ppermute | solution.py:13
  30.2 1.7 %collective-permute-done.2 = f32[5376]{0:T(1024)S(1)} collective-permute-done((f32[5376]{0:T(1024)S(1)}, f32[5376]{0:T(1024)S(1)}, u32[]{:S(2)}, u32[]{:S(2)}) %collective-permute-start.2) | collective-permute-done | bytes 21536 | tf_op jit(solution)/shard_map/ppermute | solution.py:13
  31.9 0.9 %collective-permute-done.3 = f32[5376]{0:T(1024)S(1)} collective-permute-done((f32[5376]{0:T(1024)S(1)}, f32[5376]{0:T(1024)S(1)}, u32[]{:S(2)}, u32[]{:S(2)}) %collective-permute-start.3) | collective-permute-done | bytes 21536 | tf_op jit(solution)/shard_map/ppermute | solution.py:13
  33.7 8.9 %all_to_all.36 = f32[8,1,4]{2,1,0:T(1,128)S(1)} all-to-all(f32[8,1,4]{2,1,0:T(1,128)S(1)} %broadcast_in_dim.304), channel_id=1, replica_groups=mesh['box'=8,'rep'=4] {'box'}, dimensions={0} | all-to-all | bytes 256 | tf_op jit(solution)/shard_map/all_to_all | solution.py:36
  42.7 1.3 %collective-permute-start.4 = (bf16[16,256]{1,0:T(8,128)(2,1)S(1)}, bf16[16,256]{1,0:T(8,128)(2,1)S(1)}, u32[]{:S(2)}, u32[]{:S(2)}) collective-permute-start(bf16[16,256]{1,0:T(8,128)(2,1)S(1)} %get-tuple-element.5), channel_id=1, source_target_pairs={{4,0},{8,4},{12,8},{16,12},{20,16},{24,20},{28,24},{5,1},{9,5},{13... | collective-permute-start | bytes 24584 | tf_op jit(solution)/shard_map/ppermute | solution.py:112
  44.0 2.8 %fusion.53 = f32[16,1,2,256]{3,1,2,0:T(1,128)S(1)} fusion(bf16[16,2,256,256]{3,2,1,0:T(8,128)(2,1)} %param.11, bf16[16,256,1,1]{1,0,2,3:T(8,128)(2,1)S(1)} %bitcast.101), kind=kOutput, calls=%fused_computation.94 | convolution fusion | flops 4194304 | bytes 4235264 | tf_op jit(solution)/shard_map/bsij,bi->bsj/dot_general | solution.py:88
  48.8 0.8 %copy.47 = f32[8,1,5376]{2,1,0:T(1,128)} copy(f32[8,1,5376]{2,0,1:T(8,128)S(1)} %maximum_bitcast_fusion) | data formatting | bytes 344064 | tf_op jit(solution)/shard_map/all_to_all | solution.py:119
  49.6 3.9 %all-to-all-start.2 = ((f32[8,1,5376]{2,1,0:T(1,128)}), f32[8,1,5376]{2,1,0:T(1,128)S(1)}, u32[]{:S(2)}, u32[]{:S(2)}) async-start(f32[8,1,5376]{2,1,0:T(1,128)} %copy.47), calls=%async_computation.2 | async-start | bytes 344064 | tf_op jit(solution)/shard_map/all_to_all | solution.py:119
  53.9 3.1 %fusion.1 = f32[16,256]{1,0:T(8,128)S(1)} fusion(bf16[16,2,256,256]{3,2,1,0:T(8,128)(2,1)} %param.11, f32[16,2,256]{2,1,0:T(2,128)S(1)} %mul.221), kind=kLoop, calls=%fused_computation.3 | loop fusion | flops 6287360 | bytes 4243456 | tf_op jit(solution)/shard_map/reduce_sum | solution.py:135
  57.0 4.2 %all-to-all-done.2 = f32[8,1,5376]{2,1,0:T(1,128)S(1)} async-done(((f32[8,1,5376]{2,1,0:T(1,128)}), f32[8,1,5376]{2,1,0:T(1,128)S(1)}, u32[]{:S(2)}, u32[]{:S(2)}) %all-to-all-start.2) | async-done | bytes 172064 | tf_op jit(solution)/shard_map/all_to_all | solution.py:119
  62.4 0.9 %collective-permute-start.6 = (f32[5376]{0:T(1024)S(1)}, f32[5376]{0:T(1024)S(1)}, u32[]{:S(2)}, u32[]{:S(2)}) collective-permute-start(f32[5376]{0:T(1024)S(1)} %pad_maximum_fusion.2), channel_id=1, source_target_pairs={{0,2},{1,3},{2,0},{3,1},{4,6},{5,7},{6,4},{7,5},{8,10},{9,11},{10,... | collective-permute-start | bytes 64520 | tf_op jit(solution)/shard_map/ppermute | solution.py:13
  63.3 1.3 %collective-permute-start.5 = (f32[5376]{0:T(1024)S(1)}, f32[5376]{0:T(1024)S(1)}, u32[]{:S(2)}, u32[]{:S(2)}) collective-permute-start(f32[5376]{0:T(1024)S(1)} %pad_maximum_fusion.2), channel_id=1, source_target_pairs={{0,1},{1,0},{2,3},{3,2},{4,5},{5,4},{6,7},{7,6},{8,9},{9,8},{10,11... | collective-permute-start | bytes 64520 | tf_op jit(solution)/shard_map/ppermute | solution.py:13
  64.6 1.7 %collective-permute-done.6 = f32[5376]{0:T(1024)S(1)} collective-permute-done((f32[5376]{0:T(1024)S(1)}, f32[5376]{0:T(1024)S(1)}, u32[]{:S(2)}, u32[]{:S(2)}) %collective-permute-start.6) | collective-permute-done | bytes 21536 | tf_op jit(solution)/shard_map/ppermute | solution.py:13
  68.1 0.6 broadcast_in_dim.315
  68.8 8.8 %all_to_all.37 = f32[8,1,1]{2,1,0:T(1,128)S(1)} all-to-all(f32[8,1,1]{2,1,0:T(1,128)S(1)} %broadcast_in_dim.315), channel_id=1, replica_groups=mesh['box'=8,'rep'=4] {'box'}, dimensions={0} | all-to-all | bytes 64 | tf_op jit(solution)/shard_map/all_to_all | solution.py:36
  (148 shorter events, 12.1 us)
Async XLA Ops:
  0.6 6.5 %copy-start.5 = (s32[16,2]{0,1:T(2,128)S(1)}, s32[16,2]{0,1:T(2,128)}, u32[]{:S(2)}) copy-start(s32[16,2]{0,1:T(2,128)} %param.12) | copy-start | bytes 388
  0.6 7.1 %copy-start.1 = (bf16[16,64,256]{2,1,0:T(8,128)(2,1)S(1)}, bf16[16,64,256]{2,1,0:T(8,128)(2,1)}, u32[]{:S(2)}) copy-start(bf16[16,64,256]{2,1,0:T(8,128)(2,1)} %param.13) | copy-start | bytes 1572868
  0.7 7.4 %copy-start.2 = (bf16[16,64,64]{2,1,0:T(8,128)(2,1)S(1)}, bf16[16,64,64]{2,1,0:T(8,128)(2,1)}, u32[]{:S(2)}) copy-start(bf16[16,64,64]{2,1,0:T(8,128)(2,1)} %param.14) | copy-start | bytes 393220
  1.5 18.1 %collective-permute-start = (bf16[16,256]{1,0:T(8,128)(2,1)S(1)}, bf16[16,256]{1,0:T(8,128)(2,1)S(1)}, u32[]{:S(2)}, u32[]{:S(2)}) collective-permute-start(bf16[16,256]{1,0:T(8,128)(2,1)S(1)} %get-tuple-element.16), channel_id=1, source_target_pairs={{4,0},{8,4},{12,8},{16,12},{20,16},{24,20},{28,24},{5,1},{9,5},{13... | collective-permute-start | bytes 24584 | tf_op jit(solution)/shard_map/ppermute | solution.py:112
  4.1 4.1 %copy-start.6 = (s32[16]{0:T(128)S(1)}, s32[16]{0:T(128)}, u32[]{:S(2)}) copy-start(s32[16]{0:T(128)} %param.15) | copy-start | bytes 196
  4.1 4.7 %copy-start = (bf16[20,4,64,64]{3,2,1,0:T(8,128)(2,1)S(1)}, bf16[20,4,64,64]{3,2,1,0:T(8,128)(2,1)}, u32[]{:S(2)}) copy-start(bf16[20,4,64,64]{3,2,1,0:T(8,128)(2,1)} %param.16) | copy-start | bytes 1966084
  10.7 16.0 %all-to-all-start = ((f32[8,1,5376]{2,1,0:T(1,128)}), f32[8,1,5376]{2,1,0:T(1,128)S(1)}, u32[]{:S(2)}, u32[]{:S(2)}) async-start(f32[8,1,5376]{2,1,0:T(1,128)} %all_to_all.24), calls=%async_computation | async-start | bytes 344064 | tf_op jit(solution)/shard_map/all_to_all | solution.py:119
  22.9 10.6 %copy-start.3 = (f32[16,256]{1,0:T(8,128)S(1)}, f32[16,256]{1,0:T(8,128)}, u32[]{:S(2)}) copy-start(f32[16,256]{1,0:T(8,128)} %param.9) | copy-start | bytes 49156
  22.9 10.6 %copy-start.4 = (f32[16,256]{1,0:T(8,128)S(1)}, f32[16,256]{1,0:T(8,128)}, u32[]{:S(2)}) copy-start(f32[16,256]{1,0:T(8,128)} %param.10) | copy-start | bytes 49156
  28.0 3.9 %collective-permute-start.2 = (f32[5376]{0:T(1024)S(1)}, f32[5376]{0:T(1024)S(1)}, u32[]{:S(2)}, u32[]{:S(2)}) collective-permute-start(f32[5376]{0:T(1024)S(1)} %pad_maximum_fusion.1), channel_id=1, source_target_pairs={{0,2},{1,3},{2,0},{3,1},{4,6},{5,7},{6,4},{7,5},{8,10},{9,11},{10,... | collective-permute-start | bytes 64520 | tf_op jit(solution)/shard_map/ppermute | solution.py:13
  29.5 3.3 %collective-permute-start.3 = (f32[5376]{0:T(1024)S(1)}, f32[5376]{0:T(1024)S(1)}, u32[]{:S(2)}, u32[]{:S(2)}) collective-permute-start(f32[5376]{0:T(1024)S(1)} %pad_maximum_fusion.1), channel_id=1, source_target_pairs={{0,3},{1,2},{2,1},{3,0},{4,7},{5,6},{6,5},{7,4},{8,11},{9,10},{10,... | collective-permute-start | bytes 64520 | tf_op jit(solution)/shard_map/ppermute | solution.py:13
  29.5 3.3 %collective-permute-start.1 = (f32[5376]{0:T(1024)S(1)}, f32[5376]{0:T(1024)S(1)}, u32[]{:S(2)}, u32[]{:S(2)}) collective-permute-start(f32[5376]{0:T(1024)S(1)} %pad_maximum_fusion.1), channel_id=1, source_target_pairs={{0,1},{1,0},{2,3},{3,2},{4,5},{5,4},{6,7},{7,6},{8,9},{9,8},{10,11... | collective-permute-start | bytes 64520 | tf_op jit(solution)/shard_map/ppermute | solution.py:13
  42.7 10.9 %collective-permute-start.4 = (bf16[16,256]{1,0:T(8,128)(2,1)S(1)}, bf16[16,256]{1,0:T(8,128)(2,1)S(1)}, u32[]{:S(2)}, u32[]{:S(2)}) collective-permute-start(bf16[16,256]{1,0:T(8,128)(2,1)S(1)} %get-tuple-element.5), channel_id=1, source_target_pairs={{4,0},{8,4},{12,8},{16,12},{20,16},{24,20},{28,24},{5,1},{9,5},{13... | collective-permute-start | bytes 24584 | tf_op jit(solution)/shard_map/ppermute | solution.py:112
  49.6 11.5 %all-to-all-start.2 = ((f32[8,1,5376]{2,1,0:T(1,128)}), f32[8,1,5376]{2,1,0:T(1,128)S(1)}, u32[]{:S(2)}, u32[]{:S(2)}) async-start(f32[8,1,5376]{2,1,0:T(1,128)} %copy.47), calls=%async_computation.2 | async-start | bytes 344064 | tf_op jit(solution)/shard_map/all_to_all | solution.py:119
  62.4 3.9 %collective-permute-start.6 = (f32[5376]{0:T(1024)S(1)}, f32[5376]{0:T(1024)S(1)}, u32[]{:S(2)}, u32[]{:S(2)}) collective-permute-start(f32[5376]{0:T(1024)S(1)} %pad_maximum_fusion.2), channel_id=1, source_target_pairs={{0,2},{1,3},{2,0},{3,1},{4,6},{5,7},{6,4},{7,5},{8,10},{9,11},{10,... | collective-permute-start | bytes 64520 | tf_op jit(solution)/shard_map/ppermute | solution.py:13
  63.3 3.5 %collective-permute-start.7 = (f32[5376]{0:T(1024)S(1)}, f32[5376]{0:T(1024)S(1)}, u32[]{:S(2)}, u32[]{:S(2)}) collective-permute-start(f32[5376]{0:T(1024)S(1)} %pad_maximum_fusion.2), channel_id=1, source_target_pairs={{0,3},{1,2},{2,1},{3,0},{4,7},{5,6},{6,5},{7,4},{8,11},{9,10},{10,... | collective-permute-start | bytes 64520 | tf_op jit(solution)/shard_map/ppermute | solution.py:13
  63.3 3.5 %collective-permute-start.5 = (f32[5376]{0:T(1024)S(1)}, f32[5376]{0:T(1024)S(1)}, u32[]{:S(2)}, u32[]{:S(2)}) collective-permute-start(f32[5376]{0:T(1024)S(1)} %pad_maximum_fusion.2), channel_id=1, source_target_pairs={{0,1},{1,0},{2,3},{3,2},{4,5},{5,4},{6,7},{7,6},{8,9},{9,8},{10,11... | collective-permute-start | bytes 64520 | tf_op jit(solution)/shard_map/ppermute | solution.py:13

commit v19 on v16

--- a/solution.py
+++ b/solution.py
@@ -85,8 +85,8 @@
     norm_now = None
     for iteration in range(ITERS):
         rounded = direction.astype(jnp.bfloat16)
-        mirrored = jnp.einsum(
-            "bsij,bi->bsj", near_tiles, rounded, preferred_element_type=jnp.float32
+        mirrored = jnp.sum(
+            near_tiles.astype(jnp.float32) * rounded.astype(jnp.float32)[:, None, :, None], axis=2
         )
         landed = jnp.dot(
             near_onehot, mirrored.reshape(-1, mirrored.shape[2]), precision=lax.Precision.HIGHEST

time: 78 us -> 87.3 us (1.12)
  waiting for transfers between devices: 12.9 us -> 22.5 us
  other arithmetic: 10.9 us -> 15.9 us
  matrix products: 10.3 us -> 5.53 us
    all_to_all x2, waiting for transfers between devices: 8.12 us -> 14.7 us  [local(): lax.all_to_all(jnp.concatenate([far_send.reshape(box_devices, far_size),...]
    dot_general x2 -> x0, matrix products: 5.66 us -> none  [local(): jnp.einsum('bsij,bi->bsj', near_tiles, rounded, preferred_element_type=jn...]
    ppermute x2, waiting for transfers between devices: 0.01 us -> 2.98 us  [local(): lax.ppermute(rounded, 'box', [(i, i - 1) for i in range(1, box_devices)])]
    reduce_sum x2, other arithmetic: 6.19 us -> 8.24 us  [local(): forward = jnp.sum(near_tiles.astype(jnp.float32) * near_in, axis=(1, 3))]
    reduce_sum x2, other arithmetic: 0.44 us -> 1.48 us  [local(): jnp.sum(leaf_bases.astype(jnp.float32) * rounded.astype(jnp.float32)[:, N...]
    dot_general x2, matrix products: 0.36 us -> 1.3 us  [local(): jnp.einsum('brq,br->bq', transfer, leaf_coef, preferred_element_type=jnp....]
  transfers between devices with their start and end apart: 10 -> 10, of which waited for: 6 -> 7; matrix products, arithmetic and copies ran while one was open for 23% -> 10% of each run, Pallas kernels for 0% -> 0%
where the time goes in v19:
time: 87.3 us; the launch traced here: 86.7 us
  waiting for transfers between devices  22.5 us (26%)
  starting transfers between devices  18.7 us (21%)
  blocking collectives  17.8 us (20%)
  other arithmetic  15.9 us (18%)
  matrix products  5.53 us (6%)
  local copies, waits for them, and re-layouts  5.06 us (6%)
  between operations  1.22 us (1%)
    all_to_all x2, blocking collectives, box_sum(): got = lax.all_to_all(sent, 'box', 0, 0, tiled=True)  17.8 us
    all_to_all x2, waiting for transfers between devices, local(): lax.all_to_all(jnp.concatenate([far_send.reshape(box_devices, far_size),...  14.7 us
    all_to_all x2, starting transfers between devices, local(): lax.all_to_all(jnp.concatenate([far_send.reshape(box_devices, far_size),...  11.8 us
    reduce_sum x2, other arithmetic, local(): forward = jnp.sum(near_tiles.astype(jnp.float32) * near_in, axis=(1, 3))  8.24 us
    ppermute x6, waiting for transfers between devices, rep_sum(): lax.ppermute(vector, 'rep', [(i, i ^ mask) for i in range(count)])  4.77 us
    ppermute x6, starting transfers between devices, rep_sum(): lax.ppermute(vector, 'rep', [(i, i ^ mask) for i in range(count)])  4.35 us
    ppermute x2, waiting for transfers between devices, local(): lax.ppermute(rounded, 'box', [(i, i - 1) for i in range(1, box_devices)])  2.98 us
    ppermute x2, starting transfers between devices, local(): lax.ppermute(rounded, 'box', [(i, i - 1) for i in range(1, box_devices)])  2.57 us
  transfers between devices with their start and end apart: 10, of which 7 were waited for; matrix products, arithmetic and copies ran while one was open for 10% of the time, Pallas kernels for 0%

profile of v19, /device:TPU:0, one launch (start us, length us, event | category | flops | bytes accessed | tf_op | source)
XLA Modules:
  0.0 86.7 jit_solution(2350992998933796221)
XLA Ops:
  0.6 0.8 fusion.97
  1.5 1.3 %collective-permute-start = (bf16[16,256]{1,0:T(8,128)(2,1)S(1)}, bf16[16,256]{1,0:T(8,128)(2,1)S(1)}, u32[]{:S(2)}, u32[]{:S(2)}) collective-permute-start(bf16[16,256]{1,0:T(8,128)(2,1)S(1)} %get-tuple-element.22), channel_id=1, source_target_pairs={{4,0},{8,4},{12,8},{16,12},{20,16},{24,20},{28,24},{5,1},{9,5},{13... | collective-permute-start | bytes 24584 | tf_op jit(solution)/shard_map/ppermute | solution.py:110
  2.8 0.7 broadcast_select_fusion.4
  3.6 0.7 broadcast_compare_fusion.1
  5.0 1.3 %fusion.4 = bf16[16,64]{1,0:T(8,128)(2,1)S(1)} fusion(bf16[16,64,256]{2,1,0:T(8,128)(2,1)} %param.13, f32[16,256]{1,0:T(8,128)S(1)} %get-tuple-element.21), kind=kLoop, calls=%fused_computation.14 | loop fusion | flops 785408 | bytes 542720 | tf_op jit(solution)/shard_map/reduce_sum | solution.py:94
  6.2 1.1 %fusion.67 = f32[16,1,64]{2,1,0:T(1,128)S(1)} fusion(bf16[16,64,64]{2,1,0:T(8,128)(2,1)} %param.14, bf16[16,64,1]{1,0,2:T(8,128)(2,1)S(1)} %bitcast.122), kind=kOutput, calls=%fused_computation.113 | convolution fusion | flops 131072 | bytes 137216 | tf_op jit(solution)/shard_map/brq,br->bq/dot_general | solution.py:97
  9.9 4.2 %fusion = (f32[16,256]{1,0:T(8,128)S(1)}, f32[16,2,256]{2,1,0:T(2,128)S(1)}) fusion(bf16[16,2,256,256]{3,2,1,0:T(8,128)(2,1)} %param.11, f32[16,2,256]{2,1,0:T(2,128)S(1)} %mul.150, f32[16,256]{1,0:T(8,128)S(1)} %get-tuple-element.21), kind=kLoop, calls=%fused_computation.4 | loop fusion | flops 10473472 | bytes 4292608 | tf_op jit(solution)/shard_map/reduce_sum | solution.py:133
  14.4 0.8 all_to_all.24
  15.2 8.4 %all-to-all-start = ((f32[8,1,5376]{2,1,0:T(1,128)}), f32[8,1,5376]{2,1,0:T(1,128)S(1)}, u32[]{:S(2)}, u32[]{:S(2)}) async-start(f32[8,1,5376]{2,1,0:T(1,128)} %all_to_all.24), calls=%async_computation | async-start | bytes 344064 | tf_op jit(solution)/shard_map/all_to_all | solution.py:117
  24.0 7.2 %all-to-all-done = f32[8,1,5376]{2,1,0:T(1,128)S(1)} async-done(((f32[8,1,5376]{2,1,0:T(1,128)}), f32[8,1,5376]{2,1,0:T(1,128)S(1)}, u32[]{:S(2)}, u32[]{:S(2)}) %all-to-all-start) | async-done | bytes 172064 | tf_op jit(solution)/shard_map/all_to_all | solution.py:117
  32.6 1.5 %collective-permute-start.2 = (f32[5376]{0:T(1024)S(1)}, f32[5376]{0:T(1024)S(1)}, u32[]{:S(2)}, u32[]{:S(2)}) collective-permute-start(f32[5376]{0:T(1024)S(1)} %constant_dynamic-update-slice_fusion), channel_id=1, source_target_pairs={{0,2},{1,3},{2,0},{3,1},{4,6},{5,7},{6,4},{7,5},{8,10},{9,11},{10,... | collective-permute-start | bytes 64520 | tf_op jit(solution)/shard_map/ppermute | solution.py:13
  34.8 1.7 %collective-permute-done.2 = f32[5376]{0:T(1024)S(1)} collective-permute-done((f32[5376]{0:T(1024)S(1)}, f32[5376]{0:T(1024)S(1)}, u32[]{:S(2)}, u32[]{:S(2)}) %collective-permute-start.2) | collective-permute-done | bytes 21536 | tf_op jit(solution)/shard_map/ppermute | solution.py:13
  36.4 0.9 %collective-permute-done.3 = f32[5376]{0:T(1024)S(1)} collective-permute-done((f32[5376]{0:T(1024)S(1)}, f32[5376]{0:T(1024)S(1)}, u32[]{:S(2)}, u32[]{:S(2)}) %collective-permute-start.3) | collective-permute-done | bytes 21536 | tf_op jit(solution)/shard_map/ppermute | solution.py:13
  38.3 8.9 %all_to_all.36 = f32[8,1,4]{2,1,0:T(1,128)S(1)} all-to-all(f32[8,1,4]{2,1,0:T(1,128)S(1)} %broadcast_in_dim.300), channel_id=1, replica_groups=mesh['box'=8,'rep'=4] {'box'}, dimensions={0} | all-to-all | bytes 256 | tf_op jit(solution)/shard_map/all_to_all | solution.py:36
  47.3 1.3 %collective-permute-start.4 = (bf16[16,256]{1,0:T(8,128)(2,1)S(1)}, bf16[16,256]{1,0:T(8,128)(2,1)S(1)}, u32[]{:S(2)}, u32[]{:S(2)}) collective-permute-start(bf16[16,256]{1,0:T(8,128)(2,1)S(1)} %get-tuple-element.9), channel_id=1, source_target_pairs={{4,0},{8,4},{12,8},{16,12},{20,16},{24,20},{28,24},{5,1},{9,5},{13... | collective-permute-start | bytes 24584 | tf_op jit(solution)/shard_map/ppermute | solution.py:110
  49.9 3.0 %collective-permute-done.4 = bf16[16,256]{1,0:T(8,128)(2,1)S(1)} collective-permute-done((bf16[16,256]{1,0:T(8,128)(2,1)S(1)}, bf16[16,256]{1,0:T(8,128)(2,1)S(1)}, u32[]{:S(2)}, u32[]{:S(2)}) %collective-permute-start.4) | collective-permute-done | bytes 8224 | tf_op jit(solution)/shard_map/ppermute | solution.py:110
  53.1 4.1 %fusion.2 = (f32[16,256]{1,0:T(8,128)S(1)}, f32[16,2,256]{2,1,0:T(2,128)S(1)}) fusion(bf16[16,2,256,256]{3,2,1,0:T(8,128)(2,1)} %param.11, f32[16,2,256]{2,1,0:T(2,128)S(1)} %mul.176, f32[16,256]{1,0:T(8,128)S(1)} %get-tuple-element.8), kind=kLoop, calls=%fused_computation.6 | loop fusion | flops 10473472 | bytes 4292608 | tf_op jit(solution)/shard_map/reduce_sum | solution.py:133
  57.5 0.8 copy.49
  58.3 3.4 %all-to-all-start.2 = ((f32[8,1,5376]{2,1,0:T(1,128)}), f32[8,1,5376]{2,1,0:T(1,128)S(1)}, u32[]{:S(2)}, u32[]{:S(2)}) async-start(f32[8,1,5376]{2,1,0:T(1,128)} %copy.49), calls=%async_computation.2 | async-start | bytes 344064 | tf_op jit(solution)/shard_map/all_to_all | solution.py:117
  61.8 7.5 %all-to-all-done.2 = f32[8,1,5376]{2,1,0:T(1,128)S(1)} async-done(((f32[8,1,5376]{2,1,0:T(1,128)}), f32[8,1,5376]{2,1,0:T(1,128)S(1)}, u32[]{:S(2)}, u32[]{:S(2)}) %all-to-all-start.2) | async-done | bytes 172064 | tf_op jit(solution)/shard_map/all_to_all | solution.py:117
  70.7 0.8 collective-permute-start.6
  71.5 1.3 %collective-permute-start.5 = (f32[5376]{0:T(1024)S(1)}, f32[5376]{0:T(1024)S(1)}, u32[]{:S(2)}, u32[]{:S(2)}) collective-permute-start(f32[5376]{0:T(1024)S(1)} %constant_dynamic-update-slice_fusion.1), channel_id=1, source_target_pairs={{0,1},{1,0},{2,3},{3,2},{4,5},{5,4},{6,7},{7,6},{8,9},{9,8},{10,11... | collective-permute-start | bytes 64520 | tf_op jit(solution)/shard_map/ppermute | solution.py:13
  72.8 1.7 %collective-permute-done.6 = f32[5376]{0:T(1024)S(1)} collective-permute-done((f32[5376]{0:T(1024)S(1)}, f32[5376]{0:T(1024)S(1)}, u32[]{:S(2)}, u32[]{:S(2)}) %collective-permute-start.6) | collective-permute-done | bytes 21536 | tf_op jit(solution)/shard_map/ppermute | solution.py:13
  77.0 8.8 %all_to_all.37 = f32[8,1,1]{2,1,0:T(1,128)S(1)} all-to-all(f32[8,1,1]{2,1,0:T(1,128)S(1)} %broadcast_in_dim.311), channel_id=1, replica_groups=mesh['box'=8,'rep'=4] {'box'}, dimensions={0} | all-to-all | bytes 64 | tf_op jit(solution)/shard_map/all_to_all | solution.py:36
  (140 shorter events, 13.2 us)
Async XLA Ops:
  0.6 7.9 %copy-start = (bf16[20,4,64,64]{3,2,1,0:T(8,128)(2,1)S(1)}, bf16[20,4,64,64]{3,2,1,0:T(8,128)(2,1)}, u32[]{:S(2)}) copy-start(bf16[20,4,64,64]{3,2,1,0:T(8,128)(2,1)} %param.16) | copy-start | bytes 1966084
  1.5 8.2 %collective-permute-start = (bf16[16,256]{1,0:T(8,128)(2,1)S(1)}, bf16[16,256]{1,0:T(8,128)(2,1)S(1)}, u32[]{:S(2)}, u32[]{:S(2)}) collective-permute-start(bf16[16,256]{1,0:T(8,128)(2,1)S(1)} %get-tuple-element.22), channel_id=1, source_target_pairs={{4,0},{8,4},{12,8},{16,12},{20,16},{24,20},{28,24},{5,1},{9,5},{13... | collective-permute-start | bytes 24584 | tf_op jit(solution)/shard_map/ppermute | solution.py:110
  9.9 27.7 %copy-start.4 = (bf16[16,64,64]{2,1,0:T(8,128)(2,1)S(1)}, bf16[16,64,64]{2,1,0:T(8,128)(2,1)}, u32[]{:S(2)}) copy-start(bf16[16,64,64]{2,1,0:T(8,128)(2,1)} %param.14) | copy-start | bytes 393220
  9.9 28.0 %copy-start.1 = (bf16[16,64,256]{2,1,0:T(8,128)(2,1)S(1)}, bf16[16,64,256]{2,1,0:T(8,128)(2,1)}, u32[]{:S(2)}) copy-start(bf16[16,64,256]{2,1,0:T(8,128)(2,1)} %param.13) | copy-start | bytes 1572868
  9.9 28.2 %copy-start.2 = (f32[16,256]{1,0:T(8,128)S(1)}, f32[16,256]{1,0:T(8,128)}, u32[]{:S(2)}) copy-start(f32[16,256]{1,0:T(8,128)} %param.9) | copy-start | bytes 49156
  9.9 28.2 %copy-start.3 = (f32[16,256]{1,0:T(8,128)S(1)}, f32[16,256]{1,0:T(8,128)}, u32[]{:S(2)}) copy-start(f32[16,256]{1,0:T(8,128)} %param.10) | copy-start | bytes 49156
  15.2 16.0 %all-to-all-start = ((f32[8,1,5376]{2,1,0:T(1,128)}), f32[8,1,5376]{2,1,0:T(1,128)S(1)}, u32[]{:S(2)}, u32[]{:S(2)}) async-start(f32[8,1,5376]{2,1,0:T(1,128)} %all_to_all.24), calls=%async_computation | async-start | bytes 344064 | tf_op jit(solution)/shard_map/all_to_all | solution.py:117
  32.6 3.9 %collective-permute-start.2 = (f32[5376]{0:T(1024)S(1)}, f32[5376]{0:T(1024)S(1)}, u32[]{:S(2)}, u32[]{:S(2)}) collective-permute-start(f32[5376]{0:T(1024)S(1)} %constant_dynamic-update-slice_fusion), channel_id=1, source_target_pairs={{0,2},{1,3},{2,0},{3,1},{4,6},{5,7},{6,4},{7,5},{8,10},{9,11},{10,... | collective-permute-start | bytes 64520 | tf_op jit(solution)/shard_map/ppermute | solution.py:13
  34.1 3.3 %collective-permute-start.3 = (f32[5376]{0:T(1024)S(1)}, f32[5376]{0:T(1024)S(1)}, u32[]{:S(2)}, u32[]{:S(2)}) collective-permute-start(f32[5376]{0:T(1024)S(1)} %constant_dynamic-update-slice_fusion), channel_id=1, source_target_pairs={{0,3},{1,2},{2,1},{3,0},{4,7},{5,6},{6,5},{7,4},{8,11},{9,10},{10,... | collective-permute-start | bytes 64520 | tf_op jit(solution)/shard_map/ppermute | solution.py:13
  34.1 3.3 %collective-permute-start.1 = (f32[5376]{0:T(1024)S(1)}, f32[5376]{0:T(1024)S(1)}, u32[]{:S(2)}, u32[]{:S(2)}) collective-permute-start(f32[5376]{0:T(1024)S(1)} %constant_dynamic-update-slice_fusion), channel_id=1, source_target_pairs={{0,1},{1,0},{2,3},{3,2},{4,5},{5,4},{6,7},{7,6},{8,9},{9,8},{10,11... | collective-permute-start | bytes 64520 | tf_op jit(solution)/shard_map/ppermute | solution.py:13
  47.3 5.5 %collective-permute-start.4 = (bf16[16,256]{1,0:T(8,128)(2,1)S(1)}, bf16[16,256]{1,0:T(8,128)(2,1)S(1)}, u32[]{:S(2)}, u32[]{:S(2)}) collective-permute-start(bf16[16,256]{1,0:T(8,128)(2,1)S(1)} %get-tuple-element.9), channel_id=1, source_target_pairs={{4,0},{8,4},{12,8},{16,12},{20,16},{24,20},{28,24},{5,1},{9,5},{13... | collective-permute-start | bytes 24584 | tf_op jit(solution)/shard_map/ppermute | solution.py:110
  58.3 10.9 %all-to-all-start.2 = ((f32[8,1,5376]{2,1,0:T(1,128)}), f32[8,1,5376]{2,1,0:T(1,128)S(1)}, u32[]{:S(2)}, u32[]{:S(2)}) async-start(f32[8,1,5376]{2,1,0:T(1,128)} %copy.49), calls=%async_computation.2 | async-start | bytes 344064 | tf_op jit(solution)/shard_map/all_to_all | solution.py:117
  70.7 3.9 %collective-permute-start.6 = (f32[5376]{0:T(1024)S(1)}, f32[5376]{0:T(1024)S(1)}, u32[]{:S(2)}, u32[]{:S(2)}) collective-permute-start(f32[5376]{0:T(1024)S(1)} %constant_dynamic-update-slice_fusion.1), channel_id=1, source_target_pairs={{0,2},{1,3},{2,0},{3,1},{4,6},{5,7},{6,4},{7,5},{8,10},{9,11},{10,... | collective-permute-start | bytes 64520 | tf_op jit(solution)/shard_map/ppermute | solution.py:13
  71.5 3.5 %collective-permute-start.7 = (f32[5376]{0:T(1024)S(1)}, f32[5376]{0:T(1024)S(1)}, u32[]{:S(2)}, u32[]{:S(2)}) collective-permute-start(f32[5376]{0:T(1024)S(1)} %constant_dynamic-update-slice_fusion.1), channel_id=1, source_target_pairs={{0,3},{1,2},{2,1},{3,0},{4,7},{5,6},{6,5},{7,4},{8,11},{9,10},{10,... | collective-permute-start | bytes 64520 | tf_op jit(solution)/shard_map/ppermute | solution.py:13
  71.5 3.5 %collective-permute-start.5 = (f32[5376]{0:T(1024)S(1)}, f32[5376]{0:T(1024)S(1)}, u32[]{:S(2)}, u32[]{:S(2)}) collective-permute-start(f32[5376]{0:T(1024)S(1)} %constant_dynamic-update-slice_fusion.1), channel_id=1, source_target_pairs={{0,1},{1,0},{2,3},{3,2},{4,5},{5,4},{6,7},{7,6},{8,9},{9,8},{10,11... | collective-permute-start | bytes 64520 | tf_op jit(solution)/shard_map/ppermute | solution.py:13

commit v20 on v16

--- a/solution.py
+++ b/solution.py
@@ -139,9 +139,15 @@
             "nsab,nsb->na", coupling, partner_coef, preferred_element_type=jnp.float32
         )
         far_part = far_forward + spread[box_rank] + mirror_in
-        both = rep_sum(jnp.concatenate([near_part.reshape(-1), far_part.reshape(-1)]))
-        near_total = both[:near_size].reshape(box_count, leaf)
-        far_total = both[near_size:].reshape(node_count, rank_width)
+        far_rows = far_size // leaf if far_size % leaf == 0 else None
+        if far_rows is not None:
+            both = rep_sum(jnp.concatenate([near_part, far_part.reshape(far_rows, leaf)], axis=0))
+            near_total = both[:box_count]
+            far_total = both[box_count:].reshape(node_count, rank_width)
+        else:
+            both = rep_sum(jnp.concatenate([near_part.reshape(-1), far_part.reshape(-1)]))
+            near_total = both[:near_size].reshape(box_count, leaf)
+            far_total = both[near_size:].reshape(node_count, rank_width)
         group_out = far_total[box_count:].astype(jnp.bfloat16)
         parent_pick = jnp.zeros((box_count, rank_width), jnp.bfloat16)
         for group in range(group_count):

time: 78 us -> 78.2 us (level)
  no operation moved by 1% of the time
where the time goes in v20:
time: 78.2 us; the launch traced here: 77.6 us
  starting transfers between devices  19.4 us (25%)
  blocking collectives  17.8 us (23%)
  waiting for transfers between devices  12.9 us (16%)
  other arithmetic  10.9 us (14%)
  matrix products  10.3 us (13%)
  local copies, waits for them, and re-layouts  5.1 us (7%)
  between operations  1.2 us (2%)
    all_to_all x2, blocking collectives, box_sum(): got = lax.all_to_all(sent, 'box', 0, 0, tiled=True)  17.8 us
    all_to_all x2, starting transfers between devices, local(): lax.all_to_all(jnp.concatenate([far_send.reshape(box_devices, far_size),...  12.5 us
    all_to_all x2, waiting for transfers between devices, local(): lax.all_to_all(jnp.concatenate([far_send.reshape(box_devices, far_size),...  8.15 us
    reduce_sum x2, other arithmetic, local(): forward = jnp.sum(near_tiles.astype(jnp.float32) * near_in, axis=(1, 3))  6.19 us
    dot_general x2, matrix products, local(): jnp.einsum('bsij,bi->bsj', near_tiles, rounded, preferred_element_type=jn...  5.66 us
    ppermute x6, waiting for transfers between devices, rep_sum(): lax.ppermute(vector, 'rep', [(i, i ^ mask) for i in range(count)])  4.77 us
    ppermute x6, starting transfers between devices, rep_sum(): lax.ppermute(vector, 'rep', [(i, i ^ mask) for i in range(count)])  4.41 us
    ppermute x2, starting transfers between devices, local(): lax.ppermute(rounded, 'box', [(i, i - 1) for i in range(1, box_devices)])  2.57 us
  transfers between devices with their start and end apart: 10, of which 6 were waited for; matrix products, arithmetic and copies ran while one was open for 23% of the time, Pallas kernels for 0%

profile of v20, /device:TPU:0, one launch (start us, length us, event | category | flops | bytes accessed | tf_op | source)
XLA Modules:
  0.0 77.6 jit_solution(2367477773560865192)
XLA Ops:
  0.7 0.9 %fusion.100 = (f32[16,256]{1,0:T(8,128)S(1)}, bf16[16,256]{1,0:T(8,128)(2,1)S(1)}) fusion(f32[16,256]{1,0:T(8,128)} %param.9), kind=kLoop, calls=%fused_computation.179 | loop fusion | flops 8192 | bytes 40960 | tf_op jit(solution)/shard_map/convert_element_type | solution.py:95
  1.6 1.3 %collective-permute-start = (bf16[16,256]{1,0:T(8,128)(2,1)S(1)}, bf16[16,256]{1,0:T(8,128)(2,1)S(1)}, u32[]{:S(2)}, u32[]{:S(2)}) collective-permute-start(bf16[16,256]{1,0:T(8,128)(2,1)S(1)} %get-tuple-element.18), channel_id=1, source_target_pairs={{4,0},{8,4},{12,8},{16,12},{20,16},{24,20},{28,24},{5,1},{9,5},{13... | collective-permute-start | bytes 24584 | tf_op jit(solution)/shard_map/ppermute | solution.py:110
  2.9 0.7 broadcast_select_fusion.4
  3.7 2.8 %fusion.45 = f32[16,1,2,256]{3,1,2,0:T(1,128)S(1)} fusion(bf16[16,2,256,256]{3,2,1,0:T(8,128)(2,1)} %param.11, bf16[16,256,1,1]{1,0,2,3:T(8,128)(2,1)S(1)} %bitcast.138), kind=kOutput, calls=%fused_computation.82 | convolution fusion | flops 4194304 | bytes 4235264 | tf_op jit(solution)/shard_map/bsij,bi->bsj/dot_general | solution.py:88
  9.0 0.8 %all_to_all.24 = f32[8,1,5376]{2,1,0:T(1,128)} reshape(f32[8,5376]{1,0:T(8,128)S(1)} %pad_maximum_fusion) | data formatting | bytes 344064 | tf_op jit(solution)/shard_map/all_to_all | solution.py:117
  9.7 8.5 %all-to-all-start = ((f32[8,1,5376]{2,1,0:T(1,128)}), f32[8,1,5376]{2,1,0:T(1,128)S(1)}, u32[]{:S(2)}, u32[]{:S(2)}) async-start(f32[8,1,5376]{2,1,0:T(1,128)} %all_to_all.24), calls=%async_computation | async-start | bytes 344064 | tf_op jit(solution)/shard_map/all_to_all | solution.py:117
  18.9 3.1 %fusion = f32[16,256]{1,0:T(8,128)S(1)} fusion(bf16[16,2,256,256]{3,2,1,0:T(8,128)(2,1)} %param.11, f32[16,2,256]{2,1,0:T(2,128)S(1)} %mul.134), kind=kLoop, calls=%fused_computation.2 | loop fusion | flops 6287360 | bytes 4243456 | tf_op jit(solution)/shard_map/reduce_sum | solution.py:133
  22.0 3.9 %all-to-all-done = f32[8,1,5376]{2,1,0:T(1,128)S(1)} async-done(((f32[8,1,5376]{2,1,0:T(1,128)}), f32[8,1,5376]{2,1,0:T(1,128)S(1)}, u32[]{:S(2)}, u32[]{:S(2)}) %all-to-all-start) | async-done | bytes 172064 | tf_op jit(solution)/shard_map/all_to_all | solution.py:117
  27.3 1.6 %collective-permute-start.2 = (f32[21,256]{1,0:T(8,128)S(1)}, f32[21,256]{1,0:T(8,128)S(1)}, u32[]{:S(2)}, u32[]{:S(2)}) collective-permute-start(f32[21,256]{1,0:T(8,128)S(1)} %pad_maximum_fusion.1), channel_id=1, source_target_pairs={{0,2},{1,3},{2,0},{3,1},{4,6},{5,7},{6,4},{7,5},{8,10},{9,11},{10,... | collective-permute-start | bytes 64520 | tf_op jit(solution)/shard_map/ppermute | solution.py:13
  28.8 0.6 collective-permute-start.1
  29.5 1.7 %collective-permute-done.2 = f32[21,256]{1,0:T(8,128)S(1)} collective-permute-done((f32[21,256]{1,0:T(8,128)S(1)}, f32[21,256]{1,0:T(8,128)S(1)}, u32[]{:S(2)}, u32[]{:S(2)}) %collective-permute-start.2) | collective-permute-done | bytes 21536 | tf_op jit(solution)/shard_map/ppermute | solution.py:13
  31.2 0.9 %collective-permute-done.3 = f32[21,256]{1,0:T(8,128)S(1)} collective-permute-done((f32[21,256]{1,0:T(8,128)S(1)}, f32[21,256]{1,0:T(8,128)S(1)}, u32[]{:S(2)}, u32[]{:S(2)}) %collective-permute-start.3) | collective-permute-done | bytes 21536 | tf_op jit(solution)/shard_map/ppermute | solution.py:13
  33.0 8.9 %all_to_all.36 = f32[8,1,4]{2,1,0:T(1,128)S(1)} all-to-all(f32[8,1,4]{2,1,0:T(1,128)S(1)} %broadcast_in_dim.318), channel_id=1, replica_groups=mesh['box'=8,'rep'=4] {'box'}, dimensions={0} | all-to-all | bytes 256 | tf_op jit(solution)/shard_map/all_to_all | solution.py:36
  42.0 1.3 %collective-permute-start.4 = (bf16[16,256]{1,0:T(8,128)(2,1)S(1)}, bf16[16,256]{1,0:T(8,128)(2,1)S(1)}, u32[]{:S(2)}, u32[]{:S(2)}) collective-permute-start(bf16[16,256]{1,0:T(8,128)(2,1)S(1)} %get-tuple-element.5), channel_id=1, source_target_pairs={{4,0},{8,4},{12,8},{16,12},{20,16},{24,20},{28,24},{5,1},{9,5},{13... | collective-permute-start | bytes 24584 | tf_op jit(solution)/shard_map/ppermute | solution.py:110
  43.3 2.8 %fusion.43 = f32[16,1,2,256]{3,1,2,0:T(1,128)S(1)} fusion(bf16[16,2,256,256]{3,2,1,0:T(8,128)(2,1)} %param.11, bf16[16,256,1,1]{1,0,2,3:T(8,128)(2,1)S(1)} %bitcast.139), kind=kOutput, calls=%fused_computation.80 | convolution fusion | flops 4194304 | bytes 4235264 | tf_op jit(solution)/shard_map/bsij,bi->bsj/dot_general | solution.py:88
  47.8 0.8 %copy.49 = f32[8,1,5376]{2,1,0:T(1,128)} copy(f32[8,1,5376]{2,0,1:T(8,128)S(1)} %maximum_bitcast_fusion) | data formatting | bytes 344064 | tf_op jit(solution)/shard_map/all_to_all | solution.py:117
  48.6 3.9 %all-to-all-start.2 = ((f32[8,1,5376]{2,1,0:T(1,128)}), f32[8,1,5376]{2,1,0:T(1,128)S(1)}, u32[]{:S(2)}, u32[]{:S(2)}) async-start(f32[8,1,5376]{2,1,0:T(1,128)} %copy.49), calls=%async_computation.2 | async-start | bytes 344064 | tf_op jit(solution)/shard_map/all_to_all | solution.py:117
  52.8 3.1 %fusion.1 = f32[16,256]{1,0:T(8,128)S(1)} fusion(bf16[16,2,256,256]{3,2,1,0:T(8,128)(2,1)} %param.11, f32[16,2,256]{2,1,0:T(2,128)S(1)} %mul.158), kind=kLoop, calls=%fused_computation.3 | loop fusion | flops 6287360 | bytes 4243456 | tf_op jit(solution)/shard_map/reduce_sum | solution.py:133
  55.9 4.2 %all-to-all-done.2 = f32[8,1,5376]{2,1,0:T(1,128)S(1)} async-done(((f32[8,1,5376]{2,1,0:T(1,128)}), f32[8,1,5376]{2,1,0:T(1,128)S(1)}, u32[]{:S(2)}, u32[]{:S(2)}) %all-to-all-start.2) | async-done | bytes 172064 | tf_op jit(solution)/shard_map/all_to_all | solution.py:117
  61.5 0.9 %collective-permute-start.6 = (f32[21,256]{1,0:T(8,128)S(1)}, f32[21,256]{1,0:T(8,128)S(1)}, u32[]{:S(2)}, u32[]{:S(2)}) collective-permute-start(f32[21,256]{1,0:T(8,128)S(1)} %pad_maximum_fusion.2), channel_id=1, source_target_pairs={{0,2},{1,3},{2,0},{3,1},{4,6},{5,7},{6,4},{7,5},{8,10},{9,11},{10,... | collective-permute-start | bytes 64520 | tf_op jit(solution)/shard_map/ppermute | solution.py:13
  62.4 1.3 %collective-permute-start.5 = (f32[21,256]{1,0:T(8,128)S(1)}, f32[21,256]{1,0:T(8,128)S(1)}, u32[]{:S(2)}, u32[]{:S(2)}) collective-permute-start(f32[21,256]{1,0:T(8,128)S(1)} %pad_maximum_fusion.2), channel_id=1, source_target_pairs={{0,1},{1,0},{2,3},{3,2},{4,5},{5,4},{6,7},{7,6},{8,9},{9,8},{10,11... | collective-permute-start | bytes 64520 | tf_op jit(solution)/shard_map/ppermute | solution.py:13
  63.7 1.7 %collective-permute-done.6 = f32[21,256]{1,0:T(8,128)S(1)} collective-permute-done((f32[21,256]{1,0:T(8,128)S(1)}, f32[21,256]{1,0:T(8,128)S(1)}, u32[]{:S(2)}, u32[]{:S(2)}) %collective-permute-start.6) | collective-permute-done | bytes 21536 | tf_op jit(solution)/shard_map/ppermute | solution.py:13
  67.2 0.6 broadcast_in_dim.333
  67.9 8.8 %all_to_all.37 = f32[8,1,1]{2,1,0:T(1,128)S(1)} all-to-all(f32[8,1,1]{2,1,0:T(1,128)S(1)} %broadcast_in_dim.333), channel_id=1, replica_groups=mesh['box'=8,'rep'=4] {'box'}, dimensions={0} | all-to-all | bytes 64 | tf_op jit(solution)/shard_map/all_to_all | solution.py:36
  (140 shorter events, 11.1 us)
Async XLA Ops:
  0.6 7.5 %copy-start = (bf16[20,4,64,64]{3,2,1,0:T(8,128)(2,1)S(1)}, bf16[20,4,64,64]{3,2,1,0:T(8,128)(2,1)}, u32[]{:S(2)}) copy-start(bf16[20,4,64,64]{3,2,1,0:T(8,128)(2,1)} %param.16) | copy-start | bytes 1966084
  0.6 5.9 %copy-start.4 = (s32[16,2]{0,1:T(2,128)S(1)}, s32[16,2]{0,1:T(2,128)}, u32[]{:S(2)}) copy-start(s32[16,2]{0,1:T(2,128)} %param.12) | copy-start | bytes 388
  0.7 6.5 %copy-start.1 = (bf16[16,64,256]{2,1,0:T(8,128)(2,1)S(1)}, bf16[16,64,256]{2,1,0:T(8,128)(2,1)}, u32[]{:S(2)}) copy-start(bf16[16,64,256]{2,1,0:T(8,128)(2,1)} %param.13) | copy-start | bytes 1572868
  0.7 6.7 %copy-start.6 = (bf16[16,64,64]{2,1,0:T(8,128)(2,1)S(1)}, bf16[16,64,64]{2,1,0:T(8,128)(2,1)}, u32[]{:S(2)}) copy-start(bf16[16,64,64]{2,1,0:T(8,128)(2,1)} %param.14) | copy-start | bytes 393220
  0.7 6.9 %copy-start.5 = (s32[16]{0:T(128)S(1)}, s32[16]{0:T(128)}, u32[]{:S(2)}) copy-start(s32[16]{0:T(128)} %param.15) | copy-start | bytes 196
  1.6 17.1 %collective-permute-start = (bf16[16,256]{1,0:T(8,128)(2,1)S(1)}, bf16[16,256]{1,0:T(8,128)(2,1)S(1)}, u32[]{:S(2)}, u32[]{:S(2)}) collective-permute-start(bf16[16,256]{1,0:T(8,128)(2,1)S(1)} %get-tuple-element.18), channel_id=1, source_target_pairs={{4,0},{8,4},{12,8},{16,12},{20,16},{24,20},{28,24},{5,1},{9,5},{13... | collective-permute-start | bytes 24584 | tf_op jit(solution)/shard_map/ppermute | solution.py:110
  9.7 23.1 %copy-start.2 = (f32[16,256]{1,0:T(8,128)S(1)}, f32[16,256]{1,0:T(8,128)}, u32[]{:S(2)}) copy-start(f32[16,256]{1,0:T(8,128)} %param.9) | copy-start | bytes 49156
  9.7 23.1 %copy-start.3 = (f32[16,256]{1,0:T(8,128)S(1)}, f32[16,256]{1,0:T(8,128)}, u32[]{:S(2)}) copy-start(f32[16,256]{1,0:T(8,128)} %param.10) | copy-start | bytes 49156
  9.7 16.2 %all-to-all-start = ((f32[8,1,5376]{2,1,0:T(1,128)}), f32[8,1,5376]{2,1,0:T(1,128)S(1)}, u32[]{:S(2)}, u32[]{:S(2)}) async-start(f32[8,1,5376]{2,1,0:T(1,128)} %all_to_all.24), calls=%async_computation | async-start | bytes 344064 | tf_op jit(solution)/shard_map/all_to_all | solution.py:117
  27.3 3.9 %collective-permute-start.2 = (f32[21,256]{1,0:T(8,128)S(1)}, f32[21,256]{1,0:T(8,128)S(1)}, u32[]{:S(2)}, u32[]{:S(2)}) collective-permute-start(f32[21,256]{1,0:T(8,128)S(1)} %pad_maximum_fusion.1), channel_id=1, source_target_pairs={{0,2},{1,3},{2,0},{3,1},{4,6},{5,7},{6,4},{7,5},{8,10},{9,11},{10,... | collective-permute-start | bytes 64520 | tf_op jit(solution)/shard_map/ppermute | solution.py:13
  28.8 3.3 %collective-permute-start.3 = (f32[21,256]{1,0:T(8,128)S(1)}, f32[21,256]{1,0:T(8,128)S(1)}, u32[]{:S(2)}, u32[]{:S(2)}) collective-permute-start(f32[21,256]{1,0:T(8,128)S(1)} %pad_maximum_fusion.1), channel_id=1, source_target_pairs={{0,3},{1,2},{2,1},{3,0},{4,7},{5,6},{6,5},{7,4},{8,11},{9,10},{10,... | collective-permute-start | bytes 64520 | tf_op jit(solution)/shard_map/ppermute | solution.py:13
  28.8 3.3 %collective-permute-start.1 = (f32[21,256]{1,0:T(8,128)S(1)}, f32[21,256]{1,0:T(8,128)S(1)}, u32[]{:S(2)}, u32[]{:S(2)}) collective-permute-start(f32[21,256]{1,0:T(8,128)S(1)} %pad_maximum_fusion.1), channel_id=1, source_target_pairs={{0,1},{1,0},{2,3},{3,2},{4,5},{5,4},{6,7},{7,6},{8,9},{9,8},{10,11... | collective-permute-start | bytes 64520 | tf_op jit(solution)/shard_map/ppermute | solution.py:13
  42.0 10.6 %collective-permute-start.4 = (bf16[16,256]{1,0:T(8,128)(2,1)S(1)}, bf16[16,256]{1,0:T(8,128)(2,1)S(1)}, u32[]{:S(2)}, u32[]{:S(2)}) collective-permute-start(bf16[16,256]{1,0:T(8,128)(2,1)S(1)} %get-tuple-element.5), channel_id=1, source_target_pairs={{4,0},{8,4},{12,8},{16,12},{20,16},{24,20},{28,24},{5,1},{9,5},{13... | collective-permute-start | bytes 24584 | tf_op jit(solution)/shard_map/ppermute | solution.py:110
  48.6 11.5 %all-to-all-start.2 = ((f32[8,1,5376]{2,1,0:T(1,128)}), f32[8,1,5376]{2,1,0:T(1,128)S(1)}, u32[]{:S(2)}, u32[]{:S(2)}) async-start(f32[8,1,5376]{2,1,0:T(1,128)} %copy.49), calls=%async_computation.2 | async-start | bytes 344064 | tf_op jit(solution)/shard_map/all_to_all | solution.py:117
  61.5 3.9 %collective-permute-start.6 = (f32[21,256]{1,0:T(8,128)S(1)}, f32[21,256]{1,0:T(8,128)S(1)}, u32[]{:S(2)}, u32[]{:S(2)}) collective-permute-start(f32[21,256]{1,0:T(8,128)S(1)} %pad_maximum_fusion.2), channel_id=1, source_target_pairs={{0,2},{1,3},{2,0},{3,1},{4,6},{5,7},{6,4},{7,5},{8,10},{9,11},{10,... | collective-permute-start | bytes 64520 | tf_op jit(solution)/shard_map/ppermute | solution.py:13
  62.4 3.5 %collective-permute-start.7 = (f32[21,256]{1,0:T(8,128)S(1)}, f32[21,256]{1,0:T(8,128)S(1)}, u32[]{:S(2)}, u32[]{:S(2)}) collective-permute-start(f32[21,256]{1,0:T(8,128)S(1)} %pad_maximum_fusion.2), channel_id=1, source_target_pairs={{0,3},{1,2},{2,1},{3,0},{4,7},{5,6},{6,5},{7,4},{8,11},{9,10},{10,... | collective-permute-start | bytes 64520 | tf_op jit(solution)/shard_map/ppermute | solution.py:13
  62.4 3.5 %collective-permute-start.5 = (f32[21,256]{1,0:T(8,128)S(1)}, f32[21,256]{1,0:T(8,128)S(1)}, u32[]{:S(2)}, u32[]{:S(2)}) collective-permute-start(f32[21,256]{1,0:T(8,128)S(1)} %pad_maximum_fusion.2), channel_id=1, source_target_pairs={{0,1},{1,0},{2,3},{3,2},{4,5},{5,4},{6,7},{7,6},{8,9},{9,8},{10,11... | collective-permute-start | bytes 64520 | tf_op jit(solution)/shard_map/ppermute | solution.py:13

commit v21 on v16

--- a/solution.py
+++ b/solution.py
@@ -135,8 +135,9 @@
         partner_coef = jnp.dot(
             far_pick.T.astype(jnp.bfloat16), every_coef, preferred_element_type=jnp.float32
         ).astype(jnp.bfloat16).reshape(node_count, -1, rank_width)
-        far_forward = jnp.einsum(
-            "nsab,nsb->na", coupling, partner_coef, preferred_element_type=jnp.float32
+        far_forward = jnp.sum(
+            coupling.astype(jnp.float32) * partner_coef.astype(jnp.float32)[:, :, None, :],
+            axis=(1, 3),
         )
         far_part = far_forward + spread[box_rank] + mirror_in
         both = rep_sum(jnp.concatenate([near_part.reshape(-1), far_part.reshape(-1)]))

time: 78 us -> 77.9 us (level)
  matrix products: 10.3 us -> 9.38 us
  other arithmetic: 10.9 us -> 11.7 us
    dot_general x2 -> x0, matrix products: 0.87 us -> none  [local(): jnp.einsum('nsab,nsb->na', coupling, partner_coef, preferred_element_type...]
    reduce_sum x0 -> x2, other arithmetic: none -> 0.83 us  [local(): jnp.sum(coupling.astype(jnp.float32) * partner_coef.astype(jnp.float32)[:...]
  transfers between devices with their start and end apart: 10 -> 10, of which waited for: 6 -> 6; matrix products, arithmetic and copies ran while one was open for 23% -> 24% of each run, Pallas kernels for 0% -> 0%
where the time goes in v21:
time: 77.9 us; the launch traced here: 77.3 us
  starting transfers between devices  19.3 us (25%)
  blocking collectives  17.8 us (23%)
  waiting for transfers between devices  12.7 us (16%)
  other arithmetic  11.7 us (15%)
  matrix products  9.38 us (12%)
  local copies, waits for them, and re-layouts  5.09 us (7%)
  between operations  1.28 us (2%)
    all_to_all x2, blocking collectives, box_sum(): got = lax.all_to_all(sent, 'box', 0, 0, tiled=True)  17.8 us
    all_to_all x2, starting transfers between devices, local(): lax.all_to_all(jnp.concatenate([far_send.reshape(box_devices, far_size),...  12.3 us
    all_to_all x2, waiting for transfers between devices, local(): lax.all_to_all(jnp.concatenate([far_send.reshape(box_devices, far_size),...  7.96 us
    reduce_sum x2, other arithmetic, local(): forward = jnp.sum(near_tiles.astype(jnp.float32) * near_in, axis=(1, 3))  6.19 us
    dot_general x2, matrix products, local(): jnp.einsum('bsij,bi->bsj', near_tiles, rounded, preferred_element_type=jn...  5.66 us
    ppermute x6, waiting for transfers between devices, rep_sum(): lax.ppermute(vector, 'rep', [(i, i ^ mask) for i in range(count)])  4.77 us
    ppermute x6, starting transfers between devices, rep_sum(): lax.ppermute(vector, 'rep', [(i, i ^ mask) for i in range(count)])  4.41 us
    ppermute x2, starting transfers between devices, local(): lax.ppermute(rounded, 'box', [(i, i - 1) for i in range(1, box_devices)])  2.57 us
  transfers between devices with their start and end apart: 10, of which 6 were waited for; matrix products, arithmetic and copies ran while one was open for 24% of the time, Pallas kernels for 0%

profile of v21, /device:TPU:0, one launch (start us, length us, event | category | flops | bytes accessed | tf_op | source)
XLA Modules:
  0.0 77.3 jit_solution(9522881975498811471)
XLA Ops:
  0.7 0.9 %fusion.97 = (f32[16,256]{1,0:T(8,128)S(1)}, bf16[16,256]{1,0:T(8,128)(2,1)S(1)}) fusion(f32[16,256]{1,0:T(8,128)} %param.9), kind=kLoop, calls=%fused_computation.173 | loop fusion | flops 8192 | bytes 40960 | tf_op jit(solution)/shard_map/convert_element_type | solution.py:95
  1.6 1.3 %collective-permute-start = (bf16[16,256]{1,0:T(8,128)(2,1)S(1)}, bf16[16,256]{1,0:T(8,128)(2,1)S(1)}, u32[]{:S(2)}, u32[]{:S(2)}) collective-permute-start(bf16[16,256]{1,0:T(8,128)(2,1)S(1)} %get-tuple-element.18), channel_id=1, source_target_pairs={{4,0},{8,4},{12,8},{16,12},{20,16},{24,20},{28,24},{5,1},{9,5},{13... | collective-permute-start | bytes 24584 | tf_op jit(solution)/shard_map/ppermute | solution.py:110
  2.9 0.7 broadcast_select_fusion.4
  3.7 2.8 %fusion.45 = f32[16,1,2,256]{3,1,2,0:T(1,128)S(1)} fusion(bf16[16,2,256,256]{3,2,1,0:T(8,128)(2,1)} %param.11, bf16[16,256,1,1]{1,0,2,3:T(8,128)(2,1)S(1)} %bitcast.116), kind=kOutput, calls=%fused_computation.84 | convolution fusion | flops 4194304 | bytes 4235264 | tf_op jit(solution)/shard_map/bsij,bi->bsj/dot_general | solution.py:88
  9.0 0.8 %all_to_all.24 = f32[8,1,5376]{2,1,0:T(1,128)} reshape(f32[8,5376]{1,0:T(8,128)S(1)} %pad_maximum_fusion) | data formatting | bytes 344064 | tf_op jit(solution)/shard_map/all_to_all | solution.py:117
  9.7 8.4 %all-to-all-start = ((f32[8,1,5376]{2,1,0:T(1,128)}), f32[8,1,5376]{2,1,0:T(1,128)S(1)}, u32[]{:S(2)}, u32[]{:S(2)}) async-start(f32[8,1,5376]{2,1,0:T(1,128)} %all_to_all.24), calls=%async_computation | async-start | bytes 344064 | tf_op jit(solution)/shard_map/all_to_all | solution.py:117
  18.9 3.1 %fusion = f32[16,256]{1,0:T(8,128)S(1)} fusion(bf16[16,2,256,256]{3,2,1,0:T(8,128)(2,1)} %param.11, f32[16,2,256]{2,1,0:T(2,128)S(1)} %mul.150), kind=kLoop, calls=%fused_computation.2 | loop fusion | flops 6287360 | bytes 4243456 | tf_op jit(solution)/shard_map/reduce_sum | solution.py:133
  22.0 3.8 %all-to-all-done = f32[8,1,5376]{2,1,0:T(1,128)S(1)} async-done(((f32[8,1,5376]{2,1,0:T(1,128)}), f32[8,1,5376]{2,1,0:T(1,128)S(1)}, u32[]{:S(2)}, u32[]{:S(2)}) %all-to-all-start) | async-done | bytes 172064 | tf_op jit(solution)/shard_map/all_to_all | solution.py:117
  27.0 1.6 %collective-permute-start.2 = (f32[5376]{0:T(1024)S(1)}, f32[5376]{0:T(1024)S(1)}, u32[]{:S(2)}, u32[]{:S(2)}) collective-permute-start(f32[5376]{0:T(1024)S(1)} %pad_maximum_fusion.1), channel_id=1, source_target_pairs={{0,2},{1,3},{2,0},{3,1},{4,6},{5,7},{6,4},{7,5},{8,10},{9,11},{10,... | collective-permute-start | bytes 64520 | tf_op jit(solution)/shard_map/ppermute | solution.py:13
  28.6 0.6 collective-permute-start.1
  29.2 1.7 %collective-permute-done.2 = f32[5376]{0:T(1024)S(1)} collective-permute-done((f32[5376]{0:T(1024)S(1)}, f32[5376]{0:T(1024)S(1)}, u32[]{:S(2)}, u32[]{:S(2)}) %collective-permute-start.2) | collective-permute-done | bytes 21536 | tf_op jit(solution)/shard_map/ppermute | solution.py:13
  30.9 0.9 %collective-permute-done.3 = f32[5376]{0:T(1024)S(1)} collective-permute-done((f32[5376]{0:T(1024)S(1)}, f32[5376]{0:T(1024)S(1)}, u32[]{:S(2)}, u32[]{:S(2)}) %collective-permute-start.3) | collective-permute-done | bytes 21536 | tf_op jit(solution)/shard_map/ppermute | solution.py:13
  32.7 8.9 %all_to_all.36 = f32[8,1,4]{2,1,0:T(1,128)S(1)} all-to-all(f32[8,1,4]{2,1,0:T(1,128)S(1)} %broadcast_in_dim.300), channel_id=1, replica_groups=mesh['box'=8,'rep'=4] {'box'}, dimensions={0} | all-to-all | bytes 256 | tf_op jit(solution)/shard_map/all_to_all | solution.py:36
  41.8 1.3 %collective-permute-start.4 = (bf16[16,256]{1,0:T(8,128)(2,1)S(1)}, bf16[16,256]{1,0:T(8,128)(2,1)S(1)}, u32[]{:S(2)}, u32[]{:S(2)}) collective-permute-start(bf16[16,256]{1,0:T(8,128)(2,1)S(1)} %get-tuple-element.5), channel_id=1, source_target_pairs={{4,0},{8,4},{12,8},{16,12},{20,16},{24,20},{28,24},{5,1},{9,5},{13... | collective-permute-start | bytes 24584 | tf_op jit(solution)/shard_map/ppermute | solution.py:110
  43.1 2.8 %fusion.43 = f32[16,1,2,256]{3,1,2,0:T(1,128)S(1)} fusion(bf16[16,2,256,256]{3,2,1,0:T(8,128)(2,1)} %param.11, bf16[16,256,1,1]{1,0,2,3:T(8,128)(2,1)S(1)} %bitcast.117), kind=kOutput, calls=%fused_computation.82 | convolution fusion | flops 4194304 | bytes 4235264 | tf_op jit(solution)/shard_map/bsij,bi->bsj/dot_general | solution.py:88
  47.5 0.8 %copy.51 = f32[8,1,5376]{2,1,0:T(1,128)} copy(f32[8,1,5376]{2,0,1:T(8,128)S(1)} %maximum_bitcast_fusion) | data formatting | bytes 344064 | tf_op jit(solution)/shard_map/all_to_all | solution.py:117
  48.4 3.9 %all-to-all-start.2 = ((f32[8,1,5376]{2,1,0:T(1,128)}), f32[8,1,5376]{2,1,0:T(1,128)S(1)}, u32[]{:S(2)}, u32[]{:S(2)}) async-start(f32[8,1,5376]{2,1,0:T(1,128)} %copy.51), calls=%async_computation.2 | async-start | bytes 344064 | tf_op jit(solution)/shard_map/all_to_all | solution.py:117
  52.6 3.1 %fusion.1 = f32[16,256]{1,0:T(8,128)S(1)} fusion(bf16[16,2,256,256]{3,2,1,0:T(8,128)(2,1)} %param.11, f32[16,2,256]{2,1,0:T(2,128)S(1)} %mul.176), kind=kLoop, calls=%fused_computation.3 | loop fusion | flops 6287360 | bytes 4243456 | tf_op jit(solution)/shard_map/reduce_sum | solution.py:133
  55.7 4.2 %all-to-all-done.2 = f32[8,1,5376]{2,1,0:T(1,128)S(1)} async-done(((f32[8,1,5376]{2,1,0:T(1,128)}), f32[8,1,5376]{2,1,0:T(1,128)S(1)}, u32[]{:S(2)}, u32[]{:S(2)}) %all-to-all-start.2) | async-done | bytes 172064 | tf_op jit(solution)/shard_map/all_to_all | solution.py:117
  61.2 0.9 %collective-permute-start.6 = (f32[5376]{0:T(1024)S(1)}, f32[5376]{0:T(1024)S(1)}, u32[]{:S(2)}, u32[]{:S(2)}) collective-permute-start(f32[5376]{0:T(1024)S(1)} %pad_maximum_fusion.2), channel_id=1, source_target_pairs={{0,2},{1,3},{2,0},{3,1},{4,6},{5,7},{6,4},{7,5},{8,10},{9,11},{10,... | collective-permute-start | bytes 64520 | tf_op jit(solution)/shard_map/ppermute | solution.py:13
  62.0 1.3 %collective-permute-start.5 = (f32[5376]{0:T(1024)S(1)}, f32[5376]{0:T(1024)S(1)}, u32[]{:S(2)}, u32[]{:S(2)}) collective-permute-start(f32[5376]{0:T(1024)S(1)} %pad_maximum_fusion.2), channel_id=1, source_target_pairs={{0,1},{1,0},{2,3},{3,2},{4,5},{5,4},{6,7},{7,6},{8,9},{9,8},{10,11... | collective-permute-start | bytes 64520 | tf_op jit(solution)/shard_map/ppermute | solution.py:13
  63.4 1.7 %collective-permute-done.6 = f32[5376]{0:T(1024)S(1)} collective-permute-done((f32[5376]{0:T(1024)S(1)}, f32[5376]{0:T(1024)S(1)}, u32[]{:S(2)}, u32[]{:S(2)}) %collective-permute-start.6) | collective-permute-done | bytes 21536 | tf_op jit(solution)/shard_map/ppermute | solution.py:13
  66.9 0.6 broadcast_in_dim.311
  67.5 8.8 %all_to_all.37 = f32[8,1,1]{2,1,0:T(1,128)S(1)} all-to-all(f32[8,1,1]{2,1,0:T(1,128)S(1)} %broadcast_in_dim.311), channel_id=1, replica_groups=mesh['box'=8,'rep'=4] {'box'}, dimensions={0} | all-to-all | bytes 64 | tf_op jit(solution)/shard_map/all_to_all | solution.py:36
  (148 shorter events, 11.0 us)
Async XLA Ops:
  0.6 6.8 %copy-start = (bf16[16,64,64]{2,1,0:T(8,128)(2,1)S(1)}, bf16[16,64,64]{2,1,0:T(8,128)(2,1)}, u32[]{:S(2)}) copy-start(bf16[16,64,64]{2,1,0:T(8,128)(2,1)} %param.14) | copy-start | bytes 393220
  0.6 5.9 %copy-start.5 = (s32[16,2]{0,1:T(2,128)S(1)}, s32[16,2]{0,1:T(2,128)}, u32[]{:S(2)}) copy-start(s32[16,2]{0,1:T(2,128)} %param.12) | copy-start | bytes 388
  0.7 6.5 %copy-start.2 = (bf16[16,64,256]{2,1,0:T(8,128)(2,1)S(1)}, bf16[16,64,256]{2,1,0:T(8,128)(2,1)}, u32[]{:S(2)}) copy-start(bf16[16,64,256]{2,1,0:T(8,128)(2,1)} %param.13) | copy-start | bytes 1572868
  0.7 6.9 %copy-start.6 = (s32[16]{0:T(128)S(1)}, s32[16]{0:T(128)}, u32[]{:S(2)}) copy-start(s32[16]{0:T(128)} %param.15) | copy-start | bytes 196
  0.7 7.5 %copy-start.1 = (bf16[20,4,64,64]{3,2,1,0:T(8,128)(2,1)S(1)}, bf16[20,4,64,64]{3,2,1,0:T(8,128)(2,1)}, u32[]{:S(2)}) copy-start(bf16[20,4,64,64]{3,2,1,0:T(8,128)(2,1)} %param.16) | copy-start | bytes 1966084
  1.6 17.1 %collective-permute-start = (bf16[16,256]{1,0:T(8,128)(2,1)S(1)}, bf16[16,256]{1,0:T(8,128)(2,1)S(1)}, u32[]{:S(2)}, u32[]{:S(2)}) collective-permute-start(bf16[16,256]{1,0:T(8,128)(2,1)S(1)} %get-tuple-element.18), channel_id=1, source_target_pairs={{4,0},{8,4},{12,8},{16,12},{20,16},{24,20},{28,24},{5,1},{9,5},{13... | collective-permute-start | bytes 24584 | tf_op jit(solution)/shard_map/ppermute | solution.py:110
  9.7 16.0 %all-to-all-start = ((f32[8,1,5376]{2,1,0:T(1,128)}), f32[8,1,5376]{2,1,0:T(1,128)S(1)}, u32[]{:S(2)}, u32[]{:S(2)}) async-start(f32[8,1,5376]{2,1,0:T(1,128)} %all_to_all.24), calls=%async_computation | async-start | bytes 344064 | tf_op jit(solution)/shard_map/all_to_all | solution.py:117
  18.1 14.4 %copy-start.3 = (f32[16,256]{1,0:T(8,128)S(1)}, f32[16,256]{1,0:T(8,128)}, u32[]{:S(2)}) copy-start(f32[16,256]{1,0:T(8,128)} %param.9) | copy-start | bytes 49156
  18.2 14.4 %copy-start.4 = (f32[16,256]{1,0:T(8,128)S(1)}, f32[16,256]{1,0:T(8,128)}, u32[]{:S(2)}) copy-start(f32[16,256]{1,0:T(8,128)} %param.10) | copy-start | bytes 49156
  27.0 3.9 %collective-permute-start.2 = (f32[5376]{0:T(1024)S(1)}, f32[5376]{0:T(1024)S(1)}, u32[]{:S(2)}, u32[]{:S(2)}) collective-permute-start(f32[5376]{0:T(1024)S(1)} %pad_maximum_fusion.1), channel_id=1, source_target_pairs={{0,2},{1,3},{2,0},{3,1},{4,6},{5,7},{6,4},{7,5},{8,10},{9,11},{10,... | collective-permute-start | bytes 64520 | tf_op jit(solution)/shard_map/ppermute | solution.py:13
  28.6 3.3 %collective-permute-start.3 = (f32[5376]{0:T(1024)S(1)}, f32[5376]{0:T(1024)S(1)}, u32[]{:S(2)}, u32[]{:S(2)}) collective-permute-start(f32[5376]{0:T(1024)S(1)} %pad_maximum_fusion.1), channel_id=1, source_target_pairs={{0,3},{1,2},{2,1},{3,0},{4,7},{5,6},{6,5},{7,4},{8,11},{9,10},{10,... | collective-permute-start | bytes 64520 | tf_op jit(solution)/shard_map/ppermute | solution.py:13
  28.6 3.3 %collective-permute-start.1 = (f32[5376]{0:T(1024)S(1)}, f32[5376]{0:T(1024)S(1)}, u32[]{:S(2)}, u32[]{:S(2)}) collective-permute-start(f32[5376]{0:T(1024)S(1)} %pad_maximum_fusion.1), channel_id=1, source_target_pairs={{0,1},{1,0},{2,3},{3,2},{4,5},{5,4},{6,7},{7,6},{8,9},{9,8},{10,11... | collective-permute-start | bytes 64520 | tf_op jit(solution)/shard_map/ppermute | solution.py:13
  41.8 10.6 %collective-permute-start.4 = (bf16[16,256]{1,0:T(8,128)(2,1)S(1)}, bf16[16,256]{1,0:T(8,128)(2,1)S(1)}, u32[]{:S(2)}, u32[]{:S(2)}) collective-permute-start(bf16[16,256]{1,0:T(8,128)(2,1)S(1)} %get-tuple-element.5), channel_id=1, source_target_pairs={{4,0},{8,4},{12,8},{16,12},{20,16},{24,20},{28,24},{5,1},{9,5},{13... | collective-permute-start | bytes 24584 | tf_op jit(solution)/shard_map/ppermute | solution.py:110
  48.4 11.5 %all-to-all-start.2 = ((f32[8,1,5376]{2,1,0:T(1,128)}), f32[8,1,5376]{2,1,0:T(1,128)S(1)}, u32[]{:S(2)}, u32[]{:S(2)}) async-start(f32[8,1,5376]{2,1,0:T(1,128)} %copy.51), calls=%async_computation.2 | async-start | bytes 344064 | tf_op jit(solution)/shard_map/all_to_all | solution.py:117
  61.2 3.9 %collective-permute-start.6 = (f32[5376]{0:T(1024)S(1)}, f32[5376]{0:T(1024)S(1)}, u32[]{:S(2)}, u32[]{:S(2)}) collective-permute-start(f32[5376]{0:T(1024)S(1)} %pad_maximum_fusion.2), channel_id=1, source_target_pairs={{0,2},{1,3},{2,0},{3,1},{4,6},{5,7},{6,4},{7,5},{8,10},{9,11},{10,... | collective-permute-start | bytes 64520 | tf_op jit(solution)/shard_map/ppermute | solution.py:13
  62.0 3.5 %collective-permute-start.7 = (f32[5376]{0:T(1024)S(1)}, f32[5376]{0:T(1024)S(1)}, u32[]{:S(2)}, u32[]{:S(2)}) collective-permute-start(f32[5376]{0:T(1024)S(1)} %pad_maximum_fusion.2), channel_id=1, source_target_pairs={{0,3},{1,2},{2,1},{3,0},{4,7},{5,6},{6,5},{7,4},{8,11},{9,10},{10,... | collective-permute-start | bytes 64520 | tf_op jit(solution)/shard_map/ppermute | solution.py:13
  62.0 3.5 %collective-permute-start.5 = (f32[5376]{0:T(1024)S(1)}, f32[5376]{0:T(1024)S(1)}, u32[]{:S(2)}, u32[]{:S(2)}) collective-permute-start(f32[5376]{0:T(1024)S(1)} %pad_maximum_fusion.2), channel_id=1, source_target_pairs={{0,1},{1,0},{2,3},{3,2},{4,5},{5,4},{6,7},{7,6},{8,9},{9,8},{10,11... | collective-permute-start | bytes 64520 | tf_op jit(solution)/shard_map/ppermute | solution.py:13

commit v22 on v16

--- a/solution.py
+++ b/solution.py
@@ -94,7 +94,9 @@
         leaf_coef = jnp.sum(
             leaf_bases.astype(jnp.float32) * rounded.astype(jnp.float32)[:, None, :], axis=2
         ).astype(jnp.bfloat16)
-        upward = jnp.einsum("brq,br->bq", transfer, leaf_coef, preferred_element_type=jnp.float32)
+        upward = jnp.sum(
+            transfer.astype(jnp.float32) * leaf_coef.astype(jnp.float32)[:, :, None], axis=1
+        )
         group_coef = jnp.dot(parent_onehot, upward, precision=lax.Precision.HIGHEST).astype(
             jnp.bfloat16
         )

time: 78 us -> 78.1 us (level)
  transfers between devices with their start and end apart: 10 -> 10, of which waited for: 6 -> 6; matrix products, arithmetic and copies ran while one was open for 23% -> 24% of each run, Pallas kernels for 0% -> 0%
where the time goes in v22:
time: 78.1 us; the launch traced here: 77.5 us
  starting transfers between devices  19.2 us (25%)
  blocking collectives  17.8 us (23%)
  waiting for transfers between devices  12.9 us (17%)
  other arithmetic  11.3 us (14%)
  matrix products  9.9 us (13%)
  local copies, waits for them, and re-layouts  5.11 us (7%)
  between operations  1.33 us (2%)
    all_to_all x2, blocking collectives, box_sum(): got = lax.all_to_all(sent, 'box', 0, 0, tiled=True)  17.8 us
    all_to_all x2, starting transfers between devices, local(): lax.all_to_all(jnp.concatenate([far_send.reshape(box_devices, far_size),...  12.3 us
    all_to_all x2, waiting for transfers between devices, local(): lax.all_to_all(jnp.concatenate([far_send.reshape(box_devices, far_size),...  8.12 us
    reduce_sum x2, other arithmetic, local(): forward = jnp.sum(near_tiles.astype(jnp.float32) * near_in, axis=(1, 3))  6.19 us
    dot_general x2, matrix products, local(): jnp.einsum('bsij,bi->bsj', near_tiles, rounded, preferred_element_type=jn...  5.66 us
    ppermute x6, waiting for transfers between devices, rep_sum(): lax.ppermute(vector, 'rep', [(i, i ^ mask) for i in range(count)])  4.77 us
    ppermute x6, starting transfers between devices, rep_sum(): lax.ppermute(vector, 'rep', [(i, i ^ mask) for i in range(count)])  4.35 us
    ppermute x2, starting transfers between devices, local(): lax.ppermute(rounded, 'box', [(i, i - 1) for i in range(1, box_devices)])  2.57 us
  transfers between devices with their start and end apart: 10, of which 6 were waited for; matrix products, arithmetic and copies ran while one was open for 24% of the time, Pallas kernels for 0%

profile of v22, /device:TPU:0, one launch (start us, length us, event | category | flops | bytes accessed | tf_op | source)
XLA Modules:
  0.0 77.5 jit_solution(3118928746594448503)
XLA Ops:
  0.7 0.9 %fusion.97 = (f32[16,256]{1,0:T(8,128)S(1)}, bf16[16,256]{1,0:T(8,128)(2,1)S(1)}) fusion(f32[16,256]{1,0:T(8,128)} %param.9), kind=kLoop, calls=%fused_computation.173 | loop fusion | flops 8192 | bytes 40960 | tf_op jit(solution)/shard_map/convert_element_type | solution.py:95
  1.6 1.3 %collective-permute-start = (bf16[16,256]{1,0:T(8,128)(2,1)S(1)}, bf16[16,256]{1,0:T(8,128)(2,1)S(1)}, u32[]{:S(2)}, u32[]{:S(2)}) collective-permute-start(bf16[16,256]{1,0:T(8,128)(2,1)S(1)} %get-tuple-element.18), channel_id=1, source_target_pairs={{4,0},{8,4},{12,8},{16,12},{20,16},{24,20},{28,24},{5,1},{9,5},{13... | collective-permute-start | bytes 24584 | tf_op jit(solution)/shard_map/ppermute | solution.py:112
  2.9 0.7 broadcast_select_fusion.4
  3.7 2.8 %fusion.47 = f32[16,1,2,256]{3,1,2,0:T(1,128)S(1)} fusion(bf16[16,2,256,256]{3,2,1,0:T(8,128)(2,1)} %param.11, bf16[16,256,1,1]{1,0,2,3:T(8,128)(2,1)S(1)} %bitcast.120), kind=kOutput, calls=%fused_computation.84 | convolution fusion | flops 4194304 | bytes 4235264 | tf_op jit(solution)/shard_map/bsij,bi->bsj/dot_general | solution.py:88
  9.0 0.8 %all_to_all.24 = f32[8,1,5376]{2,1,0:T(1,128)} reshape(f32[8,5376]{1,0:T(8,128)S(1)} %pad_maximum_fusion) | data formatting | bytes 344064 | tf_op jit(solution)/shard_map/all_to_all | solution.py:119
  9.8 8.4 %all-to-all-start = ((f32[8,1,5376]{2,1,0:T(1,128)}), f32[8,1,5376]{2,1,0:T(1,128)S(1)}, u32[]{:S(2)}, u32[]{:S(2)}) async-start(f32[8,1,5376]{2,1,0:T(1,128)} %all_to_all.24), calls=%async_computation | async-start | bytes 344064 | tf_op jit(solution)/shard_map/all_to_all | solution.py:119
  18.9 3.1 %fusion = f32[16,256]{1,0:T(8,128)S(1)} fusion(bf16[16,2,256,256]{3,2,1,0:T(8,128)(2,1)} %param.11, f32[16,2,256]{2,1,0:T(2,128)S(1)} %mul.150), kind=kLoop, calls=%fused_computation.2 | loop fusion | flops 6287360 | bytes 4243456 | tf_op jit(solution)/shard_map/reduce_sum | solution.py:135
  22.0 3.9 %all-to-all-done = f32[8,1,5376]{2,1,0:T(1,128)S(1)} async-done(((f32[8,1,5376]{2,1,0:T(1,128)}), f32[8,1,5376]{2,1,0:T(1,128)S(1)}, u32[]{:S(2)}, u32[]{:S(2)}) %all-to-all-start) | async-done | bytes 172064 | tf_op jit(solution)/shard_map/all_to_all | solution.py:119
  27.2 1.5 %collective-permute-start.2 = (f32[5376]{0:T(1024)S(1)}, f32[5376]{0:T(1024)S(1)}, u32[]{:S(2)}, u32[]{:S(2)}) collective-permute-start(f32[5376]{0:T(1024)S(1)} %constant_dynamic-update-slice_fusion), channel_id=1, source_target_pairs={{0,2},{1,3},{2,0},{3,1},{4,6},{5,7},{6,4},{7,5},{8,10},{9,11},{10,... | collective-permute-start | bytes 64520 | tf_op jit(solution)/shard_map/ppermute | solution.py:13
  28.7 0.6 collective-permute-start.1
  29.4 1.7 %collective-permute-done.2 = f32[5376]{0:T(1024)S(1)} collective-permute-done((f32[5376]{0:T(1024)S(1)}, f32[5376]{0:T(1024)S(1)}, u32[]{:S(2)}, u32[]{:S(2)}) %collective-permute-start.2) | collective-permute-done | bytes 21536 | tf_op jit(solution)/shard_map/ppermute | solution.py:13
  31.1 0.9 %collective-permute-done.3 = f32[5376]{0:T(1024)S(1)} collective-permute-done((f32[5376]{0:T(1024)S(1)}, f32[5376]{0:T(1024)S(1)}, u32[]{:S(2)}, u32[]{:S(2)}) %collective-permute-start.3) | collective-permute-done | bytes 21536 | tf_op jit(solution)/shard_map/ppermute | solution.py:13
  32.9 8.9 %all_to_all.36 = f32[8,1,4]{2,1,0:T(1,128)S(1)} all-to-all(f32[8,1,4]{2,1,0:T(1,128)S(1)} %broadcast_in_dim.300), channel_id=1, replica_groups=mesh['box'=8,'rep'=4] {'box'}, dimensions={0} | all-to-all | bytes 256 | tf_op jit(solution)/shard_map/all_to_all | solution.py:36
  41.9 1.3 %collective-permute-start.4 = (bf16[16,256]{1,0:T(8,128)(2,1)S(1)}, bf16[16,256]{1,0:T(8,128)(2,1)S(1)}, u32[]{:S(2)}, u32[]{:S(2)}) collective-permute-start(bf16[16,256]{1,0:T(8,128)(2,1)S(1)} %get-tuple-element.5), channel_id=1, source_target_pairs={{4,0},{8,4},{12,8},{16,12},{20,16},{24,20},{28,24},{5,1},{9,5},{13... | collective-permute-start | bytes 24584 | tf_op jit(solution)/shard_map/ppermute | solution.py:112
  43.2 2.8 %fusion.45 = f32[16,1,2,256]{3,1,2,0:T(1,128)S(1)} fusion(bf16[16,2,256,256]{3,2,1,0:T(8,128)(2,1)} %param.11, bf16[16,256,1,1]{1,0,2,3:T(8,128)(2,1)S(1)} %bitcast.121), kind=kOutput, calls=%fused_computation.82 | convolution fusion | flops 4194304 | bytes 4235264 | tf_op jit(solution)/shard_map/bsij,bi->bsj/dot_general | solution.py:88
  47.7 0.8 %copy.49 = f32[8,1,5376]{2,1,0:T(1,128)} copy(f32[8,1,5376]{2,0,1:T(8,128)S(1)} %maximum_bitcast_fusion) | data formatting | bytes 344064 | tf_op jit(solution)/shard_map/all_to_all | solution.py:119
  48.6 3.9 %all-to-all-start.2 = ((f32[8,1,5376]{2,1,0:T(1,128)}), f32[8,1,5376]{2,1,0:T(1,128)S(1)}, u32[]{:S(2)}, u32[]{:S(2)}) async-start(f32[8,1,5376]{2,1,0:T(1,128)} %copy.49), calls=%async_computation.2 | async-start | bytes 344064 | tf_op jit(solution)/shard_map/all_to_all | solution.py:119
  52.8 3.1 %fusion.1 = f32[16,256]{1,0:T(8,128)S(1)} fusion(bf16[16,2,256,256]{3,2,1,0:T(8,128)(2,1)} %param.11, f32[16,2,256]{2,1,0:T(2,128)S(1)} %mul.176), kind=kLoop, calls=%fused_computation.3 | loop fusion | flops 6287360 | bytes 4243456 | tf_op jit(solution)/shard_map/reduce_sum | solution.py:135
  55.9 4.2 %all-to-all-done.2 = f32[8,1,5376]{2,1,0:T(1,128)S(1)} async-done(((f32[8,1,5376]{2,1,0:T(1,128)}), f32[8,1,5376]{2,1,0:T(1,128)S(1)}, u32[]{:S(2)}, u32[]{:S(2)}) %all-to-all-start.2) | async-done | bytes 172064 | tf_op jit(solution)/shard_map/all_to_all | solution.py:119
  61.5 0.8 %collective-permute-start.6 = (f32[5376]{0:T(1024)S(1)}, f32[5376]{0:T(1024)S(1)}, u32[]{:S(2)}, u32[]{:S(2)}) collective-permute-start(f32[5376]{0:T(1024)S(1)} %constant_dynamic-update-slice_fusion.1), channel_id=1, source_target_pairs={{0,2},{1,3},{2,0},{3,1},{4,6},{5,7},{6,4},{7,5},{8,10},{9,11},{10,... | collective-permute-start | bytes 64520 | tf_op jit(solution)/shard_map/ppermute | solution.py:13
  62.3 1.3 %collective-permute-start.5 = (f32[5376]{0:T(1024)S(1)}, f32[5376]{0:T(1024)S(1)}, u32[]{:S(2)}, u32[]{:S(2)}) collective-permute-start(f32[5376]{0:T(1024)S(1)} %constant_dynamic-update-slice_fusion.1), channel_id=1, source_target_pairs={{0,1},{1,0},{2,3},{3,2},{4,5},{5,4},{6,7},{7,6},{8,9},{9,8},{10,11... | collective-permute-start | bytes 64520 | tf_op jit(solution)/shard_map/ppermute | solution.py:13
  63.6 1.7 %collective-permute-done.6 = f32[5376]{0:T(1024)S(1)} collective-permute-done((f32[5376]{0:T(1024)S(1)}, f32[5376]{0:T(1024)S(1)}, u32[]{:S(2)}, u32[]{:S(2)}) %collective-permute-start.6) | collective-permute-done | bytes 21536 | tf_op jit(solution)/shard_map/ppermute | solution.py:13
  67.1 0.6 broadcast_in_dim.311
  67.8 8.8 %all_to_all.37 = f32[8,1,1]{2,1,0:T(1,128)S(1)} all-to-all(f32[8,1,1]{2,1,0:T(1,128)S(1)} %broadcast_in_dim.311), channel_id=1, replica_groups=mesh['box'=8,'rep'=4] {'box'}, dimensions={0} | all-to-all | bytes 64 | tf_op jit(solution)/shard_map/all_to_all | solution.py:36
  (150 shorter events, 11.1 us)
Async XLA Ops:
  0.6 7.6 %copy-start = (bf16[20,4,64,64]{3,2,1,0:T(8,128)(2,1)S(1)}, bf16[20,4,64,64]{3,2,1,0:T(8,128)(2,1)}, u32[]{:S(2)}) copy-start(bf16[20,4,64,64]{3,2,1,0:T(8,128)(2,1)} %param.16) | copy-start | bytes 1966084
  0.6 5.9 %copy-start.5 = (s32[16,2]{0,1:T(2,128)S(1)}, s32[16,2]{0,1:T(2,128)}, u32[]{:S(2)}) copy-start(s32[16,2]{0,1:T(2,128)} %param.12) | copy-start | bytes 388
  0.7 6.5 %copy-start.1 = (bf16[16,64,256]{2,1,0:T(8,128)(2,1)S(1)}, bf16[16,64,256]{2,1,0:T(8,128)(2,1)}, u32[]{:S(2)}) copy-start(bf16[16,64,256]{2,1,0:T(8,128)(2,1)} %param.13) | copy-start | bytes 1572868
  0.7 6.8 %copy-start.2 = (bf16[16,64,64]{2,1,0:T(8,128)(2,1)S(1)}, bf16[16,64,64]{2,1,0:T(8,128)(2,1)}, u32[]{:S(2)}) copy-start(bf16[16,64,64]{2,1,0:T(8,128)(2,1)} %param.14) | copy-start | bytes 393220
  0.7 7.0 %copy-start.6 = (s32[16]{0:T(128)S(1)}, s32[16]{0:T(128)}, u32[]{:S(2)}) copy-start(s32[16]{0:T(128)} %param.15) | copy-start | bytes 196
  1.6 17.1 %collective-permute-start = (bf16[16,256]{1,0:T(8,128)(2,1)S(1)}, bf16[16,256]{1,0:T(8,128)(2,1)S(1)}, u32[]{:S(2)}, u32[]{:S(2)}) collective-permute-start(bf16[16,256]{1,0:T(8,128)(2,1)S(1)} %get-tuple-element.18), channel_id=1, source_target_pairs={{4,0},{8,4},{12,8},{16,12},{20,16},{24,20},{28,24},{5,1},{9,5},{13... | collective-permute-start | bytes 24584 | tf_op jit(solution)/shard_map/ppermute | solution.py:112
  9.8 16.0 %all-to-all-start = ((f32[8,1,5376]{2,1,0:T(1,128)}), f32[8,1,5376]{2,1,0:T(1,128)S(1)}, u32[]{:S(2)}, u32[]{:S(2)}) async-start(f32[8,1,5376]{2,1,0:T(1,128)} %all_to_all.24), calls=%async_computation | async-start | bytes 344064 | tf_op jit(solution)/shard_map/all_to_all | solution.py:119
  18.2 14.5 %copy-start.3 = (f32[16,256]{1,0:T(8,128)S(1)}, f32[16,256]{1,0:T(8,128)}, u32[]{:S(2)}) copy-start(f32[16,256]{1,0:T(8,128)} %param.9) | copy-start | bytes 49156
  18.2 14.5 %copy-start.4 = (f32[16,256]{1,0:T(8,128)S(1)}, f32[16,256]{1,0:T(8,128)}, u32[]{:S(2)}) copy-start(f32[16,256]{1,0:T(8,128)} %param.10) | copy-start | bytes 49156
  27.2 3.9 %collective-permute-start.2 = (f32[5376]{0:T(1024)S(1)}, f32[5376]{0:T(1024)S(1)}, u32[]{:S(2)}, u32[]{:S(2)}) collective-permute-start(f32[5376]{0:T(1024)S(1)} %constant_dynamic-update-slice_fusion), channel_id=1, source_target_pairs={{0,2},{1,3},{2,0},{3,1},{4,6},{5,7},{6,4},{7,5},{8,10},{9,11},{10,... | collective-permute-start | bytes 64520 | tf_op jit(solution)/shard_map/ppermute | solution.py:13
  28.7 3.3 %collective-permute-start.3 = (f32[5376]{0:T(1024)S(1)}, f32[5376]{0:T(1024)S(1)}, u32[]{:S(2)}, u32[]{:S(2)}) collective-permute-start(f32[5376]{0:T(1024)S(1)} %constant_dynamic-update-slice_fusion), channel_id=1, source_target_pairs={{0,3},{1,2},{2,1},{3,0},{4,7},{5,6},{6,5},{7,4},{8,11},{9,10},{10,... | collective-permute-start | bytes 64520 | tf_op jit(solution)/shard_map/ppermute | solution.py:13
  28.7 3.3 %collective-permute-start.1 = (f32[5376]{0:T(1024)S(1)}, f32[5376]{0:T(1024)S(1)}, u32[]{:S(2)}, u32[]{:S(2)}) collective-permute-start(f32[5376]{0:T(1024)S(1)} %constant_dynamic-update-slice_fusion), channel_id=1, source_target_pairs={{0,1},{1,0},{2,3},{3,2},{4,5},{5,4},{6,7},{7,6},{8,9},{9,8},{10,11... | collective-permute-start | bytes 64520 | tf_op jit(solution)/shard_map/ppermute | solution.py:13
  41.9 10.6 %collective-permute-start.4 = (bf16[16,256]{1,0:T(8,128)(2,1)S(1)}, bf16[16,256]{1,0:T(8,128)(2,1)S(1)}, u32[]{:S(2)}, u32[]{:S(2)}) collective-permute-start(bf16[16,256]{1,0:T(8,128)(2,1)S(1)} %get-tuple-element.5), channel_id=1, source_target_pairs={{4,0},{8,4},{12,8},{16,12},{20,16},{24,20},{28,24},{5,1},{9,5},{13... | collective-permute-start | bytes 24584 | tf_op jit(solution)/shard_map/ppermute | solution.py:112
  48.6 11.5 %all-to-all-start.2 = ((f32[8,1,5376]{2,1,0:T(1,128)}), f32[8,1,5376]{2,1,0:T(1,128)S(1)}, u32[]{:S(2)}, u32[]{:S(2)}) async-start(f32[8,1,5376]{2,1,0:T(1,128)} %copy.49), calls=%async_computation.2 | async-start | bytes 344064 | tf_op jit(solution)/shard_map/all_to_all | solution.py:119
  61.5 3.9 %collective-permute-start.6 = (f32[5376]{0:T(1024)S(1)}, f32[5376]{0:T(1024)S(1)}, u32[]{:S(2)}, u32[]{:S(2)}) collective-permute-start(f32[5376]{0:T(1024)S(1)} %constant_dynamic-update-slice_fusion.1), channel_id=1, source_target_pairs={{0,2},{1,3},{2,0},{3,1},{4,6},{5,7},{6,4},{7,5},{8,10},{9,11},{10,... | collective-permute-start | bytes 64520 | tf_op jit(solution)/shard_map/ppermute | solution.py:13
  62.3 3.5 %collective-permute-start.7 = (f32[5376]{0:T(1024)S(1)}, f32[5376]{0:T(1024)S(1)}, u32[]{:S(2)}, u32[]{:S(2)}) collective-permute-start(f32[5376]{0:T(1024)S(1)} %constant_dynamic-update-slice_fusion.1), channel_id=1, source_target_pairs={{0,3},{1,2},{2,1},{3,0},{4,7},{5,6},{6,5},{7,4},{8,11},{9,10},{10,... | collective-permute-start | bytes 64520 | tf_op jit(solution)/shard_map/ppermute | solution.py:13
  62.3 3.5 %collective-permute-start.5 = (f32[5376]{0:T(1024)S(1)}, f32[5376]{0:T(1024)S(1)}, u32[]{:S(2)}, u32[]{:S(2)}) collective-permute-start(f32[5376]{0:T(1024)S(1)} %constant_dynamic-update-slice_fusion.1), channel_id=1, source_target_pairs={{0,1},{1,0},{2,3},{3,2},{4,5},{5,4},{6,7},{7,6},{8,9},{9,8},{10,11... | collective-permute-start | bytes 64520 | tf_op jit(solution)/shard_map/ppermute | solution.py:13

commit v23 on v16

--- a/solution.py
+++ b/solution.py
@@ -143,9 +143,9 @@
         near_total = both[:near_size].reshape(box_count, leaf)
         far_total = both[near_size:].reshape(node_count, rank_width)
         group_out = far_total[box_count:].astype(jnp.bfloat16)
-        parent_pick = jnp.zeros((box_count, rank_width), jnp.bfloat16)
-        for group in range(group_count):
-            parent_pick = jnp.where((parent_local == group)[:, None], group_out[group][None], parent_pick)
+        parent_pick = jnp.dot(
+            parent_onehot.T.astype(jnp.bfloat16), group_out, preferred_element_type=jnp.float32
+        ).astype(jnp.bfloat16)
         from_parent = jnp.einsum(
             "brq,bq->br", transfer, parent_pick, preferred_element_type=jnp.float32
         )

time: 78 us -> 78.3 us (level)
  no operation moved by 1% of the time
where the time goes in v23:
time: 78.3 us; the launch traced here: 77.7 us
  starting transfers between devices  19.2 us (25%)
  blocking collectives  17.8 us (23%)
  waiting for transfers between devices  12.9 us (16%)
  other arithmetic  10.7 us (14%)
  matrix products  10.6 us (14%)
  local copies, waits for them, and re-layouts  5.13 us (7%)
  between operations  1.29 us (2%)
    all_to_all x2, blocking collectives, box_sum(): got = lax.all_to_all(sent, 'box', 0, 0, tiled=True)  17.8 us
    all_to_all x2, starting transfers between devices, local(): lax.all_to_all(jnp.concatenate([far_send.reshape(box_devices, far_size),...  12.3 us
    all_to_all x2, waiting for transfers between devices, local(): lax.all_to_all(jnp.concatenate([far_send.reshape(box_devices, far_size),...  8.12 us
    reduce_sum x2, other arithmetic, local(): forward = jnp.sum(near_tiles.astype(jnp.float32) * near_in, axis=(1, 3))  6.19 us
    dot_general x2, matrix products, local(): jnp.einsum('bsij,bi->bsj', near_tiles, rounded, preferred_element_type=jn...  5.66 us
    ppermute x6, waiting for transfers between devices, rep_sum(): lax.ppermute(vector, 'rep', [(i, i ^ mask) for i in range(count)])  4.78 us
    ppermute x6, starting transfers between devices, rep_sum(): lax.ppermute(vector, 'rep', [(i, i ^ mask) for i in range(count)])  4.35 us
    ppermute x2, starting transfers between devices, local(): lax.ppermute(rounded, 'box', [(i, i - 1) for i in range(1, box_devices)])  2.57 us
  transfers between devices with their start and end apart: 10, of which 6 were waited for; matrix products, arithmetic and copies ran while one was open for 23% of the time, Pallas kernels for 0%

profile of v23, /device:TPU:0, one launch (start us, length us, event | category | flops | bytes accessed | tf_op | source)
XLA Modules:
  0.0 77.7 jit_solution(4403085784429305101)
XLA Ops:
  0.7 0.9 %fusion.101 = (f32[16,256]{1,0:T(8,128)S(1)}, bf16[16,256]{1,0:T(8,128)(2,1)S(1)}) fusion(f32[16,256]{1,0:T(8,128)} %param.9), kind=kLoop, calls=%fused_computation.175 | loop fusion | flops 8192 | bytes 40960 | tf_op jit(solution)/shard_map/convert_element_type | solution.py:95
  1.6 1.3 %collective-permute-start = (bf16[16,256]{1,0:T(8,128)(2,1)S(1)}, bf16[16,256]{1,0:T(8,128)(2,1)S(1)}, u32[]{:S(2)}, u32[]{:S(2)}) collective-permute-start(bf16[16,256]{1,0:T(8,128)(2,1)S(1)} %get-tuple-element.12), channel_id=1, source_target_pairs={{4,0},{8,4},{12,8},{16,12},{20,16},{24,20},{28,24},{5,1},{9,5},{13... | collective-permute-start | bytes 24584 | tf_op jit(solution)/shard_map/ppermute | solution.py:110
  2.9 0.7 broadcast_select_fusion.4
  3.7 2.8 %fusion.47 = f32[16,1,2,256]{3,1,2,0:T(1,128)S(1)} fusion(bf16[16,2,256,256]{3,2,1,0:T(8,128)(2,1)} %param.11, bf16[16,256,1,1]{1,0,2,3:T(8,128)(2,1)S(1)} %bitcast.130), kind=kOutput, calls=%fused_computation.84 | convolution fusion | flops 4194304 | bytes 4235264 | tf_op jit(solution)/shard_map/bsij,bi->bsj/dot_general | solution.py:88
  9.0 0.8 %all_to_all.24 = f32[8,1,5376]{2,1,0:T(1,128)} reshape(f32[8,5376]{1,0:T(8,128)S(1)} %pad_maximum_fusion) | data formatting | bytes 344064 | tf_op jit(solution)/shard_map/all_to_all | solution.py:117
  9.8 8.4 %all-to-all-start = ((f32[8,1,5376]{2,1,0:T(1,128)}), f32[8,1,5376]{2,1,0:T(1,128)S(1)}, u32[]{:S(2)}, u32[]{:S(2)}) async-start(f32[8,1,5376]{2,1,0:T(1,128)} %all_to_all.24), calls=%async_computation | async-start | bytes 344064 | tf_op jit(solution)/shard_map/all_to_all | solution.py:117
  18.8 3.1 %fusion = f32[16,256]{1,0:T(8,128)S(1)} fusion(bf16[16,2,256,256]{3,2,1,0:T(8,128)(2,1)} %param.11, f32[16,2,256]{2,1,0:T(2,128)S(1)} %mul.134), kind=kLoop, calls=%fused_computation.2 | loop fusion | flops 6287360 | bytes 4243456 | tf_op jit(solution)/shard_map/reduce_sum | solution.py:133
  21.9 3.9 %all-to-all-done = f32[8,1,5376]{2,1,0:T(1,128)S(1)} async-done(((f32[8,1,5376]{2,1,0:T(1,128)}), f32[8,1,5376]{2,1,0:T(1,128)S(1)}, u32[]{:S(2)}, u32[]{:S(2)}) %all-to-all-start) | async-done | bytes 172064 | tf_op jit(solution)/shard_map/all_to_all | solution.py:117
  27.2 1.5 %collective-permute-start.2 = (f32[5376]{0:T(1024)S(1)}, f32[5376]{0:T(1024)S(1)}, u32[]{:S(2)}, u32[]{:S(2)}) collective-permute-start(f32[5376]{0:T(1024)S(1)} %constant_dynamic-update-slice_fusion), channel_id=1, source_target_pairs={{0,2},{1,3},{2,0},{3,1},{4,6},{5,7},{6,4},{7,5},{8,10},{9,11},{10,... | collective-permute-start | bytes 64520 | tf_op jit(solution)/shard_map/ppermute | solution.py:13
  28.7 0.6 collective-permute-start.1
  29.3 1.7 %collective-permute-done.2 = f32[5376]{0:T(1024)S(1)} collective-permute-done((f32[5376]{0:T(1024)S(1)}, f32[5376]{0:T(1024)S(1)}, u32[]{:S(2)}, u32[]{:S(2)}) %collective-permute-start.2) | collective-permute-done | bytes 21536 | tf_op jit(solution)/shard_map/ppermute | solution.py:13
  31.0 0.9 %collective-permute-done.3 = f32[5376]{0:T(1024)S(1)} collective-permute-done((f32[5376]{0:T(1024)S(1)}, f32[5376]{0:T(1024)S(1)}, u32[]{:S(2)}, u32[]{:S(2)}) %collective-permute-start.3) | collective-permute-done | bytes 21536 | tf_op jit(solution)/shard_map/ppermute | solution.py:13
  32.9 8.9 %all_to_all.36 = f32[8,1,4]{2,1,0:T(1,128)S(1)} all-to-all(f32[8,1,4]{2,1,0:T(1,128)S(1)} %broadcast_in_dim.204), channel_id=1, replica_groups=mesh['box'=8,'rep'=4] {'box'}, dimensions={0} | all-to-all | bytes 256 | tf_op jit(solution)/shard_map/all_to_all | solution.py:36
  42.0 1.3 %collective-permute-start.4 = (bf16[16,256]{1,0:T(8,128)(2,1)S(1)}, bf16[16,256]{1,0:T(8,128)(2,1)S(1)}, u32[]{:S(2)}, u32[]{:S(2)}) collective-permute-start(bf16[16,256]{1,0:T(8,128)(2,1)S(1)} %get-tuple-element.3), channel_id=1, source_target_pairs={{4,0},{8,4},{12,8},{16,12},{20,16},{24,20},{28,24},{5,1},{9,5},{13... | collective-permute-start | bytes 24584 | tf_op jit(solution)/shard_map/ppermute | solution.py:110
  43.3 2.8 %fusion.45 = f32[16,1,2,256]{3,1,2,0:T(1,128)S(1)} fusion(bf16[16,2,256,256]{3,2,1,0:T(8,128)(2,1)} %param.11, bf16[16,256,1,1]{1,0,2,3:T(8,128)(2,1)S(1)} %bitcast.131), kind=kOutput, calls=%fused_computation.82 | convolution fusion | flops 4194304 | bytes 4235264 | tf_op jit(solution)/shard_map/bsij,bi->bsj/dot_general | solution.py:88
  47.7 0.8 %copy.49 = f32[8,1,5376]{2,1,0:T(1,128)} copy(f32[8,1,5376]{2,0,1:T(8,128)S(1)} %maximum_bitcast_fusion) | data formatting | bytes 344064 | tf_op jit(solution)/shard_map/all_to_all | solution.py:117
  48.6 3.9 %all-to-all-start.2 = ((f32[8,1,5376]{2,1,0:T(1,128)}), f32[8,1,5376]{2,1,0:T(1,128)S(1)}, u32[]{:S(2)}, u32[]{:S(2)}) async-start(f32[8,1,5376]{2,1,0:T(1,128)} %copy.49), calls=%async_computation.2 | async-start | bytes 344064 | tf_op jit(solution)/shard_map/all_to_all | solution.py:117
  52.8 3.1 %fusion.1 = f32[16,256]{1,0:T(8,128)S(1)} fusion(bf16[16,2,256,256]{3,2,1,0:T(8,128)(2,1)} %param.11, f32[16,2,256]{2,1,0:T(2,128)S(1)} %mul.158), kind=kLoop, calls=%fused_computation.3 | loop fusion | flops 6287360 | bytes 4243456 | tf_op jit(solution)/shard_map/reduce_sum | solution.py:133
  55.9 4.2 %all-to-all-done.2 = f32[8,1,5376]{2,1,0:T(1,128)S(1)} async-done(((f32[8,1,5376]{2,1,0:T(1,128)}), f32[8,1,5376]{2,1,0:T(1,128)S(1)}, u32[]{:S(2)}, u32[]{:S(2)}) %all-to-all-start.2) | async-done | bytes 172064 | tf_op jit(solution)/shard_map/all_to_all | solution.py:117
  61.5 0.8 %collective-permute-start.6 = (f32[5376]{0:T(1024)S(1)}, f32[5376]{0:T(1024)S(1)}, u32[]{:S(2)}, u32[]{:S(2)}) collective-permute-start(f32[5376]{0:T(1024)S(1)} %constant_dynamic-update-slice_fusion.1), channel_id=1, source_target_pairs={{0,2},{1,3},{2,0},{3,1},{4,6},{5,7},{6,4},{7,5},{8,10},{9,11},{10,... | collective-permute-start | bytes 64520 | tf_op jit(solution)/shard_map/ppermute | solution.py:13
  62.3 1.3 %collective-permute-start.5 = (f32[5376]{0:T(1024)S(1)}, f32[5376]{0:T(1024)S(1)}, u32[]{:S(2)}, u32[]{:S(2)}) collective-permute-start(f32[5376]{0:T(1024)S(1)} %constant_dynamic-update-slice_fusion.1), channel_id=1, source_target_pairs={{0,1},{1,0},{2,3},{3,2},{4,5},{5,4},{6,7},{7,6},{8,9},{9,8},{10,11... | collective-permute-start | bytes 64520 | tf_op jit(solution)/shard_map/ppermute | solution.py:13
  63.7 1.7 %collective-permute-done.6 = f32[5376]{0:T(1024)S(1)} collective-permute-done((f32[5376]{0:T(1024)S(1)}, f32[5376]{0:T(1024)S(1)}, u32[]{:S(2)}, u32[]{:S(2)}) %collective-permute-start.6) | collective-permute-done | bytes 21536 | tf_op jit(solution)/shard_map/ppermute | solution.py:13
  67.3 0.6 broadcast_in_dim.211
  68.0 8.8 %all_to_all.37 = f32[8,1,1]{2,1,0:T(1,128)S(1)} all-to-all(f32[8,1,1]{2,1,0:T(1,128)S(1)} %broadcast_in_dim.211), channel_id=1, replica_groups=mesh['box'=8,'rep'=4] {'box'}, dimensions={0} | all-to-all | bytes 64 | tf_op jit(solution)/shard_map/all_to_all | solution.py:36
  (149 shorter events, 11.3 us)
Async XLA Ops:
  0.6 7.5 %copy-start = (bf16[20,4,64,64]{3,2,1,0:T(8,128)(2,1)S(1)}, bf16[20,4,64,64]{3,2,1,0:T(8,128)(2,1)}, u32[]{:S(2)}) copy-start(bf16[20,4,64,64]{3,2,1,0:T(8,128)(2,1)} %param.16) | copy-start | bytes 1966084
  0.6 5.9 %copy-start.4 = (s32[16,2]{0,1:T(2,128)S(1)}, s32[16,2]{0,1:T(2,128)}, u32[]{:S(2)}) copy-start(s32[16,2]{0,1:T(2,128)} %param.12) | copy-start | bytes 388
  0.7 6.5 %copy-start.1 = (bf16[16,64,256]{2,1,0:T(8,128)(2,1)S(1)}, bf16[16,64,256]{2,1,0:T(8,128)(2,1)}, u32[]{:S(2)}) copy-start(bf16[16,64,256]{2,1,0:T(8,128)(2,1)} %param.13) | copy-start | bytes 1572868
  0.7 6.8 %copy-start.5 = (bf16[16,64,64]{2,1,0:T(8,128)(2,1)S(1)}, bf16[16,64,64]{2,1,0:T(8,128)(2,1)}, u32[]{:S(2)}) copy-start(bf16[16,64,64]{2,1,0:T(8,128)(2,1)} %param.14) | copy-start | bytes 393220
  0.7 6.9 %copy-start.6 = (s32[16]{0:T(128)S(1)}, s32[16]{0:T(128)}, u32[]{:S(2)}) copy-start(s32[16]{0:T(128)} %param.15) | copy-start | bytes 196
  1.6 17.0 %collective-permute-start = (bf16[16,256]{1,0:T(8,128)(2,1)S(1)}, bf16[16,256]{1,0:T(8,128)(2,1)S(1)}, u32[]{:S(2)}, u32[]{:S(2)}) collective-permute-start(bf16[16,256]{1,0:T(8,128)(2,1)S(1)} %get-tuple-element.12), channel_id=1, source_target_pairs={{4,0},{8,4},{12,8},{16,12},{20,16},{24,20},{28,24},{5,1},{9,5},{13... | collective-permute-start | bytes 24584 | tf_op jit(solution)/shard_map/ppermute | solution.py:110
  9.8 16.0 %all-to-all-start = ((f32[8,1,5376]{2,1,0:T(1,128)}), f32[8,1,5376]{2,1,0:T(1,128)S(1)}, u32[]{:S(2)}, u32[]{:S(2)}) async-start(f32[8,1,5376]{2,1,0:T(1,128)} %all_to_all.24), calls=%async_computation | async-start | bytes 344064 | tf_op jit(solution)/shard_map/all_to_all | solution.py:117
  18.2 14.6 %copy-start.2 = (f32[16,256]{1,0:T(8,128)S(1)}, f32[16,256]{1,0:T(8,128)}, u32[]{:S(2)}) copy-start(f32[16,256]{1,0:T(8,128)} %param.9) | copy-start | bytes 49156
  18.2 14.6 %copy-start.3 = (f32[16,256]{1,0:T(8,128)S(1)}, f32[16,256]{1,0:T(8,128)}, u32[]{:S(2)}) copy-start(f32[16,256]{1,0:T(8,128)} %param.10) | copy-start | bytes 49156
  27.2 3.9 %collective-permute-start.2 = (f32[5376]{0:T(1024)S(1)}, f32[5376]{0:T(1024)S(1)}, u32[]{:S(2)}, u32[]{:S(2)}) collective-permute-start(f32[5376]{0:T(1024)S(1)} %constant_dynamic-update-slice_fusion), channel_id=1, source_target_pairs={{0,2},{1,3},{2,0},{3,1},{4,6},{5,7},{6,4},{7,5},{8,10},{9,11},{10,... | collective-permute-start | bytes 64520 | tf_op jit(solution)/shard_map/ppermute | solution.py:13
  28.7 3.3 %collective-permute-start.3 = (f32[5376]{0:T(1024)S(1)}, f32[5376]{0:T(1024)S(1)}, u32[]{:S(2)}, u32[]{:S(2)}) collective-permute-start(f32[5376]{0:T(1024)S(1)} %constant_dynamic-update-slice_fusion), channel_id=1, source_target_pairs={{0,3},{1,2},{2,1},{3,0},{4,7},{5,6},{6,5},{7,4},{8,11},{9,10},{10,... | collective-permute-start | bytes 64520 | tf_op jit(solution)/shard_map/ppermute | solution.py:13
  28.7 3.3 %collective-permute-start.1 = (f32[5376]{0:T(1024)S(1)}, f32[5376]{0:T(1024)S(1)}, u32[]{:S(2)}, u32[]{:S(2)}) collective-permute-start(f32[5376]{0:T(1024)S(1)} %constant_dynamic-update-slice_fusion), channel_id=1, source_target_pairs={{0,1},{1,0},{2,3},{3,2},{4,5},{5,4},{6,7},{7,6},{8,9},{9,8},{10,11... | collective-permute-start | bytes 64520 | tf_op jit(solution)/shard_map/ppermute | solution.py:13
  42.0 10.5 %collective-permute-start.4 = (bf16[16,256]{1,0:T(8,128)(2,1)S(1)}, bf16[16,256]{1,0:T(8,128)(2,1)S(1)}, u32[]{:S(2)}, u32[]{:S(2)}) collective-permute-start(bf16[16,256]{1,0:T(8,128)(2,1)S(1)} %get-tuple-element.3), channel_id=1, source_target_pairs={{4,0},{8,4},{12,8},{16,12},{20,16},{24,20},{28,24},{5,1},{9,5},{13... | collective-permute-start | bytes 24584 | tf_op jit(solution)/shard_map/ppermute | solution.py:110
  48.6 11.5 %all-to-all-start.2 = ((f32[8,1,5376]{2,1,0:T(1,128)}), f32[8,1,5376]{2,1,0:T(1,128)S(1)}, u32[]{:S(2)}, u32[]{:S(2)}) async-start(f32[8,1,5376]{2,1,0:T(1,128)} %copy.49), calls=%async_computation.2 | async-start | bytes 344064 | tf_op jit(solution)/shard_map/all_to_all | solution.py:117
  61.5 3.9 %collective-permute-start.6 = (f32[5376]{0:T(1024)S(1)}, f32[5376]{0:T(1024)S(1)}, u32[]{:S(2)}, u32[]{:S(2)}) collective-permute-start(f32[5376]{0:T(1024)S(1)} %constant_dynamic-update-slice_fusion.1), channel_id=1, source_target_pairs={{0,2},{1,3},{2,0},{3,1},{4,6},{5,7},{6,4},{7,5},{8,10},{9,11},{10,... | collective-permute-start | bytes 64520 | tf_op jit(solution)/shard_map/ppermute | solution.py:13
  62.3 3.5 %collective-permute-start.7 = (f32[5376]{0:T(1024)S(1)}, f32[5376]{0:T(1024)S(1)}, u32[]{:S(2)}, u32[]{:S(2)}) collective-permute-start(f32[5376]{0:T(1024)S(1)} %constant_dynamic-update-slice_fusion.1), channel_id=1, source_target_pairs={{0,3},{1,2},{2,1},{3,0},{4,7},{5,6},{6,5},{7,4},{8,11},{9,10},{10,... | collective-permute-start | bytes 64520 | tf_op jit(solution)/shard_map/ppermute | solution.py:13
  62.3 3.5 %collective-permute-start.5 = (f32[5376]{0:T(1024)S(1)}, f32[5376]{0:T(1024)S(1)}, u32[]{:S(2)}, u32[]{:S(2)}) collective-permute-start(f32[5376]{0:T(1024)S(1)} %constant_dynamic-update-slice_fusion.1), channel_id=1, source_target_pairs={{0,1},{1,0},{2,3},{3,2},{4,5},{5,4},{6,7},{7,6},{8,9},{9,8},{10,11... | collective-permute-start | bytes 64520 | tf_op jit(solution)/shard_map/ppermute | solution.py:13

commit v24 on v16

--- a/solution.py
+++ b/solution.py
@@ -34,8 +34,8 @@
     count = lax.axis_size("box")
     sent = jnp.broadcast_to(values[None, :], (count, values.shape[0]))
     got = lax.all_to_all(sent, "box", 0, 0, tiled=True)
-    wide = lax.optimization_barrier(jnp.broadcast_to(got[:, :, None], got.shape + (width,)))
-    return jnp.sum(wide, axis=0)
+    total = jnp.sum(got, axis=0)
+    return lax.optimization_barrier(jnp.broadcast_to(total[:, None], total.shape + (width,)))
 
 
 def local(

time: 78 us -> 79.1 us (1.014)
  no operation moved by 1% of the time
where the time goes in v24:
time: 79.1 us; the launch traced here: 78.5 us
  starting transfers between devices  19.2 us (24%)
  blocking collectives  17.8 us (23%)
  waiting for transfers between devices  12.9 us (16%)
  other arithmetic  11.3 us (14%)
  matrix products  10.3 us (13%)
  local copies, waits for them, and re-layouts  5.7 us (7%)
  between operations  1.3 us (2%)
    all_to_all x2, blocking collectives, box_sum(): got = lax.all_to_all(sent, 'box', 0, 0, tiled=True)  17.8 us
    all_to_all x2, starting transfers between devices, local(): lax.all_to_all(jnp.concatenate([far_send.reshape(box_devices, far_size),...  12.3 us
    all_to_all x2, waiting for transfers between devices, local(): lax.all_to_all(jnp.concatenate([far_send.reshape(box_devices, far_size),...  8.12 us
    reduce_sum x2, other arithmetic, local(): forward = jnp.sum(near_tiles.astype(jnp.float32) * near_in, axis=(1, 3))  6.19 us
    dot_general x2, matrix products, local(): jnp.einsum('bsij,bi->bsj', near_tiles, rounded, preferred_element_type=jn...  5.66 us
    ppermute x6, waiting for transfers between devices, rep_sum(): lax.ppermute(vector, 'rep', [(i, i ^ mask) for i in range(count)])  4.77 us
    ppermute x6, starting transfers between devices, rep_sum(): lax.ppermute(vector, 'rep', [(i, i ^ mask) for i in range(count)])  4.35 us
    ppermute x2, starting transfers between devices, local(): lax.ppermute(rounded, 'box', [(i, i - 1) for i in range(1, box_devices)])  2.57 us
  transfers between devices with their start and end apart: 10, of which 6 were waited for; matrix products, arithmetic and copies ran while one was open for 23% of the time, Pallas kernels for 0%

profile of v24, /device:TPU:0, one launch (start us, length us, event | category | flops | bytes accessed | tf_op | source)
XLA Modules:
  0.0 78.5 jit_solution(12434527621475457714)
XLA Ops:
  0.7 0.9 %fusion.99 = (f32[16,256]{1,0:T(8,128)S(1)}, bf16[16,256]{1,0:T(8,128)(2,1)S(1)}) fusion(f32[16,256]{1,0:T(8,128)} %param.9), kind=kLoop, calls=%fused_computation.173 | loop fusion | flops 8192 | bytes 40960 | tf_op jit(solution)/shard_map/convert_element_type | solution.py:95
  1.6 1.3 %collective-permute-start = (bf16[16,256]{1,0:T(8,128)(2,1)S(1)}, bf16[16,256]{1,0:T(8,128)(2,1)S(1)}, u32[]{:S(2)}, u32[]{:S(2)}) collective-permute-start(bf16[16,256]{1,0:T(8,128)(2,1)S(1)} %get-tuple-element.18), channel_id=1, source_target_pairs={{4,0},{8,4},{12,8},{16,12},{20,16},{24,20},{28,24},{5,1},{9,5},{13... | collective-permute-start | bytes 24584 | tf_op jit(solution)/shard_map/ppermute | solution.py:110
  2.9 0.7 broadcast_select_fusion.4
  3.7 2.8 %fusion.45 = f32[16,1,2,256]{3,1,2,0:T(1,128)S(1)} fusion(bf16[16,2,256,256]{3,2,1,0:T(8,128)(2,1)} %param.11, bf16[16,256,1,1]{1,0,2,3:T(8,128)(2,1)S(1)} %bitcast.126), kind=kOutput, calls=%fused_computation.80 | convolution fusion | flops 4194304 | bytes 4235264 | tf_op jit(solution)/shard_map/bsij,bi->bsj/dot_general | solution.py:88
  9.0 0.8 %all_to_all.24 = f32[8,1,5376]{2,1,0:T(1,128)} reshape(f32[8,5376]{1,0:T(8,128)S(1)} %pad_maximum_fusion) | data formatting | bytes 344064 | tf_op jit(solution)/shard_map/all_to_all | solution.py:117
  9.8 8.4 %all-to-all-start = ((f32[8,1,5376]{2,1,0:T(1,128)}), f32[8,1,5376]{2,1,0:T(1,128)S(1)}, u32[]{:S(2)}, u32[]{:S(2)}) async-start(f32[8,1,5376]{2,1,0:T(1,128)} %all_to_all.24), calls=%async_computation | async-start | bytes 344064 | tf_op jit(solution)/shard_map/all_to_all | solution.py:117
  18.8 3.1 %fusion = f32[16,256]{1,0:T(8,128)S(1)} fusion(bf16[16,2,256,256]{3,2,1,0:T(8,128)(2,1)} %param.11, f32[16,2,256]{2,1,0:T(2,128)S(1)} %mul.134), kind=kLoop, calls=%fused_computation.2 | loop fusion | flops 6287360 | bytes 4243456 | tf_op jit(solution)/shard_map/reduce_sum | solution.py:133
  21.9 3.9 %all-to-all-done = f32[8,1,5376]{2,1,0:T(1,128)S(1)} async-done(((f32[8,1,5376]{2,1,0:T(1,128)}), f32[8,1,5376]{2,1,0:T(1,128)S(1)}, u32[]{:S(2)}, u32[]{:S(2)}) %all-to-all-start) | async-done | bytes 172064 | tf_op jit(solution)/shard_map/all_to_all | solution.py:117
  27.2 1.5 %collective-permute-start.2 = (f32[5376]{0:T(1024)S(1)}, f32[5376]{0:T(1024)S(1)}, u32[]{:S(2)}, u32[]{:S(2)}) collective-permute-start(f32[5376]{0:T(1024)S(1)} %constant_dynamic-update-slice_fusion), channel_id=1, source_target_pairs={{0,2},{1,3},{2,0},{3,1},{4,6},{5,7},{6,4},{7,5},{8,10},{9,11},{10,... | collective-permute-start | bytes 64520 | tf_op jit(solution)/shard_map/ppermute | solution.py:13
  28.7 0.6 collective-permute-start.1
  29.3 1.7 %collective-permute-done.2 = f32[5376]{0:T(1024)S(1)} collective-permute-done((f32[5376]{0:T(1024)S(1)}, f32[5376]{0:T(1024)S(1)}, u32[]{:S(2)}, u32[]{:S(2)}) %collective-permute-start.2) | collective-permute-done | bytes 21536 | tf_op jit(solution)/shard_map/ppermute | solution.py:13
  31.0 0.9 %collective-permute-done.3 = f32[5376]{0:T(1024)S(1)} collective-permute-done((f32[5376]{0:T(1024)S(1)}, f32[5376]{0:T(1024)S(1)}, u32[]{:S(2)}, u32[]{:S(2)}) %collective-permute-start.3) | collective-permute-done | bytes 21536 | tf_op jit(solution)/shard_map/ppermute | solution.py:13
  32.8 8.9 %all_to_all.36 = f32[8,1,4]{2,1,0:T(1,128)S(1)} all-to-all(f32[8,1,4]{2,1,0:T(1,128)S(1)} %broadcast_in_dim.294), channel_id=1, replica_groups=mesh['box'=8,'rep'=4] {'box'}, dimensions={0} | all-to-all | bytes 256 | tf_op jit(solution)/shard_map/all_to_all | solution.py:36
  41.9 1.3 %collective-permute-start.4 = (bf16[16,256]{1,0:T(8,128)(2,1)S(1)}, bf16[16,256]{1,0:T(8,128)(2,1)S(1)}, u32[]{:S(2)}, u32[]{:S(2)}) collective-permute-start(bf16[16,256]{1,0:T(8,128)(2,1)S(1)} %get-tuple-element.5), channel_id=1, source_target_pairs={{4,0},{8,4},{12,8},{16,12},{20,16},{24,20},{28,24},{5,1},{9,5},{13... | collective-permute-start | bytes 24584 | tf_op jit(solution)/shard_map/ppermute | solution.py:110
  43.2 2.8 %fusion.43 = f32[16,1,2,256]{3,1,2,0:T(1,128)S(1)} fusion(bf16[16,2,256,256]{3,2,1,0:T(8,128)(2,1)} %param.11, bf16[16,256,1,1]{1,0,2,3:T(8,128)(2,1)S(1)} %bitcast.127), kind=kOutput, calls=%fused_computation.78 | convolution fusion | flops 4194304 | bytes 4235264 | tf_op jit(solution)/shard_map/bsij,bi->bsj/dot_general | solution.py:88
  47.6 0.8 %copy.54 = f32[8,1,5376]{2,1,0:T(1,128)} copy(f32[8,1,5376]{2,0,1:T(8,128)S(1)} %maximum_bitcast_fusion) | data formatting | bytes 344064 | tf_op jit(solution)/shard_map/all_to_all | solution.py:117
  48.5 3.9 %all-to-all-start.2 = ((f32[8,1,5376]{2,1,0:T(1,128)}), f32[8,1,5376]{2,1,0:T(1,128)S(1)}, u32[]{:S(2)}, u32[]{:S(2)}) async-start(f32[8,1,5376]{2,1,0:T(1,128)} %copy.54), calls=%async_computation.2 | async-start | bytes 344064 | tf_op jit(solution)/shard_map/all_to_all | solution.py:117
  52.7 3.1 %fusion.1 = f32[16,256]{1,0:T(8,128)S(1)} fusion(bf16[16,2,256,256]{3,2,1,0:T(8,128)(2,1)} %param.11, f32[16,2,256]{2,1,0:T(2,128)S(1)} %mul.158), kind=kLoop, calls=%fused_computation.3 | loop fusion | flops 6287360 | bytes 4243456 | tf_op jit(solution)/shard_map/reduce_sum | solution.py:133
  55.8 4.2 %all-to-all-done.2 = f32[8,1,5376]{2,1,0:T(1,128)S(1)} async-done(((f32[8,1,5376]{2,1,0:T(1,128)}), f32[8,1,5376]{2,1,0:T(1,128)S(1)}, u32[]{:S(2)}, u32[]{:S(2)}) %all-to-all-start.2) | async-done | bytes 172064 | tf_op jit(solution)/shard_map/all_to_all | solution.py:117
  61.4 0.8 %collective-permute-start.6 = (f32[5376]{0:T(1024)S(1)}, f32[5376]{0:T(1024)S(1)}, u32[]{:S(2)}, u32[]{:S(2)}) collective-permute-start(f32[5376]{0:T(1024)S(1)} %constant_dynamic-update-slice_fusion.1), channel_id=1, source_target_pairs={{0,2},{1,3},{2,0},{3,1},{4,6},{5,7},{6,4},{7,5},{8,10},{9,11},{10,... | collective-permute-start | bytes 64520 | tf_op jit(solution)/shard_map/ppermute | solution.py:13
  62.2 1.3 %collective-permute-start.5 = (f32[5376]{0:T(1024)S(1)}, f32[5376]{0:T(1024)S(1)}, u32[]{:S(2)}, u32[]{:S(2)}) collective-permute-start(f32[5376]{0:T(1024)S(1)} %constant_dynamic-update-slice_fusion.1), channel_id=1, source_target_pairs={{0,1},{1,0},{2,3},{3,2},{4,5},{5,4},{6,7},{7,6},{8,9},{9,8},{10,11... | collective-permute-start | bytes 64520 | tf_op jit(solution)/shard_map/ppermute | solution.py:13
  63.6 1.7 %collective-permute-done.6 = f32[5376]{0:T(1024)S(1)} collective-permute-done((f32[5376]{0:T(1024)S(1)}, f32[5376]{0:T(1024)S(1)}, u32[]{:S(2)}, u32[]{:S(2)}) %collective-permute-start.6) | collective-permute-done | bytes 21536 | tf_op jit(solution)/shard_map/ppermute | solution.py:13
  67.1 0.6 broadcast_in_dim.304
  67.7 8.8 %all_to_all.37 = f32[8,1,1]{2,1,0:T(1,128)S(1)} all-to-all(f32[8,1,1]{2,1,0:T(1,128)S(1)} %broadcast_in_dim.304), channel_id=1, replica_groups=mesh['box'=8,'rep'=4] {'box'}, dimensions={0} | all-to-all | bytes 64 | tf_op jit(solution)/shard_map/all_to_all | solution.py:36
  (147 shorter events, 12.0 us)
Async XLA Ops:
  0.6 7.5 %copy-start = (bf16[20,4,64,64]{3,2,1,0:T(8,128)(2,1)S(1)}, bf16[20,4,64,64]{3,2,1,0:T(8,128)(2,1)}, u32[]{:S(2)}) copy-start(bf16[20,4,64,64]{3,2,1,0:T(8,128)(2,1)} %param.16) | copy-start | bytes 1966084
  0.6 5.9 %copy-start.4 = (s32[16,2]{0,1:T(2,128)S(1)}, s32[16,2]{0,1:T(2,128)}, u32[]{:S(2)}) copy-start(s32[16,2]{0,1:T(2,128)} %param.12) | copy-start | bytes 388
  0.7 6.5 %copy-start.1 = (bf16[16,64,256]{2,1,0:T(8,128)(2,1)S(1)}, bf16[16,64,256]{2,1,0:T(8,128)(2,1)}, u32[]{:S(2)}) copy-start(bf16[16,64,256]{2,1,0:T(8,128)(2,1)} %param.13) | copy-start | bytes 1572868
  0.7 6.8 %copy-start.6 = (bf16[16,64,64]{2,1,0:T(8,128)(2,1)S(1)}, bf16[16,64,64]{2,1,0:T(8,128)(2,1)}, u32[]{:S(2)}) copy-start(bf16[16,64,64]{2,1,0:T(8,128)(2,1)} %param.14) | copy-start | bytes 393220
  0.7 6.9 %copy-start.5 = (s32[16]{0:T(128)S(1)}, s32[16]{0:T(128)}, u32[]{:S(2)}) copy-start(s32[16]{0:T(128)} %param.15) | copy-start | bytes 196
  1.6 17.0 %collective-permute-start = (bf16[16,256]{1,0:T(8,128)(2,1)S(1)}, bf16[16,256]{1,0:T(8,128)(2,1)S(1)}, u32[]{:S(2)}, u32[]{:S(2)}) collective-permute-start(bf16[16,256]{1,0:T(8,128)(2,1)S(1)} %get-tuple-element.18), channel_id=1, source_target_pairs={{4,0},{8,4},{12,8},{16,12},{20,16},{24,20},{28,24},{5,1},{9,5},{13... | collective-permute-start | bytes 24584 | tf_op jit(solution)/shard_map/ppermute | solution.py:110
  9.8 16.0 %all-to-all-start = ((f32[8,1,5376]{2,1,0:T(1,128)}), f32[8,1,5376]{2,1,0:T(1,128)S(1)}, u32[]{:S(2)}, u32[]{:S(2)}) async-start(f32[8,1,5376]{2,1,0:T(1,128)} %all_to_all.24), calls=%async_computation | async-start | bytes 344064 | tf_op jit(solution)/shard_map/all_to_all | solution.py:117
  18.2 14.5 %copy-start.2 = (f32[16,256]{1,0:T(8,128)S(1)}, f32[16,256]{1,0:T(8,128)}, u32[]{:S(2)}) copy-start(f32[16,256]{1,0:T(8,128)} %param.9) | copy-start | bytes 49156
  18.2 14.5 %copy-start.3 = (f32[16,256]{1,0:T(8,128)S(1)}, f32[16,256]{1,0:T(8,128)}, u32[]{:S(2)}) copy-start(f32[16,256]{1,0:T(8,128)} %param.10) | copy-start | bytes 49156
  27.2 3.9 %collective-permute-start.2 = (f32[5376]{0:T(1024)S(1)}, f32[5376]{0:T(1024)S(1)}, u32[]{:S(2)}, u32[]{:S(2)}) collective-permute-start(f32[5376]{0:T(1024)S(1)} %constant_dynamic-update-slice_fusion), channel_id=1, source_target_pairs={{0,2},{1,3},{2,0},{3,1},{4,6},{5,7},{6,4},{7,5},{8,10},{9,11},{10,... | collective-permute-start | bytes 64520 | tf_op jit(solution)/shard_map/ppermute | solution.py:13
  28.7 3.3 %collective-permute-start.3 = (f32[5376]{0:T(1024)S(1)}, f32[5376]{0:T(1024)S(1)}, u32[]{:S(2)}, u32[]{:S(2)}) collective-permute-start(f32[5376]{0:T(1024)S(1)} %constant_dynamic-update-slice_fusion), channel_id=1, source_target_pairs={{0,3},{1,2},{2,1},{3,0},{4,7},{5,6},{6,5},{7,4},{8,11},{9,10},{10,... | collective-permute-start | bytes 64520 | tf_op jit(solution)/shard_map/ppermute | solution.py:13
  28.7 3.3 %collective-permute-start.1 = (f32[5376]{0:T(1024)S(1)}, f32[5376]{0:T(1024)S(1)}, u32[]{:S(2)}, u32[]{:S(2)}) collective-permute-start(f32[5376]{0:T(1024)S(1)} %constant_dynamic-update-slice_fusion), channel_id=1, source_target_pairs={{0,1},{1,0},{2,3},{3,2},{4,5},{5,4},{6,7},{7,6},{8,9},{9,8},{10,11... | collective-permute-start | bytes 64520 | tf_op jit(solution)/shard_map/ppermute | solution.py:13
  41.9 10.6 %collective-permute-start.4 = (bf16[16,256]{1,0:T(8,128)(2,1)S(1)}, bf16[16,256]{1,0:T(8,128)(2,1)S(1)}, u32[]{:S(2)}, u32[]{:S(2)}) collective-permute-start(bf16[16,256]{1,0:T(8,128)(2,1)S(1)} %get-tuple-element.5), channel_id=1, source_target_pairs={{4,0},{8,4},{12,8},{16,12},{20,16},{24,20},{28,24},{5,1},{9,5},{13... | collective-permute-start | bytes 24584 | tf_op jit(solution)/shard_map/ppermute | solution.py:110
  48.5 11.5 %all-to-all-start.2 = ((f32[8,1,5376]{2,1,0:T(1,128)}), f32[8,1,5376]{2,1,0:T(1,128)S(1)}, u32[]{:S(2)}, u32[]{:S(2)}) async-start(f32[8,1,5376]{2,1,0:T(1,128)} %copy.54), calls=%async_computation.2 | async-start | bytes 344064 | tf_op jit(solution)/shard_map/all_to_all | solution.py:117
  61.4 3.9 %collective-permute-start.6 = (f32[5376]{0:T(1024)S(1)}, f32[5376]{0:T(1024)S(1)}, u32[]{:S(2)}, u32[]{:S(2)}) collective-permute-start(f32[5376]{0:T(1024)S(1)} %constant_dynamic-update-slice_fusion.1), channel_id=1, source_target_pairs={{0,2},{1,3},{2,0},{3,1},{4,6},{5,7},{6,4},{7,5},{8,10},{9,11},{10,... | collective-permute-start | bytes 64520 | tf_op jit(solution)/shard_map/ppermute | solution.py:13
  62.2 3.5 %collective-permute-start.7 = (f32[5376]{0:T(1024)S(1)}, f32[5376]{0:T(1024)S(1)}, u32[]{:S(2)}, u32[]{:S(2)}) collective-permute-start(f32[5376]{0:T(1024)S(1)} %constant_dynamic-update-slice_fusion.1), channel_id=1, source_target_pairs={{0,3},{1,2},{2,1},{3,0},{4,7},{5,6},{6,5},{7,4},{8,11},{9,10},{10,... | collective-permute-start | bytes 64520 | tf_op jit(solution)/shard_map/ppermute | solution.py:13
  62.2 3.5 %collective-permute-start.5 = (f32[5376]{0:T(1024)S(1)}, f32[5376]{0:T(1024)S(1)}, u32[]{:S(2)}, u32[]{:S(2)}) collective-permute-start(f32[5376]{0:T(1024)S(1)} %constant_dynamic-update-slice_fusion.1), channel_id=1, source_target_pairs={{0,1},{1,0},{2,3},{3,2},{4,5},{5,4},{6,7},{7,6},{8,9},{9,8},{10,11... | collective-permute-start | bytes 64520 | tf_op jit(solution)/shard_map/ppermute | solution.py:13

commit v25 on v17

--- a/solution.py
+++ b/solution.py
@@ -146,8 +146,8 @@
         parent_pick = jnp.zeros((box_count, rank_width), jnp.bfloat16)
         for group in range(group_count):
             parent_pick = jnp.where((parent_local == group)[:, None], group_out[group][None], parent_pick)
-        from_parent = jnp.sum(
-            transfer.astype(jnp.float32) * parent_pick.astype(jnp.float32)[:, None, :], axis=2
+        from_parent = jnp.einsum(
+            "brq,bq->br", transfer, parent_pick, preferred_element_type=jnp.float32
         )
         downward = (far_total[:box_count] + from_parent).astype(jnp.bfloat16)
         far_field = jnp.sum(

time: 78.1 us -> 78.2 us (level)
  no operation moved by 1% of the time
where the time goes in v25:
time: 78.2 us; the launch traced here: 77.6 us
  starting transfers between devices  19.2 us (25%)
  blocking collectives  17.8 us (23%)
  waiting for transfers between devices  12.9 us (16%)
  other arithmetic  11.4 us (15%)
  matrix products  9.85 us (13%)
  local copies, waits for them, and re-layouts  5.11 us (7%)
  between operations  1.31 us (2%)
    all_to_all x2, blocking collectives, box_sum(): got = lax.all_to_all(sent, 'box', 0, 0, tiled=True)  17.8 us
    all_to_all x2, starting transfers between devices, local(): lax.all_to_all(jnp.concatenate([far_send.reshape(box_devices, far_size),...  12.3 us
    all_to_all x2, waiting for transfers between devices, local(): lax.all_to_all(jnp.concatenate([far_send.reshape(box_devices, far_size),...  8.12 us
    reduce_sum x2, other arithmetic, local(): forward = jnp.sum(near_tiles.astype(jnp.float32) * near_in, axis=(1, 3))  6.19 us
    dot_general x2, matrix products, local(): jnp.einsum('bsij,bi->bsj', near_tiles, rounded, preferred_element_type=jn...  5.66 us
    ppermute x6, waiting for transfers between devices, rep_sum(): lax.ppermute(vector, 'rep', [(i, i ^ mask) for i in range(count)])  4.77 us
    ppermute x6, starting transfers between devices, rep_sum(): lax.ppermute(vector, 'rep', [(i, i ^ mask) for i in range(count)])  4.35 us
    ppermute x2, starting transfers between devices, local(): lax.ppermute(rounded, 'box', [(i, i - 1) for i in range(1, box_devices)])  2.57 us
  transfers between devices with their start and end apart: 10, of which 6 were waited for; matrix products, arithmetic and copies ran while one was open for 23% of the time, Pallas kernels for 0%

profile of v25, /device:TPU:0, one launch (start us, length us, event | category | flops | bytes accessed | tf_op | source)
XLA Modules:
  0.0 77.6 jit_solution(14864545647530613919)
XLA Ops:
  0.7 0.9 %fusion.97 = (f32[16,256]{1,0:T(8,128)S(1)}, bf16[16,256]{1,0:T(8,128)(2,1)S(1)}) fusion(f32[16,256]{1,0:T(8,128)} %param.9), kind=kLoop, calls=%fused_computation.173 | loop fusion | flops 8192 | bytes 40960 | tf_op jit(solution)/shard_map/convert_element_type | solution.py:95
  1.6 1.3 %collective-permute-start = (bf16[16,256]{1,0:T(8,128)(2,1)S(1)}, bf16[16,256]{1,0:T(8,128)(2,1)S(1)}, u32[]{:S(2)}, u32[]{:S(2)}) collective-permute-start(bf16[16,256]{1,0:T(8,128)(2,1)S(1)} %get-tuple-element.18), channel_id=1, source_target_pairs={{4,0},{8,4},{12,8},{16,12},{20,16},{24,20},{28,24},{5,1},{9,5},{13... | collective-permute-start | bytes 24584 | tf_op jit(solution)/shard_map/ppermute | solution.py:110
  2.9 0.7 broadcast_select_fusion.4
  3.7 2.8 %fusion.47 = f32[16,1,2,256]{3,1,2,0:T(1,128)S(1)} fusion(bf16[16,2,256,256]{3,2,1,0:T(8,128)(2,1)} %param.11, bf16[16,256,1,1]{1,0,2,3:T(8,128)(2,1)S(1)} %bitcast.113), kind=kOutput, calls=%fused_computation.82 | convolution fusion | flops 4194304 | bytes 4235264 | tf_op jit(solution)/shard_map/bsij,bi->bsj/dot_general | solution.py:88
  9.0 0.8 %all_to_all.24 = f32[8,1,5376]{2,1,0:T(1,128)} reshape(f32[8,5376]{1,0:T(8,128)S(1)} %pad_maximum_fusion) | data formatting | bytes 344064 | tf_op jit(solution)/shard_map/all_to_all | solution.py:117
  9.8 8.4 %all-to-all-start = ((f32[8,1,5376]{2,1,0:T(1,128)}), f32[8,1,5376]{2,1,0:T(1,128)S(1)}, u32[]{:S(2)}, u32[]{:S(2)}) async-start(f32[8,1,5376]{2,1,0:T(1,128)} %all_to_all.24), calls=%async_computation | async-start | bytes 344064 | tf_op jit(solution)/shard_map/all_to_all | solution.py:117
  18.8 3.1 %fusion = f32[16,256]{1,0:T(8,128)S(1)} fusion(bf16[16,2,256,256]{3,2,1,0:T(8,128)(2,1)} %param.11, f32[16,2,256]{2,1,0:T(2,128)S(1)} %mul.150), kind=kLoop, calls=%fused_computation.2 | loop fusion | flops 6287360 | bytes 4243456 | tf_op jit(solution)/shard_map/reduce_sum | solution.py:133
  21.9 3.9 %all-to-all-done = f32[8,1,5376]{2,1,0:T(1,128)S(1)} async-done(((f32[8,1,5376]{2,1,0:T(1,128)}), f32[8,1,5376]{2,1,0:T(1,128)S(1)}, u32[]{:S(2)}, u32[]{:S(2)}) %all-to-all-start) | async-done | bytes 172064 | tf_op jit(solution)/shard_map/all_to_all | solution.py:117
  27.2 1.5 %collective-permute-start.2 = (f32[5376]{0:T(1024)S(1)}, f32[5376]{0:T(1024)S(1)}, u32[]{:S(2)}, u32[]{:S(2)}) collective-permute-start(f32[5376]{0:T(1024)S(1)} %constant_dynamic-update-slice_fusion), channel_id=1, source_target_pairs={{0,2},{1,3},{2,0},{3,1},{4,6},{5,7},{6,4},{7,5},{8,10},{9,11},{10,... | collective-permute-start | bytes 64520 | tf_op jit(solution)/shard_map/ppermute | solution.py:13
  28.7 0.6 collective-permute-start.1
  29.3 1.7 %collective-permute-done.2 = f32[5376]{0:T(1024)S(1)} collective-permute-done((f32[5376]{0:T(1024)S(1)}, f32[5376]{0:T(1024)S(1)}, u32[]{:S(2)}, u32[]{:S(2)}) %collective-permute-start.2) | collective-permute-done | bytes 21536 | tf_op jit(solution)/shard_map/ppermute | solution.py:13
  31.0 0.9 %collective-permute-done.3 = f32[5376]{0:T(1024)S(1)} collective-permute-done((f32[5376]{0:T(1024)S(1)}, f32[5376]{0:T(1024)S(1)}, u32[]{:S(2)}, u32[]{:S(2)}) %collective-permute-start.3) | collective-permute-done | bytes 21536 | tf_op jit(solution)/shard_map/ppermute | solution.py:13
  32.9 8.9 %all_to_all.36 = f32[8,1,4]{2,1,0:T(1,128)S(1)} all-to-all(f32[8,1,4]{2,1,0:T(1,128)S(1)} %broadcast_in_dim.300), channel_id=1, replica_groups=mesh['box'=8,'rep'=4] {'box'}, dimensions={0} | all-to-all | bytes 256 | tf_op jit(solution)/shard_map/all_to_all | solution.py:36
  41.9 1.3 %collective-permute-start.4 = (bf16[16,256]{1,0:T(8,128)(2,1)S(1)}, bf16[16,256]{1,0:T(8,128)(2,1)S(1)}, u32[]{:S(2)}, u32[]{:S(2)}) collective-permute-start(bf16[16,256]{1,0:T(8,128)(2,1)S(1)} %get-tuple-element.5), channel_id=1, source_target_pairs={{4,0},{8,4},{12,8},{16,12},{20,16},{24,20},{28,24},{5,1},{9,5},{13... | collective-permute-start | bytes 24584 | tf_op jit(solution)/shard_map/ppermute | solution.py:110
  43.2 2.8 %fusion.45 = f32[16,1,2,256]{3,1,2,0:T(1,128)S(1)} fusion(bf16[16,2,256,256]{3,2,1,0:T(8,128)(2,1)} %param.11, bf16[16,256,1,1]{1,0,2,3:T(8,128)(2,1)S(1)} %bitcast.114), kind=kOutput, calls=%fused_computation.80 | convolution fusion | flops 4194304 | bytes 4235264 | tf_op jit(solution)/shard_map/bsij,bi->bsj/dot_general | solution.py:88
  47.7 0.8 %copy.49 = f32[8,1,5376]{2,1,0:T(1,128)} copy(f32[8,1,5376]{2,0,1:T(8,128)S(1)} %maximum_bitcast_fusion) | data formatting | bytes 344064 | tf_op jit(solution)/shard_map/all_to_all | solution.py:117
  48.5 3.9 %all-to-all-start.2 = ((f32[8,1,5376]{2,1,0:T(1,128)}), f32[8,1,5376]{2,1,0:T(1,128)S(1)}, u32[]{:S(2)}, u32[]{:S(2)}) async-start(f32[8,1,5376]{2,1,0:T(1,128)} %copy.49), calls=%async_computation.2 | async-start | bytes 344064 | tf_op jit(solution)/shard_map/all_to_all | solution.py:117
  52.7 3.1 %fusion.1 = f32[16,256]{1,0:T(8,128)S(1)} fusion(bf16[16,2,256,256]{3,2,1,0:T(8,128)(2,1)} %param.11, f32[16,2,256]{2,1,0:T(2,128)S(1)} %mul.176), kind=kLoop, calls=%fused_computation.3 | loop fusion | flops 6287360 | bytes 4243456 | tf_op jit(solution)/shard_map/reduce_sum | solution.py:133
  55.8 4.2 %all-to-all-done.2 = f32[8,1,5376]{2,1,0:T(1,128)S(1)} async-done(((f32[8,1,5376]{2,1,0:T(1,128)}), f32[8,1,5376]{2,1,0:T(1,128)S(1)}, u32[]{:S(2)}, u32[]{:S(2)}) %all-to-all-start.2) | async-done | bytes 172064 | tf_op jit(solution)/shard_map/all_to_all | solution.py:117
  61.4 0.8 %collective-permute-start.6 = (f32[5376]{0:T(1024)S(1)}, f32[5376]{0:T(1024)S(1)}, u32[]{:S(2)}, u32[]{:S(2)}) collective-permute-start(f32[5376]{0:T(1024)S(1)} %constant_dynamic-update-slice_fusion.1), channel_id=1, source_target_pairs={{0,2},{1,3},{2,0},{3,1},{4,6},{5,7},{6,4},{7,5},{8,10},{9,11},{10,... | collective-permute-start | bytes 64520 | tf_op jit(solution)/shard_map/ppermute | solution.py:13
  62.3 1.3 %collective-permute-start.5 = (f32[5376]{0:T(1024)S(1)}, f32[5376]{0:T(1024)S(1)}, u32[]{:S(2)}, u32[]{:S(2)}) collective-permute-start(f32[5376]{0:T(1024)S(1)} %constant_dynamic-update-slice_fusion.1), channel_id=1, source_target_pairs={{0,1},{1,0},{2,3},{3,2},{4,5},{5,4},{6,7},{7,6},{8,9},{9,8},{10,11... | collective-permute-start | bytes 64520 | tf_op jit(solution)/shard_map/ppermute | solution.py:13
  63.6 1.7 %collective-permute-done.6 = f32[5376]{0:T(1024)S(1)} collective-permute-done((f32[5376]{0:T(1024)S(1)}, f32[5376]{0:T(1024)S(1)}, u32[]{:S(2)}, u32[]{:S(2)}) %collective-permute-start.6) | collective-permute-done | bytes 21536 | tf_op jit(solution)/shard_map/ppermute | solution.py:13
  67.2 0.6 broadcast_in_dim.311
  67.8 8.8 %all_to_all.37 = f32[8,1,1]{2,1,0:T(1,128)S(1)} all-to-all(f32[8,1,1]{2,1,0:T(1,128)S(1)} %broadcast_in_dim.311), channel_id=1, replica_groups=mesh['box'=8,'rep'=4] {'box'}, dimensions={0} | all-to-all | bytes 64 | tf_op jit(solution)/shard_map/all_to_all | solution.py:36
  (148 shorter events, 11.1 us)
Async XLA Ops:
  0.6 7.5 %copy-start = (bf16[20,4,64,64]{3,2,1,0:T(8,128)(2,1)S(1)}, bf16[20,4,64,64]{3,2,1,0:T(8,128)(2,1)}, u32[]{:S(2)}) copy-start(bf16[20,4,64,64]{3,2,1,0:T(8,128)(2,1)} %param.16) | copy-start | bytes 1966084
  0.6 5.9 %copy-start.4 = (s32[16,2]{0,1:T(2,128)S(1)}, s32[16,2]{0,1:T(2,128)}, u32[]{:S(2)}) copy-start(s32[16,2]{0,1:T(2,128)} %param.12) | copy-start | bytes 388
  0.7 6.5 %copy-start.1 = (bf16[16,64,256]{2,1,0:T(8,128)(2,1)S(1)}, bf16[16,64,256]{2,1,0:T(8,128)(2,1)}, u32[]{:S(2)}) copy-start(bf16[16,64,256]{2,1,0:T(8,128)(2,1)} %param.13) | copy-start | bytes 1572868
  0.7 6.8 %copy-start.6 = (bf16[16,64,64]{2,1,0:T(8,128)(2,1)S(1)}, bf16[16,64,64]{2,1,0:T(8,128)(2,1)}, u32[]{:S(2)}) copy-start(bf16[16,64,64]{2,1,0:T(8,128)(2,1)} %param.14) | copy-start | bytes 393220
  0.7 6.9 %copy-start.5 = (s32[16]{0:T(128)S(1)}, s32[16]{0:T(128)}, u32[]{:S(2)}) copy-start(s32[16]{0:T(128)} %param.15) | copy-start | bytes 196
  1.6 17.0 %collective-permute-start = (bf16[16,256]{1,0:T(8,128)(2,1)S(1)}, bf16[16,256]{1,0:T(8,128)(2,1)S(1)}, u32[]{:S(2)}, u32[]{:S(2)}) collective-permute-start(bf16[16,256]{1,0:T(8,128)(2,1)S(1)} %get-tuple-element.18), channel_id=1, source_target_pairs={{4,0},{8,4},{12,8},{16,12},{20,16},{24,20},{28,24},{5,1},{9,5},{13... | collective-permute-start | bytes 24584 | tf_op jit(solution)/shard_map/ppermute | solution.py:110
  9.8 16.0 %all-to-all-start = ((f32[8,1,5376]{2,1,0:T(1,128)}), f32[8,1,5376]{2,1,0:T(1,128)S(1)}, u32[]{:S(2)}, u32[]{:S(2)}) async-start(f32[8,1,5376]{2,1,0:T(1,128)} %all_to_all.24), calls=%async_computation | async-start | bytes 344064 | tf_op jit(solution)/shard_map/all_to_all | solution.py:117
  18.2 14.5 %copy-start.2 = (f32[16,256]{1,0:T(8,128)S(1)}, f32[16,256]{1,0:T(8,128)}, u32[]{:S(2)}) copy-start(f32[16,256]{1,0:T(8,128)} %param.9) | copy-start | bytes 49156
  18.2 14.6 %copy-start.3 = (f32[16,256]{1,0:T(8,128)S(1)}, f32[16,256]{1,0:T(8,128)}, u32[]{:S(2)}) copy-start(f32[16,256]{1,0:T(8,128)} %param.10) | copy-start | bytes 49156
  27.2 3.9 %collective-permute-start.2 = (f32[5376]{0:T(1024)S(1)}, f32[5376]{0:T(1024)S(1)}, u32[]{:S(2)}, u32[]{:S(2)}) collective-permute-start(f32[5376]{0:T(1024)S(1)} %constant_dynamic-update-slice_fusion), channel_id=1, source_target_pairs={{0,2},{1,3},{2,0},{3,1},{4,6},{5,7},{6,4},{7,5},{8,10},{9,11},{10,... | collective-permute-start | bytes 64520 | tf_op jit(solution)/shard_map/ppermute | solution.py:13
  28.7 3.3 %collective-permute-start.3 = (f32[5376]{0:T(1024)S(1)}, f32[5376]{0:T(1024)S(1)}, u32[]{:S(2)}, u32[]{:S(2)}) collective-permute-start(f32[5376]{0:T(1024)S(1)} %constant_dynamic-update-slice_fusion), channel_id=1, source_target_pairs={{0,3},{1,2},{2,1},{3,0},{4,7},{5,6},{6,5},{7,4},{8,11},{9,10},{10,... | collective-permute-start | bytes 64520 | tf_op jit(solution)/shard_map/ppermute | solution.py:13
  28.7 3.3 %collective-permute-start.1 = (f32[5376]{0:T(1024)S(1)}, f32[5376]{0:T(1024)S(1)}, u32[]{:S(2)}, u32[]{:S(2)}) collective-permute-start(f32[5376]{0:T(1024)S(1)} %constant_dynamic-update-slice_fusion), channel_id=1, source_target_pairs={{0,1},{1,0},{2,3},{3,2},{4,5},{5,4},{6,7},{7,6},{8,9},{9,8},{10,11... | collective-permute-start | bytes 64520 | tf_op jit(solution)/shard_map/ppermute | solution.py:13
  41.9 10.5 %collective-permute-start.4 = (bf16[16,256]{1,0:T(8,128)(2,1)S(1)}, bf16[16,256]{1,0:T(8,128)(2,1)S(1)}, u32[]{:S(2)}, u32[]{:S(2)}) collective-permute-start(bf16[16,256]{1,0:T(8,128)(2,1)S(1)} %get-tuple-element.5), channel_id=1, source_target_pairs={{4,0},{8,4},{12,8},{16,12},{20,16},{24,20},{28,24},{5,1},{9,5},{13... | collective-permute-start | bytes 24584 | tf_op jit(solution)/shard_map/ppermute | solution.py:110
  48.5 11.5 %all-to-all-start.2 = ((f32[8,1,5376]{2,1,0:T(1,128)}), f32[8,1,5376]{2,1,0:T(1,128)S(1)}, u32[]{:S(2)}, u32[]{:S(2)}) async-start(f32[8,1,5376]{2,1,0:T(1,128)} %copy.49), calls=%async_computation.2 | async-start | bytes 344064 | tf_op jit(solution)/shard_map/all_to_all | solution.py:117
  61.4 3.9 %collective-permute-start.6 = (f32[5376]{0:T(1024)S(1)}, f32[5376]{0:T(1024)S(1)}, u32[]{:S(2)}, u32[]{:S(2)}) collective-permute-start(f32[5376]{0:T(1024)S(1)} %constant_dynamic-update-slice_fusion.1), channel_id=1, source_target_pairs={{0,2},{1,3},{2,0},{3,1},{4,6},{5,7},{6,4},{7,5},{8,10},{9,11},{10,... | collective-permute-start | bytes 64520 | tf_op jit(solution)/shard_map/ppermute | solution.py:13
  62.3 3.5 %collective-permute-start.7 = (f32[5376]{0:T(1024)S(1)}, f32[5376]{0:T(1024)S(1)}, u32[]{:S(2)}, u32[]{:S(2)}) collective-permute-start(f32[5376]{0:T(1024)S(1)} %constant_dynamic-update-slice_fusion.1), channel_id=1, source_target_pairs={{0,3},{1,2},{2,1},{3,0},{4,7},{5,6},{6,5},{7,4},{8,11},{9,10},{10,... | collective-permute-start | bytes 64520 | tf_op jit(solution)/shard_map/ppermute | solution.py:13
  62.3 3.5 %collective-permute-start.5 = (f32[5376]{0:T(1024)S(1)}, f32[5376]{0:T(1024)S(1)}, u32[]{:S(2)}, u32[]{:S(2)}) collective-permute-start(f32[5376]{0:T(1024)S(1)} %constant_dynamic-update-slice_fusion.1), channel_id=1, source_target_pairs={{0,1},{1,0},{2,3},{3,2},{4,5},{5,4},{6,7},{7,6},{8,9},{9,8},{10,11... | collective-permute-start | bytes 64520 | tf_op jit(solution)/shard_map/ppermute | solution.py:13
